TPU v7x, 256 devices: a whole 4x4x8 slice. The times are simulated.
256 devices in a mesh: wide: 64 (over y_lo, z, x), narrow: 4 (over y_hi, core).
Axes of the slice: x: 4, y: 4 (y_hi: 2, y_lo: 2; y = y_hi * 2 + y_lo), z: 8, core: 2. Of those that a mesh axis runs over, the one named last changes fastest.
Arguments:
- concentration: float32 [3, 512, 256, 128], P(None, 'wide', 'narrow'), may hold values from 0.5 to 2
- potential: float32 [512, 256, 128], P('wide', 'narrow'), may hold values from -6 to 6
- permittivity: float32 [512, 256, 128], P('wide', 'narrow'), may hold values from 1 to 10
- diffusivity: float32 [3], replicated, may hold values from 0.02 to 0.1
- valence: int32 [3], replicated, may hold values from -2 to 2
- charge_pos: float32 [3, 524288], P(None, ('wide', 'narrow')), may hold values from 0 to 1
- charge_q: float32 [1, 524288], P(None, ('wide', 'narrow')), may hold values from -64 to 64
- charge_tile: int32 [1, 524288], P(None, ('wide', 'narrow')), may hold values from 0 to 15
- near_index: int32 [64, 4, 512], P('wide', 'narrow'), may hold values from 0 to 65535
- brick_mask: int32 [64, 4], P('wide', 'narrow'), may hold values 0 or 1
Outputs:
- species_out: float32 [3, 512, 256, 128], P(None, 'wide', 'narrow')
- potential_out: float32 [512, 256, 128], P('wide', 'narrow')
Inputs may be any that keep to these rules, and one draw needn't show every extreme that they name: `near_index`: an index of a node of the brick. `charge_tile`: a tile of the whole y range.
All inputs are finite; a program needn't handle non-finite values. No bound on the sum of `brick_mask` on one device may be relied on, other than what follows from the above.
Results may differ from a plain program's by a relative error of at most 0.0003.
Values sent between devices are 32-bit elements; how exact they have to be, the bound alone decides.
No kernel may reach another device: no remote copies, remote signals or barrier semaphores. Data moves between devices by JAX's collectives and lax.ppermute only.
A program may use at most 64 MiB of HBM per device.

v0:
```python
import jax
import jax.numpy as jnp
from jax import lax
from jax.sharding import PartitionSpec as P

TILES_DEV = 4
STEPS = 2
SWEEPS = 6


def with_halo(cells, sides, width):
    for axis, dim in sides:
        count = lax.axis_size(axis)
        head = lax.slice_in_dim(cells, 0, width, axis=dim)
        tail = lax.slice_in_dim(cells, cells.shape[dim] - width, cells.shape[dim], axis=dim)
        cells = jnp.concatenate(
            [
                lax.ppermute(tail, axis, [(i, (i + 1) % count) for i in range(count)]),
                cells,
                lax.ppermute(head, axis, [((i + 1) % count, i) for i in range(count)]),
            ],
            axis=dim,
        )
    return cells


def relax(field_pad, perm_pad, source):
    centre = field_pad[1:-1, 1:-1]
    perm_centre = perm_pad[1:-1, 1:-1]
    numer = source
    denom = jnp.zeros_like(source)
    pairs = (
        (field_pad[2:, 1:-1], perm_pad[2:, 1:-1]),
        (field_pad[:-2, 1:-1], perm_pad[:-2, 1:-1]),
        (field_pad[1:-1, 2:], perm_pad[1:-1, 2:]),
        (field_pad[1:-1, :-2], perm_pad[1:-1, :-2]),
    )
    for other_field, other_perm in pairs:
        weight = 0.5 * (perm_centre + other_perm)
        numer = numer + weight * other_field
        denom = denom + weight
    zeros_edge = jnp.zeros_like(centre[..., :1])
    upper_field = jnp.concatenate([centre[..., 1:], zeros_edge], axis=-1)
    lower_field = jnp.concatenate([zeros_edge, centre[..., :-1]], axis=-1)
    upper_perm = jnp.concatenate([perm_centre[..., 1:], perm_centre[..., -1:]], axis=-1)
    lower_perm = jnp.concatenate([perm_centre[..., :1], perm_centre[..., :-1]], axis=-1)
    for other_field, other_perm in ((upper_field, upper_perm), (lower_field, lower_perm)):
        weight = 0.5 * (perm_centre + other_perm)
        numer = numer + weight * other_field
        denom = denom + weight
    return numer / denom


def transport(species_pad, field_pad, diffusivity, charge_num):
    centre = species_pad[:, 1:-1, 1:-1]
    field_centre = field_pad[1:-1, 1:-1]
    drift = charge_num[:, None, None, None]
    total = jnp.zeros_like(centre)
    pairs = (
        (species_pad[:, 2:, 1:-1], field_pad[2:, 1:-1]),
        (species_pad[:, :-2, 1:-1], field_pad[:-2, 1:-1]),
        (species_pad[:, 1:-1, 2:], field_pad[1:-1, 2:]),
        (species_pad[:, 1:-1, :-2], field_pad[1:-1, :-2]),
    )
    for other, other_field in pairs:
        total = (
            total + (centre - other) - drift * 0.5 * (centre + other) * (other_field - field_centre)
        )
    left = centre[..., :-1]
    right = centre[..., 1:]
    across = (
        left
        - right
        - drift * 0.5 * (left + right) * (field_centre[..., 1:] - field_centre[..., :-1])
    )
    zeros_edge = jnp.zeros_like(centre[..., :1])
    total = total + jnp.concatenate([across, zeros_edge], axis=-1)
    total = total - jnp.concatenate([zeros_edge, across], axis=-1)
    return centre - diffusivity[:, None, None, None] * total


def pair_field(
    node_z,
    node_y,
    node_x,
    node_tile,
    block,
    slab_float,
    depth,
    rows_total,
    width,
    tile_rows,
    tiles_all,
):
    charge_x = block[0] * width
    charge_y = (block[4] + block[1]) * tile_rows
    charge_z = (slab_float + block[2]) * depth
    strength = block[3]
    label = block[4]

    def one_block(nodes):
        pos_z, pos_y, pos_x, pos_tile = nodes
        offset_z = pos_z[:, None] - charge_z[None, :]
        offset_y = pos_y[:, None] - charge_y[None, :]
        offset_y = offset_y - rows_total * jnp.floor(offset_y / rows_total + 0.5)
        offset_x = pos_x[:, None] - charge_x[None, :]
        distance = jnp.sqrt(offset_z * offset_z + offset_y * offset_y + offset_x * offset_x)
        tile_gap = jnp.mod(pos_tile[:, None] - label[None, :], tiles_all)
        adjacent = (tile_gap == 0.0) | (tile_gap == 1.0) | (tile_gap == tiles_all - 1.0)
        term = (
            strength[None, :] * jnp.exp(-distance / tile_rows) / jnp.sqrt(distance * distance + 1.0)
        )
        return jnp.sum(jnp.where(adjacent, term, 0.0), axis=1)

    shaped = tuple((arr.reshape(-1, 128) for arr in (node_z, node_y, node_x, node_tile)))
    return lax.map(one_block, shaped).reshape(-1)


def per_device(
    concentration,
    potential,
    permittivity,
    diffusivity,
    valence,
    charge_pos,
    charge_q,
    charge_tile,
    near_index,
    brick_mask,
):
    depth, height, width = potential.shape
    bands = lax.axis_size("narrow")
    rows_total = float(height * bands)
    tiles_all = float(TILES_DEV * bands)
    tile_rows = height // TILES_DEV
    slab = lax.axis_index("wide")
    band = lax.axis_index("narrow")
    index = near_index[0, 0]
    local_z = index // (height * width)
    local_y = index // width % height
    local_x = index % width
    global_z = slab * depth + local_z
    global_y = band * height + local_y
    node_z = global_z.astype(jnp.float32)
    node_y = global_y.astype(jnp.float32)
    node_x = local_x.astype(jnp.float32)
    node_tile = (global_y // tile_rows).astype(jnp.float32)
    slab_float = slab.astype(jnp.float32)
    charges = jnp.concatenate([charge_pos, charge_q, charge_tile.astype(jnp.float32)], axis=0)
    values = pair_field(
        node_z,
        node_y,
        node_x,
        node_tile,
        lax.all_gather(charges, "narrow", axis=1, tiled=True),
        slab_float,
        depth,
        rows_total,
        width,
        float(tile_rows),
        tiles_all,
    )
    values = values * brick_mask[0, 0].astype(jnp.float32)
    electrode = jnp.zeros((depth * height * width,), jnp.float32).at[index].add(values)
    electrode = electrode.reshape(depth, height, width)
    charge_num = valence.astype(jnp.float32)
    perm_pad = with_halo(permittivity, (("wide", 0), ("narrow", 1)), 1)
    field = potential
    species = concentration
    for step in range(STEPS):
        source = jnp.sum(charge_num[:, None, None, None] * species, axis=0) + electrode

        def single(turn, current):
            padded = with_halo(current, (("wide", 0), ("narrow", 1)), 1)
            return relax(padded, perm_pad, source)

        field = lax.fori_loop(0, SWEEPS, single, field)
        field_pad = with_halo(field, (("wide", 0), ("narrow", 1)), 1)
        species_pad = with_halo(species, (("wide", 1), ("narrow", 2)), 1)
        species = transport(species_pad, field_pad, diffusivity, charge_num)
    return (species, field)


def solution(mesh):
    in_specs = (
        P(None, "wide", "narrow", None),
        P("wide", "narrow", None),
        P("wide", "narrow", None),
        P(),
        P(),
        P(None, ("wide", "narrow")),
        P(None, ("wide", "narrow")),
        P(None, ("wide", "narrow")),
        P("wide", "narrow", None),
        P("wide", "narrow"),
    )
    out_specs = (P(None, "wide", "narrow", None), P("wide", "narrow", None))
    return jax.shard_map(
        per_device, mesh=mesh, in_specs=in_specs, out_specs=out_specs, check_vma=False
    )
```

profile of v0, /device:TPU:1, one launch (start us, length us, event | category | flops | bytes accessed | tf_op | source)
XLA Modules:
  0.0 287.6 jit_solution(8321827700418992691)
XLA Ops:
  1.5 2.0 collective-permute-start.10
  3.5 7.7 %collective-permute-start.9 = (f32[1,64,128]{2,1,0:T(8,128)S(1)}, f32[1,64,128]{2,1,0:T(8,128)S(1)}, u32[]{:S(2)}, u32[]{:S(2)}) collective-permute-start(f32[1,64,128]{2,1,0:T(8,128)S(1)} %get-tuple-element.365), channel_id=1, source_target_pairs={{4,0},{8,4},{12,8},{16,12},{20,16},{24,20},{28,24},{32,28},{36,32}... | collective-permute-start | bytes 98312 | tf_op jit(solution)/shard_map/ppermute | solution.py:20
  11.2 1.6 fusion.123
  16.1 9.7 %all_gather.3 = f32[5,8192]{1,0:T(8,128)S(1)} all-gather(f32[5,2048]{1,0:T(8,128)S(1)} %pad_maximum_fusion.32), channel_id=1, replica_groups=mesh['wide'=64,'narrow'=4] {'narrow'}, dimensions={1}, use_global_device_ids=true | all-gather | bytes 204800 | tf_op jit(solution)/shard_map/all_gather | solution.py:155
  25.9 28.1 %while.34 = (s32[]{:T(128)}, f32[4,128]{1,0:T(4,128)S(1)}, f32[4,128]{1,0:T(4,128)S(1)}, f32[1,8192]{1,0:T(1,128)S(1)}, f32[1,8192]{1,0:T(1,128)S(1)}, /*index=5...) while((s32[]{:T(128)}, f32[4,128]{1,0:T(4,128)S(1)}, ...), condition=%wide.region_3.4_spmd, body=%wide.region_1.3_spmd.sunk | while | flops 34602880 | bytes 171665 | solution.py:116
  26.0 6.9 %select_reduce_fusion.2 = f32[128]{0:T(128)S(1)} fusion(f32[8192]{0:T(1024)S(1)} %get-tuple-element.618, f32[128]{0:T(128)S(1)} %get-tuple-element.548, f32[8192]{0:T(1024)S(1)} %get-tuple-element.616, f32[128]{0:T(128)S(1)} %get-tuple-element.549, f32[8192]{0:T(1024)S(1)} %get-tuple-element.614, f32[128]{0:T(128)S(1)} %get-tuple-element.550, ...), kind=kLoop, calls=%fused_computation.11.clone.1 | loop fusion | flops 34602880 | bytes 166400 | tf_op jit(solution)/shard_map/while/body/eval_jaxpr/reduce_sum | solution.py:113
  33.0 6.9 %select_reduce_fusion.2 = f32[128]{0:T(128)S(1)} fusion(f32[8192]{0:T(1024)S(1)} %get-tuple-element.618, f32[128]{0:T(128)S(1)} %get-tuple-element.548, f32[8192]{0:T(1024)S(1)} %get-tuple-element.616, f32[128]{0:T(128)S(1)} %get-tuple-element.549, f32[8192]{0:T(1024)S(1)} %get-tuple-element.614, f32[128]{0:T(128)S(1)} %get-tuple-element.550, ...), kind=kLoop, calls=%fused_computation.11.clone.1 | loop fusion | flops 34602880 | bytes 166400 | tf_op jit(solution)/shard_map/while/body/eval_jaxpr/reduce_sum | solution.py:113
  40.0 6.9 %select_reduce_fusion.2 = f32[128]{0:T(128)S(1)} fusion(f32[8192]{0:T(1024)S(1)} %get-tuple-element.618, f32[128]{0:T(128)S(1)} %get-tuple-element.548, f32[8192]{0:T(1024)S(1)} %get-tuple-element.616, f32[128]{0:T(128)S(1)} %get-tuple-element.549, f32[8192]{0:T(1024)S(1)} %get-tuple-element.614, f32[128]{0:T(128)S(1)} %get-tuple-element.550, ...), kind=kLoop, calls=%fused_computation.11.clone.1 | loop fusion | flops 34602880 | bytes 166400 | tf_op jit(solution)/shard_map/while/body/eval_jaxpr/reduce_sum | solution.py:113
  47.0 6.9 %select_reduce_fusion.2 = f32[128]{0:T(128)S(1)} fusion(f32[8192]{0:T(1024)S(1)} %get-tuple-element.618, f32[128]{0:T(128)S(1)} %get-tuple-element.548, f32[8192]{0:T(1024)S(1)} %get-tuple-element.616, f32[128]{0:T(128)S(1)} %get-tuple-element.549, f32[8192]{0:T(1024)S(1)} %get-tuple-element.614, f32[128]{0:T(128)S(1)} %get-tuple-element.550, ...), kind=kLoop, calls=%fused_computation.11.clone.1 | loop fusion | flops 34602880 | bytes 166400 | tf_op jit(solution)/shard_map/while/body/eval_jaxpr/reduce_sum | solution.py:113
  54.1 2.2 collective-permute-start.12
  56.3 3.5 %scatter_custom_fusion = f32[65536]{0:T(1024)S(1)} fusion(s32[512]{0:T(512)S(1)} %bitcast.41, f32[512]{0:T(512)S(1)} %multiply_bitcast_fusion, f32[]{:T(128)} %constant.138.clone.1), kind=kCustom, calls=%fused_computation.155 | custom fusion | flops 512 | bytes 262148 | tf_op jit(solution)/shard_map/scatter-add | solution.py:164
  61.4 1.5 fusion.95
  64.7 89.1 %while.35 = (s32[]{:T(128)}, f32[8,64,128]{2,1,0:T(8,128)S(1)}, f32[8,64,128]{2,1,0:T(8,128)S(1)}, f32[8,64,128]{2,1,0:T(8,128)}, f32[8,64,128]{2,1,0:T(8,128)S(...) while((s32[]{:T(128)}, f32[8,64,128]{2,1,0:T(8,128)S(1)}, ...), condition=%wide.region_6.7_spmd, body=%wide.region_5.6_spmd.sunk | while | flops 1835010 | bytes 7268641 | solution.py:177
  64.8 5.7 %collective-permute-start.1 = (f32[1,64,128]{2,1,0:T(8,128)S(1)}, f32[1,64,128]{2,1,0:T(8,128)S(1)}, u32[]{:S(2)}, u32[]{:S(2)}) collective-permute-start(f32[1,64,128]{2,1,0:T(8,128)S(1)} %get-tuple-element.562), channel_id=1, source_target_pairs={{4,0},{8,4},{12,8},{16,12},{20,16},{24,20},{28,24},{32,28},{36,32}... | collective-permute-start | bytes 98312 | tf_op jit(solution)/shard_map/while/body/eval_jaxpr/ppermute | solution.py:20
  71.9 3.5 %collective-permute-start.2 = (f32[10,1,128]{2,1,0:T(1,128)S(1)}, f32[10,1,128]{2,1,0:T(1,128)S(1)}, u32[]{:S(2)}, u32[]{:S(2)}) collective-permute-start(f32[10,1,128]{2,1,0:T(1,128)S(1)} %get-tuple-element.563), channel_id=1, source_target_pairs={{0,1},{1,2},{2,3},{3,0},{4,5},{5,6},{6,7},{7,4},{8,9},{9,10},{10,1... | collective-permute-start | bytes 15368 | tf_op jit(solution)/shard_map/while/body/eval_jaxpr/ppermute | solution.py:18
  76.2 3.8 %collective-permute-done.3 = f32[10,1,128]{2,1,0:T(1,128)S(1)} collective-permute-done((f32[10,1,128]{2,1,0:T(1,128)S(1)}, f32[10,1,128]{2,1,0:T(1,128)S(1)}, u32[]{:S(2)}, u32[]{:S(2)}) %collective-permute-start.3) | collective-permute-done | bytes 5152 | tf_op jit(solution)/shard_map/while/body/eval_jaxpr/ppermute | solution.py:20
  80.0 1.4 fusion.147
  81.6 5.7 %collective-permute-start.1 = (f32[1,64,128]{2,1,0:T(8,128)S(1)}, f32[1,64,128]{2,1,0:T(8,128)S(1)}, u32[]{:S(2)}, u32[]{:S(2)}) collective-permute-start(f32[1,64,128]{2,1,0:T(8,128)S(1)} %get-tuple-element.562), channel_id=1, source_target_pairs={{4,0},{8,4},{12,8},{16,12},{20,16},{24,20},{28,24},{32,28},{36,32}... | collective-permute-start | bytes 98312 | tf_op jit(solution)/shard_map/while/body/eval_jaxpr/ppermute | solution.py:20
  90.6 3.8 %collective-permute-done.3 = f32[10,1,128]{2,1,0:T(1,128)S(1)} collective-permute-done((f32[10,1,128]{2,1,0:T(1,128)S(1)}, f32[10,1,128]{2,1,0:T(1,128)S(1)}, u32[]{:S(2)}, u32[]{:S(2)}) %collective-permute-start.3) | collective-permute-done | bytes 5152 | tf_op jit(solution)/shard_map/while/body/eval_jaxpr/ppermute | solution.py:20
  94.4 1.4 fusion.147
  96.0 5.7 %collective-permute-start.1 = (f32[1,64,128]{2,1,0:T(8,128)S(1)}, f32[1,64,128]{2,1,0:T(8,128)S(1)}, u32[]{:S(2)}, u32[]{:S(2)}) collective-permute-start(f32[1,64,128]{2,1,0:T(8,128)S(1)} %get-tuple-element.562), channel_id=1, source_target_pairs={{4,0},{8,4},{12,8},{16,12},{20,16},{24,20},{28,24},{32,28},{36,32}... | collective-permute-start | bytes 98312 | tf_op jit(solution)/shard_map/while/body/eval_jaxpr/ppermute | solution.py:20
  105.1 3.8 %collective-permute-done.3 = f32[10,1,128]{2,1,0:T(1,128)S(1)} collective-permute-done((f32[10,1,128]{2,1,0:T(1,128)S(1)}, f32[10,1,128]{2,1,0:T(1,128)S(1)}, u32[]{:S(2)}, u32[]{:S(2)}) %collective-permute-start.3) | collective-permute-done | bytes 5152 | tf_op jit(solution)/shard_map/while/body/eval_jaxpr/ppermute | solution.py:20
  108.9 1.4 fusion.147
  110.5 5.7 %collective-permute-start.1 = (f32[1,64,128]{2,1,0:T(8,128)S(1)}, f32[1,64,128]{2,1,0:T(8,128)S(1)}, u32[]{:S(2)}, u32[]{:S(2)}) collective-permute-start(f32[1,64,128]{2,1,0:T(8,128)S(1)} %get-tuple-element.562), channel_id=1, source_target_pairs={{4,0},{8,4},{12,8},{16,12},{20,16},{24,20},{28,24},{32,28},{36,32}... | collective-permute-start | bytes 98312 | tf_op jit(solution)/shard_map/while/body/eval_jaxpr/ppermute | solution.py:20
  119.6 3.8 %collective-permute-done.3 = f32[10,1,128]{2,1,0:T(1,128)S(1)} collective-permute-done((f32[10,1,128]{2,1,0:T(1,128)S(1)}, f32[10,1,128]{2,1,0:T(1,128)S(1)}, u32[]{:S(2)}, u32[]{:S(2)}) %collective-permute-start.3) | collective-permute-done | bytes 5152 | tf_op jit(solution)/shard_map/while/body/eval_jaxpr/ppermute | solution.py:20
  123.3 1.4 fusion.147
  124.9 5.7 %collective-permute-start.1 = (f32[1,64,128]{2,1,0:T(8,128)S(1)}, f32[1,64,128]{2,1,0:T(8,128)S(1)}, u32[]{:S(2)}, u32[]{:S(2)}) collective-permute-start(f32[1,64,128]{2,1,0:T(8,128)S(1)} %get-tuple-element.562), channel_id=1, source_target_pairs={{4,0},{8,4},{12,8},{16,12},{20,16},{24,20},{28,24},{32,28},{36,32}... | collective-permute-start | bytes 98312 | tf_op jit(solution)/shard_map/while/body/eval_jaxpr/ppermute | solution.py:20
  134.1 3.8 %collective-permute-done.3 = f32[10,1,128]{2,1,0:T(1,128)S(1)} collective-permute-done((f32[10,1,128]{2,1,0:T(1,128)S(1)}, f32[10,1,128]{2,1,0:T(1,128)S(1)}, u32[]{:S(2)}, u32[]{:S(2)}) %collective-permute-start.3) | collective-permute-done | bytes 5152 | tf_op jit(solution)/shard_map/while/body/eval_jaxpr/ppermute | solution.py:20
  137.8 1.4 fusion.147
  139.4 5.7 %collective-permute-start.1 = (f32[1,64,128]{2,1,0:T(8,128)S(1)}, f32[1,64,128]{2,1,0:T(8,128)S(1)}, u32[]{:S(2)}, u32[]{:S(2)}) collective-permute-start(f32[1,64,128]{2,1,0:T(8,128)S(1)} %get-tuple-element.562), channel_id=1, source_target_pairs={{4,0},{8,4},{12,8},{16,12},{20,16},{24,20},{28,24},{32,28},{36,32}... | collective-permute-start | bytes 98312 | tf_op jit(solution)/shard_map/while/body/eval_jaxpr/ppermute | solution.py:20
  148.5 3.8 %collective-permute-done.3 = f32[10,1,128]{2,1,0:T(1,128)S(1)} collective-permute-done((f32[10,1,128]{2,1,0:T(1,128)S(1)}, f32[10,1,128]{2,1,0:T(1,128)S(1)}, u32[]{:S(2)}, u32[]{:S(2)}) %collective-permute-start.3) | collective-permute-done | bytes 5152 | tf_op jit(solution)/shard_map/while/body/eval_jaxpr/ppermute | solution.py:20
  152.3 1.4 fusion.147
  154.0 1.5 constant_dynamic-update-slice_fusion.9
  156.7 3.2 %collective-permute-start.18 = (f32[3,10,1,128]{3,2,1,0:T(1,128)S(1)}, f32[3,10,1,128]{3,2,1,0:T(1,128)S(1)}, u32[]{:S(2)}, u32[]{:S(2)}) collective-permute-start(f32[3,10,1,128]{3,2,1,0:T(1,128)S(1)} %get-tuple-element.329), channel_id=1, source_target_pairs={{0,1},{1,2},{2,3},{3,0},{4,5},{5,6},{6,7},{7,4},{8,9},{9,10},{10,1... | collective-permute-start | bytes 46088 | tf_op jit(solution)/shard_map/ppermute | solution.py:18
  159.9 5.7 %collective-permute-start.13 = (f32[1,64,128]{2,1,0:T(8,128)S(1)}, f32[1,64,128]{2,1,0:T(8,128)S(1)}, u32[]{:S(2)}, u32[]{:S(2)}) collective-permute-start(f32[1,64,128]{2,1,0:T(8,128)S(1)} %get-tuple-element.354), channel_id=1, source_target_pairs={{4,0},{8,4},{12,8},{16,12},{20,16},{24,20},{28,24},{32,28},{36,32}... | collective-permute-start | bytes 98312 | tf_op jit(solution)/shard_map/ppermute | solution.py:20
  166.7 3.2 %collective-permute-start.19 = (f32[10,1,128]{2,1,0:T(1,128)S(1)}, f32[10,1,128]{2,1,0:T(1,128)S(1)}, u32[]{:S(2)}, u32[]{:S(2)}) collective-permute-start(f32[10,1,128]{2,1,0:T(1,128)S(1)} %get-tuple-element.345), channel_id=1, source_target_pairs={{0,1},{1,2},{2,3},{3,0},{4,5},{5,6},{6,7},{7,4},{8,9},{9,10},{10,1... | collective-permute-start | bytes 15368 | tf_op jit(solution)/shard_map/ppermute | solution.py:18
  171.4 1.9 multiply_reduce_fusion
  174.1 91.0 %while.36 = (s32[]{:T(128)}, f32[8,64,128]{2,1,0:T(8,128)S(1)}, f32[8,64,128]{2,1,0:T(8,128)S(1)}, f32[8,64,128]{2,1,0:T(8,128)}, f32[8,64,128]{2,1,0:T(8,128)S(...) while((s32[]{:T(128)}, f32[8,64,128]{2,1,0:T(8,128)S(1)}, ...), condition=%wide.region_9.10_spmd, body=%wide.region_8.9_spmd.sunk | while | flops 1835010 | bytes 7268641 | solution.py:177
  174.2 6.0 %collective-permute-start.5 = (f32[1,64,128]{2,1,0:T(8,128)S(1)}, f32[1,64,128]{2,1,0:T(8,128)S(1)}, u32[]{:S(2)}, u32[]{:S(2)}) collective-permute-start(f32[1,64,128]{2,1,0:T(8,128)S(1)} %get-tuple-element.577), channel_id=1, source_target_pairs={{4,0},{8,4},{12,8},{16,12},{20,16},{24,20},{28,24},{32,28},{36,32}... | collective-permute-start | bytes 98312 | tf_op jit(solution)/shard_map/while/body/eval_jaxpr/ppermute | solution.py:20
  181.5 4.8 %collective-permute-start.6 = (f32[10,1,128]{2,1,0:T(1,128)S(1)}, f32[10,1,128]{2,1,0:T(1,128)S(1)}, u32[]{:S(2)}, u32[]{:S(2)}) collective-permute-start(f32[10,1,128]{2,1,0:T(1,128)S(1)} %get-tuple-element.578), channel_id=1, source_target_pairs={{0,1},{1,2},{2,3},{3,0},{4,5},{5,6},{6,7},{7,4},{8,9},{9,10},{10,1... | collective-permute-start | bytes 15368 | tf_op jit(solution)/shard_map/while/body/eval_jaxpr/ppermute | solution.py:18
  187.1 3.8 %collective-permute-done.7 = f32[10,1,128]{2,1,0:T(1,128)S(1)} collective-permute-done((f32[10,1,128]{2,1,0:T(1,128)S(1)}, f32[10,1,128]{2,1,0:T(1,128)S(1)}, u32[]{:S(2)}, u32[]{:S(2)}) %collective-permute-start.7) | collective-permute-done | bytes 5152 | tf_op jit(solution)/shard_map/while/body/eval_jaxpr/ppermute | solution.py:20
  190.9 1.4 fusion.151
  192.5 5.7 %collective-permute-start.5 = (f32[1,64,128]{2,1,0:T(8,128)S(1)}, f32[1,64,128]{2,1,0:T(8,128)S(1)}, u32[]{:S(2)}, u32[]{:S(2)}) collective-permute-start(f32[1,64,128]{2,1,0:T(8,128)S(1)} %get-tuple-element.577), channel_id=1, source_target_pairs={{4,0},{8,4},{12,8},{16,12},{20,16},{24,20},{28,24},{32,28},{36,32}... | collective-permute-start | bytes 98312 | tf_op jit(solution)/shard_map/while/body/eval_jaxpr/ppermute | solution.py:20
  201.6 3.8 %collective-permute-done.7 = f32[10,1,128]{2,1,0:T(1,128)S(1)} collective-permute-done((f32[10,1,128]{2,1,0:T(1,128)S(1)}, f32[10,1,128]{2,1,0:T(1,128)S(1)}, u32[]{:S(2)}, u32[]{:S(2)}) %collective-permute-start.7) | collective-permute-done | bytes 5152 | tf_op jit(solution)/shard_map/while/body/eval_jaxpr/ppermute | solution.py:20
  205.3 1.4 fusion.151
  206.9 5.7 %collective-permute-start.5 = (f32[1,64,128]{2,1,0:T(8,128)S(1)}, f32[1,64,128]{2,1,0:T(8,128)S(1)}, u32[]{:S(2)}, u32[]{:S(2)}) collective-permute-start(f32[1,64,128]{2,1,0:T(8,128)S(1)} %get-tuple-element.577), channel_id=1, source_target_pairs={{4,0},{8,4},{12,8},{16,12},{20,16},{24,20},{28,24},{32,28},{36,32}... | collective-permute-start | bytes 98312 | tf_op jit(solution)/shard_map/while/body/eval_jaxpr/ppermute | solution.py:20
  216.0 3.8 %collective-permute-done.7 = f32[10,1,128]{2,1,0:T(1,128)S(1)} collective-permute-done((f32[10,1,128]{2,1,0:T(1,128)S(1)}, f32[10,1,128]{2,1,0:T(1,128)S(1)}, u32[]{:S(2)}, u32[]{:S(2)}) %collective-permute-start.7) | collective-permute-done | bytes 5152 | tf_op jit(solution)/shard_map/while/body/eval_jaxpr/ppermute | solution.py:20
  219.8 1.4 fusion.151
  221.4 5.7 %collective-permute-start.5 = (f32[1,64,128]{2,1,0:T(8,128)S(1)}, f32[1,64,128]{2,1,0:T(8,128)S(1)}, u32[]{:S(2)}, u32[]{:S(2)}) collective-permute-start(f32[1,64,128]{2,1,0:T(8,128)S(1)} %get-tuple-element.577), channel_id=1, source_target_pairs={{4,0},{8,4},{12,8},{16,12},{20,16},{24,20},{28,24},{32,28},{36,32}... | collective-permute-start | bytes 98312 | tf_op jit(solution)/shard_map/while/body/eval_jaxpr/ppermute | solution.py:20
  230.5 3.8 %collective-permute-done.7 = f32[10,1,128]{2,1,0:T(1,128)S(1)} collective-permute-done((f32[10,1,128]{2,1,0:T(1,128)S(1)}, f32[10,1,128]{2,1,0:T(1,128)S(1)}, u32[]{:S(2)}, u32[]{:S(2)}) %collective-permute-start.7) | collective-permute-done | bytes 5152 | tf_op jit(solution)/shard_map/while/body/eval_jaxpr/ppermute | solution.py:20
  234.3 1.4 fusion.151
  235.9 5.7 %collective-permute-start.5 = (f32[1,64,128]{2,1,0:T(8,128)S(1)}, f32[1,64,128]{2,1,0:T(8,128)S(1)}, u32[]{:S(2)}, u32[]{:S(2)}) collective-permute-start(f32[1,64,128]{2,1,0:T(8,128)S(1)} %get-tuple-element.577), channel_id=1, source_target_pairs={{4,0},{8,4},{12,8},{16,12},{20,16},{24,20},{28,24},{32,28},{36,32}... | collective-permute-start | bytes 98312 | tf_op jit(solution)/shard_map/while/body/eval_jaxpr/ppermute | solution.py:20
  241.7 1.8 collective-permute-done.4
  245.3 3.8 %collective-permute-done.7 = f32[10,1,128]{2,1,0:T(1,128)S(1)} collective-permute-done((f32[10,1,128]{2,1,0:T(1,128)S(1)}, f32[10,1,128]{2,1,0:T(1,128)S(1)}, u32[]{:S(2)}, u32[]{:S(2)}) %collective-permute-start.7) | collective-permute-done | bytes 5152 | tf_op jit(solution)/shard_map/while/body/eval_jaxpr/ppermute | solution.py:20
  249.1 1.4 fusion.151
  250.7 5.7 %collective-permute-start.5 = (f32[1,64,128]{2,1,0:T(8,128)S(1)}, f32[1,64,128]{2,1,0:T(8,128)S(1)}, u32[]{:S(2)}, u32[]{:S(2)}) collective-permute-start(f32[1,64,128]{2,1,0:T(8,128)S(1)} %get-tuple-element.577), channel_id=1, source_target_pairs={{4,0},{8,4},{12,8},{16,12},{20,16},{24,20},{28,24},{32,28},{36,32}... | collective-permute-start | bytes 98312 | tf_op jit(solution)/shard_map/while/body/eval_jaxpr/ppermute | solution.py:20
  256.4 1.9 collective-permute-done.4
  259.8 3.8 %collective-permute-done.7 = f32[10,1,128]{2,1,0:T(1,128)S(1)} collective-permute-done((f32[10,1,128]{2,1,0:T(1,128)S(1)}, f32[10,1,128]{2,1,0:T(1,128)S(1)}, u32[]{:S(2)}, u32[]{:S(2)}) %collective-permute-start.7) | collective-permute-done | bytes 5152 | tf_op jit(solution)/shard_map/while/body/eval_jaxpr/ppermute | solution.py:20
  263.6 1.4 fusion.151
  265.2 5.5 %collective-permute-start.21 = (f32[1,64,128]{2,1,0:T(8,128)S(1)}, f32[1,64,128]{2,1,0:T(8,128)S(1)}, u32[]{:S(2)}, u32[]{:S(2)}) collective-permute-start(f32[1,64,128]{2,1,0:T(8,128)S(1)} %get-tuple-element.350), channel_id=1, source_target_pairs={{4,0},{8,4},{12,8},{16,12},{20,16},{24,20},{28,24},{32,28},{36,32}... | collective-permute-start | bytes 98312 | tf_op jit(solution)/shard_map/ppermute | solution.py:20
  270.8 5.8 %collective-permute-start.20 = (f32[3,1,64,128]{3,2,1,0:T(8,128)S(1)}, f32[3,1,64,128]{3,2,1,0:T(8,128)S(1)}, u32[]{:S(2)}, u32[]{:S(2)}) collective-permute-start(f32[3,1,64,128]{3,2,1,0:T(8,128)S(1)} %get-tuple-element.331), channel_id=1, source_target_pairs={{4,0},{8,4},{12,8},{16,12},{20,16},{24,20},{28,24},{32,28},{36,32}... | collective-permute-start | bytes 294920 | tf_op jit(solution)/shard_map/ppermute | solution.py:20
  277.8 1.9 collective-permute-start.25
  281.8 2.6 collective-permute-start.26
  285.9 1.7 fusion.49
  (298 shorter events, 52.4 us)
Async XLA Ops:
  1.5 52.5 %collective-permute-start.10 = (f32[1,64,128]{2,1,0:T(8,128)S(1)}, f32[1,64,128]{2,1,0:T(8,128)S(1)}, u32[]{:S(2)}, u32[]{:S(2)}) collective-permute-start(f32[1,64,128]{2,1,0:T(8,128)S(1)} %get-tuple-element.364), channel_id=1, source_target_pairs={{0,4},{4,8},{8,12},{12,16},{16,20},{20,24},{24,28},{28,32},{32,36}... | collective-permute-start | bytes 98312 | tf_op jit(solution)/shard_map/ppermute | solution.py:18
  3.5 50.5 %collective-permute-start.9 = (f32[1,64,128]{2,1,0:T(8,128)S(1)}, f32[1,64,128]{2,1,0:T(8,128)S(1)}, u32[]{:S(2)}, u32[]{:S(2)}) collective-permute-start(f32[1,64,128]{2,1,0:T(8,128)S(1)} %get-tuple-element.365), channel_id=1, source_target_pairs={{4,0},{8,4},{12,8},{16,12},{20,16},{24,20},{28,24},{32,28},{36,32}... | collective-permute-start | bytes 98312 | tf_op jit(solution)/shard_map/ppermute | solution.py:20
  12.8 141.2 %collective-permute-start.8 = (f32[3,1,64,128]{3,2,1,0:T(8,128)}, f32[3,1,64,128]{3,2,1,0:T(8,128)}, u32[]{:S(2)}, u32[]{:S(2)}) collective-permute-start(f32[3,1,64,128]{3,2,1,0:T(8,128)} %get-tuple-element.332), channel_id=1, source_target_pairs={{4,0},{8,4},{12,8},{16,12},{20,16},{24,20},{28,24},{32,28},{36,32}... | collective-permute-start | bytes 294920 | tf_op jit(solution)/shard_map/ppermute | solution.py:20
  14.2 48.8 %collective-permute-start.14 = (f32[3,1,64,128]{3,2,1,0:T(8,128)}, f32[3,1,64,128]{3,2,1,0:T(8,128)S(1)}, u32[]{:S(2)}, u32[]{:S(2)}) collective-permute-start(f32[3,1,64,128]{3,2,1,0:T(8,128)} %get-tuple-element.333), channel_id=1, source_target_pairs={{0,4},{4,8},{8,12},{12,16},{16,20},{20,24},{24,28},{28,32},{32,36}... | collective-permute-start | bytes 294920 | tf_op jit(solution)/shard_map/ppermute | solution.py:18
  54.1 5.7 %collective-permute-start.12 = (f32[10,1,128]{2,1,0:T(1,128)S(1)}, f32[10,1,128]{2,1,0:T(1,128)S(1)}, u32[]{:S(2)}, u32[]{:S(2)}) collective-permute-start(f32[10,1,128]{2,1,0:T(1,128)S(1)} %get-tuple-element.346), channel_id=1, source_target_pairs={{0,1},{1,2},{2,3},{3,0},{4,5},{5,6},{6,7},{7,4},{8,9},{9,10},{10,1... | collective-permute-start | bytes 15368 | tf_op jit(solution)/shard_map/ppermute | solution.py:18
  56.3 4.5 %collective-permute-start.11 = (f32[10,1,128]{2,1,0:T(1,128)S(1)}, f32[10,1,128]{2,1,0:T(1,128)S(1)}, u32[]{:S(2)}, u32[]{:S(2)}) collective-permute-start(f32[10,1,128]{2,1,0:T(1,128)S(1)} %get-tuple-element.347), channel_id=1, source_target_pairs={{1,0},{2,1},{3,2},{0,3},{5,4},{6,5},{7,6},{4,7},{9,8},{10,9},{11,1... | collective-permute-start | bytes 15368 | tf_op jit(solution)/shard_map/ppermute | solution.py:20
  64.7 7.1 %collective-permute-start = (f32[1,64,128]{2,1,0:T(8,128)S(1)}, f32[1,64,128]{2,1,0:T(8,128)S(1)}, u32[]{:S(2)}, u32[]{:S(2)}) collective-permute-start(f32[1,64,128]{2,1,0:T(8,128)S(1)} %get-tuple-element.561), channel_id=1, source_target_pairs={{0,4},{4,8},{8,12},{12,16},{16,20},{20,24},{24,28},{28,32},{32,36}... | collective-permute-start | bytes 98312 | tf_op jit(solution)/shard_map/while/body/eval_jaxpr/ppermute | solution.py:18
  64.8 7.0 %collective-permute-start.1 = (f32[1,64,128]{2,1,0:T(8,128)S(1)}, f32[1,64,128]{2,1,0:T(8,128)S(1)}, u32[]{:S(2)}, u32[]{:S(2)}) collective-permute-start(f32[1,64,128]{2,1,0:T(8,128)S(1)} %get-tuple-element.562), channel_id=1, source_target_pairs={{4,0},{8,4},{12,8},{16,12},{20,16},{24,20},{28,24},{32,28},{36,32}... | collective-permute-start | bytes 98312 | tf_op jit(solution)/shard_map/while/body/eval_jaxpr/ppermute | solution.py:20
  71.9 4.3 %collective-permute-start.2 = (f32[10,1,128]{2,1,0:T(1,128)S(1)}, f32[10,1,128]{2,1,0:T(1,128)S(1)}, u32[]{:S(2)}, u32[]{:S(2)}) collective-permute-start(f32[10,1,128]{2,1,0:T(1,128)S(1)} %get-tuple-element.563), channel_id=1, source_target_pairs={{0,1},{1,2},{2,3},{3,0},{4,5},{5,6},{6,7},{7,4},{8,9},{9,10},{10,1... | collective-permute-start | bytes 15368 | tf_op jit(solution)/shard_map/while/body/eval_jaxpr/ppermute | solution.py:18
  75.4 4.5 %collective-permute-start.3 = (f32[10,1,128]{2,1,0:T(1,128)S(1)}, f32[10,1,128]{2,1,0:T(1,128)S(1)}, u32[]{:S(2)}, u32[]{:S(2)}) collective-permute-start(f32[10,1,128]{2,1,0:T(1,128)S(1)} %get-tuple-element.564), channel_id=1, source_target_pairs={{1,0},{2,1},{3,2},{0,3},{5,4},{6,5},{7,6},{4,7},{9,8},{10,9},{11,1... | collective-permute-start | bytes 15368 | tf_op jit(solution)/shard_map/while/body/eval_jaxpr/ppermute | solution.py:20
  81.5 7.1 %collective-permute-start = (f32[1,64,128]{2,1,0:T(8,128)S(1)}, f32[1,64,128]{2,1,0:T(8,128)S(1)}, u32[]{:S(2)}, u32[]{:S(2)}) collective-permute-start(f32[1,64,128]{2,1,0:T(8,128)S(1)} %get-tuple-element.561), channel_id=1, source_target_pairs={{0,4},{4,8},{8,12},{12,16},{16,20},{20,24},{24,28},{28,32},{32,36}... | collective-permute-start | bytes 98312 | tf_op jit(solution)/shard_map/while/body/eval_jaxpr/ppermute | solution.py:18
  81.6 7.0 %collective-permute-start.1 = (f32[1,64,128]{2,1,0:T(8,128)S(1)}, f32[1,64,128]{2,1,0:T(8,128)S(1)}, u32[]{:S(2)}, u32[]{:S(2)}) collective-permute-start(f32[1,64,128]{2,1,0:T(8,128)S(1)} %get-tuple-element.562), channel_id=1, source_target_pairs={{4,0},{8,4},{12,8},{16,12},{20,16},{24,20},{28,24},{32,28},{36,32}... | collective-permute-start | bytes 98312 | tf_op jit(solution)/shard_map/while/body/eval_jaxpr/ppermute | solution.py:20
  88.6 2.0 collective-permute-start.2
  89.9 4.5 %collective-permute-start.3 = (f32[10,1,128]{2,1,0:T(1,128)S(1)}, f32[10,1,128]{2,1,0:T(1,128)S(1)}, u32[]{:S(2)}, u32[]{:S(2)}) collective-permute-start(f32[10,1,128]{2,1,0:T(1,128)S(1)} %get-tuple-element.564), channel_id=1, source_target_pairs={{1,0},{2,1},{3,2},{0,3},{5,4},{6,5},{7,6},{4,7},{9,8},{10,9},{11,1... | collective-permute-start | bytes 15368 | tf_op jit(solution)/shard_map/while/body/eval_jaxpr/ppermute | solution.py:20
  95.9 7.1 %collective-permute-start = (f32[1,64,128]{2,1,0:T(8,128)S(1)}, f32[1,64,128]{2,1,0:T(8,128)S(1)}, u32[]{:S(2)}, u32[]{:S(2)}) collective-permute-start(f32[1,64,128]{2,1,0:T(8,128)S(1)} %get-tuple-element.561), channel_id=1, source_target_pairs={{0,4},{4,8},{8,12},{12,16},{16,20},{20,24},{24,28},{28,32},{32,36}... | collective-permute-start | bytes 98312 | tf_op jit(solution)/shard_map/while/body/eval_jaxpr/ppermute | solution.py:18
  96.0 7.0 %collective-permute-start.1 = (f32[1,64,128]{2,1,0:T(8,128)S(1)}, f32[1,64,128]{2,1,0:T(8,128)S(1)}, u32[]{:S(2)}, u32[]{:S(2)}) collective-permute-start(f32[1,64,128]{2,1,0:T(8,128)S(1)} %get-tuple-element.562), channel_id=1, source_target_pairs={{4,0},{8,4},{12,8},{16,12},{20,16},{24,20},{28,24},{32,28},{36,32}... | collective-permute-start | bytes 98312 | tf_op jit(solution)/shard_map/while/body/eval_jaxpr/ppermute | solution.py:20
  104.3 4.5 %collective-permute-start.3 = (f32[10,1,128]{2,1,0:T(1,128)S(1)}, f32[10,1,128]{2,1,0:T(1,128)S(1)}, u32[]{:S(2)}, u32[]{:S(2)}) collective-permute-start(f32[10,1,128]{2,1,0:T(1,128)S(1)} %get-tuple-element.564), channel_id=1, source_target_pairs={{1,0},{2,1},{3,2},{0,3},{5,4},{6,5},{7,6},{4,7},{9,8},{10,9},{11,1... | collective-permute-start | bytes 15368 | tf_op jit(solution)/shard_map/while/body/eval_jaxpr/ppermute | solution.py:20
  110.4 7.1 %collective-permute-start = (f32[1,64,128]{2,1,0:T(8,128)S(1)}, f32[1,64,128]{2,1,0:T(8,128)S(1)}, u32[]{:S(2)}, u32[]{:S(2)}) collective-permute-start(f32[1,64,128]{2,1,0:T(8,128)S(1)} %get-tuple-element.561), channel_id=1, source_target_pairs={{0,4},{4,8},{8,12},{12,16},{16,20},{20,24},{24,28},{28,32},{32,36}... | collective-permute-start | bytes 98312 | tf_op jit(solution)/shard_map/while/body/eval_jaxpr/ppermute | solution.py:18
  110.5 7.0 %collective-permute-start.1 = (f32[1,64,128]{2,1,0:T(8,128)S(1)}, f32[1,64,128]{2,1,0:T(8,128)S(1)}, u32[]{:S(2)}, u32[]{:S(2)}) collective-permute-start(f32[1,64,128]{2,1,0:T(8,128)S(1)} %get-tuple-element.562), channel_id=1, source_target_pairs={{4,0},{8,4},{12,8},{16,12},{20,16},{24,20},{28,24},{32,28},{36,32}... | collective-permute-start | bytes 98312 | tf_op jit(solution)/shard_map/while/body/eval_jaxpr/ppermute | solution.py:20
  118.8 4.5 %collective-permute-start.3 = (f32[10,1,128]{2,1,0:T(1,128)S(1)}, f32[10,1,128]{2,1,0:T(1,128)S(1)}, u32[]{:S(2)}, u32[]{:S(2)}) collective-permute-start(f32[10,1,128]{2,1,0:T(1,128)S(1)} %get-tuple-element.564), channel_id=1, source_target_pairs={{1,0},{2,1},{3,2},{0,3},{5,4},{6,5},{7,6},{4,7},{9,8},{10,9},{11,1... | collective-permute-start | bytes 15368 | tf_op jit(solution)/shard_map/while/body/eval_jaxpr/ppermute | solution.py:20
  124.9 7.1 %collective-permute-start = (f32[1,64,128]{2,1,0:T(8,128)S(1)}, f32[1,64,128]{2,1,0:T(8,128)S(1)}, u32[]{:S(2)}, u32[]{:S(2)}) collective-permute-start(f32[1,64,128]{2,1,0:T(8,128)S(1)} %get-tuple-element.561), channel_id=1, source_target_pairs={{0,4},{4,8},{8,12},{12,16},{16,20},{20,24},{24,28},{28,32},{32,36}... | collective-permute-start | bytes 98312 | tf_op jit(solution)/shard_map/while/body/eval_jaxpr/ppermute | solution.py:18
  124.9 7.0 %collective-permute-start.1 = (f32[1,64,128]{2,1,0:T(8,128)S(1)}, f32[1,64,128]{2,1,0:T(8,128)S(1)}, u32[]{:S(2)}, u32[]{:S(2)}) collective-permute-start(f32[1,64,128]{2,1,0:T(8,128)S(1)} %get-tuple-element.562), channel_id=1, source_target_pairs={{4,0},{8,4},{12,8},{16,12},{20,16},{24,20},{28,24},{32,28},{36,32}... | collective-permute-start | bytes 98312 | tf_op jit(solution)/shard_map/while/body/eval_jaxpr/ppermute | solution.py:20
  132.0 2.1 collective-permute-start.2
  133.3 4.5 %collective-permute-start.3 = (f32[10,1,128]{2,1,0:T(1,128)S(1)}, f32[10,1,128]{2,1,0:T(1,128)S(1)}, u32[]{:S(2)}, u32[]{:S(2)}) collective-permute-start(f32[10,1,128]{2,1,0:T(1,128)S(1)} %get-tuple-element.564), channel_id=1, source_target_pairs={{1,0},{2,1},{3,2},{0,3},{5,4},{6,5},{7,6},{4,7},{9,8},{10,9},{11,1... | collective-permute-start | bytes 15368 | tf_op jit(solution)/shard_map/while/body/eval_jaxpr/ppermute | solution.py:20
  139.3 7.1 %collective-permute-start = (f32[1,64,128]{2,1,0:T(8,128)S(1)}, f32[1,64,128]{2,1,0:T(8,128)S(1)}, u32[]{:S(2)}, u32[]{:S(2)}) collective-permute-start(f32[1,64,128]{2,1,0:T(8,128)S(1)} %get-tuple-element.561), channel_id=1, source_target_pairs={{0,4},{4,8},{8,12},{12,16},{16,20},{20,24},{24,28},{28,32},{32,36}... | collective-permute-start | bytes 98312 | tf_op jit(solution)/shard_map/while/body/eval_jaxpr/ppermute | solution.py:18
  139.4 7.0 %collective-permute-start.1 = (f32[1,64,128]{2,1,0:T(8,128)S(1)}, f32[1,64,128]{2,1,0:T(8,128)S(1)}, u32[]{:S(2)}, u32[]{:S(2)}) collective-permute-start(f32[1,64,128]{2,1,0:T(8,128)S(1)} %get-tuple-element.562), channel_id=1, source_target_pairs={{4,0},{8,4},{12,8},{16,12},{20,16},{24,20},{28,24},{32,28},{36,32}... | collective-permute-start | bytes 98312 | tf_op jit(solution)/shard_map/while/body/eval_jaxpr/ppermute | solution.py:20
  146.5 2.1 collective-permute-start.2
  147.8 4.5 %collective-permute-start.3 = (f32[10,1,128]{2,1,0:T(1,128)S(1)}, f32[10,1,128]{2,1,0:T(1,128)S(1)}, u32[]{:S(2)}, u32[]{:S(2)}) collective-permute-start(f32[10,1,128]{2,1,0:T(1,128)S(1)} %get-tuple-element.564), channel_id=1, source_target_pairs={{1,0},{2,1},{3,2},{0,3},{5,4},{6,5},{7,6},{4,7},{9,8},{10,9},{11,1... | collective-permute-start | bytes 15368 | tf_op jit(solution)/shard_map/while/body/eval_jaxpr/ppermute | solution.py:20
  153.9 11.6 %collective-permute-start.15 = (f32[1,64,128]{2,1,0:T(8,128)S(1)}, f32[1,64,128]{2,1,0:T(8,128)S(1)}, u32[]{:S(2)}, u32[]{:S(2)}) collective-permute-start(f32[1,64,128]{2,1,0:T(8,128)S(1)} %get-tuple-element.355), channel_id=1, source_target_pairs={{0,4},{4,8},{8,12},{12,16},{16,20},{20,24},{24,28},{28,32},{32,36}... | collective-permute-start | bytes 98312 | tf_op jit(solution)/shard_map/ppermute | solution.py:18
  156.6 14.8 %collective-permute-start.16 = (f32[3,10,1,128]{3,2,1,0:T(1,128)S(1)}, f32[3,10,1,128]{3,2,1,0:T(1,128)S(1)}, u32[]{:S(2)}, u32[]{:S(2)}) collective-permute-start(f32[3,10,1,128]{3,2,1,0:T(1,128)S(1)} %get-tuple-element.328), channel_id=1, source_target_pairs={{1,0},{2,1},{3,2},{0,3},{5,4},{6,5},{7,6},{4,7},{9,8},{10,9},{11,1... | collective-permute-start | bytes 46088 | tf_op jit(solution)/shard_map/ppermute | solution.py:20
  156.7 14.7 %collective-permute-start.18 = (f32[3,10,1,128]{3,2,1,0:T(1,128)S(1)}, f32[3,10,1,128]{3,2,1,0:T(1,128)S(1)}, u32[]{:S(2)}, u32[]{:S(2)}) collective-permute-start(f32[3,10,1,128]{3,2,1,0:T(1,128)S(1)} %get-tuple-element.329), channel_id=1, source_target_pairs={{0,1},{1,2},{2,3},{3,0},{4,5},{5,6},{6,7},{7,4},{8,9},{9,10},{10,1... | collective-permute-start | bytes 46088 | tf_op jit(solution)/shard_map/ppermute | solution.py:18
  159.9 6.7 %collective-permute-start.13 = (f32[1,64,128]{2,1,0:T(8,128)S(1)}, f32[1,64,128]{2,1,0:T(8,128)S(1)}, u32[]{:S(2)}, u32[]{:S(2)}) collective-permute-start(f32[1,64,128]{2,1,0:T(8,128)S(1)} %get-tuple-element.354), channel_id=1, source_target_pairs={{4,0},{8,4},{12,8},{16,12},{20,16},{24,20},{28,24},{32,28},{36,32}... | collective-permute-start | bytes 98312 | tf_op jit(solution)/shard_map/ppermute | solution.py:20
  166.6 4.6 %collective-permute-start.17 = (f32[10,1,128]{2,1,0:T(1,128)S(1)}, f32[10,1,128]{2,1,0:T(1,128)S(1)}, u32[]{:S(2)}, u32[]{:S(2)}) collective-permute-start(f32[10,1,128]{2,1,0:T(1,128)S(1)} %get-tuple-element.344), channel_id=1, source_target_pairs={{1,0},{2,1},{3,2},{0,3},{5,4},{6,5},{7,6},{4,7},{9,8},{10,9},{11,1... | collective-permute-start | bytes 15368 | tf_op jit(solution)/shard_map/ppermute | solution.py:20
  166.7 4.5 %collective-permute-start.19 = (f32[10,1,128]{2,1,0:T(1,128)S(1)}, f32[10,1,128]{2,1,0:T(1,128)S(1)}, u32[]{:S(2)}, u32[]{:S(2)}) collective-permute-start(f32[10,1,128]{2,1,0:T(1,128)S(1)} %get-tuple-element.345), channel_id=1, source_target_pairs={{0,1},{1,2},{2,3},{3,0},{4,5},{5,6},{6,7},{7,4},{8,9},{9,10},{10,1... | collective-permute-start | bytes 15368 | tf_op jit(solution)/shard_map/ppermute | solution.py:18
  174.1 7.3 %collective-permute-start.4 = (f32[1,64,128]{2,1,0:T(8,128)S(1)}, f32[1,64,128]{2,1,0:T(8,128)S(1)}, u32[]{:S(2)}, u32[]{:S(2)}) collective-permute-start(f32[1,64,128]{2,1,0:T(8,128)S(1)} %get-tuple-element.576), channel_id=1, source_target_pairs={{0,4},{4,8},{8,12},{12,16},{16,20},{20,24},{24,28},{28,32},{32,36}... | collective-permute-start | bytes 98312 | tf_op jit(solution)/shard_map/while/body/eval_jaxpr/ppermute | solution.py:18
  174.2 7.3 %collective-permute-start.5 = (f32[1,64,128]{2,1,0:T(8,128)S(1)}, f32[1,64,128]{2,1,0:T(8,128)S(1)}, u32[]{:S(2)}, u32[]{:S(2)}) collective-permute-start(f32[1,64,128]{2,1,0:T(8,128)S(1)} %get-tuple-element.577), channel_id=1, source_target_pairs={{4,0},{8,4},{12,8},{16,12},{20,16},{24,20},{28,24},{32,28},{36,32}... | collective-permute-start | bytes 98312 | tf_op jit(solution)/shard_map/while/body/eval_jaxpr/ppermute | solution.py:20
  181.5 5.6 %collective-permute-start.6 = (f32[10,1,128]{2,1,0:T(1,128)S(1)}, f32[10,1,128]{2,1,0:T(1,128)S(1)}, u32[]{:S(2)}, u32[]{:S(2)}) collective-permute-start(f32[10,1,128]{2,1,0:T(1,128)S(1)} %get-tuple-element.578), channel_id=1, source_target_pairs={{0,1},{1,2},{2,3},{3,0},{4,5},{5,6},{6,7},{7,4},{8,9},{9,10},{10,1... | collective-permute-start | bytes 15368 | tf_op jit(solution)/shard_map/while/body/eval_jaxpr/ppermute | solution.py:18
  186.3 4.5 %collective-permute-start.7 = (f32[10,1,128]{2,1,0:T(1,128)S(1)}, f32[10,1,128]{2,1,0:T(1,128)S(1)}, u32[]{:S(2)}, u32[]{:S(2)}) collective-permute-start(f32[10,1,128]{2,1,0:T(1,128)S(1)} %get-tuple-element.579), channel_id=1, source_target_pairs={{1,0},{2,1},{3,2},{0,3},{5,4},{6,5},{7,6},{4,7},{9,8},{10,9},{11,1... | collective-permute-start | bytes 15368 | tf_op jit(solution)/shard_map/while/body/eval_jaxpr/ppermute | solution.py:20
  192.4 7.1 %collective-permute-start.4 = (f32[1,64,128]{2,1,0:T(8,128)S(1)}, f32[1,64,128]{2,1,0:T(8,128)S(1)}, u32[]{:S(2)}, u32[]{:S(2)}) collective-permute-start(f32[1,64,128]{2,1,0:T(8,128)S(1)} %get-tuple-element.576), channel_id=1, source_target_pairs={{0,4},{4,8},{8,12},{12,16},{16,20},{20,24},{24,28},{28,32},{32,36}... | collective-permute-start | bytes 98312 | tf_op jit(solution)/shard_map/while/body/eval_jaxpr/ppermute | solution.py:18
  192.5 7.0 %collective-permute-start.5 = (f32[1,64,128]{2,1,0:T(8,128)S(1)}, f32[1,64,128]{2,1,0:T(8,128)S(1)}, u32[]{:S(2)}, u32[]{:S(2)}) collective-permute-start(f32[1,64,128]{2,1,0:T(8,128)S(1)} %get-tuple-element.577), channel_id=1, source_target_pairs={{4,0},{8,4},{12,8},{16,12},{20,16},{24,20},{28,24},{32,28},{36,32}... | collective-permute-start | bytes 98312 | tf_op jit(solution)/shard_map/while/body/eval_jaxpr/ppermute | solution.py:20
  199.5 2.1 collective-permute-start.6
  200.8 4.5 %collective-permute-start.7 = (f32[10,1,128]{2,1,0:T(1,128)S(1)}, f32[10,1,128]{2,1,0:T(1,128)S(1)}, u32[]{:S(2)}, u32[]{:S(2)}) collective-permute-start(f32[10,1,128]{2,1,0:T(1,128)S(1)} %get-tuple-element.579), channel_id=1, source_target_pairs={{1,0},{2,1},{3,2},{0,3},{5,4},{6,5},{7,6},{4,7},{9,8},{10,9},{11,1... | collective-permute-start | bytes 15368 | tf_op jit(solution)/shard_map/while/body/eval_jaxpr/ppermute | solution.py:20
  206.8 7.1 %collective-permute-start.4 = (f32[1,64,128]{2,1,0:T(8,128)S(1)}, f32[1,64,128]{2,1,0:T(8,128)S(1)}, u32[]{:S(2)}, u32[]{:S(2)}) collective-permute-start(f32[1,64,128]{2,1,0:T(8,128)S(1)} %get-tuple-element.576), channel_id=1, source_target_pairs={{0,4},{4,8},{8,12},{12,16},{16,20},{20,24},{24,28},{28,32},{32,36}... | collective-permute-start | bytes 98312 | tf_op jit(solution)/shard_map/while/body/eval_jaxpr/ppermute | solution.py:18
  206.9 7.0 %collective-permute-start.5 = (f32[1,64,128]{2,1,0:T(8,128)S(1)}, f32[1,64,128]{2,1,0:T(8,128)S(1)}, u32[]{:S(2)}, u32[]{:S(2)}) collective-permute-start(f32[1,64,128]{2,1,0:T(8,128)S(1)} %get-tuple-element.577), channel_id=1, source_target_pairs={{4,0},{8,4},{12,8},{16,12},{20,16},{24,20},{28,24},{32,28},{36,32}... | collective-permute-start | bytes 98312 | tf_op jit(solution)/shard_map/while/body/eval_jaxpr/ppermute | solution.py:20
  214.0 2.1 collective-permute-start.6
  215.3 4.5 %collective-permute-start.7 = (f32[10,1,128]{2,1,0:T(1,128)S(1)}, f32[10,1,128]{2,1,0:T(1,128)S(1)}, u32[]{:S(2)}, u32[]{:S(2)}) collective-permute-start(f32[10,1,128]{2,1,0:T(1,128)S(1)} %get-tuple-element.579), channel_id=1, source_target_pairs={{1,0},{2,1},{3,2},{0,3},{5,4},{6,5},{7,6},{4,7},{9,8},{10,9},{11,1... | collective-permute-start | bytes 15368 | tf_op jit(solution)/shard_map/while/body/eval_jaxpr/ppermute | solution.py:20
  221.3 7.1 %collective-permute-start.4 = (f32[1,64,128]{2,1,0:T(8,128)S(1)}, f32[1,64,128]{2,1,0:T(8,128)S(1)}, u32[]{:S(2)}, u32[]{:S(2)}) collective-permute-start(f32[1,64,128]{2,1,0:T(8,128)S(1)} %get-tuple-element.576), channel_id=1, source_target_pairs={{0,4},{4,8},{8,12},{12,16},{16,20},{20,24},{24,28},{28,32},{32,36}... | collective-permute-start | bytes 98312 | tf_op jit(solution)/shard_map/while/body/eval_jaxpr/ppermute | solution.py:18
  221.4 7.0 %collective-permute-start.5 = (f32[1,64,128]{2,1,0:T(8,128)S(1)}, f32[1,64,128]{2,1,0:T(8,128)S(1)}, u32[]{:S(2)}, u32[]{:S(2)}) collective-permute-start(f32[1,64,128]{2,1,0:T(8,128)S(1)} %get-tuple-element.577), channel_id=1, source_target_pairs={{4,0},{8,4},{12,8},{16,12},{20,16},{24,20},{28,24},{32,28},{36,32}... | collective-permute-start | bytes 98312 | tf_op jit(solution)/shard_map/while/body/eval_jaxpr/ppermute | solution.py:20
  228.5 2.1 collective-permute-start.6
  229.8 4.5 %collective-permute-start.7 = (f32[10,1,128]{2,1,0:T(1,128)S(1)}, f32[10,1,128]{2,1,0:T(1,128)S(1)}, u32[]{:S(2)}, u32[]{:S(2)}) collective-permute-start(f32[10,1,128]{2,1,0:T(1,128)S(1)} %get-tuple-element.579), channel_id=1, source_target_pairs={{1,0},{2,1},{3,2},{0,3},{5,4},{6,5},{7,6},{4,7},{9,8},{10,9},{11,1... | collective-permute-start | bytes 15368 | tf_op jit(solution)/shard_map/while/body/eval_jaxpr/ppermute | solution.py:20
  235.8 7.6 %collective-permute-start.4 = (f32[1,64,128]{2,1,0:T(8,128)S(1)}, f32[1,64,128]{2,1,0:T(8,128)S(1)}, u32[]{:S(2)}, u32[]{:S(2)}) collective-permute-start(f32[1,64,128]{2,1,0:T(8,128)S(1)} %get-tuple-element.576), channel_id=1, source_target_pairs={{0,4},{4,8},{8,12},{12,16},{16,20},{20,24},{24,28},{28,32},{32,36}... | collective-permute-start | bytes 98312 | tf_op jit(solution)/shard_map/while/body/eval_jaxpr/ppermute | solution.py:18
  235.9 7.6 %collective-permute-start.5 = (f32[1,64,128]{2,1,0:T(8,128)S(1)}, f32[1,64,128]{2,1,0:T(8,128)S(1)}, u32[]{:S(2)}, u32[]{:S(2)}) collective-permute-start(f32[1,64,128]{2,1,0:T(8,128)S(1)} %get-tuple-element.577), channel_id=1, source_target_pairs={{4,0},{8,4},{12,8},{16,12},{20,16},{24,20},{28,24},{32,28},{36,32}... | collective-permute-start | bytes 98312 | tf_op jit(solution)/shard_map/while/body/eval_jaxpr/ppermute | solution.py:20
  244.5 4.5 %collective-permute-start.7 = (f32[10,1,128]{2,1,0:T(1,128)S(1)}, f32[10,1,128]{2,1,0:T(1,128)S(1)}, u32[]{:S(2)}, u32[]{:S(2)}) collective-permute-start(f32[10,1,128]{2,1,0:T(1,128)S(1)} %get-tuple-element.579), channel_id=1, source_target_pairs={{1,0},{2,1},{3,2},{0,3},{5,4},{6,5},{7,6},{4,7},{9,8},{10,9},{11,1... | collective-permute-start | bytes 15368 | tf_op jit(solution)/shard_map/while/body/eval_jaxpr/ppermute | solution.py:20
  250.6 7.7 %collective-permute-start.4 = (f32[1,64,128]{2,1,0:T(8,128)S(1)}, f32[1,64,128]{2,1,0:T(8,128)S(1)}, u32[]{:S(2)}, u32[]{:S(2)}) collective-permute-start(f32[1,64,128]{2,1,0:T(8,128)S(1)} %get-tuple-element.576), channel_id=1, source_target_pairs={{0,4},{4,8},{8,12},{12,16},{16,20},{20,24},{24,28},{28,32},{32,36}... | collective-permute-start | bytes 98312 | tf_op jit(solution)/shard_map/while/body/eval_jaxpr/ppermute | solution.py:18
  250.7 7.6 %collective-permute-start.5 = (f32[1,64,128]{2,1,0:T(8,128)S(1)}, f32[1,64,128]{2,1,0:T(8,128)S(1)}, u32[]{:S(2)}, u32[]{:S(2)}) collective-permute-start(f32[1,64,128]{2,1,0:T(8,128)S(1)} %get-tuple-element.577), channel_id=1, source_target_pairs={{4,0},{8,4},{12,8},{16,12},{20,16},{24,20},{28,24},{32,28},{36,32}... | collective-permute-start | bytes 98312 | tf_op jit(solution)/shard_map/while/body/eval_jaxpr/ppermute | solution.py:20
  259.0 4.5 %collective-permute-start.7 = (f32[10,1,128]{2,1,0:T(1,128)S(1)}, f32[10,1,128]{2,1,0:T(1,128)S(1)}, u32[]{:S(2)}, u32[]{:S(2)}) collective-permute-start(f32[10,1,128]{2,1,0:T(1,128)S(1)} %get-tuple-element.579), channel_id=1, source_target_pairs={{1,0},{2,1},{3,2},{0,3},{5,4},{6,5},{7,6},{4,7},{9,8},{10,9},{11,1... | collective-permute-start | bytes 15368 | tf_op jit(solution)/shard_map/while/body/eval_jaxpr/ppermute | solution.py:20
  265.2 12.5 %collective-permute-start.21 = (f32[1,64,128]{2,1,0:T(8,128)S(1)}, f32[1,64,128]{2,1,0:T(8,128)S(1)}, u32[]{:S(2)}, u32[]{:S(2)}) collective-permute-start(f32[1,64,128]{2,1,0:T(8,128)S(1)} %get-tuple-element.350), channel_id=1, source_target_pairs={{4,0},{8,4},{12,8},{16,12},{20,16},{24,20},{28,24},{32,28},{36,32}... | collective-permute-start | bytes 98312 | tf_op jit(solution)/shard_map/ppermute | solution.py:20
  270.7 7.0 %collective-permute-start.23 = (f32[1,64,128]{2,1,0:T(8,128)S(1)}, f32[1,64,128]{2,1,0:T(8,128)S(1)}, u32[]{:S(2)}, u32[]{:S(2)}) collective-permute-start(f32[1,64,128]{2,1,0:T(8,128)S(1)} %get-tuple-element.351), channel_id=1, source_target_pairs={{0,4},{4,8},{8,12},{12,16},{16,20},{20,24},{24,28},{28,32},{32,36}... | collective-permute-start | bytes 98312 | tf_op jit(solution)/shard_map/ppermute | solution.py:18
  270.7 10.4 %collective-permute-start.22 = (f32[3,1,64,128]{3,2,1,0:T(8,128)S(1)}, f32[3,1,64,128]{3,2,1,0:T(8,128)S(1)}, u32[]{:S(2)}, u32[]{:S(2)}) collective-permute-start(f32[3,1,64,128]{3,2,1,0:T(8,128)S(1)} %get-tuple-element.330), channel_id=1, source_target_pairs={{0,4},{4,8},{8,12},{12,16},{16,20},{20,24},{24,28},{28,32},{32,36}... | collective-permute-start | bytes 294920 | tf_op jit(solution)/shard_map/ppermute | solution.py:18
  270.8 10.3 %collective-permute-start.20 = (f32[3,1,64,128]{3,2,1,0:T(8,128)S(1)}, f32[3,1,64,128]{3,2,1,0:T(8,128)S(1)}, u32[]{:S(2)}, u32[]{:S(2)}) collective-permute-start(f32[3,1,64,128]{3,2,1,0:T(8,128)S(1)} %get-tuple-element.331), channel_id=1, source_target_pairs={{4,0},{8,4},{12,8},{16,12},{20,16},{24,20},{28,24},{32,28},{36,32}... | collective-permute-start | bytes 294920 | tf_op jit(solution)/shard_map/ppermute | solution.py:20
  277.8 6.7 %collective-permute-start.25 = (f32[10,1,128]{2,1,0:T(1,128)S(1)}, f32[10,1,128]{2,1,0:T(1,128)S(1)}, u32[]{:S(2)}, u32[]{:S(2)}) collective-permute-start(f32[10,1,128]{2,1,0:T(1,128)S(1)} %get-tuple-element.342), channel_id=1, source_target_pairs={{1,0},{2,1},{3,2},{0,3},{5,4},{6,5},{7,6},{4,7},{9,8},{10,9},{11,1... | collective-permute-start | bytes 15368 | tf_op jit(solution)/shard_map/ppermute | solution.py:20
  279.6 4.8 %collective-permute-start.27 = (f32[10,1,128]{2,1,0:T(1,128)S(1)}, f32[10,1,128]{2,1,0:T(1,128)S(1)}, u32[]{:S(2)}, u32[]{:S(2)}) collective-permute-start(f32[10,1,128]{2,1,0:T(1,128)S(1)} %get-tuple-element.343), channel_id=1, source_target_pairs={{0,1},{1,2},{2,3},{3,0},{4,5},{5,6},{6,7},{7,4},{8,9},{9,10},{10,1... | collective-permute-start | bytes 15368 | tf_op jit(solution)/shard_map/ppermute | solution.py:18
  281.1 4.7 %collective-permute-start.24 = (f32[3,10,1,128]{3,2,1,0:T(1,128)S(1)}, f32[3,10,1,128]{3,2,1,0:T(1,128)S(1)}, u32[]{:S(2)}, u32[]{:S(2)}) collective-permute-start(f32[3,10,1,128]{3,2,1,0:T(1,128)S(1)} %get-tuple-element.326), channel_id=1, source_target_pairs={{1,0},{2,1},{3,2},{0,3},{5,4},{6,5},{7,6},{4,7},{9,8},{10,9},{11,1... | collective-permute-start | bytes 46088 | tf_op jit(solution)/shard_map/ppermute | solution.py:20
  281.8 4.0 %collective-permute-start.26 = (f32[3,10,1,128]{3,2,1,0:T(1,128)S(1)}, f32[3,10,1,128]{3,2,1,0:T(1,128)S(1)}, u32[]{:S(2)}, u32[]{:S(2)}) collective-permute-start(f32[3,10,1,128]{3,2,1,0:T(1,128)S(1)} %get-tuple-element.327), channel_id=1, source_target_pairs={{0,1},{1,2},{2,3},{3,0},{4,5},{5,6},{6,7},{7,4},{8,9},{9,10},{10,1... | collective-permute-start | bytes 46088 | tf_op jit(solution)/shard_map/ppermute | solution.py:18
  (36 other events, 128.2 us)
where the time goes:
time: 289 us; the launch traced here: 288 us
  starting transfers between devices  134 us (46%)
  waiting for transfers between devices  74.2 us (26%)
  other arithmetic  56.7 us (20%)
  local copies, waits for them, and re-layouts  10.2 us (4%)
  blocking collectives  9.67 us (3%)
    ppermute x34, starting transfers between devices, with_halo(): lax.ppermute(head, axis, [((i + 1) % count, i) for i in range(count)])  97.7 us
    ppermute x34, waiting for transfers between devices, with_halo(): lax.ppermute(head, axis, [((i + 1) % count, i) for i in range(count)])  49.7 us
    ppermute x34, starting transfers between devices, with_halo(): lax.ppermute(tail, axis, [(i, (i + 1) % count) for i in range(count)])  36.3 us
    reduce_sum x4, other arithmetic, one_block(): return jnp.sum(jnp.where(adjacent, term, 0.0), axis=1)  27.7 us
    ppermute x34, waiting for transfers between devices, with_halo(): lax.ppermute(tail, axis, [(i, (i + 1) % count) for i in range(count)])  24.5 us
    div x12, other arithmetic, relax(): return numer / denom  17.3 us
    all_gather x1, blocking collectives, per_device(): lax.all_gather(charges, 'narrow', axis=1, tiled=True)  9.67 us
  transfers between devices with their start and end apart: 68, of which 41 were waited for; matrix products, arithmetic and copies ran while one was open for 18% of the time, Pallas kernels for 0%

commit v1 on v0

--- a/solution.py
+++ b/solution.py
@@ -114,6 +114,42 @@
 
     shaped = tuple((arr.reshape(-1, 128) for arr in (node_z, node_y, node_x, node_tile)))
     return lax.map(one_block, shaped).reshape(-1)
+
+
+def ring(x, axis, shift):
+    count = lax.axis_size(axis)
+    return lax.ppermute(x, axis, [(i, (i + shift) % count) for i in range(count)])
+
+
+def deep_halo(items, axis_z, axis_y):
+    for back, axis in ((3, axis_z), (2, axis_y)):
+        tops, bots = [], []
+        for a, w in items:
+            dim = a.ndim - back
+            n = a.shape[dim]
+            tops.append(lax.slice_in_dim(a, n - w, n, axis=dim))
+            bots.append(lax.slice_in_dim(a, 0, w, axis=dim))
+        minor = items[0][0].shape[-1]
+        top = jnp.concatenate([t.reshape(-1, minor) for t in tops], axis=0)
+        bot = jnp.concatenate([b.reshape(-1, minor) for b in bots], axis=0)
+        below = ring(top, axis, 1)
+        above = ring(bot, axis, -1)
+        out, at = [], 0
+        for (a, w), t in zip(items, tops):
+            size = t.size // minor
+            lo = below[at:at + size].reshape(t.shape)
+            hi = above[at:at + size].reshape(t.shape)
+            at += size
+            out.append((jnp.concatenate([lo, a, hi], axis=a.ndim - back), w))
+        items = out
+    return [a for a, _ in items]
+
+
+def box(a, have, want):
+    cut = have - want
+    if cut == 0:
+        return a
+    return a[..., cut:a.shape[-3] - cut, cut:a.shape[-2] - cut, :]
 
 
 def per_device(
@@ -164,20 +200,25 @@
     electrode = jnp.zeros((depth * height * width,), jnp.float32).at[index].add(values)
     electrode = electrode.reshape(depth, height, width)
     charge_num = valence.astype(jnp.float32)
-    perm_pad = with_halo(permittivity, (("wide", 0), ("narrow", 1)), 1)
+    deep = SWEEPS + 1
     field = potential
     species = concentration
+    perm_ext = None
     for step in range(STEPS):
         source = jnp.sum(charge_num[:, None, None, None] * species, axis=0) + electrode
-
-        def single(turn, current):
-            padded = with_halo(current, (("wide", 0), ("narrow", 1)), 1)
-            return relax(padded, perm_pad, source)
-
-        field = lax.fori_loop(0, SWEEPS, single, field)
-        field_pad = with_halo(field, (("wide", 0), ("narrow", 1)), 1)
-        species_pad = with_halo(species, (("wide", 1), ("narrow", 2)), 1)
-        species = transport(species_pad, field_pad, diffusivity, charge_num)
+        items = [(field, deep), (source, deep - 1), (species, 1)]
+        if perm_ext is None:
+            items.append((permittivity, deep))
+        got = deep_halo(items, "wide", "narrow")
+        field_e, source_e, species_e = got[0], got[1], got[2]
+        if perm_ext is None:
+            perm_ext = got[3]
+        have = deep
+        for sweep in range(SWEEPS):
+            field_e = relax(field_e, box(perm_ext, deep, have), box(source_e, deep - 1, have - 1))
+            have -= 1
+        species = transport(species_e, field_e, diffusivity, charge_num)
+        field = field_e[1:-1, 1:-1]
     return (species, field)
 
 

time: 289 us -> 199 us (0.69)
  starting transfers between devices: 134 us -> 19.3 us
  local copies, waits for them, and re-layouts: 10.2 us -> 61.8 us
  waiting for transfers between devices: 74.2 us -> 43.4 us
  other arithmetic: 56.7 us -> 60.1 us
    ppermute x68 -> x8, starting transfers between devices: 134 us -> 19.3 us  [ring(): lax.ppermute(x, axis, [(i, (i + shift) % count) for i in range(count)])]
    ppermute x68 -> x8, waiting for transfers between devices: 74.2 us -> 43.4 us  [ring(): lax.ppermute(x, axis, [(i, (i + shift) % count) for i in range(count)])]
    slice x35 -> x43, local copies, waits for them, and re-layouts: 4.71 us -> 28.8 us  [the longest x6 7.3 us: relax(): perm_centre[..., -1:]]
    unnamed x47 -> x188, local copies, waits for them, and re-layouts: 1.5 us -> 21.7 us
    reshape x0 -> x28, local copies, waits for them, and re-layouts: none -> 6.04 us  [the longest x7 3.65 us: deep_halo(): lo = below[at:at + size].reshape(t.shape)]
    concatenate x0 -> x14, other arithmetic: none -> 4.42 us  [the longest x6 4.18 us: deep_halo(): out.append((jnp.concatenate([lo, a, hi], axis=a.ndim - back), w))]
    slice x12, local copies, waits for them, and re-layouts: 1.55 us -> 4.97 us  [relax(): upper_field = jnp.concatenate([centre[..., 1:], zeros_edge], axis=-1)]
  transfers between devices with their start and end apart: 68 -> 8, of which waited for: 41 -> 6; matrix products, arithmetic and copies ran while one was open for 18% -> 0% of each run, Pallas kernels for 0% -> 0%
where the time goes in v1:
time: 199 us; the launch traced here: 198 us
  local copies, waits for them, and re-layouts  61.8 us (31%)
  other arithmetic  60.1 us (30%)
  waiting for transfers between devices  43.4 us (22%)
  starting transfers between devices  19.3 us (10%)
  blocking collectives  10.4 us (5%)
  between operations  2.68 us (1%)
    ppermute x8, waiting for transfers between devices, ring(): lax.ppermute(x, axis, [(i, (i + shift) % count) for i in range(count)])  43.4 us
    reduce_sum x4, other arithmetic, one_block(): return jnp.sum(jnp.where(adjacent, term, 0.0), axis=1)  27.7 us
    unnamed x188, local copies, waits for them, and re-layouts  21.7 us
    ppermute x8, starting transfers between devices, ring(): lax.ppermute(x, axis, [(i, (i + shift) % count) for i in range(count)])  19.3 us
    div x12, other arithmetic, relax(): return numer / denom  18.1 us
    all_gather x1, blocking collectives, per_device(): lax.all_gather(charges, 'narrow', axis=1, tiled=True)  10.4 us
    slice x6, local copies, waits for them, and re-layouts, relax(): perm_centre[..., -1:]  7.3 us
    slice x6, local copies, waits for them, and re-layouts, relax(): perm_centre[..., 1:]  7.26 us
  transfers between devices with their start and end apart: 8, of which 6 were waited for; matrix products, arithmetic and copies ran while one was open for 0% of the time, Pallas kernels for 0%

profile of v1, /device:TPU:1, one launch (start us, length us, event | category | flops | bytes accessed | tf_op | source)
XLA Modules:
  0.0 197.7 jit_solution(9004602825562309416)
XLA Ops:
  1.4 1.1 fusion.248
  3.3 10.4 %all_gather.3 = f32[5,8192]{1,0:T(8,128)S(1)} all-gather(f32[5,2048]{1,0:T(8,128)S(1)} %pad_maximum_fusion.50), channel_id=1, replica_groups=mesh['wide'=64,'narrow'=4] {'narrow'}, dimensions={1}, use_global_device_ids=true | all-gather | bytes 204800 | tf_op jit(solution)/shard_map/all_gather | solution.py:191
  13.8 28.1 %while.10 = (s32[]{:T(128)}, f32[4,128]{1,0:T(4,128)S(1)}, f32[4,128]{1,0:T(4,128)S(1)}, f32[1,8192]{1,0:T(1,128)S(1)}, f32[1,8192]{1,0:T(1,128)S(1)}, /*index=5...) while((s32[]{:T(128)}, f32[4,128]{1,0:T(4,128)S(1)}, ...), condition=%wide.region_3.4_spmd, body=%wide.region_1.3_spmd.sunk | while | flops 34602880 | bytes 171665 | solution.py:116
  13.9 6.9 %select_reduce_fusion.2 = f32[128]{0:T(128)S(1)} fusion(f32[8192]{0:T(1024)S(1)} %get-tuple-element.307, f32[128]{0:T(128)S(1)} %get-tuple-element.267, f32[8192]{0:T(1024)S(1)} %get-tuple-element.305, f32[128]{0:T(128)S(1)} %get-tuple-element.268, f32[8192]{0:T(1024)S(1)} %get-tuple-element.303, f32[128]{0:T(128)S(1)} %get-tuple-element.269, ...), kind=kLoop, calls=%fused_computation.11.clone.1 | loop fusion | flops 34602880 | bytes 166400 | tf_op jit(solution)/shard_map/while/body/eval_jaxpr/reduce_sum | solution.py:113
  20.9 6.9 %select_reduce_fusion.2 = f32[128]{0:T(128)S(1)} fusion(f32[8192]{0:T(1024)S(1)} %get-tuple-element.307, f32[128]{0:T(128)S(1)} %get-tuple-element.267, f32[8192]{0:T(1024)S(1)} %get-tuple-element.305, f32[128]{0:T(128)S(1)} %get-tuple-element.268, f32[8192]{0:T(1024)S(1)} %get-tuple-element.303, f32[128]{0:T(128)S(1)} %get-tuple-element.269, ...), kind=kLoop, calls=%fused_computation.11.clone.1 | loop fusion | flops 34602880 | bytes 166400 | tf_op jit(solution)/shard_map/while/body/eval_jaxpr/reduce_sum | solution.py:113
  27.9 6.9 %select_reduce_fusion.2 = f32[128]{0:T(128)S(1)} fusion(f32[8192]{0:T(1024)S(1)} %get-tuple-element.307, f32[128]{0:T(128)S(1)} %get-tuple-element.267, f32[8192]{0:T(1024)S(1)} %get-tuple-element.305, f32[128]{0:T(128)S(1)} %get-tuple-element.268, f32[8192]{0:T(1024)S(1)} %get-tuple-element.303, f32[128]{0:T(128)S(1)} %get-tuple-element.269, ...), kind=kLoop, calls=%fused_computation.11.clone.1 | loop fusion | flops 34602880 | bytes 166400 | tf_op jit(solution)/shard_map/while/body/eval_jaxpr/reduce_sum | solution.py:113
  34.9 6.9 %select_reduce_fusion.2 = f32[128]{0:T(128)S(1)} fusion(f32[8192]{0:T(1024)S(1)} %get-tuple-element.307, f32[128]{0:T(128)S(1)} %get-tuple-element.267, f32[8192]{0:T(1024)S(1)} %get-tuple-element.305, f32[128]{0:T(128)S(1)} %get-tuple-element.268, f32[8192]{0:T(1024)S(1)} %get-tuple-element.303, f32[128]{0:T(128)S(1)} %get-tuple-element.269, ...), kind=kLoop, calls=%fused_computation.11.clone.1 | loop fusion | flops 34602880 | bytes 166400 | tf_op jit(solution)/shard_map/while/body/eval_jaxpr/reduce_sum | solution.py:113
  42.5 3.3 %scatter_custom_fusion = f32[65536]{0:T(1024)S(1)} fusion(s32[512]{0:T(512)S(1)} %bitcast.117, f32[512]{0:T(512)S(1)} %multiply_bitcast_fusion, f32[]{:T(128)} %constant.114.clone.1), kind=kCustom, calls=%fused_computation.342 | custom fusion | flops 512 | bytes 262148 | tf_op jit(solution)/shard_map/scatter-add | solution.py:200
  46.6 7.1 %collective-permute-start = (f32[1472,128]{1,0:T(8,128)S(1)}, f32[1472,128]{1,0:T(8,128)S(1)}, u32[]{:S(2)}, u32[]{:S(2)}) collective-permute-start(f32[1472,128]{1,0:T(8,128)S(1)} %pad_maximum_fusion.21), channel_id=1, source_target_pairs={{0,252},{4,0},{8,4},{12,8},{16,12},{20,16},{24,20},{28,24},{32,28}... | collective-permute-start | bytes 2261000 | tf_op jit(solution)/shard_map/ppermute | solution.py:121
  53.9 15.9 %collective-permute-done = f32[1472,128]{1,0:T(8,128)S(1)} collective-permute-done((f32[1472,128]{1,0:T(8,128)S(1)}, f32[1472,128]{1,0:T(8,128)S(1)}, u32[]{:S(2)}, u32[]{:S(2)}) %collective-permute-start) | collective-permute-done | bytes 753696 | tf_op jit(solution)/shard_map/ppermute | solution.py:121
  69.9 6.2 %collective-permute-done.1 = f32[1472,128]{1,0:T(8,128)S(1)} collective-permute-done((f32[1472,128]{1,0:T(8,128)S(1)}, f32[1472,128]{1,0:T(8,128)S(1)}, u32[]{:S(2)}, u32[]{:S(2)}) %collective-permute-start.1) | collective-permute-done | bytes 753696 | tf_op jit(solution)/shard_map/ppermute | solution.py:121
  77.1 0.9 slice.1072
  78.2 1.0 slice.1070
  80.0 1.4 collective-permute-start.3
  81.4 2.8 %collective-permute-start.2 = (f32[458,128]{1,0:T(8,128)S(1)}, f32[458,128]{1,0:T(8,128)S(1)}, u32[]{:S(2)}, u32[]{:S(2)}) collective-permute-start(f32[458,128]{1,0:T(8,128)S(1)} %pad_maximum_fusion.31), channel_id=1, source_target_pairs={{0,1},{1,2},{2,3},{3,0},{4,5},{5,6},{6,7},{7,4},{8,9},{9,10},{10,1... | collective-permute-start | bytes 703496 | tf_op jit(solution)/shard_map/ppermute | solution.py:121
  84.8 3.5 %collective-permute-done.3 = f32[458,128]{1,0:T(8,128)S(1)} collective-permute-done((f32[458,128]{1,0:T(8,128)S(1)}, f32[458,128]{1,0:T(8,128)S(1)}, u32[]{:S(2)}, u32[]{:S(2)}) %collective-permute-start.3) | collective-permute-done | bytes 234528 | tf_op jit(solution)/shard_map/ppermute | solution.py:121
  90.5 1.5 pad_maximum_fusion
  92.0 1.5 fusion.226
  93.5 1.5 fusion.227
  95.0 1.4 fusion.224
  96.3 1.4 fusion.225
  97.7 1.2 fusion.222
  98.9 1.3 fusion.223
  100.2 1.2 fusion.220
  101.4 1.1 fusion.221
  102.5 0.9 fusion.218
  103.4 1.1 fusion.219
  104.5 1.0 fusion.216
  105.5 1.0 fusion.217
  106.5 1.5 fusion.228
  108.0 1.5 slice.1076
  109.5 1.5 reshape.275
  110.9 1.5 slice.1075
  112.4 1.5 reshape.270
  113.9 1.3 pad_maximum_fusion.3
  115.5 3.5 %fusion.29 = f32[20,76,128]{2,1,0:T(8,128)S(1)} fusion(f32[22,78,128]{2,1,0:T(8,128)S(1)} %get-tuple-element.195, f32[20,76,127]{2,1,0:T(8,128)} %get-tuple-element.126, f32[20,76,127]{2,1,0:T(8,128)} %get-tuple-element.125, f32[22,78,128]{2,1,0:T(8,128)S(1)} %get-tuple-element.194, f32[20,76,127]{2,1,0:T(8,128)S(1)} %copy-done.3, ...), kind=kLoop, calls=%fused_computation.47 | loop fusion | flops 7004160 | bytes 11661440 | tf_op jit(solution)/shard_map/div | solution.py:51
  120.8 1.4 fusion.103
  123.8 1.1 fusion.123
  126.4 1.0 fusion.143
  128.7 0.9 fusion.163
  130.9 1.6 fusion.183
  132.6 0.9 fusion.243
  133.5 0.8 fusion.244
  136.9 0.9 multiply_reduce_fusion
  138.9 1.5 collective-permute-start.5
  140.5 10.0 %collective-permute-done.4 = f32[1024,128]{1,0:T(8,128)S(1)} collective-permute-done((f32[1024,128]{1,0:T(8,128)S(1)}, f32[1024,128]{1,0:T(8,128)S(1)}, u32[]{:S(2)}, u32[]{:S(2)}) %collective-permute-start.4) | collective-permute-done | bytes 524320 | tf_op jit(solution)/shard_map/ppermute | solution.py:121
  150.5 4.4 %collective-permute-done.5 = f32[1024,128]{1,0:T(8,128)S(1)} collective-permute-done((f32[1024,128]{1,0:T(8,128)S(1)}, f32[1024,128]{1,0:T(8,128)S(1)}, u32[]{:S(2)}, u32[]{:S(2)}) %collective-permute-start.5) | collective-permute-done | bytes 524320 | tf_op jit(solution)/shard_map/ppermute | solution.py:121
  155.5 0.9 slice.1193
  156.5 1.0 slice.1191
  158.3 2.8 %collective-permute-start.7 = (f32[304,128]{1,0:T(8,128)S(1)}, f32[304,128]{1,0:T(8,128)S(1)}, u32[]{:S(2)}, u32[]{:S(2)}) collective-permute-start(f32[304,128]{1,0:T(8,128)S(1)} %pad_maximum_fusion.34), channel_id=1, source_target_pairs={{0,3},{1,0},{2,1},{3,2},{4,7},{5,4},{6,5},{7,6},{8,11},{9,8},{10,9... | collective-permute-start | bytes 466952 | tf_op jit(solution)/shard_map/ppermute | solution.py:121
  161.1 3.5 %collective-permute-start.6 = (f32[304,128]{1,0:T(8,128)S(1)}, f32[304,128]{1,0:T(8,128)S(1)}, u32[]{:S(2)}, u32[]{:S(2)}) collective-permute-start(f32[304,128]{1,0:T(8,128)S(1)} %pad_maximum_fusion.33), channel_id=1, source_target_pairs={{0,1},{1,2},{2,3},{3,0},{4,5},{5,6},{6,7},{7,4},{8,9},{9,10},{10,1... | collective-permute-start | bytes 466952 | tf_op jit(solution)/shard_map/ppermute | solution.py:121
  164.6 3.4 %collective-permute-done.7 = f32[304,128]{1,0:T(8,128)S(1)} collective-permute-done((f32[304,128]{1,0:T(8,128)S(1)}, f32[304,128]{1,0:T(8,128)S(1)}, u32[]{:S(2)}, u32[]{:S(2)}) %collective-permute-start.7) | collective-permute-done | bytes 155680 | tf_op jit(solution)/shard_map/ppermute | solution.py:121
  169.4 1.3 pad_maximum_fusion.2
  170.7 1.4 fusion.215
  172.1 0.8 slice.1196
  173.0 1.5 slice.1195
  174.4 0.8 reshape.297
  175.4 1.0 copy-done.2
  176.7 3.7 %fusion.22 = f32[20,76,128]{2,1,0:T(8,128)S(1)} fusion(f32[22,78,128]{2,1,0:T(8,128)S(1)} %pad_maximum_fusion.2, f32[20,76,127]{2,1,0:T(8,128)} %get-tuple-element.100, f32[20,76,127]{2,1,0:T(8,128)} %get-tuple-element.99, f32[22,78,128]{2,1,0:T(8,128)S(1)} %get-tuple-element.194, f32[20,76,127]{2,1,0:T(8,128)S(1)} %copy-done.4, ...), kind=kLoop, calls=%fused_computation.36 | loop fusion | flops 7004160 | bytes 11661440 | tf_op jit(solution)/shard_map/div | solution.py:51
  182.1 1.4 fusion.96
  185.1 1.1 fusion.116
  187.7 1.0 fusion.136
  190.1 0.9 fusion.156
  196.0 1.8 fusion.47
  (295 shorter events, 32.7 us)
Async XLA Ops:
  0.6 1.8 copy-start
  1.4 1.3 copy-start.91
  42.5 3.4 %copy-start.38 = (f32[8,64,128]{2,1,0:T(8,128)S(1)}, f32[8,64,128]{2,1,0:T(8,128)}, u32[]{:S(2)}) copy-start(f32[8,64,128]{2,1,0:T(8,128)} %param.13) | copy-start | bytes 786436
  46.6 23.2 %collective-permute-start = (f32[1472,128]{1,0:T(8,128)S(1)}, f32[1472,128]{1,0:T(8,128)S(1)}, u32[]{:S(2)}, u32[]{:S(2)}) collective-permute-start(f32[1472,128]{1,0:T(8,128)S(1)} %pad_maximum_fusion.21), channel_id=1, source_target_pairs={{0,252},{4,0},{8,4},{12,8},{16,12},{20,16},{24,20},{28,24},{32,28}... | collective-permute-start | bytes 2261000 | tf_op jit(solution)/shard_map/ppermute | solution.py:121
  53.8 23.1 %copy-start.13 = (f32[8,64,128]{2,1,0:T(8,128)S(1)}, f32[8,64,128]{2,1,0:T(8,128)}, u32[]{:S(2)}) copy-start(f32[8,64,128]{2,1,0:T(8,128)} %param.14) | copy-start | bytes 786436
  53.8 22.3 %collective-permute-start.1 = (f32[1472,128]{1,0:T(8,128)S(1)}, f32[1472,128]{1,0:T(8,128)S(1)}, u32[]{:S(2)}, u32[]{:S(2)}) collective-permute-start(f32[1472,128]{1,0:T(8,128)S(1)} %pad_maximum_fusion.22), channel_id=1, source_target_pairs={{0,4},{4,8},{8,12},{12,16},{16,20},{20,24},{24,28},{28,32},{32,36}... | collective-permute-start | bytes 2261000 | tf_op jit(solution)/shard_map/ppermute | solution.py:121
  69.9 7.0 %copy-start.39 = (f32[448,128]{1,0:T(8,128)}, f32[448,128]{1,0:T(8,128)S(1)}, u32[]{:S(2)}) copy-start(f32[448,128]{1,0:T(8,128)S(1)} %get-tuple-element.138) | copy-start | bytes 688132
  69.9 10.0 %copy-start.56 = (f32[448,128]{1,0:T(8,128)}, f32[448,128]{1,0:T(8,128)S(1)}, u32[]{:S(2)}) copy-start(f32[448,128]{1,0:T(8,128)S(1)} %get-tuple-element.137) | copy-start | bytes 688132
  76.1 3.8 %copy-start.57 = (f32[448,128]{1,0:T(8,128)}, f32[448,128]{1,0:T(8,128)S(1)}, u32[]{:S(2)}) copy-start(f32[448,128]{1,0:T(8,128)S(1)} %get-tuple-element.135) | copy-start | bytes 688132
  77.1 2.1 %copy-start.66 = (f32[192,128]{1,0:T(8,128)}, f32[192,128]{1,0:T(8,128)S(1)}, u32[]{:S(2)}) copy-start(f32[192,128]{1,0:T(8,128)S(1)} %slice.1066) | copy-start | bytes 294916
  78.0 1.2 copy-start.68
  79.9 4.3 %copy-start.93 = (s32[3]{0:T(128)S(1)}, s32[3]{0:T(128)}, u32[]{:S(2)}) copy-start(s32[3]{0:T(128)} %param.16) | copy-start | bytes 40
  80.0 8.3 %collective-permute-start.3 = (f32[458,128]{1,0:T(8,128)S(1)}, f32[458,128]{1,0:T(8,128)S(1)}, u32[]{:S(2)}, u32[]{:S(2)}) collective-permute-start(f32[458,128]{1,0:T(8,128)S(1)} %pad_maximum_fusion.32), channel_id=1, source_target_pairs={{0,3},{1,0},{2,1},{3,2},{4,7},{5,4},{6,5},{7,6},{8,11},{9,8},{10,9... | collective-permute-start | bytes 703496 | tf_op jit(solution)/shard_map/ppermute | solution.py:121
  81.4 7.6 %collective-permute-start.2 = (f32[458,128]{1,0:T(8,128)S(1)}, f32[458,128]{1,0:T(8,128)S(1)}, u32[]{:S(2)}, u32[]{:S(2)}) collective-permute-start(f32[458,128]{1,0:T(8,128)S(1)} %pad_maximum_fusion.31), channel_id=1, source_target_pairs={{0,1},{1,2},{2,3},{3,0},{4,5},{5,6},{6,7},{7,4},{8,9},{9,10},{10,1... | collective-permute-start | bytes 703496 | tf_op jit(solution)/shard_map/ppermute | solution.py:121
  89.0 3.0 %copy-start.72 = (f32[22,7,128]{2,1,0:T(8,128)}, f32[22,7,128]{2,1,0:T(8,128)S(1)}, u32[]{:S(2)}) copy-start(f32[22,7,128]{2,1,0:T(8,128)S(1)} %reshape.277) | copy-start | bytes 236548
  89.0 2.9 %copy-start.74 = (f32[22,7,128]{2,1,0:T(8,128)}, f32[22,7,128]{2,1,0:T(8,128)S(1)}, u32[]{:S(2)}) copy-start(f32[22,7,128]{2,1,0:T(8,128)S(1)} %reshape.276) | copy-start | bytes 236548
  103.4 24.2 %copy-start.30 = (f32[12,68,127]{2,1,0:T(8,128)}, f32[12,68,127]{2,1,0:T(8,128)S(1)}, u32[]{:S(2)}) copy-start(f32[12,68,127]{2,1,0:T(8,128)S(1)} %get-tuple-element.105) | copy-start | bytes 1243588
  113.9 1.4 copy-start.1
  113.9 1.7 copy-start.3
  119.0 1.1 copy-start.5
  119.0 1.3 copy-start.7
  119.0 1.5 copy-start.9
  119.1 1.8 copy-start.11
  122.2 1.2 copy-start.16
  122.2 1.4 copy-start.18
  122.2 1.6 copy-start.20
  124.9 1.2 copy-start.24
  124.9 1.3 copy-start.26
  125.0 1.5 copy-start.28
  127.4 1.1 copy-start.34
  127.5 1.3 copy-start.36
  128.7 1.1 copy-start.49
  129.6 1.2 copy-start.43
  129.6 1.3 copy-start.45
  129.6 1.3 copy-start.73
  129.6 1.3 copy-start.75
  133.5 24.0 %copy-start.53 = (f32[8,64,128]{2,1,0:T(8,128)}, f32[8,64,128]{2,1,0:T(8,128)S(1)}, u32[]{:S(2)}) copy-start(f32[8,64,128]{2,1,0:T(8,128)S(1)} %get-tuple-element.168) | copy-start | bytes 786436
  133.5 2.4 %copy-start.86 = (f32[3]{0:T(128)S(1)}, f32[3]{0:T(128)}, u32[]{:S(2)}) copy-start(f32[3]{0:T(128)} %broadcast_multiply_fusion) | copy-start | bytes 40
  138.8 11.7 %collective-permute-start.4 = (f32[1024,128]{1,0:T(8,128)S(1)}, f32[1024,128]{1,0:T(8,128)S(1)}, u32[]{:S(2)}, u32[]{:S(2)}) collective-permute-start(f32[1024,128]{1,0:T(8,128)S(1)} %pad_maximum_fusion.23), channel_id=1, source_target_pairs={{0,252},{4,0},{8,4},{12,8},{16,12},{20,16},{24,20},{28,24},{32,28}... | collective-permute-start | bytes 1572872 | tf_op jit(solution)/shard_map/ppermute | solution.py:121
  138.9 15.9 %collective-permute-start.5 = (f32[1024,128]{1,0:T(8,128)S(1)}, f32[1024,128]{1,0:T(8,128)S(1)}, u32[]{:S(2)}, u32[]{:S(2)}) collective-permute-start(f32[1024,128]{1,0:T(8,128)S(1)} %pad_maximum_fusion.24), channel_id=1, source_target_pairs={{0,4},{4,8},{8,12},{12,16},{16,20},{20,24},{24,28},{28,32},{32,36}... | collective-permute-start | bytes 1572872 | tf_op jit(solution)/shard_map/ppermute | solution.py:121
  150.5 4.4 %copy-start.77 = (f32[1024,128]{1,0:T(8,128)}, f32[1024,128]{1,0:T(8,128)S(1)}, u32[]{:S(2)}) copy-start(f32[1024,128]{1,0:T(8,128)S(1)} %collective-permute-done.4) | copy-start | bytes 1572868
  158.3 9.7 %collective-permute-start.7 = (f32[304,128]{1,0:T(8,128)S(1)}, f32[304,128]{1,0:T(8,128)S(1)}, u32[]{:S(2)}, u32[]{:S(2)}) collective-permute-start(f32[304,128]{1,0:T(8,128)S(1)} %pad_maximum_fusion.34), channel_id=1, source_target_pairs={{0,3},{1,0},{2,1},{3,2},{4,7},{5,4},{6,5},{7,6},{8,11},{9,8},{10,9... | collective-permute-start | bytes 466952 | tf_op jit(solution)/shard_map/ppermute | solution.py:121
  161.1 6.9 %collective-permute-start.6 = (f32[304,128]{1,0:T(8,128)S(1)}, f32[304,128]{1,0:T(8,128)S(1)}, u32[]{:S(2)}, u32[]{:S(2)}) collective-permute-start(f32[304,128]{1,0:T(8,128)S(1)} %pad_maximum_fusion.33), channel_id=1, source_target_pairs={{0,1},{1,2},{2,3},{3,0},{4,5},{5,6},{6,7},{7,4},{8,9},{9,10},{10,1... | collective-permute-start | bytes 466952 | tf_op jit(solution)/shard_map/ppermute | solution.py:121
  175.3 1.1 copy-start.2
  175.3 1.4 copy-start.4
  180.3 1.1 copy-start.6
  180.4 1.3 copy-start.8
  180.4 1.5 copy-start.10
  180.4 1.8 copy-start.12
  183.5 1.2 copy-start.17
  183.5 1.4 copy-start.19
  183.5 1.6 copy-start.21
  186.2 1.2 copy-start.25
  186.2 1.3 copy-start.27
  186.2 1.5 copy-start.29
  188.7 1.1 copy-start.33
  188.7 1.3 copy-start.35
  188.7 1.4 copy-start.37
  190.1 1.1 copy-start.61
  191.0 1.1 copy-start.46
  191.0 1.2 copy-start.48
  191.0 1.3 copy-start.50
  193.0 1.7 copy-start.88
  193.2 1.8 copy-start.63
  (38 other events, 34.0 us)

commit v2 on v1

--- a/solution.py
+++ b/solution.py
@@ -2,6 +2,8 @@
 import jax.numpy as jnp
 from jax import lax
 from jax.sharding import PartitionSpec as P
+from jax.experimental import pallas as pl
+from jax.experimental.pallas import tpu as pltpu
 
 TILES_DEV = 4
 STEPS = 2
@@ -122,27 +124,137 @@
 
 
 def deep_halo(items, axis_z, axis_y):
-    for back, axis in ((3, axis_z), (2, axis_y)):
+    for back, axis, pick in ((3, axis_z, 1), (2, axis_y, 2)):
         tops, bots = [], []
-        for a, w in items:
+        for item in items:
+            a, w = item[0], item[pick]
             dim = a.ndim - back
             n = a.shape[dim]
             tops.append(lax.slice_in_dim(a, n - w, n, axis=dim))
             bots.append(lax.slice_in_dim(a, 0, w, axis=dim))
         minor = items[0][0].shape[-1]
         top = jnp.concatenate([t.reshape(-1, minor) for t in tops], axis=0)
-        bot = jnp.concatenate([b.reshape(-1, minor) for b in bots], axis=0)
+        bot = jnp.concatenate([t.reshape(-1, minor) for t in bots], axis=0)
         below = ring(top, axis, 1)
         above = ring(bot, axis, -1)
         out, at = [], 0
-        for (a, w), t in zip(items, tops):
+        for item, t in zip(items, tops):
+            a = item[0]
             size = t.size // minor
             lo = below[at:at + size].reshape(t.shape)
             hi = above[at:at + size].reshape(t.shape)
             at += size
-            out.append((jnp.concatenate([lo, a, hi], axis=a.ndim - back), w))
+            out.append((jnp.concatenate([lo, a, hi], axis=a.ndim - back),) + tuple(item[1:]))
         items = out
-    return [a for a, _ in items]
+    return [item[0] for item in items]
+
+
+def step_kernel(dif_ref, val_ref, f_ref, p_ref, s_ref, c_ref, fo_ref, co_ref, fa, fb, w_ref):
+    planes, rows, lanes = f_ref.shape
+    species, inner = c_ref.shape[0], c_ref.shape[1] - 2
+    hz = (planes - inner) // 2
+    hy = (rows - co_ref.shape[2]) // 2
+    out_rows = co_ref.shape[2]
+    lane = lax.broadcasted_iota(jnp.int32, (rows, lanes), 1)
+    top = lane == lanes - 1
+    bot = lane == 0
+
+    def ysh(a, d):
+        return pltpu.roll(a, (-d) % rows, 0)
+
+    def xsh(a, d):
+        return pltpu.roll(a, (-d) % lanes, 1)
+
+    def weights(z, carry):
+        pc = p_ref[z]
+        ws = (
+            0.5 * (pc + p_ref[z + 1]),
+            0.5 * (pc + p_ref[z - 1]),
+            0.5 * (pc + ysh(pc, 1)),
+            0.5 * (pc + ysh(pc, -1)),
+            0.5 * (pc + jnp.where(top, pc, xsh(pc, 1))),
+            0.5 * (pc + jnp.where(bot, pc, xsh(pc, -1))),
+        )
+        den = jnp.zeros_like(pc)
+        for k, w in enumerate(ws):
+            w_ref[k, z] = w
+            den = den + w
+        w_ref[6, z] = den
+        return carry
+
+    lax.fori_loop(1, planes - 1, weights, 0)
+    bufs = (fa, fb)
+    sweeps = hz - 1
+    for k in range(sweeps):
+        rd = f_ref if k == 0 else bufs[(k - 1) % 2]
+        wr = bufs[k % 2]
+
+        def sweep(z, carry, rd=rd, wr=wr):
+            fc = rd[z]
+            numer = s_ref[z]
+            numer = numer + w_ref[0, z] * rd[z + 1]
+            numer = numer + w_ref[1, z] * rd[z - 1]
+            numer = numer + w_ref[2, z] * ysh(fc, 1)
+            numer = numer + w_ref[3, z] * ysh(fc, -1)
+            numer = numer + w_ref[4, z] * jnp.where(top, 0.0, xsh(fc, 1))
+            numer = numer + w_ref[5, z] * jnp.where(bot, 0.0, xsh(fc, -1))
+            wr[z] = numer / w_ref[6, z]
+            return carry
+
+        lax.fori_loop(k + 1, planes - k - 1, sweep, 0)
+    final = bufs[(sweeps - 1) % 2]
+
+    def move(z, carry):
+        zf = z + hz
+        fc = final[zf]
+        fo_ref[z] = fc[hy:hy + out_rows]
+        pairs_field = (final[zf + 1], final[zf - 1], ysh(fc, 1), ysh(fc, -1))
+        fr = xsh(fc, 1)
+        for s in range(species):
+            drift = val_ref[s]
+            c = c_ref[s, z + 1]
+            others = (c_ref[s, z + 2], c_ref[s, z], ysh(c, 1), ysh(c, -1))
+            total = jnp.zeros_like(c)
+            for other, other_field in zip(others, pairs_field):
+                total = total + (c - other) - drift * 0.5 * (c + other) * (other_field - fc)
+            right = xsh(c, 1)
+            across = c - right - drift * 0.5 * (c + right) * (fr - fc)
+            across = jnp.where(top, 0.0, across)
+            total = total + across
+            total = total - xsh(across, -1)
+            new = c - dif_ref[s] * total
+            co_ref[s, z] = new[hy:hy + out_rows]
+        return carry
+
+    lax.fori_loop(0, inner, move, 0)
+
+
+def time_step(diffusivity, charge_num, field_e, perm_e, source_e, species_e):
+    planes, rows, lanes = field_e.shape
+    species, inner = species_e.shape[0], species_e.shape[1] - 2
+    out_rows = rows - 2 * (SWEEPS + 2)
+    smem = pl.BlockSpec(memory_space=pltpu.SMEM)
+    vmem = pl.BlockSpec(memory_space=pltpu.VMEM)
+    points = planes * rows * lanes
+    return pl.pallas_call(
+        step_kernel,
+        out_shape=(
+            jax.ShapeDtypeStruct((inner, out_rows, lanes), jnp.float32),
+            jax.ShapeDtypeStruct((species, inner, out_rows, lanes), jnp.float32),
+        ),
+        in_specs=[smem, smem, vmem, vmem, vmem, vmem],
+        out_specs=(vmem, vmem),
+        scratch_shapes=[
+            pltpu.VMEM((planes, rows, lanes), jnp.float32),
+            pltpu.VMEM((planes, rows, lanes), jnp.float32),
+            pltpu.VMEM((7, planes, rows, lanes), jnp.float32),
+        ],
+        cost_estimate=pl.CostEstimate(
+            flops=points * (20 * SWEEPS + 20) + species_e.size * 30,
+            transcendentals=0,
+            bytes_accessed=4 * (3 * points + species_e.size + inner * out_rows * lanes * (species + 1)),
+        ),
+    )(diffusivity, charge_num, field_e, perm_e, source_e, species_e)
 
 
 def box(a, have, want):
@@ -201,24 +313,19 @@
     electrode = electrode.reshape(depth, height, width)
     charge_num = valence.astype(jnp.float32)
     deep = SWEEPS + 1
+    wide_y = SWEEPS + 2
     field = potential
     species = concentration
     perm_ext = None
     for step in range(STEPS):
         source = jnp.sum(charge_num[:, None, None, None] * species, axis=0) + electrode
-        items = [(field, deep), (source, deep - 1), (species, 1)]
+        items = [(field, deep, wide_y), (source, deep, wide_y), (species, 1, wide_y)]
         if perm_ext is None:
-            items.append((permittivity, deep))
+            items.append((permittivity, deep, wide_y))
         got = deep_halo(items, "wide", "narrow")
-        field_e, source_e, species_e = got[0], got[1], got[2]
         if perm_ext is None:
             perm_ext = got[3]
-        have = deep
-        for sweep in range(SWEEPS):
-            field_e = relax(field_e, box(perm_ext, deep, have), box(source_e, deep - 1, have - 1))
-            have -= 1
-        species = transport(species_e, field_e, diffusivity, charge_num)
-        field = field_e[1:-1, 1:-1]
+        field, species = time_step(diffusivity, charge_num, got[0], perm_ext, got[1], got[2])
     return (species, field)
 
 

time: 199 us -> 162 us (0.81)
  local copies, waits for them, and re-layouts: 61.8 us -> 3.56 us
  Pallas kernels: 0 us -> 30.1 us
  other arithmetic: 60.1 us -> 44 us
  waiting for transfers between devices: 43.4 us -> 52.9 us
    pallas_call x0 -> x2, Pallas kernels: none -> 30.1 us  [time_step(): pl.pallas_call(step_kernel, out_shape=(jax.ShapeDtypeStruct((inner, out_r...]
    unnamed x188 -> x14, local copies, waits for them, and re-layouts: 21.7 us -> 1.88 us
    slice x24 -> x0, local copies, waits for them, and re-layouts: 19.5 us -> none  [the longest x6 7.3 us: relax(): perm_centre[..., -1:]]
    div x12 -> x0, other arithmetic: 18.1 us -> none  [relax(): return numer / denom]
    ppermute x8, waiting for transfers between devices: 43.4 us -> 52.9 us  [ring(): lax.ppermute(x, axis, [(i, (i + shift) % count) for i in range(count)])]
    slice x12 -> x6, local copies, waits for them, and re-layouts: 6.46 us -> 0.11 us  [deep_halo(): lo = below[at:at + size].reshape(t.shape)]
    slice x12 -> x6, local copies, waits for them, and re-layouts: 5.73 us -> 0.11 us  [deep_halo(): hi = above[at:at + size].reshape(t.shape)]
    reshape x7 -> x2, local copies, waits for them, and re-layouts: 3.65 us -> 0.03 us  [deep_halo(): lo = below[at:at + size].reshape(t.shape)]
  transfers between devices with their start and end apart: 8 -> 8, of which waited for: 6 -> 7; matrix products, arithmetic and copies ran while one was open for 0% -> 0% of each run, Pallas kernels for 0% -> 0%
where the time goes in v2:
time: 162 us
  waiting for transfers between devices  52.9 us (33%)
  other arithmetic  44 us (27%)
  Pallas kernels  30.1 us (19%)
  starting transfers between devices  19.2 us (12%)
  blocking collectives  10.4 us (6%)
  local copies, waits for them, and re-layouts  3.56 us (2%)
  between operations  1.68 us (1%)
    ppermute x8, waiting for transfers between devices, ring(): lax.ppermute(x, axis, [(i, (i + shift) % count) for i in range(count)])  52.9 us
    pallas_call x2, Pallas kernels, time_step(): pl.pallas_call(step_kernel, out_shape=(jax.ShapeDtypeStruct((inner, out_r...  30.1 us
    reduce_sum x4, other arithmetic, one_block(): return jnp.sum(jnp.where(adjacent, term, 0.0), axis=1)  27.7 us
    ppermute x8, starting transfers between devices, ring(): lax.ppermute(x, axis, [(i, (i + shift) % count) for i in range(count)])  19.2 us
    all_gather x1, blocking collectives, per_device(): lax.all_gather(charges, 'narrow', axis=1, tiled=True)  10.4 us
    concatenate x7, other arithmetic, deep_halo(): jnp.concatenate([lo, a, hi], axis=a.ndim - back)  7.31 us
    scatter-add x1, other arithmetic, per_device(): jnp.zeros((depth * height * width,), jnp.float32).at[index].add(values)  3.33 us
  transfers between devices with their start and end apart: 8, of which 7 were waited for; matrix products, arithmetic and copies ran while one was open for 0% of the time, Pallas kernels for 0%

profile of v2, /device:TPU:1, one launch (start us, length us, event | category | flops | bytes accessed | tf_op | source)
XLA Modules:
  0.0 161.9 jit_solution(5754135155458575680)
XLA Ops:
  1.3 0.7 convert_element_type.31.val_ref
  2.0 0.0 copy-start.5
  2.0 0.7 compare_select_fusion
  2.6 0.7 fusion.37
  3.4 0.7 convert_element_type.33
  4.1 0.8 pad_maximum_fusion.31
  4.9 10.4 %all_gather.3 = f32[5,8192]{1,0:T(8,128)S(1)} all-gather(f32[5,2048]{1,0:T(8,128)S(1)} %pad_maximum_fusion.31), channel_id=1, replica_groups=mesh['wide'=64,'narrow'=4] {'narrow'}, dimensions={1}, use_global_device_ids=true | all-gather | bytes 204800 | tf_op jit(solution)/shard_map/all_gather | solution.py:303
  15.2 0.1 slice_multiply_fusion
  15.4 0.0 copy-start
  15.4 28.1 %while.10 = (s32[]{:T(128)}, f32[4,128]{1,0:T(4,128)S(1)}, f32[4,128]{1,0:T(4,128)S(1)}, f32[1,8192]{1,0:T(1,128)S(1)}, f32[1,8192]{1,0:T(1,128)S(1)}, /*index=5...) while((s32[]{:T(128)}, f32[4,128]{1,0:T(4,128)S(1)}, ...), condition=%wide.region_3.4_spmd, body=%wide.region_1.3_spmd.sunk | while | flops 34602880 | bytes 171665 | solution.py:118
  15.4 6.9 %select_reduce_fusion.2 = f32[128]{0:T(128)S(1)} fusion(f32[8192]{0:T(1024)S(1)} %get-tuple-element.264, f32[128]{0:T(128)S(1)} %get-tuple-element.224, f32[8192]{0:T(1024)S(1)} %get-tuple-element.262, f32[128]{0:T(128)S(1)} %get-tuple-element.225, f32[8192]{0:T(1024)S(1)} %get-tuple-element.260, f32[128]{0:T(128)S(1)} %get-tuple-element.226, ...), kind=kLoop, calls=%fused_computation.11.clone.1 | loop fusion | flops 34602880 | bytes 166400 | tf_op jit(solution)/shard_map/while/body/eval_jaxpr/reduce_sum | solution.py:115
  22.4 6.9 %select_reduce_fusion.2 = f32[128]{0:T(128)S(1)} fusion(f32[8192]{0:T(1024)S(1)} %get-tuple-element.264, f32[128]{0:T(128)S(1)} %get-tuple-element.224, f32[8192]{0:T(1024)S(1)} %get-tuple-element.262, f32[128]{0:T(128)S(1)} %get-tuple-element.225, f32[8192]{0:T(1024)S(1)} %get-tuple-element.260, f32[128]{0:T(128)S(1)} %get-tuple-element.226, ...), kind=kLoop, calls=%fused_computation.11.clone.1 | loop fusion | flops 34602880 | bytes 166400 | tf_op jit(solution)/shard_map/while/body/eval_jaxpr/reduce_sum | solution.py:115
  29.5 6.9 %select_reduce_fusion.2 = f32[128]{0:T(128)S(1)} fusion(f32[8192]{0:T(1024)S(1)} %get-tuple-element.264, f32[128]{0:T(128)S(1)} %get-tuple-element.224, f32[8192]{0:T(1024)S(1)} %get-tuple-element.262, f32[128]{0:T(128)S(1)} %get-tuple-element.225, f32[8192]{0:T(1024)S(1)} %get-tuple-element.260, f32[128]{0:T(128)S(1)} %get-tuple-element.226, ...), kind=kLoop, calls=%fused_computation.11.clone.1 | loop fusion | flops 34602880 | bytes 166400 | tf_op jit(solution)/shard_map/while/body/eval_jaxpr/reduce_sum | solution.py:115
  36.5 6.9 %select_reduce_fusion.2 = f32[128]{0:T(128)S(1)} fusion(f32[8192]{0:T(1024)S(1)} %get-tuple-element.264, f32[128]{0:T(128)S(1)} %get-tuple-element.224, f32[8192]{0:T(1024)S(1)} %get-tuple-element.262, f32[128]{0:T(128)S(1)} %get-tuple-element.225, f32[8192]{0:T(1024)S(1)} %get-tuple-element.260, f32[128]{0:T(128)S(1)} %get-tuple-element.226, ...), kind=kLoop, calls=%fused_computation.11.clone.1 | loop fusion | flops 34602880 | bytes 166400 | tf_op jit(solution)/shard_map/while/body/eval_jaxpr/reduce_sum | solution.py:115
  43.4 0.0 copy-done
  43.5 0.0 copy-done.5
  43.5 0.1 multiply_reduce_fusion.1
  43.6 0.0 copy-start.3
  43.6 3.3 %scatter_custom_fusion = f32[65536]{0:T(1024)S(1)} fusion(s32[512]{0:T(512)S(1)} %bitcast.167, f32[512]{0:T(512)S(1)} %multiply_bitcast_fusion, f32[]{:T(128)} %constant.100.clone.1), kind=kCustom, calls=%fused_computation.46 | custom fusion | flops 512 | bytes 262148 | tf_op jit(solution)/shard_map/scatter-add | solution.py:312
  47.0 0.0 copy-start.2
  47.1 0.0 copy-done.3
  47.1 0.8 copy-done.2
  48.0 0.1 pad_maximum_fusion.8
  48.0 7.1 %collective-permute-start.1 = (f32[1536,128]{1,0:T(8,128)S(1)}, f32[1536,128]{1,0:T(8,128)S(1)}, u32[]{:S(2)}, u32[]{:S(2)}) collective-permute-start(f32[1536,128]{1,0:T(8,128)S(1)} %pad_maximum_fusion.8), channel_id=1, source_target_pairs={{0,252},{4,0},{8,4},{12,8},{16,12},{20,16},{24,20},{28,24},{32,28}... | collective-permute-start | bytes 2359304 | tf_op jit(solution)/shard_map/ppermute | solution.py:123
  55.2 0.1 pad_maximum_fusion.7
  55.2 0.1 collective-permute-start
  55.3 16.6 %collective-permute-done.1 = f32[1536,128]{1,0:T(8,128)S(1)} collective-permute-done((f32[1536,128]{1,0:T(8,128)S(1)}, f32[1536,128]{1,0:T(8,128)S(1)}, u32[]{:S(2)}, u32[]{:S(2)}) %collective-permute-start.1) | collective-permute-done | bytes 786464 | tf_op jit(solution)/shard_map/ppermute | solution.py:123
  72.0 6.2 %collective-permute-done = f32[1536,128]{1,0:T(8,128)S(1)} collective-permute-done((f32[1536,128]{1,0:T(8,128)S(1)}, f32[1536,128]{1,0:T(8,128)S(1)}, u32[]{:S(2)}, u32[]{:S(2)}) %collective-permute-start) | collective-permute-done | bytes 786464 | tf_op jit(solution)/shard_map/ppermute | solution.py:123
  78.4 1.4 collective-permute-start.3
  79.8 2.6 %collective-permute-start.2 = (f32[768,128]{1,0:T(8,128)S(1)}, f32[768,128]{1,0:T(8,128)S(1)}, u32[]{:S(2)}, u32[]{:S(2)}) collective-permute-start(f32[768,128]{1,0:T(8,128)S(1)} %pad_maximum_fusion.11), channel_id=1, source_target_pairs={{0,1},{1,2},{2,3},{3,0},{4,5},{5,6},{6,7},{7,4},{8,9},{9,10},{10,1... | collective-permute-start | bytes 1179656 | tf_op jit(solution)/shard_map/ppermute | solution.py:123
  82.4 7.9 %collective-permute-done.3 = f32[768,128]{1,0:T(8,128)S(1)} collective-permute-done((f32[768,128]{1,0:T(8,128)S(1)}, f32[768,128]{1,0:T(8,128)S(1)}, u32[]{:S(2)}, u32[]{:S(2)}) %collective-permute-start.3) | collective-permute-done | bytes 393248 | tf_op jit(solution)/shard_map/ppermute | solution.py:123
  90.3 0.3 collective-permute-done.2
  90.6 1.0 pad_maximum_fusion.4.s_ref
  91.6 1.0 pad_maximum_fusion.3.p_ref
  92.6 1.0 pad_maximum_fusion.2.f_ref
  93.7 1.1 pad_maximum_fusion.c_ref
  94.8 0.0 copy-start.6
  94.8 15.1 %shard_map.113 = (f32[8,64,128]{2,1,0:T(8,128)}, f32[3,8,64,128]{3,2,1,0:T(8,128)}) custom-call(f32[3]{0:T(128)} %dif_ref.3, f32[3]{0:T(128)} %copy-done.5, f32[22,80,128]{2,1,0:T(8,128)} %pad_maximum_fusion.2.f_ref, f32[22,80,128]{2,1,0:T(8,128)} %pad_maximum_fusion.3.p_ref, f32[22,80,128]{2,1,0:T(8,128)} %pad_maximum_fusion.4.s_ref, ...), custom_call_target="tpu_custom_call" | custom-call | flops 40755200 | bytes 4980736 | tf_op jit(solution)/shard_map/pallas_call | solution.py:239
  109.9 1.0 fusion.39
  110.8 0.0 copy-done.6
  110.8 0.0 copy-start.4
  110.8 1.3 multiply_reduce_fusion
  112.3 0.0 copy-done.4
  112.4 0.1 collective-permute-start.5
  112.5 1.7 %collective-permute-start.4 = (f32[1088,128]{1,0:T(8,128)S(1)}, f32[1088,128]{1,0:T(8,128)S(1)}, u32[]{:S(2)}, u32[]{:S(2)}) collective-permute-start(f32[1088,128]{1,0:T(8,128)S(1)} %pad_maximum_fusion.9), channel_id=1, source_target_pairs={{0,4},{4,8},{8,12},{12,16},{16,20},{20,24},{24,28},{28,32},{32,36}... | collective-permute-start | bytes 1671176 | tf_op jit(solution)/shard_map/ppermute | solution.py:123
  114.2 10.3 %collective-permute-done.5 = f32[1088,128]{1,0:T(8,128)S(1)} collective-permute-done((f32[1088,128]{1,0:T(8,128)S(1)}, f32[1088,128]{1,0:T(8,128)S(1)}, u32[]{:S(2)}, u32[]{:S(2)}) %collective-permute-start.5) | collective-permute-done | bytes 557088 | tf_op jit(solution)/shard_map/ppermute | solution.py:123
  124.6 4.5 %collective-permute-done.4 = f32[1088,128]{1,0:T(8,128)S(1)} collective-permute-done((f32[1088,128]{1,0:T(8,128)S(1)}, f32[1088,128]{1,0:T(8,128)S(1)}, u32[]{:S(2)}, u32[]{:S(2)}) %collective-permute-start.4) | collective-permute-done | bytes 557088 | tf_op jit(solution)/shard_map/ppermute | solution.py:123
  129.1 0.0 copy-start.1
  129.2 1.0 copy-done.1
  130.3 3.0 %collective-permute-start.7 = (f32[592,128]{1,0:T(8,128)S(1)}, f32[592,128]{1,0:T(8,128)S(1)}, u32[]{:S(2)}, u32[]{:S(2)}) collective-permute-start(f32[592,128]{1,0:T(8,128)S(1)} %pad_maximum_fusion.14), channel_id=1, source_target_pairs={{0,3},{1,0},{2,1},{3,2},{4,7},{5,4},{6,5},{7,6},{8,11},{9,8},{10,9... | collective-permute-start | bytes 909320 | tf_op jit(solution)/shard_map/ppermute | solution.py:123
  133.3 3.2 %collective-permute-start.6 = (f32[592,128]{1,0:T(8,128)S(1)}, f32[592,128]{1,0:T(8,128)S(1)}, u32[]{:S(2)}, u32[]{:S(2)}) collective-permute-start(f32[592,128]{1,0:T(8,128)S(1)} %pad_maximum_fusion.13), channel_id=1, source_target_pairs={{0,1},{1,2},{2,3},{3,0},{4,5},{5,6},{6,7},{7,4},{8,9},{9,10},{10,1... | collective-permute-start | bytes 909320 | tf_op jit(solution)/shard_map/ppermute | solution.py:123
  136.6 7.1 %collective-permute-done.7 = f32[592,128]{1,0:T(8,128)S(1)} collective-permute-done((f32[592,128]{1,0:T(8,128)S(1)}, f32[592,128]{1,0:T(8,128)S(1)}, u32[]{:S(2)}, u32[]{:S(2)}) %collective-permute-start.7) | collective-permute-done | bytes 303136 | tf_op jit(solution)/shard_map/ppermute | solution.py:123
  143.6 0.0 collective-permute-done.6
  143.7 1.0 pad_maximum_fusion.6.s_ref
  144.7 1.1 pad_maximum_fusion.1.c_ref
  145.9 1.0 pad_maximum_fusion.5.f_ref
  146.9 15.1 %shard_map.114 = (f32[8,64,128]{2,1,0:T(8,128)}, f32[3,8,64,128]{3,2,1,0:T(8,128)}) custom-call(f32[3]{0:T(128)} %dif_ref.3, f32[3]{0:T(128)} %copy-done.5, f32[22,80,128]{2,1,0:T(8,128)} %pad_maximum_fusion.5.f_ref, f32[22,80,128]{2,1,0:T(8,128)} %pad_maximum_fusion.3.p_ref, f32[22,80,128]{2,1,0:T(8,128)} %pad_maximum_fusion.6.s_ref, ...), custom_call_target="tpu_custom_call" | custom-call | flops 40755200 | bytes 4980736 | tf_op jit(solution)/shard_map/pallas_call | solution.py:239
  (51 shorter events, 1.1 us)
Async XLA Ops:
  2.0 41.5 %copy-start.5 = (f32[3]{0:T(128)}, f32[3]{0:T(128)S(1)}, u32[]{:S(2)}) copy-start(f32[3]{0:T(128)S(1)} %convert_element_type.31.val_ref) | copy-start | bytes 40
  15.4 28.1 %copy-start = (f32[3,8,64,128]{3,2,1,0:T(8,128)S(1)}, f32[3,8,64,128]{3,2,1,0:T(8,128)}, u32[]{:S(2)}) copy-start(f32[3,8,64,128]{3,2,1,0:T(8,128)} %param.12) | copy-start | bytes 2359300
  43.6 3.5 %copy-start.3 = (f32[8,64,128]{2,1,0:T(8,128)S(1)}, f32[8,64,128]{2,1,0:T(8,128)}, u32[]{:S(2)}) copy-start(f32[8,64,128]{2,1,0:T(8,128)} %param.13) | copy-start | bytes 786436
  47.0 1.0 copy-start.2
  48.0 23.9 %collective-permute-start.1 = (f32[1536,128]{1,0:T(8,128)S(1)}, f32[1536,128]{1,0:T(8,128)S(1)}, u32[]{:S(2)}, u32[]{:S(2)}) collective-permute-start(f32[1536,128]{1,0:T(8,128)S(1)} %pad_maximum_fusion.8), channel_id=1, source_target_pairs={{0,252},{4,0},{8,4},{12,8},{16,12},{20,16},{24,20},{28,24},{32,28}... | collective-permute-start | bytes 2359304 | tf_op jit(solution)/shard_map/ppermute | solution.py:123
  55.2 23.0 %collective-permute-start = (f32[1536,128]{1,0:T(8,128)S(1)}, f32[1536,128]{1,0:T(8,128)S(1)}, u32[]{:S(2)}, u32[]{:S(2)}) collective-permute-start(f32[1536,128]{1,0:T(8,128)S(1)} %pad_maximum_fusion.7), channel_id=1, source_target_pairs={{0,4},{4,8},{8,12},{12,16},{16,20},{20,24},{24,28},{28,32},{32,36}... | collective-permute-start | bytes 2359304 | tf_op jit(solution)/shard_map/ppermute | solution.py:123
  78.4 11.9 %collective-permute-start.3 = (f32[768,128]{1,0:T(8,128)S(1)}, f32[768,128]{1,0:T(8,128)S(1)}, u32[]{:S(2)}, u32[]{:S(2)}) collective-permute-start(f32[768,128]{1,0:T(8,128)S(1)} %pad_maximum_fusion.12), channel_id=1, source_target_pairs={{0,3},{1,0},{2,1},{3,2},{4,7},{5,4},{6,5},{7,6},{8,11},{9,8},{10,9... | collective-permute-start | bytes 1179656 | tf_op jit(solution)/shard_map/ppermute | solution.py:123
  79.8 10.8 %collective-permute-start.2 = (f32[768,128]{1,0:T(8,128)S(1)}, f32[768,128]{1,0:T(8,128)S(1)}, u32[]{:S(2)}, u32[]{:S(2)}) collective-permute-start(f32[768,128]{1,0:T(8,128)S(1)} %pad_maximum_fusion.11), channel_id=1, source_target_pairs={{0,1},{1,2},{2,3},{3,0},{4,5},{5,6},{6,7},{7,4},{8,9},{9,10},{10,1... | collective-permute-start | bytes 1179656 | tf_op jit(solution)/shard_map/ppermute | solution.py:123
  94.8 16.0 %copy-start.6 = (f32[3]{0:T(128)S(1)}, f32[3]{0:T(128)}, u32[]{:S(2)}) copy-start(f32[3]{0:T(128)} %copy-done.5) | copy-start | bytes 40
  110.8 1.4 copy-start.4
  112.4 12.2 %collective-permute-start.5 = (f32[1088,128]{1,0:T(8,128)S(1)}, f32[1088,128]{1,0:T(8,128)S(1)}, u32[]{:S(2)}, u32[]{:S(2)}) collective-permute-start(f32[1088,128]{1,0:T(8,128)S(1)} %pad_maximum_fusion.10), channel_id=1, source_target_pairs={{0,252},{4,0},{8,4},{12,8},{16,12},{20,16},{24,20},{28,24},{32,28}... | collective-permute-start | bytes 1671176 | tf_op jit(solution)/shard_map/ppermute | solution.py:123
  112.5 16.6 %collective-permute-start.4 = (f32[1088,128]{1,0:T(8,128)S(1)}, f32[1088,128]{1,0:T(8,128)S(1)}, u32[]{:S(2)}, u32[]{:S(2)}) collective-permute-start(f32[1088,128]{1,0:T(8,128)S(1)} %pad_maximum_fusion.9), channel_id=1, source_target_pairs={{0,4},{4,8},{8,12},{12,16},{16,20},{20,24},{24,28},{28,32},{32,36}... | collective-permute-start | bytes 1671176 | tf_op jit(solution)/shard_map/ppermute | solution.py:123
  129.1 1.1 copy-start.1
  130.3 13.3 %collective-permute-start.7 = (f32[592,128]{1,0:T(8,128)S(1)}, f32[592,128]{1,0:T(8,128)S(1)}, u32[]{:S(2)}, u32[]{:S(2)}) collective-permute-start(f32[592,128]{1,0:T(8,128)S(1)} %pad_maximum_fusion.14), channel_id=1, source_target_pairs={{0,3},{1,0},{2,1},{3,2},{4,7},{5,4},{6,5},{7,6},{8,11},{9,8},{10,9... | collective-permute-start | bytes 909320 | tf_op jit(solution)/shard_map/ppermute | solution.py:123
  133.3 10.3 %collective-permute-start.6 = (f32[592,128]{1,0:T(8,128)S(1)}, f32[592,128]{1,0:T(8,128)S(1)}, u32[]{:S(2)}, u32[]{:S(2)}) collective-permute-start(f32[592,128]{1,0:T(8,128)S(1)} %pad_maximum_fusion.13), channel_id=1, source_target_pairs={{0,1},{1,2},{2,3},{3,0},{4,5},{5,6},{6,7},{7,4},{8,9},{9,10},{10,1... | collective-permute-start | bytes 909320 | tf_op jit(solution)/shard_map/ppermute | solution.py:123

commit v3 on v2

--- a/solution.py
+++ b/solution.py
@@ -114,8 +114,9 @@
         )
         return jnp.sum(jnp.where(adjacent, term, 0.0), axis=1)
 
-    shaped = tuple((arr.reshape(-1, 128) for arr in (node_z, node_y, node_x, node_tile)))
-    return lax.map(one_block, shaped).reshape(-1)
+    half = node_z.shape[0] // 2
+    parts = [one_block(tuple(arr[k * half:(k + 1) * half] for arr in (node_z, node_y, node_x, node_tile))) for k in range(2)]
+    return jnp.concatenate(parts)
 
 
 def ring(x, axis, shift):
@@ -294,6 +295,13 @@
     node_x = local_x.astype(jnp.float32)
     node_tile = (global_y // tile_rows).astype(jnp.float32)
     slab_float = slab.astype(jnp.float32)
+    deep = SWEEPS + 1
+    wide_y = SWEEPS + 2
+    first = deep_halo(
+        [(potential, deep, wide_y), (permittivity, deep, wide_y), (concentration, 1, wide_y)],
+        "wide",
+        "narrow",
+    )
     charges = jnp.concatenate([charge_pos, charge_q, charge_tile.astype(jnp.float32)], axis=0)
     values = pair_field(
         node_z,
@@ -312,20 +320,19 @@
     electrode = jnp.zeros((depth * height * width,), jnp.float32).at[index].add(values)
     electrode = electrode.reshape(depth, height, width)
     charge_num = valence.astype(jnp.float32)
-    deep = SWEEPS + 1
-    wide_y = SWEEPS + 2
     field = potential
     species = concentration
-    perm_ext = None
+    perm_ext = first[1]
     for step in range(STEPS):
         source = jnp.sum(charge_num[:, None, None, None] * species, axis=0) + electrode
-        items = [(field, deep, wide_y), (source, deep, wide_y), (species, 1, wide_y)]
-        if perm_ext is None:
-            items.append((permittivity, deep, wide_y))
-        got = deep_halo(items, "wide", "narrow")
-        if perm_ext is None:
-            perm_ext = got[3]
-        field, species = time_step(diffusivity, charge_num, got[0], perm_ext, got[1], got[2])
+        if step == 0:
+            field_e, species_e = first[0], first[2]
+            (source_e,) = deep_halo([(source, deep, wide_y)], "wide", "narrow")
+        else:
+            field_e, source_e, species_e = deep_halo(
+                [(field, deep, wide_y), (source, deep, wide_y), (species, 1, wide_y)], "wide", "narrow"
+            )
+        field, species = time_step(diffusivity, charge_num, field_e, perm_ext, source_e, species_e)
     return (species, field)
 
 

time: 162 us -> 157 us (0.969)
  waiting for transfers between devices: 52.9 us -> 34.4 us
  starting transfers between devices: 19.2 us -> 29.4 us
  blocking collectives: 10.4 us -> 16.6 us
  other arithmetic: 44 us -> 39.9 us
    ppermute x8 -> x12, waiting for transfers between devices: 52.9 us -> 34.4 us  [ring(): lax.ppermute(x, axis, [(i, (i + shift) % count) for i in range(count)])]
    ppermute x8 -> x12, starting transfers between devices: 19.2 us -> 29.4 us  [ring(): lax.ppermute(x, axis, [(i, (i + shift) % count) for i in range(count)])]
    all_gather x1, blocking collectives: 10.4 us -> 16.6 us  [per_device(): lax.all_gather(charges, 'narrow', axis=1, tiled=True)]
    slice x7, local copies, waits for them, and re-layouts: 1.15 us -> 3.19 us  [deep_halo(): tops.append(lax.slice_in_dim(a, n - w, n, axis=dim))]
    reduce_sum x4 -> x1, other arithmetic: 27.7 us -> 27.2 us  [one_block(): return jnp.sum(jnp.where(adjacent, term, 0.0), axis=1)]
  transfers between devices with their start and end apart: 8 -> 12, of which waited for: 7 -> 7; matrix products, arithmetic and copies ran while one was open for 0% -> 21% of each run, Pallas kernels for 0% -> 0%
where the time goes in v3:
time: 157 us
  other arithmetic  39.9 us (25%)
  waiting for transfers between devices  34.4 us (22%)
  Pallas kernels  30.1 us (19%)
  starting transfers between devices  29.4 us (19%)
  blocking collectives  16.6 us (11%)
  local copies, waits for them, and re-layouts  4.56 us (3%)
  between operations  1.82 us (1%)
    ppermute x12, waiting for transfers between devices, ring(): lax.ppermute(x, axis, [(i, (i + shift) % count) for i in range(count)])  34.4 us
    pallas_call x2, Pallas kernels, time_step(): pl.pallas_call(step_kernel, out_shape=(jax.ShapeDtypeStruct((inner, out_r...  30.1 us
    ppermute x12, starting transfers between devices, ring(): lax.ppermute(x, axis, [(i, (i + shift) % count) for i in range(count)])  29.4 us
    reduce_sum x1, other arithmetic, one_block(): return jnp.sum(jnp.where(adjacent, term, 0.0), axis=1)  27.2 us
    all_gather x1, blocking collectives, per_device(): lax.all_gather(charges, 'narrow', axis=1, tiled=True)  16.6 us
    concatenate x7, other arithmetic, deep_halo(): jnp.concatenate([lo, a, hi], axis=a.ndim - back)  7.25 us
    scatter-add x1, other arithmetic, per_device(): jnp.zeros((depth * height * width,), jnp.float32).at[index].add(values)  3.33 us
    slice x7, local copies, waits for them, and re-layouts, deep_halo(): tops.append(lax.slice_in_dim(a, n - w, n, axis=dim))  3.19 us
  transfers between devices with their start and end apart: 12, of which 7 were waited for; matrix products, arithmetic and copies ran while one was open for 21% of the time, Pallas kernels for 0%

profile of v3, /device:TPU:1, one launch (start us, length us, event | category | flops | bytes accessed | tf_op | source)
XLA Modules:
  0.0 156.7 jit_solution(11422895771494487027)
XLA Ops:
  0.6 0.0 copy-start.2
  0.6 1.0 fusion.50
  1.6 1.1 fusion.59
  2.7 0.0 copy-done.2
  2.8 0.0 copy-start.11
  2.8 0.0 copy-start.10
  2.8 0.0 copy-start.9
  2.8 0.0 copy-start.5
  2.8 0.0 copy-start.8
  2.9 9.7 %collective-permute-start.1 = (f32[1088,128]{1,0:T(8,128)S(1)}, f32[1088,128]{1,0:T(8,128)S(1)}, u32[]{:S(2)}, u32[]{:S(2)}) collective-permute-start(f32[1088,128]{1,0:T(8,128)S(1)} %pad_maximum_fusion.8), channel_id=1, source_target_pairs={{0,252},{4,0},{8,4},{12,8},{16,12},{20,16},{24,20},{28,24},{32,28}... | collective-permute-start | bytes 1671176 | tf_op jit(solution)/shard_map/ppermute | solution.py:124
  12.6 0.1 collective-permute-start
  13.4 0.0 copy-done.11
  13.4 0.0 copy-start.6
  13.4 0.0 copy-done.10
  13.5 0.0 copy-done.9
  13.5 0.0 copy-done.5
  13.5 0.0 copy-done.8
  13.5 16.6 %all_gather.3 = f32[5,8192]{1,0:T(8,128)S(1)} all-gather(f32[5,2048]{1,0:T(8,128)S(1)} %pad_maximum_fusion.31), channel_id=1, replica_groups=mesh['wide'=64,'narrow'=4] {'narrow'}, dimensions={1}, use_global_device_ids=true | all-gather | bytes 204800 | tf_op jit(solution)/shard_map/all_gather | solution.py:311
  30.2 0.1 fusion.58
  30.3 0.0 copy-start
  30.3 27.2 %select_reduce_fusion.1 = (f32[256]{0:T(256)S(1)}, f32[256]{0:T(256)S(1)}) fusion(f32[8192]{0:T(1024)S(1)} %bitcast.140, f32[256]{0:T(256)S(1)} %get-tuple-element.79, f32[8192]{0:T(1024)S(1)} %bitcast.141, f32[256]{0:T(256)S(1)} %get-tuple-element.68, f32[8192]{0:T(1024)S(1)} %bitcast.142, f32[256]{0:T(256)S(1)} %get-tuple-element.77, ...), kind=kLoop, calls=%fused_computation.28 | loop fusion | flops 138411520 | bytes 174080 | tf_op jit(solution)/shard_map/reduce_sum | solution.py:115
  57.5 3.3 %scatter_custom_fusion = f32[65536]{0:T(1024)S(1)} fusion(s32[512]{0:T(512)S(1)} %bitcast.145, f32[512]{0:T(512)S(1)} %maximum_multiply_fusion, f32[]{:T(128)} %constant.81.clone.1), kind=kCustom, calls=%fused_computation.58 | custom fusion | flops 512 | bytes 262148 | tf_op jit(solution)/shard_map/scatter-add | solution.py:320
  60.9 0.0 copy-done.6
  60.9 0.0 copy-done
  60.9 0.1 multiply_reduce_fusion.1
  61.1 0.0 copy-start.3
  61.1 4.9 %collective-permute-start.5 = (f32[448,128]{1,0:T(8,128)S(1)}, f32[448,128]{1,0:T(8,128)S(1)}, u32[]{:S(2)}, u32[]{:S(2)}) collective-permute-start(f32[448,128]{1,0:T(8,128)S(1)} %bitcast.136), channel_id=1, source_target_pairs={{0,252},{4,0},{8,4},{12,8},{16,12},{20,16},{24,20},{28,24},{32,28}... | collective-permute-start | bytes 688136 | tf_op jit(solution)/shard_map/ppermute | solution.py:124
  66.0 0.0 collective-permute-start.4
  66.0 0.0 collective-permute-done.1
  66.1 0.0 collective-permute-done
  66.1 0.0 copy-done.3
  66.2 0.5 collective-permute-start.3
  66.8 4.1 %collective-permute-done.5 = f32[448,128]{1,0:T(8,128)S(1)} collective-permute-done((f32[448,128]{1,0:T(8,128)S(1)}, f32[448,128]{1,0:T(8,128)S(1)}, u32[]{:S(2)}, u32[]{:S(2)}) %collective-permute-start.5) | collective-permute-done | bytes 229408 | tf_op jit(solution)/shard_map/ppermute | solution.py:124
  70.9 6.1 %collective-permute-done.4 = f32[448,128]{1,0:T(8,128)S(1)} collective-permute-done((f32[448,128]{1,0:T(8,128)S(1)}, f32[448,128]{1,0:T(8,128)S(1)}, u32[]{:S(2)}, u32[]{:S(2)}) %collective-permute-start.4) | collective-permute-done | bytes 229408 | tf_op jit(solution)/shard_map/ppermute | solution.py:124
  77.0 2.6 %collective-permute-start.6 = (f32[176,128]{1,0:T(8,128)S(1)}, f32[176,128]{1,0:T(8,128)S(1)}, u32[]{:S(2)}, u32[]{:S(2)}) collective-permute-start(f32[176,128]{1,0:T(8,128)S(1)} %get-tuple-element.26), channel_id=1, source_target_pairs={{0,1},{1,2},{2,3},{3,0},{4,5},{5,6},{6,7},{7,4},{8,9},{9,10},{10,1... | collective-permute-start | bytes 270344 | tf_op jit(solution)/shard_map/ppermute | solution.py:124
  79.6 0.0 collective-permute-start.7
  79.6 3.3 %collective-permute-start.2 = (f32[592,128]{1,0:T(8,128)S(1)}, f32[592,128]{1,0:T(8,128)S(1)}, u32[]{:S(2)}, u32[]{:S(2)}) collective-permute-start(f32[592,128]{1,0:T(8,128)S(1)} %pad_maximum_fusion.11), channel_id=1, source_target_pairs={{0,1},{1,2},{2,3},{3,0},{4,5},{5,6},{6,7},{7,4},{8,9},{9,10},{10,1... | collective-permute-start | bytes 909320 | tf_op jit(solution)/shard_map/ppermute | solution.py:124
  83.0 0.0 collective-permute-done.6
  83.0 2.1 %collective-permute-done.7 = f32[176,128]{1,0:T(8,128)S(1)} collective-permute-done((f32[176,128]{1,0:T(8,128)S(1)}, f32[176,128]{1,0:T(8,128)S(1)}, u32[]{:S(2)}, u32[]{:S(2)}) %collective-permute-start.7) | collective-permute-done | bytes 90144 | tf_op jit(solution)/shard_map/ppermute | solution.py:124
  85.1 1.0 pad_maximum_fusion.4.s_ref
  86.1 0.0 collective-permute-done.3
  86.1 0.6 collective-permute-done.2
  86.7 1.0 pad_maximum_fusion.3.p_ref
  87.7 1.0 pad_maximum_fusion.2.f_ref
  88.7 1.2 pad_maximum_fusion.c_ref
  89.9 15.1 %shard_map.113 = (f32[8,64,128]{2,1,0:T(8,128)}, f32[3,8,64,128]{3,2,1,0:T(8,128)}) custom-call(f32[3]{0:T(128)} %dif_ref.3, f32[3]{0:T(128)} %copy-done.6, f32[22,80,128]{2,1,0:T(8,128)} %pad_maximum_fusion.2.f_ref, f32[22,80,128]{2,1,0:T(8,128)} %pad_maximum_fusion.3.p_ref, f32[22,80,128]{2,1,0:T(8,128)} %pad_maximum_fusion.4.s_ref, ...), custom_call_target="tpu_custom_call" | custom-call | flops 40755200 | bytes 4980736 | tf_op jit(solution)/shard_map/pallas_call | solution.py:240
  104.9 1.0 fusion.49
  105.9 0.0 copy-done.7
  105.9 0.0 copy-start.4
  105.9 1.3 multiply_reduce_fusion
  107.4 0.1 collective-permute-start.9
  107.6 1.5 collective-permute-start.8
  109.1 9.7 %collective-permute-done.9 = f32[1088,128]{1,0:T(8,128)S(1)} collective-permute-done((f32[1088,128]{1,0:T(8,128)S(1)}, f32[1088,128]{1,0:T(8,128)S(1)}, u32[]{:S(2)}, u32[]{:S(2)}) %collective-permute-start.9) | collective-permute-done | bytes 557088 | tf_op jit(solution)/shard_map/ppermute | solution.py:124
  118.9 4.1 %collective-permute-done.8 = f32[1088,128]{1,0:T(8,128)S(1)} collective-permute-done((f32[1088,128]{1,0:T(8,128)S(1)}, f32[1088,128]{1,0:T(8,128)S(1)}, u32[]{:S(2)}, u32[]{:S(2)}) %collective-permute-start.8) | collective-permute-done | bytes 557088 | tf_op jit(solution)/shard_map/ppermute | solution.py:124
  122.9 0.0 copy-start.1
  123.0 1.0 copy-done.1
  124.1 4.1 %collective-permute-start.11 = (f32[592,128]{1,0:T(8,128)S(1)}, f32[592,128]{1,0:T(8,128)S(1)}, u32[]{:S(2)}, u32[]{:S(2)}) collective-permute-start(f32[592,128]{1,0:T(8,128)S(1)} %pad_maximum_fusion.14), channel_id=1, source_target_pairs={{0,3},{1,0},{2,1},{3,2},{4,7},{5,4},{6,5},{7,6},{8,11},{9,8},{10,9... | collective-permute-start | bytes 909320 | tf_op jit(solution)/shard_map/ppermute | solution.py:124
  128.2 2.5 %collective-permute-start.10 = (f32[592,128]{1,0:T(8,128)S(1)}, f32[592,128]{1,0:T(8,128)S(1)}, u32[]{:S(2)}, u32[]{:S(2)}) collective-permute-start(f32[592,128]{1,0:T(8,128)S(1)} %pad_maximum_fusion.13), channel_id=1, source_target_pairs={{0,1},{1,2},{2,3},{3,0},{4,5},{5,6},{6,7},{7,4},{8,9},{9,10},{10,1... | collective-permute-start | bytes 909320 | tf_op jit(solution)/shard_map/ppermute | solution.py:124
  130.8 7.7 %collective-permute-done.11 = f32[592,128]{1,0:T(8,128)S(1)} collective-permute-done((f32[592,128]{1,0:T(8,128)S(1)}, f32[592,128]{1,0:T(8,128)S(1)}, u32[]{:S(2)}, u32[]{:S(2)}) %collective-permute-start.11) | collective-permute-done | bytes 303136 | tf_op jit(solution)/shard_map/ppermute | solution.py:124
  138.5 0.0 collective-permute-done.10
  138.5 1.0 pad_maximum_fusion.6.s_ref
  139.5 1.2 pad_maximum_fusion.1.c_ref
  140.7 1.0 pad_maximum_fusion.5.f_ref
  141.7 15.1 %shard_map.114 = (f32[8,64,128]{2,1,0:T(8,128)}, f32[3,8,64,128]{3,2,1,0:T(8,128)}) custom-call(f32[3]{0:T(128)} %dif_ref.3, f32[3]{0:T(128)} %copy-done.6, f32[22,80,128]{2,1,0:T(8,128)} %pad_maximum_fusion.5.f_ref, f32[22,80,128]{2,1,0:T(8,128)} %pad_maximum_fusion.3.p_ref, f32[22,80,128]{2,1,0:T(8,128)} %pad_maximum_fusion.6.s_ref, ...), custom_call_target="tpu_custom_call" | custom-call | flops 40755200 | bytes 4980736 | tf_op jit(solution)/shard_map/pallas_call | solution.py:240
  (47 shorter events, 0.9 us)
Async XLA Ops:
  0.6 2.1 %copy-start.2 = (f32[8,64,128]{2,1,0:T(8,128)S(1)}, f32[8,64,128]{2,1,0:T(8,128)}, u32[]{:S(2)}) copy-start(f32[8,64,128]{2,1,0:T(8,128)} %param.12) | copy-start | bytes 786436
  2.8 10.6 %copy-start.11 = (s32[3]{0:T(128)S(1)}, s32[3]{0:T(128)}, u32[]{:S(2)}) copy-start(s32[3]{0:T(128)} %param.14) | copy-start | bytes 40
  2.8 10.6 %copy-start.10 = (s32[1,1,512]{2,1,0:T(1,128)S(1)}, s32[1,1,512]{2,1,0:T(1,128)}, u32[]{:S(2)}) copy-start(s32[1,1,512]{2,1,0:T(1,128)} %param.18) | copy-start | bytes 6148
  2.8 10.6 %copy-start.9 = (s32[1,2048]{1,0:T(1,128)S(1)}, s32[1,2048]{1,0:T(1,128)}, u32[]{:S(2)}) copy-start(s32[1,2048]{1,0:T(1,128)} %param.17) | copy-start | bytes 24580
  2.8 10.7 %copy-start.5 = (f32[3,2048]{1,0:T(4,128)S(1)}, f32[3,2048]{1,0:T(4,128)}, u32[]{:S(2)}) copy-start(f32[3,2048]{1,0:T(4,128)} %param.15) | copy-start | bytes 73732
  2.8 10.7 %copy-start.8 = (f32[1,2048]{1,0:T(1,128)S(1)}, f32[1,2048]{1,0:T(1,128)}, u32[]{:S(2)}) copy-start(f32[1,2048]{1,0:T(1,128)} %param.16) | copy-start | bytes 24580
  2.9 63.1 %collective-permute-start.1 = (f32[1088,128]{1,0:T(8,128)S(1)}, f32[1088,128]{1,0:T(8,128)S(1)}, u32[]{:S(2)}, u32[]{:S(2)}) collective-permute-start(f32[1088,128]{1,0:T(8,128)S(1)} %pad_maximum_fusion.8), channel_id=1, source_target_pairs={{0,252},{4,0},{8,4},{12,8},{16,12},{20,16},{24,20},{28,24},{32,28}... | collective-permute-start | bytes 1671176 | tf_op jit(solution)/shard_map/ppermute | solution.py:124
  12.6 53.4 %collective-permute-start = (f32[1088,128]{1,0:T(8,128)S(1)}, f32[1088,128]{1,0:T(8,128)S(1)}, u32[]{:S(2)}, u32[]{:S(2)}) collective-permute-start(f32[1088,128]{1,0:T(8,128)S(1)} %pad_maximum_fusion.7), channel_id=1, source_target_pairs={{0,4},{4,8},{8,12},{12,16},{16,20},{20,24},{24,28},{28,32},{32,36}... | collective-permute-start | bytes 1671176 | tf_op jit(solution)/shard_map/ppermute | solution.py:124
  13.4 47.5 %copy-start.6 = (f32[3]{0:T(128)}, f32[3]{0:T(128)S(1)}, u32[]{:S(2)}) copy-start(f32[3]{0:T(128)S(1)} %convert_element_type.27.val_ref) | copy-start | bytes 40
  30.3 30.6 %copy-start = (f32[3,8,64,128]{3,2,1,0:T(8,128)S(1)}, f32[3,8,64,128]{3,2,1,0:T(8,128)}, u32[]{:S(2)}) copy-start(f32[3,8,64,128]{3,2,1,0:T(8,128)} %param.10) | copy-start | bytes 2359300
  61.1 5.0 %copy-start.3 = (f32[8,64,128]{2,1,0:T(8,128)S(1)}, f32[8,64,128]{2,1,0:T(8,128)}, u32[]{:S(2)}) copy-start(f32[8,64,128]{2,1,0:T(8,128)} %param.11) | copy-start | bytes 786436
  61.1 9.7 %collective-permute-start.5 = (f32[448,128]{1,0:T(8,128)S(1)}, f32[448,128]{1,0:T(8,128)S(1)}, u32[]{:S(2)}, u32[]{:S(2)}) collective-permute-start(f32[448,128]{1,0:T(8,128)S(1)} %bitcast.136), channel_id=1, source_target_pairs={{0,252},{4,0},{8,4},{12,8},{16,12},{20,16},{24,20},{28,24},{32,28}... | collective-permute-start | bytes 688136 | tf_op jit(solution)/shard_map/ppermute | solution.py:124
  66.0 11.0 %collective-permute-start.4 = (f32[448,128]{1,0:T(8,128)S(1)}, f32[448,128]{1,0:T(8,128)S(1)}, u32[]{:S(2)}, u32[]{:S(2)}) collective-permute-start(f32[448,128]{1,0:T(8,128)S(1)} %bitcast.135), channel_id=1, source_target_pairs={{0,4},{4,8},{8,12},{12,16},{16,20},{20,24},{24,28},{28,32},{32,36}... | collective-permute-start | bytes 688136 | tf_op jit(solution)/shard_map/ppermute | solution.py:124
  66.2 19.8 %collective-permute-start.3 = (f32[592,128]{1,0:T(8,128)S(1)}, f32[592,128]{1,0:T(8,128)S(1)}, u32[]{:S(2)}, u32[]{:S(2)}) collective-permute-start(f32[592,128]{1,0:T(8,128)S(1)} %pad_maximum_fusion.12), channel_id=1, source_target_pairs={{0,3},{1,0},{2,1},{3,2},{4,7},{5,4},{6,5},{7,6},{8,11},{9,8},{10,9... | collective-permute-start | bytes 909320 | tf_op jit(solution)/shard_map/ppermute | solution.py:124
  77.0 6.0 %collective-permute-start.6 = (f32[176,128]{1,0:T(8,128)S(1)}, f32[176,128]{1,0:T(8,128)S(1)}, u32[]{:S(2)}, u32[]{:S(2)}) collective-permute-start(f32[176,128]{1,0:T(8,128)S(1)} %get-tuple-element.26), channel_id=1, source_target_pairs={{0,1},{1,2},{2,3},{3,0},{4,5},{5,6},{6,7},{7,4},{8,9},{9,10},{10,1... | collective-permute-start | bytes 270344 | tf_op jit(solution)/shard_map/ppermute | solution.py:124
  79.6 5.5 %collective-permute-start.7 = (f32[176,128]{1,0:T(8,128)S(1)}, f32[176,128]{1,0:T(8,128)S(1)}, u32[]{:S(2)}, u32[]{:S(2)}) collective-permute-start(f32[176,128]{1,0:T(8,128)S(1)} %get-tuple-element.27), channel_id=1, source_target_pairs={{0,3},{1,0},{2,1},{3,2},{4,7},{5,4},{6,5},{7,6},{8,11},{9,8},{10,9... | collective-permute-start | bytes 270344 | tf_op jit(solution)/shard_map/ppermute | solution.py:124
  79.6 7.1 %collective-permute-start.2 = (f32[592,128]{1,0:T(8,128)S(1)}, f32[592,128]{1,0:T(8,128)S(1)}, u32[]{:S(2)}, u32[]{:S(2)}) collective-permute-start(f32[592,128]{1,0:T(8,128)S(1)} %pad_maximum_fusion.11), channel_id=1, source_target_pairs={{0,1},{1,2},{2,3},{3,0},{4,5},{5,6},{6,7},{7,4},{8,9},{9,10},{10,1... | collective-permute-start | bytes 909320 | tf_op jit(solution)/shard_map/ppermute | solution.py:124
  89.9 16.0 %copy-start.7 = (f32[3]{0:T(128)S(1)}, f32[3]{0:T(128)}, u32[]{:S(2)}) copy-start(f32[3]{0:T(128)} %copy-done.6) | copy-start | bytes 40
  105.9 1.4 copy-start.4
  107.4 11.4 %collective-permute-start.9 = (f32[1088,128]{1,0:T(8,128)S(1)}, f32[1088,128]{1,0:T(8,128)S(1)}, u32[]{:S(2)}, u32[]{:S(2)}) collective-permute-start(f32[1088,128]{1,0:T(8,128)S(1)} %pad_maximum_fusion.10), channel_id=1, source_target_pairs={{0,252},{4,0},{8,4},{12,8},{16,12},{20,16},{24,20},{28,24},{32,28}... | collective-permute-start | bytes 1671176 | tf_op jit(solution)/shard_map/ppermute | solution.py:124
  107.6 15.3 %collective-permute-start.8 = (f32[1088,128]{1,0:T(8,128)S(1)}, f32[1088,128]{1,0:T(8,128)S(1)}, u32[]{:S(2)}, u32[]{:S(2)}) collective-permute-start(f32[1088,128]{1,0:T(8,128)S(1)} %pad_maximum_fusion.9), channel_id=1, source_target_pairs={{0,4},{4,8},{8,12},{12,16},{16,20},{20,24},{24,28},{28,32},{32,36}... | collective-permute-start | bytes 1671176 | tf_op jit(solution)/shard_map/ppermute | solution.py:124
  122.9 1.1 copy-start.1
  124.1 14.3 %collective-permute-start.11 = (f32[592,128]{1,0:T(8,128)S(1)}, f32[592,128]{1,0:T(8,128)S(1)}, u32[]{:S(2)}, u32[]{:S(2)}) collective-permute-start(f32[592,128]{1,0:T(8,128)S(1)} %pad_maximum_fusion.14), channel_id=1, source_target_pairs={{0,3},{1,0},{2,1},{3,2},{4,7},{5,4},{6,5},{7,6},{8,11},{9,8},{10,9... | collective-permute-start | bytes 909320 | tf_op jit(solution)/shard_map/ppermute | solution.py:124
  128.2 10.3 %collective-permute-start.10 = (f32[592,128]{1,0:T(8,128)S(1)}, f32[592,128]{1,0:T(8,128)S(1)}, u32[]{:S(2)}, u32[]{:S(2)}) collective-permute-start(f32[592,128]{1,0:T(8,128)S(1)} %pad_maximum_fusion.13), channel_id=1, source_target_pairs={{0,1},{1,2},{2,3},{3,0},{4,5},{5,6},{6,7},{7,4},{8,9},{9,10},{10,1... | collective-permute-start | bytes 909320 | tf_op jit(solution)/shard_map/ppermute | solution.py:124

commit v4 on v3

--- a/solution.py
+++ b/solution.py
@@ -180,7 +180,7 @@
         for k, w in enumerate(ws):
             w_ref[k, z] = w
             den = den + w
-        w_ref[6, z] = den
+        w_ref[6, z] = 1.0 / den
         return carry
 
     lax.fori_loop(1, planes - 1, weights, 0)
@@ -199,7 +199,7 @@
             numer = numer + w_ref[3, z] * ysh(fc, -1)
             numer = numer + w_ref[4, z] * jnp.where(top, 0.0, xsh(fc, 1))
             numer = numer + w_ref[5, z] * jnp.where(bot, 0.0, xsh(fc, -1))
-            wr[z] = numer / w_ref[6, z]
+            wr[z] = numer * w_ref[6, z]
             return carry
 
         lax.fori_loop(k + 1, planes - k - 1, sweep, 0)
@@ -297,18 +297,22 @@
     slab_float = slab.astype(jnp.float32)
     deep = SWEEPS + 1
     wide_y = SWEEPS + 2
+    charges = jnp.concatenate([charge_pos, charge_q, charge_tile.astype(jnp.float32)], axis=0)
+    gathered = lax.all_gather(charges, "narrow", axis=1, tiled=True)
+    gathered, potential, permittivity, concentration = lax.optimization_barrier(
+        (gathered, potential, permittivity, concentration)
+    )
     first = deep_halo(
         [(potential, deep, wide_y), (permittivity, deep, wide_y), (concentration, 1, wide_y)],
         "wide",
         "narrow",
     )
-    charges = jnp.concatenate([charge_pos, charge_q, charge_tile.astype(jnp.float32)], axis=0)
     values = pair_field(
         node_z,
         node_y,
         node_x,
         node_tile,
-        lax.all_gather(charges, "narrow", axis=1, tiled=True),
+        gathered,
         slab_float,
         depth,
         rows_total,

time: 157 us -> 150 us (0.955)
  blocking collectives: 16.6 us -> 10.4 us
  starting transfers between devices: 29.4 us -> 26.3 us
    all_gather x1, blocking collectives: 16.6 us -> 10.4 us  [per_device(): gathered = lax.all_gather(charges, 'narrow', axis=1, tiled=True)]
    ppermute x12, starting transfers between devices: 29.4 us -> 26.3 us  [ring(): lax.ppermute(x, axis, [(i, (i + shift) % count) for i in range(count)])]
    concatenate x7 -> x6, other arithmetic: 7.25 us -> 6.61 us  [deep_halo(): jnp.concatenate([lo, a, hi], axis=a.ndim - back)]
  transfers between devices with their start and end apart: 12 -> 12, of which waited for: 7 -> 6; matrix products, arithmetic and copies ran while one was open for 21% -> 22% of each run, Pallas kernels for 0% -> 0%
where the time goes in v4:
time: 150 us; the launch traced here: 149 us
  other arithmetic  40.8 us (27%)
  waiting for transfers between devices  34.5 us (23%)
  Pallas kernels  30.4 us (20%)
  starting transfers between devices  26.3 us (18%)
  blocking collectives  10.4 us (7%)
  local copies, waits for them, and re-layouts  5.32 us (4%)
  between operations  1.76 us (1%)
    ppermute x12, waiting for transfers between devices, ring(): lax.ppermute(x, axis, [(i, (i + shift) % count) for i in range(count)])  34.5 us
    pallas_call x2, Pallas kernels, time_step(): pl.pallas_call(step_kernel, out_shape=(jax.ShapeDtypeStruct((inner, out_r...  30.4 us
    reduce_sum x1, other arithmetic, one_block(): return jnp.sum(jnp.where(adjacent, term, 0.0), axis=1)  27.2 us
    ppermute x12, starting transfers between devices, ring(): lax.ppermute(x, axis, [(i, (i + shift) % count) for i in range(count)])  26.3 us
    all_gather x1, blocking collectives, per_device(): gathered = lax.all_gather(charges, 'narrow', axis=1, tiled=True)  10.4 us
    concatenate x6, other arithmetic, deep_halo(): jnp.concatenate([lo, a, hi], axis=a.ndim - back)  6.61 us
    scatter-add x1, other arithmetic, per_device(): jnp.zeros((depth * height * width,), jnp.float32).at[index].add(values)  3.33 us
    slice x7, local copies, waits for them, and re-layouts, deep_halo(): tops.append(lax.slice_in_dim(a, n - w, n, axis=dim))  3.15 us
  transfers between devices with their start and end apart: 12, of which 6 were waited for; matrix products, arithmetic and copies ran while one was open for 22% of the time, Pallas kernels for 0%

profile of v4, /device:TPU:1, one launch (start us, length us, event | category | flops | bytes accessed | tf_op | source)
XLA Modules:
  0.0 149.3 jit_solution(16523658598631744915)
XLA Ops:
  0.6 0.0 copy-start.2
  0.6 0.7 convert_element_type.28
  1.4 0.8 pad_maximum_fusion.31
  2.2 10.4 %all_gather.3 = f32[5,8192]{1,0:T(8,128)S(1)} all-gather(f32[5,2048]{1,0:T(8,128)S(1)} %pad_maximum_fusion.31), channel_id=1, replica_groups=mesh['wide'=64,'narrow'=4] {'narrow'}, dimensions={1}, use_global_device_ids=true | all-gather | bytes 204800 | tf_op jit(solution)/shard_map/all_gather | solution.py:301
  12.6 1.0 fusion.48
  13.5 1.1 fusion.57
  14.6 0.0 copy-done.2
  14.7 0.0 copy-start.8
  14.7 0.0 copy-start.7
  14.7 7.1 %collective-permute-start.1 = (f32[1088,128]{1,0:T(8,128)S(1)}, f32[1088,128]{1,0:T(8,128)S(1)}, u32[]{:S(2)}, u32[]{:S(2)}) collective-permute-start(f32[1088,128]{1,0:T(8,128)S(1)} %pad_maximum_fusion.8), channel_id=1, source_target_pairs={{0,252},{4,0},{8,4},{12,8},{16,12},{20,16},{24,20},{28,24},{32,28}... | collective-permute-start | bytes 1671176 | tf_op jit(solution)/shard_map/ppermute | solution.py:124
  21.9 0.1 collective-permute-start
  22.6 0.0 copy-done.8
  22.7 0.0 copy-start.5
  22.7 0.0 copy-done.7
  22.8 0.1 fusion.56
  22.9 0.0 copy-start
  22.9 27.2 %select_reduce_fusion.1 = (f32[256]{0:T(256)S(1)}, f32[256]{0:T(256)S(1)}) fusion(f32[8192]{0:T(1024)S(1)} %bitcast.140, f32[256]{0:T(256)S(1)} %get-tuple-element.87, f32[8192]{0:T(1024)S(1)} %bitcast.141, f32[256]{0:T(256)S(1)} %get-tuple-element.76, f32[8192]{0:T(1024)S(1)} %bitcast.142, f32[256]{0:T(256)S(1)} %get-tuple-element.85, ...), kind=kLoop, calls=%fused_computation.28 | loop fusion | flops 138411520 | bytes 174080 | tf_op jit(solution)/shard_map/reduce_sum | solution.py:115
  50.1 3.3 %scatter_custom_fusion = f32[65536]{0:T(1024)S(1)} fusion(s32[512]{0:T(512)S(1)} %bitcast.145, f32[512]{0:T(512)S(1)} %maximum_multiply_fusion, f32[]{:T(128)} %constant.81.clone.1), kind=kCustom, calls=%fused_computation.58 | custom fusion | flops 512 | bytes 262148 | tf_op jit(solution)/shard_map/scatter-add | solution.py:324
  53.5 0.0 copy-done.5
  53.5 0.0 copy-done
  53.5 0.1 multiply_reduce_fusion.1
  53.7 5.7 %collective-permute-start.5 = (f32[448,128]{1,0:T(8,128)S(1)}, f32[448,128]{1,0:T(8,128)S(1)}, u32[]{:S(2)}, u32[]{:S(2)}) collective-permute-start(f32[448,128]{1,0:T(8,128)S(1)} %bitcast.136), channel_id=1, source_target_pairs={{0,252},{4,0},{8,4},{12,8},{16,12},{20,16},{24,20},{28,24},{32,28}... | collective-permute-start | bytes 688136 | tf_op jit(solution)/shard_map/ppermute | solution.py:124
  59.5 0.0 copy-start.3
  59.5 0.0 collective-permute-start.4
  59.5 0.0 collective-permute-done.1
  59.5 0.0 collective-permute-done
  59.6 0.8 copy-done.3
  60.5 1.1 collective-permute-start.3
  61.6 2.6 %collective-permute-start.2 = (f32[592,128]{1,0:T(8,128)S(1)}, f32[592,128]{1,0:T(8,128)S(1)}, u32[]{:S(2)}, u32[]{:S(2)}) collective-permute-start(f32[592,128]{1,0:T(8,128)S(1)} %pad_maximum_fusion.11), channel_id=1, source_target_pairs={{0,1},{1,2},{2,3},{3,0},{4,5},{5,6},{6,7},{7,4},{8,9},{9,10},{10,1... | collective-permute-start | bytes 909320 | tf_op jit(solution)/shard_map/ppermute | solution.py:124
  64.2 0.0 collective-permute-done.5
  64.2 5.6 %collective-permute-done.4 = f32[448,128]{1,0:T(8,128)S(1)} collective-permute-done((f32[448,128]{1,0:T(8,128)S(1)}, f32[448,128]{1,0:T(8,128)S(1)}, u32[]{:S(2)}, u32[]{:S(2)}) %collective-permute-start.4) | collective-permute-done | bytes 229408 | tf_op jit(solution)/shard_map/ppermute | solution.py:124
  69.8 4.6 %collective-permute-start.6 = (f32[176,128]{1,0:T(8,128)S(1)}, f32[176,128]{1,0:T(8,128)S(1)}, u32[]{:S(2)}, u32[]{:S(2)}) collective-permute-start(f32[176,128]{1,0:T(8,128)S(1)} %get-tuple-element.34), channel_id=1, source_target_pairs={{0,1},{1,2},{2,3},{3,0},{4,5},{5,6},{6,7},{7,4},{8,9},{9,10},{10,1... | collective-permute-start | bytes 270344 | tf_op jit(solution)/shard_map/ppermute | solution.py:124
  74.4 0.0 collective-permute-start.7
  74.4 3.0 %collective-permute-done.6 = f32[176,128]{1,0:T(8,128)S(1)} collective-permute-done((f32[176,128]{1,0:T(8,128)S(1)}, f32[176,128]{1,0:T(8,128)S(1)}, u32[]{:S(2)}, u32[]{:S(2)}) %collective-permute-start.6) | collective-permute-done | bytes 90144 | tf_op jit(solution)/shard_map/ppermute | solution.py:124
  77.5 2.4 %collective-permute-done.7 = f32[176,128]{1,0:T(8,128)S(1)} collective-permute-done((f32[176,128]{1,0:T(8,128)S(1)}, f32[176,128]{1,0:T(8,128)S(1)}, u32[]{:S(2)}, u32[]{:S(2)}) %collective-permute-start.7) | collective-permute-done | bytes 90144 | tf_op jit(solution)/shard_map/ppermute | solution.py:124
  79.9 1.0 pad_maximum_fusion.4.s_ref
  80.9 0.0 collective-permute-done.3
  80.9 0.0 collective-permute-done.2
  80.9 1.2 pad_maximum_fusion.c_ref
  82.1 1.3 pad_maximum_fusion.2
  83.4 0.0 copy-start.6
  83.4 15.2 %shard_map.113 = (f32[8,64,128]{2,1,0:T(8,128)}, f32[3,8,64,128]{3,2,1,0:T(8,128)}) custom-call(f32[3]{0:T(128)} %dif_ref.3, f32[3]{0:T(128)} %copy-done.5, f32[22,80,128]{2,1,0:T(8,128)} %get-tuple-element.83.f_ref, f32[22,80,128]{2,1,0:T(8,128)} %get-tuple-element.84.p_ref, f32[22,80,128]{2,1,0:T(8,128)} %pad_maximum_fusion.4.s_ref, ...), custom_call_target="tpu_custom_call" | custom-call | flops 40755200 | bytes 4980736 | tf_op jit(solution)/shard_map/pallas_call | solution.py:240
  98.6 1.0 fusion.47
  99.6 0.0 copy-done.6
  99.6 0.0 copy-start.4
  99.6 1.3 multiply_reduce_fusion
  101.0 0.0 copy-done.4
  101.1 0.9 collective-permute-start.9
  102.0 0.8 collective-permute-start.8
  102.8 12.1 %collective-permute-done.9 = f32[1088,128]{1,0:T(8,128)S(1)} collective-permute-done((f32[1088,128]{1,0:T(8,128)S(1)}, f32[1088,128]{1,0:T(8,128)S(1)}, u32[]{:S(2)}, u32[]{:S(2)}) %collective-permute-start.9) | collective-permute-done | bytes 557088 | tf_op jit(solution)/shard_map/ppermute | solution.py:124
  114.9 4.8 %collective-permute-done.8 = f32[1088,128]{1,0:T(8,128)S(1)} collective-permute-done((f32[1088,128]{1,0:T(8,128)S(1)}, f32[1088,128]{1,0:T(8,128)S(1)}, u32[]{:S(2)}, u32[]{:S(2)}) %collective-permute-start.8) | collective-permute-done | bytes 557088 | tf_op jit(solution)/shard_map/ppermute | solution.py:124
  119.7 0.0 copy-start.1
  119.8 1.0 copy-done.1
  120.9 1.7 %collective-permute-start.11 = (f32[592,128]{1,0:T(8,128)S(1)}, f32[592,128]{1,0:T(8,128)S(1)}, u32[]{:S(2)}, u32[]{:S(2)}) collective-permute-start(f32[592,128]{1,0:T(8,128)S(1)} %pad_maximum_fusion.14), channel_id=1, source_target_pairs={{0,3},{1,0},{2,1},{3,2},{4,7},{5,4},{6,5},{7,6},{8,11},{9,8},{10,9... | collective-permute-start | bytes 909320 | tf_op jit(solution)/shard_map/ppermute | solution.py:124
  122.7 1.7 %collective-permute-start.10 = (f32[592,128]{1,0:T(8,128)S(1)}, f32[592,128]{1,0:T(8,128)S(1)}, u32[]{:S(2)}, u32[]{:S(2)}) collective-permute-start(f32[592,128]{1,0:T(8,128)S(1)} %pad_maximum_fusion.13), channel_id=1, source_target_pairs={{0,1},{1,2},{2,3},{3,0},{4,5},{5,6},{6,7},{7,4},{8,9},{9,10},{10,1... | collective-permute-start | bytes 909320 | tf_op jit(solution)/shard_map/ppermute | solution.py:124
  124.3 6.6 %collective-permute-done.11 = f32[592,128]{1,0:T(8,128)S(1)} collective-permute-done((f32[592,128]{1,0:T(8,128)S(1)}, f32[592,128]{1,0:T(8,128)S(1)}, u32[]{:S(2)}, u32[]{:S(2)}) %collective-permute-start.11) | collective-permute-done | bytes 303136 | tf_op jit(solution)/shard_map/ppermute | solution.py:124
  131.0 0.0 collective-permute-done.10
  131.0 1.0 pad_maximum_fusion.6.s_ref
  132.0 1.2 pad_maximum_fusion.1.c_ref
  133.2 1.0 pad_maximum_fusion.5.f_ref
  134.2 15.2 %shard_map.114 = (f32[8,64,128]{2,1,0:T(8,128)}, f32[3,8,64,128]{3,2,1,0:T(8,128)}) custom-call(f32[3]{0:T(128)} %dif_ref.3, f32[3]{0:T(128)} %copy-done.5, f32[22,80,128]{2,1,0:T(8,128)} %pad_maximum_fusion.5.f_ref, f32[22,80,128]{2,1,0:T(8,128)} %get-tuple-element.84.p_ref, f32[22,80,128]{2,1,0:T(8,128)} %pad_maximum_fusion.6.s_ref, ...), custom_call_target="tpu_custom_call" | custom-call | flops 40755200 | bytes 4980736 | tf_op jit(solution)/shard_map/pallas_call | solution.py:240
  (44 shorter events, 0.9 us)
Async XLA Ops:
  0.6 14.0 %copy-start.2 = (f32[8,64,128]{2,1,0:T(8,128)S(1)}, f32[8,64,128]{2,1,0:T(8,128)}, u32[]{:S(2)}) copy-start(f32[8,64,128]{2,1,0:T(8,128)} %param.12) | copy-start | bytes 786436
  14.7 8.0 %copy-start.8 = (s32[3]{0:T(128)S(1)}, s32[3]{0:T(128)}, u32[]{:S(2)}) copy-start(s32[3]{0:T(128)} %param.14) | copy-start | bytes 40
  14.7 8.0 %copy-start.7 = (s32[1,1,512]{2,1,0:T(1,128)S(1)}, s32[1,1,512]{2,1,0:T(1,128)}, u32[]{:S(2)}) copy-start(s32[1,1,512]{2,1,0:T(1,128)} %param.18) | copy-start | bytes 6148
  14.7 44.7 %collective-permute-start.1 = (f32[1088,128]{1,0:T(8,128)S(1)}, f32[1088,128]{1,0:T(8,128)S(1)}, u32[]{:S(2)}, u32[]{:S(2)}) collective-permute-start(f32[1088,128]{1,0:T(8,128)S(1)} %pad_maximum_fusion.8), channel_id=1, source_target_pairs={{0,252},{4,0},{8,4},{12,8},{16,12},{20,16},{24,20},{28,24},{32,28}... | collective-permute-start | bytes 1671176 | tf_op jit(solution)/shard_map/ppermute | solution.py:124
  21.9 37.6 %collective-permute-start = (f32[1088,128]{1,0:T(8,128)S(1)}, f32[1088,128]{1,0:T(8,128)S(1)}, u32[]{:S(2)}, u32[]{:S(2)}) collective-permute-start(f32[1088,128]{1,0:T(8,128)S(1)} %pad_maximum_fusion.7), channel_id=1, source_target_pairs={{0,4},{4,8},{8,12},{12,16},{16,20},{20,24},{24,28},{28,32},{32,36}... | collective-permute-start | bytes 1671176 | tf_op jit(solution)/shard_map/ppermute | solution.py:124
  22.7 30.8 %copy-start.5 = (f32[3]{0:T(128)}, f32[3]{0:T(128)S(1)}, u32[]{:S(2)}) copy-start(f32[3]{0:T(128)S(1)} %convert_element_type.27.val_ref) | copy-start | bytes 40
  22.9 30.6 %copy-start = (f32[3,8,64,128]{3,2,1,0:T(8,128)S(1)}, f32[3,8,64,128]{3,2,1,0:T(8,128)}, u32[]{:S(2)}) copy-start(f32[3,8,64,128]{3,2,1,0:T(8,128)} %param.10) | copy-start | bytes 2359300
  53.7 10.5 %collective-permute-start.5 = (f32[448,128]{1,0:T(8,128)S(1)}, f32[448,128]{1,0:T(8,128)S(1)}, u32[]{:S(2)}, u32[]{:S(2)}) collective-permute-start(f32[448,128]{1,0:T(8,128)S(1)} %bitcast.136), channel_id=1, source_target_pairs={{0,252},{4,0},{8,4},{12,8},{16,12},{20,16},{24,20},{28,24},{32,28}... | collective-permute-start | bytes 688136 | tf_op jit(solution)/shard_map/ppermute | solution.py:124
  59.5 0.9 copy-start.3
  59.5 10.3 %collective-permute-start.4 = (f32[448,128]{1,0:T(8,128)S(1)}, f32[448,128]{1,0:T(8,128)S(1)}, u32[]{:S(2)}, u32[]{:S(2)}) collective-permute-start(f32[448,128]{1,0:T(8,128)S(1)} %bitcast.135), channel_id=1, source_target_pairs={{0,4},{4,8},{8,12},{12,16},{16,20},{20,24},{24,28},{28,32},{32,36}... | collective-permute-start | bytes 688136 | tf_op jit(solution)/shard_map/ppermute | solution.py:124
  60.5 20.3 %collective-permute-start.3 = (f32[592,128]{1,0:T(8,128)S(1)}, f32[592,128]{1,0:T(8,128)S(1)}, u32[]{:S(2)}, u32[]{:S(2)}) collective-permute-start(f32[592,128]{1,0:T(8,128)S(1)} %pad_maximum_fusion.12), channel_id=1, source_target_pairs={{0,3},{1,0},{2,1},{3,2},{4,7},{5,4},{6,5},{7,6},{8,11},{9,8},{10,9... | collective-permute-start | bytes 909320 | tf_op jit(solution)/shard_map/ppermute | solution.py:124
  61.6 19.2 %collective-permute-start.2 = (f32[592,128]{1,0:T(8,128)S(1)}, f32[592,128]{1,0:T(8,128)S(1)}, u32[]{:S(2)}, u32[]{:S(2)}) collective-permute-start(f32[592,128]{1,0:T(8,128)S(1)} %pad_maximum_fusion.11), channel_id=1, source_target_pairs={{0,1},{1,2},{2,3},{3,0},{4,5},{5,6},{6,7},{7,4},{8,9},{9,10},{10,1... | collective-permute-start | bytes 909320 | tf_op jit(solution)/shard_map/ppermute | solution.py:124
  69.8 7.6 %collective-permute-start.6 = (f32[176,128]{1,0:T(8,128)S(1)}, f32[176,128]{1,0:T(8,128)S(1)}, u32[]{:S(2)}, u32[]{:S(2)}) collective-permute-start(f32[176,128]{1,0:T(8,128)S(1)} %get-tuple-element.34), channel_id=1, source_target_pairs={{0,1},{1,2},{2,3},{3,0},{4,5},{5,6},{6,7},{7,4},{8,9},{9,10},{10,1... | collective-permute-start | bytes 270344 | tf_op jit(solution)/shard_map/ppermute | solution.py:124
  74.4 5.5 %collective-permute-start.7 = (f32[176,128]{1,0:T(8,128)S(1)}, f32[176,128]{1,0:T(8,128)S(1)}, u32[]{:S(2)}, u32[]{:S(2)}) collective-permute-start(f32[176,128]{1,0:T(8,128)S(1)} %get-tuple-element.35), channel_id=1, source_target_pairs={{0,3},{1,0},{2,1},{3,2},{4,7},{5,4},{6,5},{7,6},{8,11},{9,8},{10,9... | collective-permute-start | bytes 270344 | tf_op jit(solution)/shard_map/ppermute | solution.py:124
  83.4 16.1 %copy-start.6 = (f32[3]{0:T(128)S(1)}, f32[3]{0:T(128)}, u32[]{:S(2)}) copy-start(f32[3]{0:T(128)} %copy-done.5) | copy-start | bytes 40
  99.6 1.4 copy-start.4
  101.1 13.7 %collective-permute-start.9 = (f32[1088,128]{1,0:T(8,128)S(1)}, f32[1088,128]{1,0:T(8,128)S(1)}, u32[]{:S(2)}, u32[]{:S(2)}) collective-permute-start(f32[1088,128]{1,0:T(8,128)S(1)} %pad_maximum_fusion.10), channel_id=1, source_target_pairs={{0,252},{4,0},{8,4},{12,8},{16,12},{20,16},{24,20},{28,24},{32,28}... | collective-permute-start | bytes 1671176 | tf_op jit(solution)/shard_map/ppermute | solution.py:124
  102.0 17.7 %collective-permute-start.8 = (f32[1088,128]{1,0:T(8,128)S(1)}, f32[1088,128]{1,0:T(8,128)S(1)}, u32[]{:S(2)}, u32[]{:S(2)}) collective-permute-start(f32[1088,128]{1,0:T(8,128)S(1)} %pad_maximum_fusion.9), channel_id=1, source_target_pairs={{0,4},{4,8},{8,12},{12,16},{16,20},{20,24},{24,28},{28,32},{32,36}... | collective-permute-start | bytes 1671176 | tf_op jit(solution)/shard_map/ppermute | solution.py:124
  119.7 1.1 copy-start.1
  120.9 10.0 %collective-permute-start.11 = (f32[592,128]{1,0:T(8,128)S(1)}, f32[592,128]{1,0:T(8,128)S(1)}, u32[]{:S(2)}, u32[]{:S(2)}) collective-permute-start(f32[592,128]{1,0:T(8,128)S(1)} %pad_maximum_fusion.14), channel_id=1, source_target_pairs={{0,3},{1,0},{2,1},{3,2},{4,7},{5,4},{6,5},{7,6},{8,11},{9,8},{10,9... | collective-permute-start | bytes 909320 | tf_op jit(solution)/shard_map/ppermute | solution.py:124
  122.7 8.3 %collective-permute-start.10 = (f32[592,128]{1,0:T(8,128)S(1)}, f32[592,128]{1,0:T(8,128)S(1)}, u32[]{:S(2)}, u32[]{:S(2)}) collective-permute-start(f32[592,128]{1,0:T(8,128)S(1)} %pad_maximum_fusion.13), channel_id=1, source_target_pairs={{0,1},{1,2},{2,3},{3,0},{4,5},{5,6},{6,7},{7,4},{8,9},{9,10},{10,1... | collective-permute-start | bytes 909320 | tf_op jit(solution)/shard_map/ppermute | solution.py:124

commit v5 on v4

--- a/solution.py
+++ b/solution.py
@@ -150,7 +150,15 @@
     return [item[0] for item in items]
 
 
-def step_kernel(dif_ref, val_ref, f_ref, p_ref, s_ref, c_ref, fo_ref, co_ref, fa, fb, w_ref):
+def step_kernel(
+    dif_ref, val_ref, f_hbm, p_hbm, s_hbm, c_hbm, fo_ref, co_ref, f_ref, p_ref, s_ref, c_ref, fa, fb, w_ref, sems
+):
+    copies = [
+        pltpu.make_async_copy(src, dst, sems.at[k])
+        for k, (src, dst) in enumerate(((p_hbm, p_ref), (f_hbm, f_ref), (s_hbm, s_ref), (c_hbm, c_ref)))
+    ]
+    for copy in copies:
+        copy.start()
     planes, rows, lanes = f_ref.shape
     species, inner = c_ref.shape[0], c_ref.shape[1] - 2
     hz = (planes - inner) // 2
@@ -183,7 +191,10 @@
         w_ref[6, z] = 1.0 / den
         return carry
 
+    copies[0].wait()
     lax.fori_loop(1, planes - 1, weights, 0)
+    copies[1].wait()
+    copies[2].wait()
     bufs = (fa, fb)
     sweeps = hz - 1
     for k in range(sweeps):
@@ -204,6 +215,7 @@
 
         lax.fori_loop(k + 1, planes - k - 1, sweep, 0)
     final = bufs[(sweeps - 1) % 2]
+    copies[3].wait()
 
     def move(z, carry):
         zf = z + hz
@@ -236,6 +248,7 @@
     out_rows = rows - 2 * (SWEEPS + 2)
     smem = pl.BlockSpec(memory_space=pltpu.SMEM)
     vmem = pl.BlockSpec(memory_space=pltpu.VMEM)
+    hbm = pl.BlockSpec(memory_space=pl.ANY)
     points = planes * rows * lanes
     return pl.pallas_call(
         step_kernel,
@@ -243,12 +256,17 @@
             jax.ShapeDtypeStruct((inner, out_rows, lanes), jnp.float32),
             jax.ShapeDtypeStruct((species, inner, out_rows, lanes), jnp.float32),
         ),
-        in_specs=[smem, smem, vmem, vmem, vmem, vmem],
+        in_specs=[smem, smem, hbm, hbm, hbm, hbm],
         out_specs=(vmem, vmem),
         scratch_shapes=[
             pltpu.VMEM((planes, rows, lanes), jnp.float32),
             pltpu.VMEM((planes, rows, lanes), jnp.float32),
+            pltpu.VMEM((planes, rows, lanes), jnp.float32),
+            pltpu.VMEM(species_e.shape, jnp.float32),
+            pltpu.VMEM((planes, rows, lanes), jnp.float32),
+            pltpu.VMEM((planes, rows, lanes), jnp.float32),
             pltpu.VMEM((7, planes, rows, lanes), jnp.float32),
+            pltpu.SemaphoreType.DMA((4,)),
         ],
         cost_estimate=pl.CostEstimate(
             flops=points * (20 * SWEEPS + 20) + species_e.size * 30,

time: 150 us -> 150 us (level)
  no operation moved by 1% of the time
where the time goes in v5:
time: 150 us; the launch traced here: 149 us
  other arithmetic  40.8 us (27%)
  waiting for transfers between devices  34.5 us (23%)
  Pallas kernels  29.9 us (20%)
  starting transfers between devices  26.3 us (18%)
  blocking collectives  10.4 us (7%)
  local copies, waits for them, and re-layouts  5.33 us (4%)
  between operations  1.95 us (1%)
    ppermute x12, waiting for transfers between devices, ring(): lax.ppermute(x, axis, [(i, (i + shift) % count) for i in range(count)])  34.5 us
    pallas_call x2, Pallas kernels, time_step(): pl.pallas_call(step_kernel, out_shape=(jax.ShapeDtypeStruct((inner, out_r...  29.9 us
    reduce_sum x1, other arithmetic, one_block(): return jnp.sum(jnp.where(adjacent, term, 0.0), axis=1)  27.2 us
    ppermute x12, starting transfers between devices, ring(): lax.ppermute(x, axis, [(i, (i + shift) % count) for i in range(count)])  26.3 us
    all_gather x1, blocking collectives, per_device(): gathered = lax.all_gather(charges, 'narrow', axis=1, tiled=True)  10.4 us
    concatenate x6, other arithmetic, deep_halo(): jnp.concatenate([lo, a, hi], axis=a.ndim - back)  6.61 us
    scatter-add x1, other arithmetic, per_device(): jnp.zeros((depth * height * width,), jnp.float32).at[index].add(values)  3.33 us
    slice x7, local copies, waits for them, and re-layouts, deep_halo(): tops.append(lax.slice_in_dim(a, n - w, n, axis=dim))  3.15 us
  transfers between devices with their start and end apart: 12, of which 6 were waited for; matrix products, arithmetic and copies ran while one was open for 22% of the time, Pallas kernels for 0%

profile of v5, /device:TPU:1, one launch (start us, length us, event | category | flops | bytes accessed | tf_op | source)
XLA Modules:
  0.0 149.1 jit_solution(5429675717453727116)
XLA Ops:
  0.6 0.0 copy-start.2
  0.6 0.7 convert_element_type.28
  1.4 0.8 pad_maximum_fusion.31
  2.2 10.4 %all_gather.3 = f32[5,8192]{1,0:T(8,128)S(1)} all-gather(f32[5,2048]{1,0:T(8,128)S(1)} %pad_maximum_fusion.31), channel_id=1, replica_groups=mesh['wide'=64,'narrow'=4] {'narrow'}, dimensions={1}, use_global_device_ids=true | all-gather | bytes 204800 | tf_op jit(solution)/shard_map/all_gather | solution.py:319
  12.6 1.0 fusion.48
  13.5 1.1 fusion.57
  14.6 0.0 copy-done.2
  14.7 0.0 copy-start.8
  14.7 0.0 copy-start.7
  14.7 7.1 %collective-permute-start.1 = (f32[1088,128]{1,0:T(8,128)S(1)}, f32[1088,128]{1,0:T(8,128)S(1)}, u32[]{:S(2)}, u32[]{:S(2)}) collective-permute-start(f32[1088,128]{1,0:T(8,128)S(1)} %pad_maximum_fusion.8), channel_id=1, source_target_pairs={{0,252},{4,0},{8,4},{12,8},{16,12},{20,16},{24,20},{28,24},{32,28}... | collective-permute-start | bytes 1671176 | tf_op jit(solution)/shard_map/ppermute | solution.py:124
  21.9 0.1 collective-permute-start
  22.6 0.0 copy-done.8
  22.7 0.0 copy-start.5
  22.7 0.0 copy-done.7
  22.8 0.1 fusion.56
  22.9 0.0 copy-start
  22.9 27.2 %select_reduce_fusion.1 = (f32[256]{0:T(256)S(1)}, f32[256]{0:T(256)S(1)}) fusion(f32[8192]{0:T(1024)S(1)} %bitcast.140, f32[256]{0:T(256)S(1)} %get-tuple-element.87, f32[8192]{0:T(1024)S(1)} %bitcast.141, f32[256]{0:T(256)S(1)} %get-tuple-element.76, f32[8192]{0:T(1024)S(1)} %bitcast.142, f32[256]{0:T(256)S(1)} %get-tuple-element.85, ...), kind=kLoop, calls=%fused_computation.28 | loop fusion | flops 138411520 | bytes 174080 | tf_op jit(solution)/shard_map/reduce_sum | solution.py:115
  50.1 3.3 %scatter_custom_fusion = f32[65536]{0:T(1024)S(1)} fusion(s32[512]{0:T(512)S(1)} %bitcast.145, f32[512]{0:T(512)S(1)} %maximum_multiply_fusion, f32[]{:T(128)} %constant.81.clone.1), kind=kCustom, calls=%fused_computation.58 | custom fusion | flops 512 | bytes 262148 | tf_op jit(solution)/shard_map/scatter-add | solution.py:342
  53.5 0.0 copy-done.5
  53.5 0.0 copy-done
  53.5 0.1 multiply_reduce_fusion.1
  53.7 5.7 %collective-permute-start.5 = (f32[448,128]{1,0:T(8,128)S(1)}, f32[448,128]{1,0:T(8,128)S(1)}, u32[]{:S(2)}, u32[]{:S(2)}) collective-permute-start(f32[448,128]{1,0:T(8,128)S(1)} %bitcast.136), channel_id=1, source_target_pairs={{0,252},{4,0},{8,4},{12,8},{16,12},{20,16},{24,20},{28,24},{32,28}... | collective-permute-start | bytes 688136 | tf_op jit(solution)/shard_map/ppermute | solution.py:124
  59.5 0.0 copy-start.3
  59.5 0.0 collective-permute-start.4
  59.5 0.0 collective-permute-done.1
  59.5 0.0 collective-permute-done
  59.6 0.8 copy-done.3
  60.5 1.1 collective-permute-start.3
  61.6 2.6 %collective-permute-start.2 = (f32[592,128]{1,0:T(8,128)S(1)}, f32[592,128]{1,0:T(8,128)S(1)}, u32[]{:S(2)}, u32[]{:S(2)}) collective-permute-start(f32[592,128]{1,0:T(8,128)S(1)} %pad_maximum_fusion.11), channel_id=1, source_target_pairs={{0,1},{1,2},{2,3},{3,0},{4,5},{5,6},{6,7},{7,4},{8,9},{9,10},{10,1... | collective-permute-start | bytes 909320 | tf_op jit(solution)/shard_map/ppermute | solution.py:124
  64.2 0.0 collective-permute-done.5
  64.2 5.6 %collective-permute-done.4 = f32[448,128]{1,0:T(8,128)S(1)} collective-permute-done((f32[448,128]{1,0:T(8,128)S(1)}, f32[448,128]{1,0:T(8,128)S(1)}, u32[]{:S(2)}, u32[]{:S(2)}) %collective-permute-start.4) | collective-permute-done | bytes 229408 | tf_op jit(solution)/shard_map/ppermute | solution.py:124
  69.8 4.6 %collective-permute-start.6 = (f32[176,128]{1,0:T(8,128)S(1)}, f32[176,128]{1,0:T(8,128)S(1)}, u32[]{:S(2)}, u32[]{:S(2)}) collective-permute-start(f32[176,128]{1,0:T(8,128)S(1)} %get-tuple-element.34), channel_id=1, source_target_pairs={{0,1},{1,2},{2,3},{3,0},{4,5},{5,6},{6,7},{7,4},{8,9},{9,10},{10,1... | collective-permute-start | bytes 270344 | tf_op jit(solution)/shard_map/ppermute | solution.py:124
  74.4 0.0 collective-permute-start.7
  74.4 3.0 %collective-permute-done.6 = f32[176,128]{1,0:T(8,128)S(1)} collective-permute-done((f32[176,128]{1,0:T(8,128)S(1)}, f32[176,128]{1,0:T(8,128)S(1)}, u32[]{:S(2)}, u32[]{:S(2)}) %collective-permute-start.6) | collective-permute-done | bytes 90144 | tf_op jit(solution)/shard_map/ppermute | solution.py:124
  77.5 2.4 %collective-permute-done.7 = f32[176,128]{1,0:T(8,128)S(1)} collective-permute-done((f32[176,128]{1,0:T(8,128)S(1)}, f32[176,128]{1,0:T(8,128)S(1)}, u32[]{:S(2)}, u32[]{:S(2)}) %collective-permute-start.7) | collective-permute-done | bytes 90144 | tf_op jit(solution)/shard_map/ppermute | solution.py:124
  79.9 1.0 pad_maximum_fusion.4.s_hbm
  80.9 0.0 collective-permute-done.3
  80.9 0.0 collective-permute-done.2
  80.9 1.2 pad_maximum_fusion.c_hbm
  82.1 1.3 pad_maximum_fusion.2
  83.4 0.0 copy-start.6
  83.4 15.0 %shard_map.113 = (f32[8,64,128]{2,1,0:T(8,128)}, f32[3,8,64,128]{3,2,1,0:T(8,128)}) custom-call(f32[3]{0:T(128)} %dif_ref.3, f32[3]{0:T(128)} %copy-done.5, f32[22,80,128]{2,1,0:T(8,128)} %get-tuple-element.83.f_hbm, f32[22,80,128]{2,1,0:T(8,128)} %get-tuple-element.84.p_hbm, f32[22,80,128]{2,1,0:T(8,128)} %pad_maximum_fusion.4.s_hbm, ...), custom_call_target="tpu_custom_call" | custom-call | flops 40755200 | bytes 4980736 | tf_op jit(solution)/shard_map/pallas_call | solution.py:253
  98.4 1.0 fusion.47
  99.4 0.0 copy-done.6
  99.4 0.0 copy-start.4
  99.4 1.3 multiply_reduce_fusion
  100.9 0.0 copy-done.4
  101.0 0.9 collective-permute-start.9
  101.9 0.8 collective-permute-start.8
  102.6 12.1 %collective-permute-done.9 = f32[1088,128]{1,0:T(8,128)S(1)} collective-permute-done((f32[1088,128]{1,0:T(8,128)S(1)}, f32[1088,128]{1,0:T(8,128)S(1)}, u32[]{:S(2)}, u32[]{:S(2)}) %collective-permute-start.9) | collective-permute-done | bytes 557088 | tf_op jit(solution)/shard_map/ppermute | solution.py:124
  114.7 4.8 %collective-permute-done.8 = f32[1088,128]{1,0:T(8,128)S(1)} collective-permute-done((f32[1088,128]{1,0:T(8,128)S(1)}, f32[1088,128]{1,0:T(8,128)S(1)}, u32[]{:S(2)}, u32[]{:S(2)}) %collective-permute-start.8) | collective-permute-done | bytes 557088 | tf_op jit(solution)/shard_map/ppermute | solution.py:124
  119.6 0.0 copy-start.1
  119.7 1.0 copy-done.1
  120.8 1.7 %collective-permute-start.11 = (f32[592,128]{1,0:T(8,128)S(1)}, f32[592,128]{1,0:T(8,128)S(1)}, u32[]{:S(2)}, u32[]{:S(2)}) collective-permute-start(f32[592,128]{1,0:T(8,128)S(1)} %pad_maximum_fusion.14), channel_id=1, source_target_pairs={{0,3},{1,0},{2,1},{3,2},{4,7},{5,4},{6,5},{7,6},{8,11},{9,8},{10,9... | collective-permute-start | bytes 909320 | tf_op jit(solution)/shard_map/ppermute | solution.py:124
  122.5 1.7 %collective-permute-start.10 = (f32[592,128]{1,0:T(8,128)S(1)}, f32[592,128]{1,0:T(8,128)S(1)}, u32[]{:S(2)}, u32[]{:S(2)}) collective-permute-start(f32[592,128]{1,0:T(8,128)S(1)} %pad_maximum_fusion.13), channel_id=1, source_target_pairs={{0,1},{1,2},{2,3},{3,0},{4,5},{5,6},{6,7},{7,4},{8,9},{9,10},{10,1... | collective-permute-start | bytes 909320 | tf_op jit(solution)/shard_map/ppermute | solution.py:124
  124.2 6.6 %collective-permute-done.11 = f32[592,128]{1,0:T(8,128)S(1)} collective-permute-done((f32[592,128]{1,0:T(8,128)S(1)}, f32[592,128]{1,0:T(8,128)S(1)}, u32[]{:S(2)}, u32[]{:S(2)}) %collective-permute-start.11) | collective-permute-done | bytes 303136 | tf_op jit(solution)/shard_map/ppermute | solution.py:124
  130.8 0.0 collective-permute-done.10
  130.8 1.0 pad_maximum_fusion.6.s_hbm
  131.8 1.2 pad_maximum_fusion.1.c_hbm
  133.0 1.0 pad_maximum_fusion.5.f_hbm
  134.0 14.9 %shard_map.114 = (f32[8,64,128]{2,1,0:T(8,128)}, f32[3,8,64,128]{3,2,1,0:T(8,128)}) custom-call(f32[3]{0:T(128)} %dif_ref.3, f32[3]{0:T(128)} %copy-done.5, f32[22,80,128]{2,1,0:T(8,128)} %pad_maximum_fusion.5.f_hbm, f32[22,80,128]{2,1,0:T(8,128)} %get-tuple-element.84.p_hbm, f32[22,80,128]{2,1,0:T(8,128)} %pad_maximum_fusion.6.s_hbm, ...), custom_call_target="tpu_custom_call" | custom-call | flops 40755200 | bytes 4980736 | tf_op jit(solution)/shard_map/pallas_call | solution.py:253
  (44 shorter events, 0.9 us)
Async XLA Ops:
  0.6 14.0 %copy-start.2 = (f32[8,64,128]{2,1,0:T(8,128)S(1)}, f32[8,64,128]{2,1,0:T(8,128)}, u32[]{:S(2)}) copy-start(f32[8,64,128]{2,1,0:T(8,128)} %param.12) | copy-start | bytes 786436
  14.7 8.0 %copy-start.8 = (s32[3]{0:T(128)S(1)}, s32[3]{0:T(128)}, u32[]{:S(2)}) copy-start(s32[3]{0:T(128)} %param.14) | copy-start | bytes 40
  14.7 8.0 %copy-start.7 = (s32[1,1,512]{2,1,0:T(1,128)S(1)}, s32[1,1,512]{2,1,0:T(1,128)}, u32[]{:S(2)}) copy-start(s32[1,1,512]{2,1,0:T(1,128)} %param.18) | copy-start | bytes 6148
  14.7 44.7 %collective-permute-start.1 = (f32[1088,128]{1,0:T(8,128)S(1)}, f32[1088,128]{1,0:T(8,128)S(1)}, u32[]{:S(2)}, u32[]{:S(2)}) collective-permute-start(f32[1088,128]{1,0:T(8,128)S(1)} %pad_maximum_fusion.8), channel_id=1, source_target_pairs={{0,252},{4,0},{8,4},{12,8},{16,12},{20,16},{24,20},{28,24},{32,28}... | collective-permute-start | bytes 1671176 | tf_op jit(solution)/shard_map/ppermute | solution.py:124
  21.9 37.6 %collective-permute-start = (f32[1088,128]{1,0:T(8,128)S(1)}, f32[1088,128]{1,0:T(8,128)S(1)}, u32[]{:S(2)}, u32[]{:S(2)}) collective-permute-start(f32[1088,128]{1,0:T(8,128)S(1)} %pad_maximum_fusion.7), channel_id=1, source_target_pairs={{0,4},{4,8},{8,12},{12,16},{16,20},{20,24},{24,28},{28,32},{32,36}... | collective-permute-start | bytes 1671176 | tf_op jit(solution)/shard_map/ppermute | solution.py:124
  22.7 30.8 %copy-start.5 = (f32[3]{0:T(128)}, f32[3]{0:T(128)S(1)}, u32[]{:S(2)}) copy-start(f32[3]{0:T(128)S(1)} %convert_element_type.27.val_ref) | copy-start | bytes 40
  22.9 30.6 %copy-start = (f32[3,8,64,128]{3,2,1,0:T(8,128)S(1)}, f32[3,8,64,128]{3,2,1,0:T(8,128)}, u32[]{:S(2)}) copy-start(f32[3,8,64,128]{3,2,1,0:T(8,128)} %param.10) | copy-start | bytes 2359300
  53.7 10.5 %collective-permute-start.5 = (f32[448,128]{1,0:T(8,128)S(1)}, f32[448,128]{1,0:T(8,128)S(1)}, u32[]{:S(2)}, u32[]{:S(2)}) collective-permute-start(f32[448,128]{1,0:T(8,128)S(1)} %bitcast.136), channel_id=1, source_target_pairs={{0,252},{4,0},{8,4},{12,8},{16,12},{20,16},{24,20},{28,24},{32,28}... | collective-permute-start | bytes 688136 | tf_op jit(solution)/shard_map/ppermute | solution.py:124
  59.5 0.9 copy-start.3
  59.5 10.3 %collective-permute-start.4 = (f32[448,128]{1,0:T(8,128)S(1)}, f32[448,128]{1,0:T(8,128)S(1)}, u32[]{:S(2)}, u32[]{:S(2)}) collective-permute-start(f32[448,128]{1,0:T(8,128)S(1)} %bitcast.135), channel_id=1, source_target_pairs={{0,4},{4,8},{8,12},{12,16},{16,20},{20,24},{24,28},{28,32},{32,36}... | collective-permute-start | bytes 688136 | tf_op jit(solution)/shard_map/ppermute | solution.py:124
  60.5 20.3 %collective-permute-start.3 = (f32[592,128]{1,0:T(8,128)S(1)}, f32[592,128]{1,0:T(8,128)S(1)}, u32[]{:S(2)}, u32[]{:S(2)}) collective-permute-start(f32[592,128]{1,0:T(8,128)S(1)} %pad_maximum_fusion.12), channel_id=1, source_target_pairs={{0,3},{1,0},{2,1},{3,2},{4,7},{5,4},{6,5},{7,6},{8,11},{9,8},{10,9... | collective-permute-start | bytes 909320 | tf_op jit(solution)/shard_map/ppermute | solution.py:124
  61.6 19.2 %collective-permute-start.2 = (f32[592,128]{1,0:T(8,128)S(1)}, f32[592,128]{1,0:T(8,128)S(1)}, u32[]{:S(2)}, u32[]{:S(2)}) collective-permute-start(f32[592,128]{1,0:T(8,128)S(1)} %pad_maximum_fusion.11), channel_id=1, source_target_pairs={{0,1},{1,2},{2,3},{3,0},{4,5},{5,6},{6,7},{7,4},{8,9},{9,10},{10,1... | collective-permute-start | bytes 909320 | tf_op jit(solution)/shard_map/ppermute | solution.py:124
  69.8 7.6 %collective-permute-start.6 = (f32[176,128]{1,0:T(8,128)S(1)}, f32[176,128]{1,0:T(8,128)S(1)}, u32[]{:S(2)}, u32[]{:S(2)}) collective-permute-start(f32[176,128]{1,0:T(8,128)S(1)} %get-tuple-element.34), channel_id=1, source_target_pairs={{0,1},{1,2},{2,3},{3,0},{4,5},{5,6},{6,7},{7,4},{8,9},{9,10},{10,1... | collective-permute-start | bytes 270344 | tf_op jit(solution)/shard_map/ppermute | solution.py:124
  74.4 5.5 %collective-permute-start.7 = (f32[176,128]{1,0:T(8,128)S(1)}, f32[176,128]{1,0:T(8,128)S(1)}, u32[]{:S(2)}, u32[]{:S(2)}) collective-permute-start(f32[176,128]{1,0:T(8,128)S(1)} %get-tuple-element.35), channel_id=1, source_target_pairs={{0,3},{1,0},{2,1},{3,2},{4,7},{5,4},{6,5},{7,6},{8,11},{9,8},{10,9... | collective-permute-start | bytes 270344 | tf_op jit(solution)/shard_map/ppermute | solution.py:124
  83.4 16.0 %copy-start.6 = (f32[3]{0:T(128)S(1)}, f32[3]{0:T(128)}, u32[]{:S(2)}) copy-start(f32[3]{0:T(128)} %copy-done.5) | copy-start | bytes 40
  99.4 1.4 copy-start.4
  101.0 13.7 %collective-permute-start.9 = (f32[1088,128]{1,0:T(8,128)S(1)}, f32[1088,128]{1,0:T(8,128)S(1)}, u32[]{:S(2)}, u32[]{:S(2)}) collective-permute-start(f32[1088,128]{1,0:T(8,128)S(1)} %pad_maximum_fusion.10), channel_id=1, source_target_pairs={{0,252},{4,0},{8,4},{12,8},{16,12},{20,16},{24,20},{28,24},{32,28}... | collective-permute-start | bytes 1671176 | tf_op jit(solution)/shard_map/ppermute | solution.py:124
  101.9 17.7 %collective-permute-start.8 = (f32[1088,128]{1,0:T(8,128)S(1)}, f32[1088,128]{1,0:T(8,128)S(1)}, u32[]{:S(2)}, u32[]{:S(2)}) collective-permute-start(f32[1088,128]{1,0:T(8,128)S(1)} %pad_maximum_fusion.9), channel_id=1, source_target_pairs={{0,4},{4,8},{8,12},{12,16},{16,20},{20,24},{24,28},{28,32},{32,36}... | collective-permute-start | bytes 1671176 | tf_op jit(solution)/shard_map/ppermute | solution.py:124
  119.6 1.1 copy-start.1
  120.8 10.0 %collective-permute-start.11 = (f32[592,128]{1,0:T(8,128)S(1)}, f32[592,128]{1,0:T(8,128)S(1)}, u32[]{:S(2)}, u32[]{:S(2)}) collective-permute-start(f32[592,128]{1,0:T(8,128)S(1)} %pad_maximum_fusion.14), channel_id=1, source_target_pairs={{0,3},{1,0},{2,1},{3,2},{4,7},{5,4},{6,5},{7,6},{8,11},{9,8},{10,9... | collective-permute-start | bytes 909320 | tf_op jit(solution)/shard_map/ppermute | solution.py:124
  122.5 8.3 %collective-permute-start.10 = (f32[592,128]{1,0:T(8,128)S(1)}, f32[592,128]{1,0:T(8,128)S(1)}, u32[]{:S(2)}, u32[]{:S(2)}) collective-permute-start(f32[592,128]{1,0:T(8,128)S(1)} %pad_maximum_fusion.13), channel_id=1, source_target_pairs={{0,1},{1,2},{2,3},{3,0},{4,5},{5,6},{6,7},{7,4},{8,9},{9,10},{10,1... | collective-permute-start | bytes 909320 | tf_op jit(solution)/shard_map/ppermute | solution.py:124

commit v6 on v5

--- a/solution.py
+++ b/solution.py
@@ -106,12 +106,11 @@
         offset_y = pos_y[:, None] - charge_y[None, :]
         offset_y = offset_y - rows_total * jnp.floor(offset_y / rows_total + 0.5)
         offset_x = pos_x[:, None] - charge_x[None, :]
-        distance = jnp.sqrt(offset_z * offset_z + offset_y * offset_y + offset_x * offset_x)
-        tile_gap = jnp.mod(pos_tile[:, None] - label[None, :], tiles_all)
-        adjacent = (tile_gap == 0.0) | (tile_gap == 1.0) | (tile_gap == tiles_all - 1.0)
-        term = (
-            strength[None, :] * jnp.exp(-distance / tile_rows) / jnp.sqrt(distance * distance + 1.0)
-        )
+        squared = offset_z * offset_z + offset_y * offset_y + offset_x * offset_x
+        distance = jnp.sqrt(squared)
+        tile_gap = jnp.abs(pos_tile[:, None] - label[None, :])
+        adjacent = (tile_gap <= 1.0) | (tile_gap >= tiles_all - 1.0)
+        term = strength[None, :] * jnp.exp(-distance / tile_rows) * lax.rsqrt(squared + 1.0)
         return jnp.sum(jnp.where(adjacent, term, 0.0), axis=1)
 
     half = node_z.shape[0] // 2
@@ -185,16 +184,20 @@
             0.5 * (pc + jnp.where(bot, pc, xsh(pc, -1))),
         )
         den = jnp.zeros_like(pc)
-        for k, w in enumerate(ws):
-            w_ref[k, z] = w
+        for w in ws:
             den = den + w
-        w_ref[6, z] = 1.0 / den
+        inv = 1.0 / den
+        for k in range(4):
+            w_ref[k, z] = ws[k] * inv
+        w_ref[4, z] = jnp.where(top, 0.0, ws[4]) * inv
+        w_ref[5, z] = jnp.where(bot, 0.0, ws[5]) * inv
+        w_ref[6, z] = s_ref[z] * inv
         return carry
 
     copies[0].wait()
+    copies[2].wait()
     lax.fori_loop(1, planes - 1, weights, 0)
     copies[1].wait()
-    copies[2].wait()
     bufs = (fa, fb)
     sweeps = hz - 1
     for k in range(sweeps):
@@ -203,14 +206,14 @@
 
         def sweep(z, carry, rd=rd, wr=wr):
             fc = rd[z]
-            numer = s_ref[z]
-            numer = numer + w_ref[0, z] * rd[z + 1]
-            numer = numer + w_ref[1, z] * rd[z - 1]
-            numer = numer + w_ref[2, z] * ysh(fc, 1)
-            numer = numer + w_ref[3, z] * ysh(fc, -1)
-            numer = numer + w_ref[4, z] * jnp.where(top, 0.0, xsh(fc, 1))
-            numer = numer + w_ref[5, z] * jnp.where(bot, 0.0, xsh(fc, -1))
-            wr[z] = numer * w_ref[6, z]
+            new = w_ref[6, z]
+            new = new + w_ref[0, z] * rd[z + 1]
+            new = new + w_ref[1, z] * rd[z - 1]
+            new = new + w_ref[2, z] * ysh(fc, 1)
+            new = new + w_ref[3, z] * ysh(fc, -1)
+            new = new + w_ref[4, z] * xsh(fc, 1)
+            new = new + w_ref[5, z] * xsh(fc, -1)
+            wr[z] = new
             return carry
 
         lax.fori_loop(k + 1, planes - k - 1, sweep, 0)

time: 150 us -> 142 us (0.947)
  other arithmetic: 40.8 us -> 31.7 us
    reduce_sum x1, other arithmetic: 27.2 us -> 18.2 us  [one_block(): return jnp.sum(jnp.where(adjacent, term, 0.0), axis=1)]
  transfers between devices with their start and end apart: 12 -> 12, of which waited for: 6 -> 6; matrix products, arithmetic and copies ran while one was open for 22% -> 16% of each run, Pallas kernels for 0% -> 0%
where the time goes in v6:
time: 142 us; the launch traced here: 141 us
  waiting for transfers between devices  34.5 us (24%)
  other arithmetic  31.7 us (22%)
  Pallas kernels  31 us (22%)
  starting transfers between devices  26.3 us (19%)
  blocking collectives  10.4 us (7%)
  local copies, waits for them, and re-layouts  5.33 us (4%)
  between operations  1.92 us (1%)
    ppermute x12, waiting for transfers between devices, ring(): lax.ppermute(x, axis, [(i, (i + shift) % count) for i in range(count)])  34.5 us
    pallas_call x2, Pallas kernels, time_step(): pl.pallas_call(step_kernel, out_shape=(jax.ShapeDtypeStruct((inner, out_r...  31 us
    ppermute x12, starting transfers between devices, ring(): lax.ppermute(x, axis, [(i, (i + shift) % count) for i in range(count)])  26.3 us
    reduce_sum x1, other arithmetic, one_block(): return jnp.sum(jnp.where(adjacent, term, 0.0), axis=1)  18.2 us
    all_gather x1, blocking collectives, per_device(): gathered = lax.all_gather(charges, 'narrow', axis=1, tiled=True)  10.4 us
    concatenate x6, other arithmetic, deep_halo(): jnp.concatenate([lo, a, hi], axis=a.ndim - back)  6.61 us
    scatter-add x1, other arithmetic, per_device(): jnp.zeros((depth * height * width,), jnp.float32).at[index].add(values)  3.33 us
    slice x7, local copies, waits for them, and re-layouts, deep_halo(): tops.append(lax.slice_in_dim(a, n - w, n, axis=dim))  3.15 us
  transfers between devices with their start and end apart: 12, of which 6 were waited for; matrix products, arithmetic and copies ran while one was open for 16% of the time, Pallas kernels for 0%

profile of v6, /device:TPU:1, one launch (start us, length us, event | category | flops | bytes accessed | tf_op | source)
XLA Modules:
  0.0 141.1 jit_solution(12638702936988680390)
XLA Ops:
  0.6 0.0 copy-start.2
  0.6 0.7 convert_element_type.28
  1.4 0.8 pad_maximum_fusion.31
  2.2 10.4 %all_gather.3 = f32[5,8192]{1,0:T(8,128)S(1)} all-gather(f32[5,2048]{1,0:T(8,128)S(1)} %pad_maximum_fusion.31), channel_id=1, replica_groups=mesh['wide'=64,'narrow'=4] {'narrow'}, dimensions={1}, use_global_device_ids=true | all-gather | bytes 204800 | tf_op jit(solution)/shard_map/all_gather | solution.py:322
  12.6 1.0 fusion.36
  13.5 1.1 fusion.45
  14.6 0.0 copy-done.2
  14.7 0.0 copy-start.8
  14.7 0.0 copy-start.7
  14.7 7.1 %collective-permute-start.1 = (f32[1088,128]{1,0:T(8,128)S(1)}, f32[1088,128]{1,0:T(8,128)S(1)}, u32[]{:S(2)}, u32[]{:S(2)}) collective-permute-start(f32[1088,128]{1,0:T(8,128)S(1)} %pad_maximum_fusion.8), channel_id=1, source_target_pairs={{0,252},{4,0},{8,4},{12,8},{16,12},{20,16},{24,20},{28,24},{32,28}... | collective-permute-start | bytes 1671176 | tf_op jit(solution)/shard_map/ppermute | solution.py:123
  21.9 0.1 collective-permute-start
  22.6 0.0 copy-done.8
  22.7 0.0 copy-start.5
  22.7 0.0 copy-done.7
  22.8 0.1 fusion.44
  22.9 0.0 copy-start
  22.9 18.2 %select_reduce_fusion.1 = (f32[256]{0:T(256)S(1)}, f32[256]{0:T(256)S(1)}) fusion(f32[8192]{0:T(1024)S(1)} %bitcast.140, f32[256]{0:T(256)S(1)} %get-tuple-element.87, f32[8192]{0:T(1024)S(1)} %bitcast.141, f32[256]{0:T(256)S(1)} %get-tuple-element.76, f32[8192]{0:T(1024)S(1)} %bitcast.142, f32[256]{0:T(256)S(1)} %get-tuple-element.85, ...), kind=kLoop, calls=%fused_computation.21 | loop fusion | flops 104857088 | bytes 174080 | tf_op jit(solution)/shard_map/reduce_sum | solution.py:114
  41.1 3.3 %scatter_custom_fusion = f32[65536]{0:T(1024)S(1)} fusion(s32[512]{0:T(512)S(1)} %bitcast.145, f32[512]{0:T(512)S(1)} %maximum_multiply_fusion, f32[]{:T(128)} %constant.72.clone.1), kind=kCustom, calls=%fused_computation.44 | custom fusion | flops 512 | bytes 262148 | tf_op jit(solution)/shard_map/scatter-add | solution.py:345
  44.5 0.0 copy-done.5
  44.5 0.0 copy-done
  44.5 0.1 multiply_reduce_fusion.1
  44.7 5.7 %collective-permute-start.5 = (f32[448,128]{1,0:T(8,128)S(1)}, f32[448,128]{1,0:T(8,128)S(1)}, u32[]{:S(2)}, u32[]{:S(2)}) collective-permute-start(f32[448,128]{1,0:T(8,128)S(1)} %bitcast.136), channel_id=1, source_target_pairs={{0,252},{4,0},{8,4},{12,8},{16,12},{20,16},{24,20},{28,24},{32,28}... | collective-permute-start | bytes 688136 | tf_op jit(solution)/shard_map/ppermute | solution.py:123
  50.5 0.0 copy-start.3
  50.5 0.0 collective-permute-start.4
  50.5 0.0 collective-permute-done.1
  50.5 0.0 collective-permute-done
  50.6 0.8 copy-done.3
  51.5 1.1 collective-permute-start.3
  52.6 2.6 %collective-permute-start.2 = (f32[592,128]{1,0:T(8,128)S(1)}, f32[592,128]{1,0:T(8,128)S(1)}, u32[]{:S(2)}, u32[]{:S(2)}) collective-permute-start(f32[592,128]{1,0:T(8,128)S(1)} %pad_maximum_fusion.11), channel_id=1, source_target_pairs={{0,1},{1,2},{2,3},{3,0},{4,5},{5,6},{6,7},{7,4},{8,9},{9,10},{10,1... | collective-permute-start | bytes 909320 | tf_op jit(solution)/shard_map/ppermute | solution.py:123
  55.2 0.0 collective-permute-done.5
  55.2 5.6 %collective-permute-done.4 = f32[448,128]{1,0:T(8,128)S(1)} collective-permute-done((f32[448,128]{1,0:T(8,128)S(1)}, f32[448,128]{1,0:T(8,128)S(1)}, u32[]{:S(2)}, u32[]{:S(2)}) %collective-permute-start.4) | collective-permute-done | bytes 229408 | tf_op jit(solution)/shard_map/ppermute | solution.py:123
  60.8 4.6 %collective-permute-start.6 = (f32[176,128]{1,0:T(8,128)S(1)}, f32[176,128]{1,0:T(8,128)S(1)}, u32[]{:S(2)}, u32[]{:S(2)}) collective-permute-start(f32[176,128]{1,0:T(8,128)S(1)} %get-tuple-element.34), channel_id=1, source_target_pairs={{0,1},{1,2},{2,3},{3,0},{4,5},{5,6},{6,7},{7,4},{8,9},{9,10},{10,1... | collective-permute-start | bytes 270344 | tf_op jit(solution)/shard_map/ppermute | solution.py:123
  65.4 0.0 collective-permute-start.7
  65.4 3.0 %collective-permute-done.6 = f32[176,128]{1,0:T(8,128)S(1)} collective-permute-done((f32[176,128]{1,0:T(8,128)S(1)}, f32[176,128]{1,0:T(8,128)S(1)}, u32[]{:S(2)}, u32[]{:S(2)}) %collective-permute-start.6) | collective-permute-done | bytes 90144 | tf_op jit(solution)/shard_map/ppermute | solution.py:123
  68.4 2.4 %collective-permute-done.7 = f32[176,128]{1,0:T(8,128)S(1)} collective-permute-done((f32[176,128]{1,0:T(8,128)S(1)}, f32[176,128]{1,0:T(8,128)S(1)}, u32[]{:S(2)}, u32[]{:S(2)}) %collective-permute-start.7) | collective-permute-done | bytes 90144 | tf_op jit(solution)/shard_map/ppermute | solution.py:123
  70.9 1.0 pad_maximum_fusion.4.s_hbm
  71.8 0.0 collective-permute-done.3
  71.9 0.0 collective-permute-done.2
  71.9 1.2 pad_maximum_fusion.c_hbm
  73.1 1.3 pad_maximum_fusion.2
  74.4 0.0 copy-start.6
  74.4 15.5 %shard_map.113 = (f32[8,64,128]{2,1,0:T(8,128)}, f32[3,8,64,128]{3,2,1,0:T(8,128)}) custom-call(f32[3]{0:T(128)} %dif_ref.3, f32[3]{0:T(128)} %copy-done.5, f32[22,80,128]{2,1,0:T(8,128)} %get-tuple-element.83.f_hbm, f32[22,80,128]{2,1,0:T(8,128)} %get-tuple-element.84.p_hbm, f32[22,80,128]{2,1,0:T(8,128)} %pad_maximum_fusion.4.s_hbm, ...), custom_call_target="tpu_custom_call" | custom-call | flops 40755200 | bytes 4980736 | tf_op jit(solution)/shard_map/pallas_call | solution.py:256
  89.9 1.0 fusion.35
  90.9 0.0 copy-done.6
  90.9 0.0 copy-start.4
  90.9 1.3 multiply_reduce_fusion
  92.4 0.0 copy-done.4
  92.5 0.9 collective-permute-start.9
  93.4 0.8 collective-permute-start.8
  94.1 12.1 %collective-permute-done.9 = f32[1088,128]{1,0:T(8,128)S(1)} collective-permute-done((f32[1088,128]{1,0:T(8,128)S(1)}, f32[1088,128]{1,0:T(8,128)S(1)}, u32[]{:S(2)}, u32[]{:S(2)}) %collective-permute-start.9) | collective-permute-done | bytes 557088 | tf_op jit(solution)/shard_map/ppermute | solution.py:123
  106.2 4.8 %collective-permute-done.8 = f32[1088,128]{1,0:T(8,128)S(1)} collective-permute-done((f32[1088,128]{1,0:T(8,128)S(1)}, f32[1088,128]{1,0:T(8,128)S(1)}, u32[]{:S(2)}, u32[]{:S(2)}) %collective-permute-start.8) | collective-permute-done | bytes 557088 | tf_op jit(solution)/shard_map/ppermute | solution.py:123
  111.1 0.0 copy-start.1
  111.2 1.0 copy-done.1
  112.3 1.7 %collective-permute-start.11 = (f32[592,128]{1,0:T(8,128)S(1)}, f32[592,128]{1,0:T(8,128)S(1)}, u32[]{:S(2)}, u32[]{:S(2)}) collective-permute-start(f32[592,128]{1,0:T(8,128)S(1)} %pad_maximum_fusion.14), channel_id=1, source_target_pairs={{0,3},{1,0},{2,1},{3,2},{4,7},{5,4},{6,5},{7,6},{8,11},{9,8},{10,9... | collective-permute-start | bytes 909320 | tf_op jit(solution)/shard_map/ppermute | solution.py:123
  114.0 1.7 %collective-permute-start.10 = (f32[592,128]{1,0:T(8,128)S(1)}, f32[592,128]{1,0:T(8,128)S(1)}, u32[]{:S(2)}, u32[]{:S(2)}) collective-permute-start(f32[592,128]{1,0:T(8,128)S(1)} %pad_maximum_fusion.13), channel_id=1, source_target_pairs={{0,1},{1,2},{2,3},{3,0},{4,5},{5,6},{6,7},{7,4},{8,9},{9,10},{10,1... | collective-permute-start | bytes 909320 | tf_op jit(solution)/shard_map/ppermute | solution.py:123
  115.7 6.6 %collective-permute-done.11 = f32[592,128]{1,0:T(8,128)S(1)} collective-permute-done((f32[592,128]{1,0:T(8,128)S(1)}, f32[592,128]{1,0:T(8,128)S(1)}, u32[]{:S(2)}, u32[]{:S(2)}) %collective-permute-start.11) | collective-permute-done | bytes 303136 | tf_op jit(solution)/shard_map/ppermute | solution.py:123
  122.3 0.0 collective-permute-done.10
  122.3 1.0 pad_maximum_fusion.6.s_hbm
  123.3 1.2 pad_maximum_fusion.1.c_hbm
  124.5 1.0 pad_maximum_fusion.5.f_hbm
  125.5 15.5 %shard_map.114 = (f32[8,64,128]{2,1,0:T(8,128)}, f32[3,8,64,128]{3,2,1,0:T(8,128)}) custom-call(f32[3]{0:T(128)} %dif_ref.3, f32[3]{0:T(128)} %copy-done.5, f32[22,80,128]{2,1,0:T(8,128)} %pad_maximum_fusion.5.f_hbm, f32[22,80,128]{2,1,0:T(8,128)} %get-tuple-element.84.p_hbm, f32[22,80,128]{2,1,0:T(8,128)} %pad_maximum_fusion.6.s_hbm, ...), custom_call_target="tpu_custom_call" | custom-call | flops 40755200 | bytes 4980736 | tf_op jit(solution)/shard_map/pallas_call | solution.py:256
  (44 shorter events, 0.9 us)
Async XLA Ops:
  0.6 14.0 %copy-start.2 = (f32[8,64,128]{2,1,0:T(8,128)S(1)}, f32[8,64,128]{2,1,0:T(8,128)}, u32[]{:S(2)}) copy-start(f32[8,64,128]{2,1,0:T(8,128)} %param.12) | copy-start | bytes 786436
  14.7 8.0 %copy-start.8 = (s32[3]{0:T(128)S(1)}, s32[3]{0:T(128)}, u32[]{:S(2)}) copy-start(s32[3]{0:T(128)} %param.14) | copy-start | bytes 40
  14.7 8.0 %copy-start.7 = (s32[1,1,512]{2,1,0:T(1,128)S(1)}, s32[1,1,512]{2,1,0:T(1,128)}, u32[]{:S(2)}) copy-start(s32[1,1,512]{2,1,0:T(1,128)} %param.18) | copy-start | bytes 6148
  14.7 35.7 %collective-permute-start.1 = (f32[1088,128]{1,0:T(8,128)S(1)}, f32[1088,128]{1,0:T(8,128)S(1)}, u32[]{:S(2)}, u32[]{:S(2)}) collective-permute-start(f32[1088,128]{1,0:T(8,128)S(1)} %pad_maximum_fusion.8), channel_id=1, source_target_pairs={{0,252},{4,0},{8,4},{12,8},{16,12},{20,16},{24,20},{28,24},{32,28}... | collective-permute-start | bytes 1671176 | tf_op jit(solution)/shard_map/ppermute | solution.py:123
  21.9 28.6 %collective-permute-start = (f32[1088,128]{1,0:T(8,128)S(1)}, f32[1088,128]{1,0:T(8,128)S(1)}, u32[]{:S(2)}, u32[]{:S(2)}) collective-permute-start(f32[1088,128]{1,0:T(8,128)S(1)} %pad_maximum_fusion.7), channel_id=1, source_target_pairs={{0,4},{4,8},{8,12},{12,16},{16,20},{20,24},{24,28},{28,32},{32,36}... | collective-permute-start | bytes 1671176 | tf_op jit(solution)/shard_map/ppermute | solution.py:123
  22.7 21.8 %copy-start.5 = (f32[3]{0:T(128)}, f32[3]{0:T(128)S(1)}, u32[]{:S(2)}) copy-start(f32[3]{0:T(128)S(1)} %convert_element_type.27.val_ref) | copy-start | bytes 40
  22.9 21.6 %copy-start = (f32[3,8,64,128]{3,2,1,0:T(8,128)S(1)}, f32[3,8,64,128]{3,2,1,0:T(8,128)}, u32[]{:S(2)}) copy-start(f32[3,8,64,128]{3,2,1,0:T(8,128)} %param.10) | copy-start | bytes 2359300
  44.7 10.5 %collective-permute-start.5 = (f32[448,128]{1,0:T(8,128)S(1)}, f32[448,128]{1,0:T(8,128)S(1)}, u32[]{:S(2)}, u32[]{:S(2)}) collective-permute-start(f32[448,128]{1,0:T(8,128)S(1)} %bitcast.136), channel_id=1, source_target_pairs={{0,252},{4,0},{8,4},{12,8},{16,12},{20,16},{24,20},{28,24},{32,28}... | collective-permute-start | bytes 688136 | tf_op jit(solution)/shard_map/ppermute | solution.py:123
  50.5 0.9 copy-start.3
  50.5 10.3 %collective-permute-start.4 = (f32[448,128]{1,0:T(8,128)S(1)}, f32[448,128]{1,0:T(8,128)S(1)}, u32[]{:S(2)}, u32[]{:S(2)}) collective-permute-start(f32[448,128]{1,0:T(8,128)S(1)} %bitcast.135), channel_id=1, source_target_pairs={{0,4},{4,8},{8,12},{12,16},{16,20},{20,24},{24,28},{28,32},{32,36}... | collective-permute-start | bytes 688136 | tf_op jit(solution)/shard_map/ppermute | solution.py:123
  51.5 20.3 %collective-permute-start.3 = (f32[592,128]{1,0:T(8,128)S(1)}, f32[592,128]{1,0:T(8,128)S(1)}, u32[]{:S(2)}, u32[]{:S(2)}) collective-permute-start(f32[592,128]{1,0:T(8,128)S(1)} %pad_maximum_fusion.12), channel_id=1, source_target_pairs={{0,3},{1,0},{2,1},{3,2},{4,7},{5,4},{6,5},{7,6},{8,11},{9,8},{10,9... | collective-permute-start | bytes 909320 | tf_op jit(solution)/shard_map/ppermute | solution.py:123
  52.6 19.2 %collective-permute-start.2 = (f32[592,128]{1,0:T(8,128)S(1)}, f32[592,128]{1,0:T(8,128)S(1)}, u32[]{:S(2)}, u32[]{:S(2)}) collective-permute-start(f32[592,128]{1,0:T(8,128)S(1)} %pad_maximum_fusion.11), channel_id=1, source_target_pairs={{0,1},{1,2},{2,3},{3,0},{4,5},{5,6},{6,7},{7,4},{8,9},{9,10},{10,1... | collective-permute-start | bytes 909320 | tf_op jit(solution)/shard_map/ppermute | solution.py:123
  60.8 7.6 %collective-permute-start.6 = (f32[176,128]{1,0:T(8,128)S(1)}, f32[176,128]{1,0:T(8,128)S(1)}, u32[]{:S(2)}, u32[]{:S(2)}) collective-permute-start(f32[176,128]{1,0:T(8,128)S(1)} %get-tuple-element.34), channel_id=1, source_target_pairs={{0,1},{1,2},{2,3},{3,0},{4,5},{5,6},{6,7},{7,4},{8,9},{9,10},{10,1... | collective-permute-start | bytes 270344 | tf_op jit(solution)/shard_map/ppermute | solution.py:123
  65.4 5.5 %collective-permute-start.7 = (f32[176,128]{1,0:T(8,128)S(1)}, f32[176,128]{1,0:T(8,128)S(1)}, u32[]{:S(2)}, u32[]{:S(2)}) collective-permute-start(f32[176,128]{1,0:T(8,128)S(1)} %get-tuple-element.35), channel_id=1, source_target_pairs={{0,3},{1,0},{2,1},{3,2},{4,7},{5,4},{6,5},{7,6},{8,11},{9,8},{10,9... | collective-permute-start | bytes 270344 | tf_op jit(solution)/shard_map/ppermute | solution.py:123
  74.4 16.5 %copy-start.6 = (f32[3]{0:T(128)S(1)}, f32[3]{0:T(128)}, u32[]{:S(2)}) copy-start(f32[3]{0:T(128)} %copy-done.5) | copy-start | bytes 40
  90.9 1.4 %copy-start.4 = (f32[8,64,128]{2,1,0:T(8,128)S(1)}, f32[8,64,128]{2,1,0:T(8,128)}, u32[]{:S(2)}) copy-start(f32[8,64,128]{2,1,0:T(8,128)} %get-tuple-element.14) | copy-start | bytes 786436
  92.5 13.7 %collective-permute-start.9 = (f32[1088,128]{1,0:T(8,128)S(1)}, f32[1088,128]{1,0:T(8,128)S(1)}, u32[]{:S(2)}, u32[]{:S(2)}) collective-permute-start(f32[1088,128]{1,0:T(8,128)S(1)} %pad_maximum_fusion.10), channel_id=1, source_target_pairs={{0,252},{4,0},{8,4},{12,8},{16,12},{20,16},{24,20},{28,24},{32,28}... | collective-permute-start | bytes 1671176 | tf_op jit(solution)/shard_map/ppermute | solution.py:123
  93.4 17.7 %collective-permute-start.8 = (f32[1088,128]{1,0:T(8,128)S(1)}, f32[1088,128]{1,0:T(8,128)S(1)}, u32[]{:S(2)}, u32[]{:S(2)}) collective-permute-start(f32[1088,128]{1,0:T(8,128)S(1)} %pad_maximum_fusion.9), channel_id=1, source_target_pairs={{0,4},{4,8},{8,12},{12,16},{16,20},{20,24},{24,28},{28,32},{32,36}... | collective-permute-start | bytes 1671176 | tf_op jit(solution)/shard_map/ppermute | solution.py:123
  111.1 1.1 copy-start.1
  112.3 10.0 %collective-permute-start.11 = (f32[592,128]{1,0:T(8,128)S(1)}, f32[592,128]{1,0:T(8,128)S(1)}, u32[]{:S(2)}, u32[]{:S(2)}) collective-permute-start(f32[592,128]{1,0:T(8,128)S(1)} %pad_maximum_fusion.14), channel_id=1, source_target_pairs={{0,3},{1,0},{2,1},{3,2},{4,7},{5,4},{6,5},{7,6},{8,11},{9,8},{10,9... | collective-permute-start | bytes 909320 | tf_op jit(solution)/shard_map/ppermute | solution.py:123
  114.0 8.3 %collective-permute-start.10 = (f32[592,128]{1,0:T(8,128)S(1)}, f32[592,128]{1,0:T(8,128)S(1)}, u32[]{:S(2)}, u32[]{:S(2)}) collective-permute-start(f32[592,128]{1,0:T(8,128)S(1)} %pad_maximum_fusion.13), channel_id=1, source_target_pairs={{0,1},{1,2},{2,3},{3,0},{4,5},{5,6},{6,7},{7,4},{8,9},{9,10},{10,1... | collective-permute-start | bytes 909320 | tf_op jit(solution)/shard_map/ppermute | solution.py:123

commit v7 on v6

--- a/solution.py
+++ b/solution.py
@@ -154,11 +154,13 @@
 ):
     copies = [
         pltpu.make_async_copy(src, dst, sems.at[k])
-        for k, (src, dst) in enumerate(((p_hbm, p_ref), (f_hbm, f_ref), (s_hbm, s_ref), (c_hbm, c_ref)))
+        for k, (src, dst) in enumerate(
+            ((p_hbm, p_ref), (f_hbm, f_ref.at[:, 8:88, :]), (s_hbm, s_ref), (c_hbm, c_ref))
+        )
     ]
     for copy in copies:
         copy.start()
-    planes, rows, lanes = f_ref.shape
+    planes, rows, lanes = p_ref.shape
     species, inner = c_ref.shape[0], c_ref.shape[1] - 2
     hz = (planes - inner) // 2
     hy = (rows - co_ref.shape[2]) // 2
@@ -196,8 +198,12 @@
 
     copies[0].wait()
     copies[2].wait()
-    lax.fori_loop(1, planes - 1, weights, 0)
+    lax.fori_loop(1, planes - 1, weights, 0, unroll=2)
     copies[1].wait()
+    pad = jnp.zeros((planes, 8, lanes), jnp.float32)
+    for buf in (f_ref, fa, fb):
+        buf[:, 0:8, :] = pad
+        buf[:, 88:96, :] = pad
     bufs = (fa, fb)
     sweeps = hz - 1
     for k in range(sweeps):
@@ -205,26 +211,22 @@
         wr = bufs[k % 2]
 
         def sweep(z, carry, rd=rd, wr=wr):
-            fc = rd[z]
-            new = w_ref[6, z]
-            new = new + w_ref[0, z] * rd[z + 1]
-            new = new + w_ref[1, z] * rd[z - 1]
-            new = new + w_ref[2, z] * ysh(fc, 1)
-            new = new + w_ref[3, z] * ysh(fc, -1)
-            new = new + w_ref[4, z] * xsh(fc, 1)
-            new = new + w_ref[5, z] * xsh(fc, -1)
-            wr[z] = new
+            fc = rd[z, 8:88]
+            near_z = (w_ref[6, z] + w_ref[0, z] * rd[z + 1, 8:88]) + w_ref[1, z] * rd[z - 1, 8:88]
+            near_y = w_ref[2, z] * rd[z, pl.ds(9, rows)] + w_ref[3, z] * rd[z, pl.ds(7, rows)]
+            near_x = w_ref[4, z] * xsh(fc, 1) + w_ref[5, z] * xsh(fc, -1)
+            wr[z, 8:88] = near_z + (near_y + near_x)
             return carry
 
-        lax.fori_loop(k + 1, planes - k - 1, sweep, 0)
+        lax.fori_loop(k + 1, planes - k - 1, sweep, 0, unroll=2)
     final = bufs[(sweeps - 1) % 2]
     copies[3].wait()
 
     def move(z, carry):
         zf = z + hz
-        fc = final[zf]
+        fc = final[zf, 8:88]
         fo_ref[z] = fc[hy:hy + out_rows]
-        pairs_field = (final[zf + 1], final[zf - 1], ysh(fc, 1), ysh(fc, -1))
+        pairs_field = (final[zf + 1, 8:88], final[zf - 1, 8:88], ysh(fc, 1), ysh(fc, -1))
         fr = xsh(fc, 1)
         for s in range(species):
             drift = val_ref[s]
@@ -242,7 +244,7 @@
             co_ref[s, z] = new[hy:hy + out_rows]
         return carry
 
-    lax.fori_loop(0, inner, move, 0)
+    lax.fori_loop(0, inner, move, 0, unroll=2)
 
 
 def time_step(diffusivity, charge_num, field_e, perm_e, source_e, species_e):
@@ -262,12 +264,12 @@
         in_specs=[smem, smem, hbm, hbm, hbm, hbm],
         out_specs=(vmem, vmem),
         scratch_shapes=[
-            pltpu.VMEM((planes, rows, lanes), jnp.float32),
+            pltpu.VMEM((planes, rows + 16, lanes), jnp.float32),
             pltpu.VMEM((planes, rows, lanes), jnp.float32),
             pltpu.VMEM((planes, rows, lanes), jnp.float32),
             pltpu.VMEM(species_e.shape, jnp.float32),
-            pltpu.VMEM((planes, rows, lanes), jnp.float32),
-            pltpu.VMEM((planes, rows, lanes), jnp.float32),
+            pltpu.VMEM((planes, rows + 16, lanes), jnp.float32),
+            pltpu.VMEM((planes, rows + 16, lanes), jnp.float32),
             pltpu.VMEM((7, planes, rows, lanes), jnp.float32),
             pltpu.SemaphoreType.DMA((4,)),
         ],

time: 142 us -> 134 us (0.944)
  Pallas kernels: 31 us -> 23.2 us
    pallas_call x2, Pallas kernels: 31 us -> 23.2 us  [time_step(): pl.pallas_call(step_kernel, out_shape=(jax.ShapeDtypeStruct((inner, out_r...]
  transfers between devices with their start and end apart: 12 -> 12, of which waited for: 6 -> 6; matrix products, arithmetic and copies ran while one was open for 16% -> 17% of each run, Pallas kernels for 0% -> 0%
where the time goes in v7:
time: 134 us; the launch traced here: 133 us
  waiting for transfers between devices  34.5 us (26%)
  other arithmetic  31.7 us (24%)
  starting transfers between devices  26.3 us (20%)
  Pallas kernels  23.2 us (17%)
  blocking collectives  10.4 us (8%)
  local copies, waits for them, and re-layouts  5.33 us (4%)
  between operations  1.92 us (1%)
    ppermute x12, waiting for transfers between devices, ring(): lax.ppermute(x, axis, [(i, (i + shift) % count) for i in range(count)])  34.5 us
    ppermute x12, starting transfers between devices, ring(): lax.ppermute(x, axis, [(i, (i + shift) % count) for i in range(count)])  26.3 us
    pallas_call x2, Pallas kernels, time_step(): pl.pallas_call(step_kernel, out_shape=(jax.ShapeDtypeStruct((inner, out_r...  23.2 us
    reduce_sum x1, other arithmetic, one_block(): return jnp.sum(jnp.where(adjacent, term, 0.0), axis=1)  18.2 us
    all_gather x1, blocking collectives, per_device(): gathered = lax.all_gather(charges, 'narrow', axis=1, tiled=True)  10.4 us
    concatenate x6, other arithmetic, deep_halo(): jnp.concatenate([lo, a, hi], axis=a.ndim - back)  6.61 us
    scatter-add x1, other arithmetic, per_device(): jnp.zeros((depth * height * width,), jnp.float32).at[index].add(values)  3.33 us
    slice x7, local copies, waits for them, and re-layouts, deep_halo(): tops.append(lax.slice_in_dim(a, n - w, n, axis=dim))  3.15 us
  transfers between devices with their start and end apart: 12, of which 6 were waited for; matrix products, arithmetic and copies ran while one was open for 17% of the time, Pallas kernels for 0%

profile of v7, /device:TPU:1, one launch (start us, length us, event | category | flops | bytes accessed | tf_op | source)
XLA Modules:
  0.0 133.3 jit_solution(4877785429789702966)
XLA Ops:
  0.6 0.0 copy-start.2
  0.6 0.7 convert_element_type.28
  1.4 0.8 pad_maximum_fusion.31
  2.2 10.4 %all_gather.3 = f32[5,8192]{1,0:T(8,128)S(1)} all-gather(f32[5,2048]{1,0:T(8,128)S(1)} %pad_maximum_fusion.31), channel_id=1, replica_groups=mesh['wide'=64,'narrow'=4] {'narrow'}, dimensions={1}, use_global_device_ids=true | all-gather | bytes 204800 | tf_op jit(solution)/shard_map/all_gather | solution.py:324
  12.6 1.0 fusion.36
  13.5 1.1 fusion.45
  14.6 0.0 copy-done.2
  14.7 0.0 copy-start.8
  14.7 0.0 copy-start.7
  14.7 7.1 %collective-permute-start.1 = (f32[1088,128]{1,0:T(8,128)S(1)}, f32[1088,128]{1,0:T(8,128)S(1)}, u32[]{:S(2)}, u32[]{:S(2)}) collective-permute-start(f32[1088,128]{1,0:T(8,128)S(1)} %pad_maximum_fusion.8), channel_id=1, source_target_pairs={{0,252},{4,0},{8,4},{12,8},{16,12},{20,16},{24,20},{28,24},{32,28}... | collective-permute-start | bytes 1671176 | tf_op jit(solution)/shard_map/ppermute | solution.py:123
  21.9 0.1 collective-permute-start
  22.6 0.0 copy-done.8
  22.7 0.0 copy-start.5
  22.7 0.0 copy-done.7
  22.8 0.1 fusion.44
  22.9 0.0 copy-start
  22.9 18.2 %select_reduce_fusion.1 = (f32[256]{0:T(256)S(1)}, f32[256]{0:T(256)S(1)}) fusion(f32[8192]{0:T(1024)S(1)} %bitcast.140, f32[256]{0:T(256)S(1)} %get-tuple-element.87, f32[8192]{0:T(1024)S(1)} %bitcast.141, f32[256]{0:T(256)S(1)} %get-tuple-element.76, f32[8192]{0:T(1024)S(1)} %bitcast.142, f32[256]{0:T(256)S(1)} %get-tuple-element.85, ...), kind=kLoop, calls=%fused_computation.21 | loop fusion | flops 104857088 | bytes 174080 | tf_op jit(solution)/shard_map/reduce_sum | solution.py:114
  41.1 3.3 %scatter_custom_fusion = f32[65536]{0:T(1024)S(1)} fusion(s32[512]{0:T(512)S(1)} %bitcast.145, f32[512]{0:T(512)S(1)} %maximum_multiply_fusion, f32[]{:T(128)} %constant.72.clone.1), kind=kCustom, calls=%fused_computation.44 | custom fusion | flops 512 | bytes 262148 | tf_op jit(solution)/shard_map/scatter-add | solution.py:347
  44.5 0.0 copy-done.5
  44.5 0.0 copy-done
  44.5 0.1 multiply_reduce_fusion.1
  44.7 5.7 %collective-permute-start.5 = (f32[448,128]{1,0:T(8,128)S(1)}, f32[448,128]{1,0:T(8,128)S(1)}, u32[]{:S(2)}, u32[]{:S(2)}) collective-permute-start(f32[448,128]{1,0:T(8,128)S(1)} %bitcast.136), channel_id=1, source_target_pairs={{0,252},{4,0},{8,4},{12,8},{16,12},{20,16},{24,20},{28,24},{32,28}... | collective-permute-start | bytes 688136 | tf_op jit(solution)/shard_map/ppermute | solution.py:123
  50.5 0.0 copy-start.3
  50.5 0.0 collective-permute-start.4
  50.5 0.0 collective-permute-done.1
  50.5 0.0 collective-permute-done
  50.6 0.8 copy-done.3
  51.5 1.1 collective-permute-start.3
  52.6 2.6 %collective-permute-start.2 = (f32[592,128]{1,0:T(8,128)S(1)}, f32[592,128]{1,0:T(8,128)S(1)}, u32[]{:S(2)}, u32[]{:S(2)}) collective-permute-start(f32[592,128]{1,0:T(8,128)S(1)} %pad_maximum_fusion.11), channel_id=1, source_target_pairs={{0,1},{1,2},{2,3},{3,0},{4,5},{5,6},{6,7},{7,4},{8,9},{9,10},{10,1... | collective-permute-start | bytes 909320 | tf_op jit(solution)/shard_map/ppermute | solution.py:123
  55.2 0.0 collective-permute-done.5
  55.2 5.6 %collective-permute-done.4 = f32[448,128]{1,0:T(8,128)S(1)} collective-permute-done((f32[448,128]{1,0:T(8,128)S(1)}, f32[448,128]{1,0:T(8,128)S(1)}, u32[]{:S(2)}, u32[]{:S(2)}) %collective-permute-start.4) | collective-permute-done | bytes 229408 | tf_op jit(solution)/shard_map/ppermute | solution.py:123
  60.8 4.6 %collective-permute-start.6 = (f32[176,128]{1,0:T(8,128)S(1)}, f32[176,128]{1,0:T(8,128)S(1)}, u32[]{:S(2)}, u32[]{:S(2)}) collective-permute-start(f32[176,128]{1,0:T(8,128)S(1)} %get-tuple-element.34), channel_id=1, source_target_pairs={{0,1},{1,2},{2,3},{3,0},{4,5},{5,6},{6,7},{7,4},{8,9},{9,10},{10,1... | collective-permute-start | bytes 270344 | tf_op jit(solution)/shard_map/ppermute | solution.py:123
  65.4 0.0 collective-permute-start.7
  65.4 3.0 %collective-permute-done.6 = f32[176,128]{1,0:T(8,128)S(1)} collective-permute-done((f32[176,128]{1,0:T(8,128)S(1)}, f32[176,128]{1,0:T(8,128)S(1)}, u32[]{:S(2)}, u32[]{:S(2)}) %collective-permute-start.6) | collective-permute-done | bytes 90144 | tf_op jit(solution)/shard_map/ppermute | solution.py:123
  68.4 2.4 %collective-permute-done.7 = f32[176,128]{1,0:T(8,128)S(1)} collective-permute-done((f32[176,128]{1,0:T(8,128)S(1)}, f32[176,128]{1,0:T(8,128)S(1)}, u32[]{:S(2)}, u32[]{:S(2)}) %collective-permute-start.7) | collective-permute-done | bytes 90144 | tf_op jit(solution)/shard_map/ppermute | solution.py:123
  70.9 1.0 pad_maximum_fusion.4.s_hbm
  71.8 0.0 collective-permute-done.3
  71.9 0.0 collective-permute-done.2
  71.9 1.2 pad_maximum_fusion.c_hbm
  73.1 1.3 pad_maximum_fusion.2
  74.4 0.0 copy-start.6
  74.4 11.6 %shard_map.113 = (f32[8,64,128]{2,1,0:T(8,128)}, f32[3,8,64,128]{3,2,1,0:T(8,128)}) custom-call(f32[3]{0:T(128)} %dif_ref.3, f32[3]{0:T(128)} %copy-done.5, f32[22,80,128]{2,1,0:T(8,128)} %get-tuple-element.83.f_hbm, f32[22,80,128]{2,1,0:T(8,128)} %get-tuple-element.84.p_hbm, f32[22,80,128]{2,1,0:T(8,128)} %pad_maximum_fusion.4.s_hbm, ...), custom_call_target="tpu_custom_call" | custom-call | flops 40755200 | bytes 4980736 | tf_op jit(solution)/shard_map/pallas_call | solution.py:258
  86.0 1.0 fusion.35
  87.0 0.0 copy-done.6
  87.0 0.0 copy-start.4
  87.0 1.3 %multiply_reduce_fusion = f32[8,64,128]{2,1,0:T(8,128)S(1)} fusion(f32[3,8,64,128]{3,2,1,0:T(8,128)} %get-tuple-element.15, f32[3]{0:T(128)S(1)} %copy-done.6), kind=kLoop, calls=%fused_computation.34 | loop fusion | flops 327680 | bytes 1048588 | tf_op jit(solution)/shard_map/reduce_sum | solution.py:354
  88.5 0.0 copy-done.4
  88.6 0.9 collective-permute-start.9
  89.5 0.8 collective-permute-start.8
  90.2 12.1 %collective-permute-done.9 = f32[1088,128]{1,0:T(8,128)S(1)} collective-permute-done((f32[1088,128]{1,0:T(8,128)S(1)}, f32[1088,128]{1,0:T(8,128)S(1)}, u32[]{:S(2)}, u32[]{:S(2)}) %collective-permute-start.9) | collective-permute-done | bytes 557088 | tf_op jit(solution)/shard_map/ppermute | solution.py:123
  102.3 4.8 %collective-permute-done.8 = f32[1088,128]{1,0:T(8,128)S(1)} collective-permute-done((f32[1088,128]{1,0:T(8,128)S(1)}, f32[1088,128]{1,0:T(8,128)S(1)}, u32[]{:S(2)}, u32[]{:S(2)}) %collective-permute-start.8) | collective-permute-done | bytes 557088 | tf_op jit(solution)/shard_map/ppermute | solution.py:123
  107.2 0.0 copy-start.1
  107.3 1.0 copy-done.1
  108.3 1.7 %collective-permute-start.11 = (f32[592,128]{1,0:T(8,128)S(1)}, f32[592,128]{1,0:T(8,128)S(1)}, u32[]{:S(2)}, u32[]{:S(2)}) collective-permute-start(f32[592,128]{1,0:T(8,128)S(1)} %pad_maximum_fusion.14), channel_id=1, source_target_pairs={{0,3},{1,0},{2,1},{3,2},{4,7},{5,4},{6,5},{7,6},{8,11},{9,8},{10,9... | collective-permute-start | bytes 909320 | tf_op jit(solution)/shard_map/ppermute | solution.py:123
  110.1 1.7 %collective-permute-start.10 = (f32[592,128]{1,0:T(8,128)S(1)}, f32[592,128]{1,0:T(8,128)S(1)}, u32[]{:S(2)}, u32[]{:S(2)}) collective-permute-start(f32[592,128]{1,0:T(8,128)S(1)} %pad_maximum_fusion.13), channel_id=1, source_target_pairs={{0,1},{1,2},{2,3},{3,0},{4,5},{5,6},{6,7},{7,4},{8,9},{9,10},{10,1... | collective-permute-start | bytes 909320 | tf_op jit(solution)/shard_map/ppermute | solution.py:123
  111.8 6.6 %collective-permute-done.11 = f32[592,128]{1,0:T(8,128)S(1)} collective-permute-done((f32[592,128]{1,0:T(8,128)S(1)}, f32[592,128]{1,0:T(8,128)S(1)}, u32[]{:S(2)}, u32[]{:S(2)}) %collective-permute-start.11) | collective-permute-done | bytes 303136 | tf_op jit(solution)/shard_map/ppermute | solution.py:123
  118.4 0.0 collective-permute-done.10
  118.4 1.0 pad_maximum_fusion.6.s_hbm
  119.4 1.2 pad_maximum_fusion.1.c_hbm
  120.6 1.0 pad_maximum_fusion.5.f_hbm
  121.6 11.6 %shard_map.114 = (f32[8,64,128]{2,1,0:T(8,128)}, f32[3,8,64,128]{3,2,1,0:T(8,128)}) custom-call(f32[3]{0:T(128)} %dif_ref.3, f32[3]{0:T(128)} %copy-done.5, f32[22,80,128]{2,1,0:T(8,128)} %pad_maximum_fusion.5.f_hbm, f32[22,80,128]{2,1,0:T(8,128)} %get-tuple-element.84.p_hbm, f32[22,80,128]{2,1,0:T(8,128)} %pad_maximum_fusion.6.s_hbm, ...), custom_call_target="tpu_custom_call" | custom-call | flops 40755200 | bytes 4980736 | tf_op jit(solution)/shard_map/pallas_call | solution.py:258
  (44 shorter events, 0.9 us)
Async XLA Ops:
  0.6 14.0 %copy-start.2 = (f32[8,64,128]{2,1,0:T(8,128)S(1)}, f32[8,64,128]{2,1,0:T(8,128)}, u32[]{:S(2)}) copy-start(f32[8,64,128]{2,1,0:T(8,128)} %param.12) | copy-start | bytes 786436
  14.7 8.0 %copy-start.8 = (s32[3]{0:T(128)S(1)}, s32[3]{0:T(128)}, u32[]{:S(2)}) copy-start(s32[3]{0:T(128)} %param.14) | copy-start | bytes 40
  14.7 8.0 %copy-start.7 = (s32[1,1,512]{2,1,0:T(1,128)S(1)}, s32[1,1,512]{2,1,0:T(1,128)}, u32[]{:S(2)}) copy-start(s32[1,1,512]{2,1,0:T(1,128)} %param.18) | copy-start | bytes 6148
  14.7 35.7 %collective-permute-start.1 = (f32[1088,128]{1,0:T(8,128)S(1)}, f32[1088,128]{1,0:T(8,128)S(1)}, u32[]{:S(2)}, u32[]{:S(2)}) collective-permute-start(f32[1088,128]{1,0:T(8,128)S(1)} %pad_maximum_fusion.8), channel_id=1, source_target_pairs={{0,252},{4,0},{8,4},{12,8},{16,12},{20,16},{24,20},{28,24},{32,28}... | collective-permute-start | bytes 1671176 | tf_op jit(solution)/shard_map/ppermute | solution.py:123
  21.9 28.6 %collective-permute-start = (f32[1088,128]{1,0:T(8,128)S(1)}, f32[1088,128]{1,0:T(8,128)S(1)}, u32[]{:S(2)}, u32[]{:S(2)}) collective-permute-start(f32[1088,128]{1,0:T(8,128)S(1)} %pad_maximum_fusion.7), channel_id=1, source_target_pairs={{0,4},{4,8},{8,12},{12,16},{16,20},{20,24},{24,28},{28,32},{32,36}... | collective-permute-start | bytes 1671176 | tf_op jit(solution)/shard_map/ppermute | solution.py:123
  22.7 21.8 %copy-start.5 = (f32[3]{0:T(128)}, f32[3]{0:T(128)S(1)}, u32[]{:S(2)}) copy-start(f32[3]{0:T(128)S(1)} %convert_element_type.27.val_ref) | copy-start | bytes 40
  22.9 21.6 %copy-start = (f32[3,8,64,128]{3,2,1,0:T(8,128)S(1)}, f32[3,8,64,128]{3,2,1,0:T(8,128)}, u32[]{:S(2)}) copy-start(f32[3,8,64,128]{3,2,1,0:T(8,128)} %param.10) | copy-start | bytes 2359300
  44.7 10.5 %collective-permute-start.5 = (f32[448,128]{1,0:T(8,128)S(1)}, f32[448,128]{1,0:T(8,128)S(1)}, u32[]{:S(2)}, u32[]{:S(2)}) collective-permute-start(f32[448,128]{1,0:T(8,128)S(1)} %bitcast.136), channel_id=1, source_target_pairs={{0,252},{4,0},{8,4},{12,8},{16,12},{20,16},{24,20},{28,24},{32,28}... | collective-permute-start | bytes 688136 | tf_op jit(solution)/shard_map/ppermute | solution.py:123
  50.5 0.9 copy-start.3
  50.5 10.3 %collective-permute-start.4 = (f32[448,128]{1,0:T(8,128)S(1)}, f32[448,128]{1,0:T(8,128)S(1)}, u32[]{:S(2)}, u32[]{:S(2)}) collective-permute-start(f32[448,128]{1,0:T(8,128)S(1)} %bitcast.135), channel_id=1, source_target_pairs={{0,4},{4,8},{8,12},{12,16},{16,20},{20,24},{24,28},{28,32},{32,36}... | collective-permute-start | bytes 688136 | tf_op jit(solution)/shard_map/ppermute | solution.py:123
  51.5 20.3 %collective-permute-start.3 = (f32[592,128]{1,0:T(8,128)S(1)}, f32[592,128]{1,0:T(8,128)S(1)}, u32[]{:S(2)}, u32[]{:S(2)}) collective-permute-start(f32[592,128]{1,0:T(8,128)S(1)} %pad_maximum_fusion.12), channel_id=1, source_target_pairs={{0,3},{1,0},{2,1},{3,2},{4,7},{5,4},{6,5},{7,6},{8,11},{9,8},{10,9... | collective-permute-start | bytes 909320 | tf_op jit(solution)/shard_map/ppermute | solution.py:123
  52.6 19.2 %collective-permute-start.2 = (f32[592,128]{1,0:T(8,128)S(1)}, f32[592,128]{1,0:T(8,128)S(1)}, u32[]{:S(2)}, u32[]{:S(2)}) collective-permute-start(f32[592,128]{1,0:T(8,128)S(1)} %pad_maximum_fusion.11), channel_id=1, source_target_pairs={{0,1},{1,2},{2,3},{3,0},{4,5},{5,6},{6,7},{7,4},{8,9},{9,10},{10,1... | collective-permute-start | bytes 909320 | tf_op jit(solution)/shard_map/ppermute | solution.py:123
  60.8 7.6 %collective-permute-start.6 = (f32[176,128]{1,0:T(8,128)S(1)}, f32[176,128]{1,0:T(8,128)S(1)}, u32[]{:S(2)}, u32[]{:S(2)}) collective-permute-start(f32[176,128]{1,0:T(8,128)S(1)} %get-tuple-element.34), channel_id=1, source_target_pairs={{0,1},{1,2},{2,3},{3,0},{4,5},{5,6},{6,7},{7,4},{8,9},{9,10},{10,1... | collective-permute-start | bytes 270344 | tf_op jit(solution)/shard_map/ppermute | solution.py:123
  65.4 5.5 %collective-permute-start.7 = (f32[176,128]{1,0:T(8,128)S(1)}, f32[176,128]{1,0:T(8,128)S(1)}, u32[]{:S(2)}, u32[]{:S(2)}) collective-permute-start(f32[176,128]{1,0:T(8,128)S(1)} %get-tuple-element.35), channel_id=1, source_target_pairs={{0,3},{1,0},{2,1},{3,2},{4,7},{5,4},{6,5},{7,6},{8,11},{9,8},{10,9... | collective-permute-start | bytes 270344 | tf_op jit(solution)/shard_map/ppermute | solution.py:123
  74.4 12.6 %copy-start.6 = (f32[3]{0:T(128)S(1)}, f32[3]{0:T(128)}, u32[]{:S(2)}) copy-start(f32[3]{0:T(128)} %copy-done.5) | copy-start | bytes 40
  87.0 1.4 %copy-start.4 = (f32[8,64,128]{2,1,0:T(8,128)S(1)}, f32[8,64,128]{2,1,0:T(8,128)}, u32[]{:S(2)}) copy-start(f32[8,64,128]{2,1,0:T(8,128)} %get-tuple-element.14) | copy-start | bytes 786436
  88.6 13.7 %collective-permute-start.9 = (f32[1088,128]{1,0:T(8,128)S(1)}, f32[1088,128]{1,0:T(8,128)S(1)}, u32[]{:S(2)}, u32[]{:S(2)}) collective-permute-start(f32[1088,128]{1,0:T(8,128)S(1)} %pad_maximum_fusion.10), channel_id=1, source_target_pairs={{0,252},{4,0},{8,4},{12,8},{16,12},{20,16},{24,20},{28,24},{32,28}... | collective-permute-start | bytes 1671176 | tf_op jit(solution)/shard_map/ppermute | solution.py:123
  89.5 17.7 %collective-permute-start.8 = (f32[1088,128]{1,0:T(8,128)S(1)}, f32[1088,128]{1,0:T(8,128)S(1)}, u32[]{:S(2)}, u32[]{:S(2)}) collective-permute-start(f32[1088,128]{1,0:T(8,128)S(1)} %pad_maximum_fusion.9), channel_id=1, source_target_pairs={{0,4},{4,8},{8,12},{12,16},{16,20},{20,24},{24,28},{28,32},{32,36}... | collective-permute-start | bytes 1671176 | tf_op jit(solution)/shard_map/ppermute | solution.py:123
  107.2 1.1 copy-start.1
  108.3 10.0 %collective-permute-start.11 = (f32[592,128]{1,0:T(8,128)S(1)}, f32[592,128]{1,0:T(8,128)S(1)}, u32[]{:S(2)}, u32[]{:S(2)}) collective-permute-start(f32[592,128]{1,0:T(8,128)S(1)} %pad_maximum_fusion.14), channel_id=1, source_target_pairs={{0,3},{1,0},{2,1},{3,2},{4,7},{5,4},{6,5},{7,6},{8,11},{9,8},{10,9... | collective-permute-start | bytes 909320 | tf_op jit(solution)/shard_map/ppermute | solution.py:123
  110.1 8.3 %collective-permute-start.10 = (f32[592,128]{1,0:T(8,128)S(1)}, f32[592,128]{1,0:T(8,128)S(1)}, u32[]{:S(2)}, u32[]{:S(2)}) collective-permute-start(f32[592,128]{1,0:T(8,128)S(1)} %pad_maximum_fusion.13), channel_id=1, source_target_pairs={{0,1},{1,2},{2,3},{3,0},{4,5},{5,6},{6,7},{7,4},{8,9},{9,10},{10,1... | collective-permute-start | bytes 909320 | tf_op jit(solution)/shard_map/ppermute | solution.py:123

commit v8 on v7

--- a/solution.py
+++ b/solution.py
@@ -193,7 +193,7 @@
             w_ref[k, z] = ws[k] * inv
         w_ref[4, z] = jnp.where(top, 0.0, ws[4]) * inv
         w_ref[5, z] = jnp.where(bot, 0.0, ws[5]) * inv
-        w_ref[6, z] = s_ref[z] * inv
+        w_ref[6, z] = s_ref[z - 1] * inv
         return carry
 
     copies[0].wait()
@@ -266,7 +266,7 @@
         scratch_shapes=[
             pltpu.VMEM((planes, rows + 16, lanes), jnp.float32),
             pltpu.VMEM((planes, rows, lanes), jnp.float32),
-            pltpu.VMEM((planes, rows, lanes), jnp.float32),
+            pltpu.VMEM(source_e.shape, jnp.float32),
             pltpu.VMEM(species_e.shape, jnp.float32),
             pltpu.VMEM((planes, rows + 16, lanes), jnp.float32),
             pltpu.VMEM((planes, rows + 16, lanes), jnp.float32),
@@ -354,10 +354,10 @@
         source = jnp.sum(charge_num[:, None, None, None] * species, axis=0) + electrode
         if step == 0:
             field_e, species_e = first[0], first[2]
-            (source_e,) = deep_halo([(source, deep, wide_y)], "wide", "narrow")
+            (source_e,) = deep_halo([(source, deep - 1, wide_y)], "wide", "narrow")
         else:
             field_e, source_e, species_e = deep_halo(
-                [(field, deep, wide_y), (source, deep, wide_y), (species, 1, wide_y)], "wide", "narrow"
+                [(field, deep, wide_y), (source, deep - 1, wide_y), (species, 1, wide_y)], "wide", "narrow"
             )
         field, species = time_step(diffusivity, charge_num, field_e, perm_ext, source_e, species_e)
     return (species, field)

time: 134 us -> 132 us (0.985)
  waiting for transfers between devices: 34.5 us -> 32.6 us
    ppermute x12, waiting for transfers between devices: 34.5 us -> 32.6 us  [ring(): lax.ppermute(x, axis, [(i, (i + shift) % count) for i in range(count)])]
  transfers between devices with their start and end apart: 12 -> 12, of which waited for: 6 -> 6; matrix products, arithmetic and copies ran while one was open for 17% -> 18% of each run, Pallas kernels for 0% -> 0%
where the time goes in v8:
time: 132 us; the launch traced here: 131 us
  waiting for transfers between devices  32.6 us (25%)
  other arithmetic  31.7 us (24%)
  starting transfers between devices  26.3 us (20%)
  Pallas kernels  23.1 us (18%)
  blocking collectives  10.4 us (8%)
  local copies, waits for them, and re-layouts  5.29 us (4%)
  between operations  1.93 us (1%)
    ppermute x12, waiting for transfers between devices, ring(): lax.ppermute(x, axis, [(i, (i + shift) % count) for i in range(count)])  32.6 us
    ppermute x12, starting transfers between devices, ring(): lax.ppermute(x, axis, [(i, (i + shift) % count) for i in range(count)])  26.3 us
    pallas_call x2, Pallas kernels, time_step(): pl.pallas_call(step_kernel, out_shape=(jax.ShapeDtypeStruct((inner, out_r...  23.1 us
    reduce_sum x1, other arithmetic, one_block(): return jnp.sum(jnp.where(adjacent, term, 0.0), axis=1)  18.2 us
    all_gather x1, blocking collectives, per_device(): gathered = lax.all_gather(charges, 'narrow', axis=1, tiled=True)  10.4 us
    concatenate x6, other arithmetic, deep_halo(): jnp.concatenate([lo, a, hi], axis=a.ndim - back)  6.56 us
    scatter-add x1, other arithmetic, per_device(): jnp.zeros((depth * height * width,), jnp.float32).at[index].add(values)  3.33 us
    slice x7, local copies, waits for them, and re-layouts, deep_halo(): tops.append(lax.slice_in_dim(a, n - w, n, axis=dim))  3.14 us
  transfers between devices with their start and end apart: 12, of which 6 were waited for; matrix products, arithmetic and copies ran while one was open for 18% of the time, Pallas kernels for 0%

profile of v8, /device:TPU:1, one launch (start us, length us, event | category | flops | bytes accessed | tf_op | source)
XLA Modules:
  0.0 131.2 jit_solution(2729123060242627535)
XLA Ops:
  0.6 0.0 copy-start.2
  0.6 0.7 convert_element_type.28
  1.4 0.8 pad_maximum_fusion.31
  2.2 10.4 %all_gather.3 = f32[5,8192]{1,0:T(8,128)S(1)} all-gather(f32[5,2048]{1,0:T(8,128)S(1)} %pad_maximum_fusion.31), channel_id=1, replica_groups=mesh['wide'=64,'narrow'=4] {'narrow'}, dimensions={1}, use_global_device_ids=true | all-gather | bytes 204800 | tf_op jit(solution)/shard_map/all_gather | solution.py:324
  12.6 1.0 fusion.36
  13.5 1.1 fusion.43
  14.6 0.0 copy-done.2
  14.7 0.0 copy-start.8
  14.7 0.0 copy-start.7
  14.7 7.1 %collective-permute-start.1 = (f32[1088,128]{1,0:T(8,128)S(1)}, f32[1088,128]{1,0:T(8,128)S(1)}, u32[]{:S(2)}, u32[]{:S(2)}) collective-permute-start(f32[1088,128]{1,0:T(8,128)S(1)} %pad_maximum_fusion.8), channel_id=1, source_target_pairs={{0,252},{4,0},{8,4},{12,8},{16,12},{20,16},{24,20},{28,24},{32,28}... | collective-permute-start | bytes 1671176 | tf_op jit(solution)/shard_map/ppermute | solution.py:123
  21.9 0.1 collective-permute-start
  22.6 0.0 copy-done.8
  22.7 0.0 copy-start.5
  22.7 0.0 copy-done.7
  22.8 0.1 fusion.42
  22.9 0.0 copy-start
  22.9 18.2 %select_reduce_fusion.1 = (f32[256]{0:T(256)S(1)}, f32[256]{0:T(256)S(1)}) fusion(f32[8192]{0:T(1024)S(1)} %bitcast.140, f32[256]{0:T(256)S(1)} %get-tuple-element.79, f32[8192]{0:T(1024)S(1)} %bitcast.141, f32[256]{0:T(256)S(1)} %get-tuple-element.68, f32[8192]{0:T(1024)S(1)} %bitcast.142, f32[256]{0:T(256)S(1)} %get-tuple-element.77, ...), kind=kLoop, calls=%fused_computation.21 | loop fusion | flops 104857088 | bytes 174080 | tf_op jit(solution)/shard_map/reduce_sum | solution.py:114
  41.1 3.3 %scatter_custom_fusion = f32[65536]{0:T(1024)S(1)} fusion(s32[512]{0:T(512)S(1)} %bitcast.145, f32[512]{0:T(512)S(1)} %maximum_multiply_fusion, f32[]{:T(128)} %constant.72.clone.1), kind=kCustom, calls=%fused_computation.44 | custom fusion | flops 512 | bytes 262148 | tf_op jit(solution)/shard_map/scatter-add | solution.py:347
  44.5 0.0 copy-done.5
  44.5 0.0 copy-done
  44.5 0.1 multiply_reduce_fusion.1
  44.7 5.7 %collective-permute-start.5 = (f32[384,128]{1,0:T(8,128)S(1)}, f32[384,128]{1,0:T(8,128)S(1)}, u32[]{:S(2)}, u32[]{:S(2)}) collective-permute-start(f32[384,128]{1,0:T(8,128)S(1)} %bitcast.136), channel_id=1, source_target_pairs={{0,252},{4,0},{8,4},{12,8},{16,12},{20,16},{24,20},{28,24},{32,28}... | collective-permute-start | bytes 589832 | tf_op jit(solution)/shard_map/ppermute | solution.py:123
  50.4 0.0 copy-start.3
  50.4 0.0 collective-permute-start.4
  50.4 0.0 collective-permute-done.1
  50.5 0.0 collective-permute-done
  50.6 0.8 copy-done.3
  51.5 1.1 collective-permute-start.3
  52.6 2.6 %collective-permute-start.2 = (f32[592,128]{1,0:T(8,128)S(1)}, f32[592,128]{1,0:T(8,128)S(1)}, u32[]{:S(2)}, u32[]{:S(2)}) collective-permute-start(f32[592,128]{1,0:T(8,128)S(1)} %pad_maximum_fusion.11), channel_id=1, source_target_pairs={{0,1},{1,2},{2,3},{3,0},{4,5},{5,6},{6,7},{7,4},{8,9},{9,10},{10,1... | collective-permute-start | bytes 909320 | tf_op jit(solution)/shard_map/ppermute | solution.py:123
  55.2 0.0 collective-permute-done.5
  55.2 4.9 %collective-permute-done.4 = f32[384,128]{1,0:T(8,128)S(1)} collective-permute-done((f32[384,128]{1,0:T(8,128)S(1)}, f32[384,128]{1,0:T(8,128)S(1)}, u32[]{:S(2)}, u32[]{:S(2)}) %collective-permute-start.4) | collective-permute-done | bytes 196640 | tf_op jit(solution)/shard_map/ppermute | solution.py:123
  60.1 4.6 %collective-permute-start.6 = (f32[160,128]{1,0:T(8,128)S(1)}, f32[160,128]{1,0:T(8,128)S(1)}, u32[]{:S(2)}, u32[]{:S(2)}) collective-permute-start(f32[160,128]{1,0:T(8,128)S(1)} %get-tuple-element.38), channel_id=1, source_target_pairs={{0,1},{1,2},{2,3},{3,0},{4,5},{5,6},{6,7},{7,4},{8,9},{9,10},{10,1... | collective-permute-start | bytes 245768 | tf_op jit(solution)/shard_map/ppermute | solution.py:123
  64.7 0.0 collective-permute-start.7
  64.7 2.9 %collective-permute-done.6 = f32[160,128]{1,0:T(8,128)S(1)} collective-permute-done((f32[160,128]{1,0:T(8,128)S(1)}, f32[160,128]{1,0:T(8,128)S(1)}, u32[]{:S(2)}, u32[]{:S(2)}) %collective-permute-start.6) | collective-permute-done | bytes 81952 | tf_op jit(solution)/shard_map/ppermute | solution.py:123
  67.6 2.5 %collective-permute-done.7 = f32[160,128]{1,0:T(8,128)S(1)} collective-permute-done((f32[160,128]{1,0:T(8,128)S(1)}, f32[160,128]{1,0:T(8,128)S(1)}, u32[]{:S(2)}, u32[]{:S(2)}) %collective-permute-start.7) | collective-permute-done | bytes 81952 | tf_op jit(solution)/shard_map/ppermute | solution.py:123
  70.1 1.0 pad_maximum_fusion.5.s_hbm
  71.0 0.0 collective-permute-done.3
  71.0 0.0 collective-permute-done.2
  71.1 1.1 pad_maximum_fusion.c_hbm
  72.2 1.3 %pad_maximum_fusion.2 = (f32[22,80,128]{2,1,0:T(8,128)}, f32[22,80,128]{2,1,0:T(8,128)}) fusion(f32[22,8,128]{2,1,0:T(8,128)S(1)} %get-tuple-element.47, f32[7,64,128]{2,1,0:T(8,128)S(1)} %bitcast.88, f32[8,64,128]{2,1,0:T(8,128)S(1)} %copy-done.3, f32[7,64,128]{2,1,0:T(8,128)S(1)} %bitcast.92, f32[22,8,128]{2,1,0:T(8,128)S(1)} %get-tuple-element.45, ...), kind=kLoop, calls=%fused_computation.29 | loop fusion | flops 1802240 | bytes 3604480 | tf_op jit(solution)/shard_map/concatenate | solution.py:147
  73.6 0.0 copy-start.6
  73.6 11.6 %shard_map.113 = (f32[8,64,128]{2,1,0:T(8,128)}, f32[3,8,64,128]{3,2,1,0:T(8,128)}) custom-call(f32[3]{0:T(128)} %dif_ref.3, f32[3]{0:T(128)} %copy-done.5, f32[22,80,128]{2,1,0:T(8,128)} %get-tuple-element.75.f_hbm, f32[22,80,128]{2,1,0:T(8,128)} %get-tuple-element.76.p_hbm, f32[20,80,128]{2,1,0:T(8,128)} %pad_maximum_fusion.5.s_hbm, ...), custom_call_target="tpu_custom_call" | custom-call | flops 40755200 | bytes 4980736 | tf_op jit(solution)/shard_map/pallas_call | solution.py:258
  85.2 1.0 fusion.35
  86.1 0.0 copy-done.6
  86.1 0.0 copy-start.4
  86.2 1.3 %multiply_reduce_fusion = f32[8,64,128]{2,1,0:T(8,128)S(1)} fusion(f32[3,8,64,128]{3,2,1,0:T(8,128)} %get-tuple-element.15, f32[3]{0:T(128)S(1)} %copy-done.6), kind=kLoop, calls=%fused_computation.34 | loop fusion | flops 327680 | bytes 1048588 | tf_op jit(solution)/shard_map/reduce_sum | solution.py:354
  87.6 0.0 copy-done.4
  87.7 0.7 collective-permute-start.9
  88.4 0.9 collective-permute-start.8
  89.3 11.4 %collective-permute-done.9 = f32[1024,128]{1,0:T(8,128)S(1)} collective-permute-done((f32[1024,128]{1,0:T(8,128)S(1)}, f32[1024,128]{1,0:T(8,128)S(1)}, u32[]{:S(2)}, u32[]{:S(2)}) %collective-permute-start.9) | collective-permute-done | bytes 524320 | tf_op jit(solution)/shard_map/ppermute | solution.py:123
  100.7 4.6 %collective-permute-done.8 = f32[1024,128]{1,0:T(8,128)S(1)} collective-permute-done((f32[1024,128]{1,0:T(8,128)S(1)}, f32[1024,128]{1,0:T(8,128)S(1)}, u32[]{:S(2)}, u32[]{:S(2)}) %collective-permute-start.8) | collective-permute-done | bytes 524320 | tf_op jit(solution)/shard_map/ppermute | solution.py:123
  105.4 0.0 copy-start.1
  105.5 1.0 copy-done.1
  106.5 1.8 %collective-permute-start.11 = (f32[576,128]{1,0:T(8,128)S(1)}, f32[576,128]{1,0:T(8,128)S(1)}, u32[]{:S(2)}, u32[]{:S(2)}) collective-permute-start(f32[576,128]{1,0:T(8,128)S(1)} %pad_maximum_fusion.14), channel_id=1, source_target_pairs={{0,3},{1,0},{2,1},{3,2},{4,7},{5,4},{6,5},{7,6},{8,11},{9,8},{10,9... | collective-permute-start | bytes 884744 | tf_op jit(solution)/shard_map/ppermute | solution.py:123
  108.4 1.6 %collective-permute-start.10 = (f32[576,128]{1,0:T(8,128)S(1)}, f32[576,128]{1,0:T(8,128)S(1)}, u32[]{:S(2)}, u32[]{:S(2)}) collective-permute-start(f32[576,128]{1,0:T(8,128)S(1)} %pad_maximum_fusion.13), channel_id=1, source_target_pairs={{0,1},{1,2},{2,3},{3,0},{4,5},{5,6},{6,7},{7,4},{8,9},{9,10},{10,1... | collective-permute-start | bytes 884744 | tf_op jit(solution)/shard_map/ppermute | solution.py:123
  110.0 6.4 %collective-permute-done.11 = f32[576,128]{1,0:T(8,128)S(1)} collective-permute-done((f32[576,128]{1,0:T(8,128)S(1)}, f32[576,128]{1,0:T(8,128)S(1)}, u32[]{:S(2)}, u32[]{:S(2)}) %collective-permute-start.11) | collective-permute-done | bytes 294944 | tf_op jit(solution)/shard_map/ppermute | solution.py:123
  116.3 0.0 collective-permute-done.10
  116.4 1.0 pad_maximum_fusion.6.s_hbm
  117.4 1.1 pad_maximum_fusion.1.c_hbm
  118.5 1.0 pad_maximum_fusion.4.f_hbm
  119.5 11.5 %shard_map.114 = (f32[8,64,128]{2,1,0:T(8,128)}, f32[3,8,64,128]{3,2,1,0:T(8,128)}) custom-call(f32[3]{0:T(128)} %dif_ref.3, f32[3]{0:T(128)} %copy-done.5, f32[22,80,128]{2,1,0:T(8,128)} %pad_maximum_fusion.4.f_hbm, f32[22,80,128]{2,1,0:T(8,128)} %get-tuple-element.76.p_hbm, f32[20,80,128]{2,1,0:T(8,128)} %pad_maximum_fusion.6.s_hbm, ...), custom_call_target="tpu_custom_call" | custom-call | flops 40755200 | bytes 4980736 | tf_op jit(solution)/shard_map/pallas_call | solution.py:258
  (48 shorter events, 0.9 us)
Async XLA Ops:
  0.6 14.0 %copy-start.2 = (f32[8,64,128]{2,1,0:T(8,128)S(1)}, f32[8,64,128]{2,1,0:T(8,128)}, u32[]{:S(2)}) copy-start(f32[8,64,128]{2,1,0:T(8,128)} %param.12) | copy-start | bytes 786436
  14.7 8.0 %copy-start.8 = (s32[3]{0:T(128)S(1)}, s32[3]{0:T(128)}, u32[]{:S(2)}) copy-start(s32[3]{0:T(128)} %param.14) | copy-start | bytes 40
  14.7 8.0 %copy-start.7 = (s32[1,1,512]{2,1,0:T(1,128)S(1)}, s32[1,1,512]{2,1,0:T(1,128)}, u32[]{:S(2)}) copy-start(s32[1,1,512]{2,1,0:T(1,128)} %param.18) | copy-start | bytes 6148
  14.7 35.7 %collective-permute-start.1 = (f32[1088,128]{1,0:T(8,128)S(1)}, f32[1088,128]{1,0:T(8,128)S(1)}, u32[]{:S(2)}, u32[]{:S(2)}) collective-permute-start(f32[1088,128]{1,0:T(8,128)S(1)} %pad_maximum_fusion.8), channel_id=1, source_target_pairs={{0,252},{4,0},{8,4},{12,8},{16,12},{20,16},{24,20},{28,24},{32,28}... | collective-permute-start | bytes 1671176 | tf_op jit(solution)/shard_map/ppermute | solution.py:123
  21.9 28.6 %collective-permute-start = (f32[1088,128]{1,0:T(8,128)S(1)}, f32[1088,128]{1,0:T(8,128)S(1)}, u32[]{:S(2)}, u32[]{:S(2)}) collective-permute-start(f32[1088,128]{1,0:T(8,128)S(1)} %pad_maximum_fusion.7), channel_id=1, source_target_pairs={{0,4},{4,8},{8,12},{12,16},{16,20},{20,24},{24,28},{28,32},{32,36}... | collective-permute-start | bytes 1671176 | tf_op jit(solution)/shard_map/ppermute | solution.py:123
  22.7 21.8 %copy-start.5 = (f32[3]{0:T(128)}, f32[3]{0:T(128)S(1)}, u32[]{:S(2)}) copy-start(f32[3]{0:T(128)S(1)} %convert_element_type.27.val_ref) | copy-start | bytes 40
  22.9 21.6 %copy-start = (f32[3,8,64,128]{3,2,1,0:T(8,128)S(1)}, f32[3,8,64,128]{3,2,1,0:T(8,128)}, u32[]{:S(2)}) copy-start(f32[3,8,64,128]{3,2,1,0:T(8,128)} %param.10) | copy-start | bytes 2359300
  44.7 10.5 %collective-permute-start.5 = (f32[384,128]{1,0:T(8,128)S(1)}, f32[384,128]{1,0:T(8,128)S(1)}, u32[]{:S(2)}, u32[]{:S(2)}) collective-permute-start(f32[384,128]{1,0:T(8,128)S(1)} %bitcast.136), channel_id=1, source_target_pairs={{0,252},{4,0},{8,4},{12,8},{16,12},{20,16},{24,20},{28,24},{32,28}... | collective-permute-start | bytes 589832 | tf_op jit(solution)/shard_map/ppermute | solution.py:123
  50.4 0.9 copy-start.3
  50.4 9.6 %collective-permute-start.4 = (f32[384,128]{1,0:T(8,128)S(1)}, f32[384,128]{1,0:T(8,128)S(1)}, u32[]{:S(2)}, u32[]{:S(2)}) collective-permute-start(f32[384,128]{1,0:T(8,128)S(1)} %bitcast.135), channel_id=1, source_target_pairs={{0,4},{4,8},{8,12},{12,16},{16,20},{20,24},{24,28},{28,32},{32,36}... | collective-permute-start | bytes 589832 | tf_op jit(solution)/shard_map/ppermute | solution.py:123
  51.5 19.5 %collective-permute-start.3 = (f32[592,128]{1,0:T(8,128)S(1)}, f32[592,128]{1,0:T(8,128)S(1)}, u32[]{:S(2)}, u32[]{:S(2)}) collective-permute-start(f32[592,128]{1,0:T(8,128)S(1)} %pad_maximum_fusion.12), channel_id=1, source_target_pairs={{0,3},{1,0},{2,1},{3,2},{4,7},{5,4},{6,5},{7,6},{8,11},{9,8},{10,9... | collective-permute-start | bytes 909320 | tf_op jit(solution)/shard_map/ppermute | solution.py:123
  52.6 18.4 %collective-permute-start.2 = (f32[592,128]{1,0:T(8,128)S(1)}, f32[592,128]{1,0:T(8,128)S(1)}, u32[]{:S(2)}, u32[]{:S(2)}) collective-permute-start(f32[592,128]{1,0:T(8,128)S(1)} %pad_maximum_fusion.11), channel_id=1, source_target_pairs={{0,1},{1,2},{2,3},{3,0},{4,5},{5,6},{6,7},{7,4},{8,9},{9,10},{10,1... | collective-permute-start | bytes 909320 | tf_op jit(solution)/shard_map/ppermute | solution.py:123
  60.1 7.5 %collective-permute-start.6 = (f32[160,128]{1,0:T(8,128)S(1)}, f32[160,128]{1,0:T(8,128)S(1)}, u32[]{:S(2)}, u32[]{:S(2)}) collective-permute-start(f32[160,128]{1,0:T(8,128)S(1)} %get-tuple-element.38), channel_id=1, source_target_pairs={{0,1},{1,2},{2,3},{3,0},{4,5},{5,6},{6,7},{7,4},{8,9},{9,10},{10,1... | collective-permute-start | bytes 245768 | tf_op jit(solution)/shard_map/ppermute | solution.py:123
  64.7 5.4 %collective-permute-start.7 = (f32[160,128]{1,0:T(8,128)S(1)}, f32[160,128]{1,0:T(8,128)S(1)}, u32[]{:S(2)}, u32[]{:S(2)}) collective-permute-start(f32[160,128]{1,0:T(8,128)S(1)} %get-tuple-element.39), channel_id=1, source_target_pairs={{0,3},{1,0},{2,1},{3,2},{4,7},{5,4},{6,5},{7,6},{8,11},{9,8},{10,9... | collective-permute-start | bytes 245768 | tf_op jit(solution)/shard_map/ppermute | solution.py:123
  73.6 12.6 %copy-start.6 = (f32[3]{0:T(128)S(1)}, f32[3]{0:T(128)}, u32[]{:S(2)}) copy-start(f32[3]{0:T(128)} %copy-done.5) | copy-start | bytes 40
  86.1 1.4 %copy-start.4 = (f32[8,64,128]{2,1,0:T(8,128)S(1)}, f32[8,64,128]{2,1,0:T(8,128)}, u32[]{:S(2)}) copy-start(f32[8,64,128]{2,1,0:T(8,128)} %get-tuple-element.14) | copy-start | bytes 786436
  87.7 13.0 %collective-permute-start.9 = (f32[1024,128]{1,0:T(8,128)S(1)}, f32[1024,128]{1,0:T(8,128)S(1)}, u32[]{:S(2)}, u32[]{:S(2)}) collective-permute-start(f32[1024,128]{1,0:T(8,128)S(1)} %pad_maximum_fusion.10), channel_id=1, source_target_pairs={{0,252},{4,0},{8,4},{12,8},{16,12},{20,16},{24,20},{28,24},{32,28}... | collective-permute-start | bytes 1572872 | tf_op jit(solution)/shard_map/ppermute | solution.py:123
  88.4 16.9 %collective-permute-start.8 = (f32[1024,128]{1,0:T(8,128)S(1)}, f32[1024,128]{1,0:T(8,128)S(1)}, u32[]{:S(2)}, u32[]{:S(2)}) collective-permute-start(f32[1024,128]{1,0:T(8,128)S(1)} %pad_maximum_fusion.9), channel_id=1, source_target_pairs={{0,4},{4,8},{8,12},{12,16},{16,20},{20,24},{24,28},{28,32},{32,36}... | collective-permute-start | bytes 1572872 | tf_op jit(solution)/shard_map/ppermute | solution.py:123
  105.4 1.1 copy-start.1
  106.5 9.8 %collective-permute-start.11 = (f32[576,128]{1,0:T(8,128)S(1)}, f32[576,128]{1,0:T(8,128)S(1)}, u32[]{:S(2)}, u32[]{:S(2)}) collective-permute-start(f32[576,128]{1,0:T(8,128)S(1)} %pad_maximum_fusion.14), channel_id=1, source_target_pairs={{0,3},{1,0},{2,1},{3,2},{4,7},{5,4},{6,5},{7,6},{8,11},{9,8},{10,9... | collective-permute-start | bytes 884744 | tf_op jit(solution)/shard_map/ppermute | solution.py:123
  108.4 8.0 %collective-permute-start.10 = (f32[576,128]{1,0:T(8,128)S(1)}, f32[576,128]{1,0:T(8,128)S(1)}, u32[]{:S(2)}, u32[]{:S(2)}) collective-permute-start(f32[576,128]{1,0:T(8,128)S(1)} %pad_maximum_fusion.13), channel_id=1, source_target_pairs={{0,1},{1,2},{2,3},{3,0},{4,5},{5,6},{6,7},{7,4},{8,9},{9,10},{10,1... | collective-permute-start | bytes 884744 | tf_op jit(solution)/shard_map/ppermute | solution.py:123

commit v9 on v8

--- a/solution.py
+++ b/solution.py
@@ -1,3 +1,5 @@
+import functools
+
 import jax
 import jax.numpy as jnp
 from jax import lax
@@ -124,42 +126,74 @@
 
 
 def deep_halo(items, axis_z, axis_y):
-    for back, axis, pick in ((3, axis_z, 1), (2, axis_y, 2)):
-        tops, bots = [], []
-        for item in items:
-            a, w = item[0], item[pick]
-            dim = a.ndim - back
-            n = a.shape[dim]
-            tops.append(lax.slice_in_dim(a, n - w, n, axis=dim))
-            bots.append(lax.slice_in_dim(a, 0, w, axis=dim))
-        minor = items[0][0].shape[-1]
-        top = jnp.concatenate([t.reshape(-1, minor) for t in tops], axis=0)
-        bot = jnp.concatenate([t.reshape(-1, minor) for t in bots], axis=0)
-        below = ring(top, axis, 1)
-        above = ring(bot, axis, -1)
-        out, at = [], 0
-        for item, t in zip(items, tops):
-            a = item[0]
-            size = t.size // minor
-            lo = below[at:at + size].reshape(t.shape)
-            hi = above[at:at + size].reshape(t.shape)
-            at += size
-            out.append((jnp.concatenate([lo, a, hi], axis=a.ndim - back),) + tuple(item[1:]))
-        items = out
-    return [item[0] for item in items]
-
-
-def step_kernel(
-    dif_ref, val_ref, f_hbm, p_hbm, s_hbm, c_hbm, fo_ref, co_ref, f_ref, p_ref, s_ref, c_ref, fa, fb, w_ref, sems
-):
-    copies = [
-        pltpu.make_async_copy(src, dst, sems.at[k])
-        for k, (src, dst) in enumerate(
-            ((p_hbm, p_ref), (f_hbm, f_ref.at[:, 8:88, :]), (s_hbm, s_ref), (c_hbm, c_ref))
+    minor = items[0][0].shape[-1]
+    rows = items[0][0].shape[-2]
+    tops, bots = [], []
+    for a, wz, _ in items:
+        dim = a.ndim - 3
+        n = a.shape[dim]
+        tops.append(lax.slice_in_dim(a, n - wz, n, axis=dim))
+        bots.append(lax.slice_in_dim(a, 0, wz, axis=dim))
+    z_lo = ring(jnp.concatenate([t.reshape(-1, minor) for t in tops], axis=0), axis_z, 1)
+    z_hi = ring(jnp.concatenate([t.reshape(-1, minor) for t in bots], axis=0), axis_z, -1)
+    y_tops, y_bots, z_offs, at = [], [], [], 0
+    for (a, wz, wy), t in zip(items, tops):
+        size = t.size // minor
+        z_offs.append(at // rows)
+        ext = jnp.concatenate(
+            [z_lo[at:at + size].reshape(t.shape), a, z_hi[at:at + size].reshape(t.shape)], axis=a.ndim - 3
         )
-    ]
-    for copy in copies:
-        copy.start()
+        at += size
+        y_tops.append(ext[..., rows - wy:rows, :])
+        y_bots.append(ext[..., 0:wy, :])
+    wy = items[0][2]
+    y_lo = ring(jnp.concatenate([t.reshape(-1, minor) for t in y_tops], axis=0), axis_y, 1)
+    y_hi = ring(jnp.concatenate([t.reshape(-1, minor) for t in y_bots], axis=0), axis_y, -1)
+    y_offs, at = [], 0
+    for t in y_tops:
+        y_offs.append(at // wy)
+        at += t.size // minor
+    bufs = (
+        z_lo.reshape(-1, rows, minor),
+        z_hi.reshape(-1, rows, minor),
+        y_lo.reshape(-1, wy, minor),
+        y_hi.reshape(-1, wy, minor),
+    )
+    return [(a,) + bufs + (zo, yo, wz) for (a, wz, _), zo, yo in zip(items, z_offs, y_offs)]
+
+
+def step_kernel(plan, dif_ref, val_ref, *refs):
+    hbm = refs[:20]
+    fo_ref, co_ref, f_ref, p_ref, s_ref, c_ref, fa, fb, w_ref, sems = refs[20:]
+    targets = (f_ref, p_ref, s_ref, c_ref)
+    copies = [[] for _ in targets]
+    count = 0
+    for k, (lead, z_off, y_off, wz, r0) in enumerate(plan):
+        inner_ref, z_lo, z_hi, y_lo, y_hi = hbm[5 * k:5 * k + 5]
+        target = targets[k]
+        span = 2 * wz + inner_ref.shape[-3]
+        mid = slice(r0 + 8, r0 + 8 + inner_ref.shape[-2])
+        moves = [(inner_ref, target.at[..., wz:span - wz, mid, :])]
+        for s in range(lead):
+            part = target.at[s] if lead > 1 or target.ndim == 4 else target
+            zs = slice(z_off + s * wz, z_off + (s + 1) * wz)
+            ys = slice(y_off + s * span, y_off + (s + 1) * span)
+            moves += [
+                (z_lo.at[zs], part.at[0:wz, mid, :]),
+                (z_hi.at[zs], part.at[span - wz:span, mid, :]),
+                (y_lo.at[ys], part.at[:, r0:r0 + 8, :]),
+                (y_hi.at[ys], part.at[:, mid.stop:mid.stop + 8, :]),
+            ]
+        for src, dst in moves:
+            copy = pltpu.make_async_copy(src, dst, sems.at[count])
+            copy.start()
+            copies[k].append(copy)
+            count += 1
+
+    def wait(k):
+        for copy in copies[k]:
+            copy.wait()
+
     planes, rows, lanes = p_ref.shape
     species, inner = c_ref.shape[0], c_ref.shape[1] - 2
     hz = (planes - inner) // 2
@@ -196,10 +230,10 @@
         w_ref[6, z] = s_ref[z - 1] * inv
         return carry
 
-    copies[0].wait()
-    copies[2].wait()
+    wait(1)
+    wait(2)
     lax.fori_loop(1, planes - 1, weights, 0, unroll=2)
-    copies[1].wait()
+    wait(0)
     pad = jnp.zeros((planes, 8, lanes), jnp.float32)
     for buf in (f_ref, fa, fb):
         buf[:, 0:8, :] = pad
@@ -220,7 +254,7 @@
 
         lax.fori_loop(k + 1, planes - k - 1, sweep, 0, unroll=2)
     final = bufs[(sweeps - 1) % 2]
-    copies[3].wait()
+    wait(3)
 
     def move(z, carry):
         zf = z + hz
@@ -247,38 +281,44 @@
     lax.fori_loop(0, inner, move, 0, unroll=2)
 
 
-def time_step(diffusivity, charge_num, field_e, perm_e, source_e, species_e):
-    planes, rows, lanes = field_e.shape
-    species, inner = species_e.shape[0], species_e.shape[1] - 2
-    out_rows = rows - 2 * (SWEEPS + 2)
+def time_step(diffusivity, charge_num, field_p, perm_p, source_p, species_p):
+    species, inner, out_rows, lanes = species_p[0].shape
+    planes = inner + 2 * field_p[7]
+    rows = out_rows + 2 * (SWEEPS + 2)
+    plan, operands, boxes = [], [], []
+    for pieces, r0 in ((field_p, 8), (perm_p, 0), (source_p, 0), (species_p, 0)):
+        inner_arr, z_lo, z_hi, y_lo, y_hi, z_off, y_off, wz = pieces
+        lead = inner_arr.shape[0] if inner_arr.ndim == 4 else 1
+        plan.append((lead, z_off, y_off, wz, r0))
+        operands += [inner_arr, z_lo, z_hi, y_lo, y_hi]
+        box_shape = (inner + 2 * wz, rows + 2 * r0, lanes)
+        boxes.append(box_shape if inner_arr.ndim == 3 else (lead,) + box_shape)
     smem = pl.BlockSpec(memory_space=pltpu.SMEM)
     vmem = pl.BlockSpec(memory_space=pltpu.VMEM)
     hbm = pl.BlockSpec(memory_space=pl.ANY)
     points = planes * rows * lanes
+    moves = sum(1 + 4 * p[0] for p in plan)
     return pl.pallas_call(
-        step_kernel,
+        functools.partial(step_kernel, tuple(plan)),
         out_shape=(
             jax.ShapeDtypeStruct((inner, out_rows, lanes), jnp.float32),
             jax.ShapeDtypeStruct((species, inner, out_rows, lanes), jnp.float32),
         ),
-        in_specs=[smem, smem, hbm, hbm, hbm, hbm],
+        in_specs=[smem, smem] + [hbm] * len(operands),
         out_specs=(vmem, vmem),
-        scratch_shapes=[
-            pltpu.VMEM((planes, rows + 16, lanes), jnp.float32),
-            pltpu.VMEM((planes, rows, lanes), jnp.float32),
-            pltpu.VMEM(source_e.shape, jnp.float32),
-            pltpu.VMEM(species_e.shape, jnp.float32),
+        scratch_shapes=[pltpu.VMEM(shape, jnp.float32) for shape in boxes]
+        + [
             pltpu.VMEM((planes, rows + 16, lanes), jnp.float32),
             pltpu.VMEM((planes, rows + 16, lanes), jnp.float32),
             pltpu.VMEM((7, planes, rows, lanes), jnp.float32),
-            pltpu.SemaphoreType.DMA((4,)),
+            pltpu.SemaphoreType.DMA((moves,)),
         ],
         cost_estimate=pl.CostEstimate(
-            flops=points * (20 * SWEEPS + 20) + species_e.size * 30,
+            flops=points * (20 * SWEEPS + 20) + species * (inner + 2) * rows * lanes * 30,
             transcendentals=0,
-            bytes_accessed=4 * (3 * points + species_e.size + inner * out_rows * lanes * (species + 1)),
+            bytes_accessed=4 * (3 * points + inner * out_rows * lanes * (2 * species + 1)),
         ),
-    )(diffusivity, charge_num, field_e, perm_e, source_e, species_e)
+    )(diffusivity, charge_num, *operands)
 
 
 def box(a, have, want):
@@ -349,17 +389,17 @@
     charge_num = valence.astype(jnp.float32)
     field = potential
     species = concentration
-    perm_ext = first[1]
+    perm_p = first[1]
     for step in range(STEPS):
         source = jnp.sum(charge_num[:, None, None, None] * species, axis=0) + electrode
         if step == 0:
-            field_e, species_e = first[0], first[2]
-            (source_e,) = deep_halo([(source, deep - 1, wide_y)], "wide", "narrow")
+            field_p, species_p = first[0], first[2]
+            (source_p,) = deep_halo([(source, deep - 1, wide_y)], "wide", "narrow")
         else:
-            field_e, source_e, species_e = deep_halo(
+            field_p, source_p, species_p = deep_halo(
                 [(field, deep, wide_y), (source, deep - 1, wide_y), (species, 1, wide_y)], "wide", "narrow"
             )
-        field, species = time_step(diffusivity, charge_num, field_e, perm_ext, source_e, species_e)
+        field, species = time_step(diffusivity, charge_num, field_p, perm_p, source_p, species_p)
     return (species, field)
 
 

time: 132 us -> 124 us (0.939)
  waiting for transfers between devices: 32.6 us -> 25.5 us
  other arithmetic: 31.7 us -> 26.7 us
  starting transfers between devices: 26.3 us -> 29.2 us
    ppermute x12, waiting for transfers between devices: 32.6 us -> 25.5 us  [ring(): lax.ppermute(x, axis, [(i, (i + shift) % count) for i in range(count)])]
    concatenate x14 -> x10, other arithmetic: 6.79 us -> 1.89 us  [the longest x2 0.89 us: deep_halo(): jnp.concatenate([t.reshape(-1, minor) for t in bots], axis=0)]
    ppermute x12, starting transfers between devices: 26.3 us -> 29.2 us  [ring(): lax.ppermute(x, axis, [(i, (i + shift) % count) for i in range(count)])]
    unnamed x18 -> x46, local copies, waits for them, and re-layouts: 1.89 us -> 4.18 us
    slice x21 -> x17, local copies, waits for them, and re-layouts: 3.33 us -> 2.24 us  [the longest x7 2.09 us: deep_halo(): bots.append(lax.slice_in_dim(a, 0, wz, axis=dim))]
  transfers between devices with their start and end apart: 12 -> 12, of which waited for: 6 -> 4; matrix products, arithmetic and copies ran while one was open for 18% -> 19% of each run, Pallas kernels for 0% -> 0%
where the time goes in v9:
time: 124 us
  starting transfers between devices  29.2 us (24%)
  other arithmetic  26.7 us (22%)
  waiting for transfers between devices  25.5 us (21%)
  Pallas kernels  23.7 us (19%)
  blocking collectives  10.5 us (8%)
  local copies, waits for them, and re-layouts  6.44 us (5%)
  between operations  2.02 us (2%)
    ppermute x12, starting transfers between devices, ring(): lax.ppermute(x, axis, [(i, (i + shift) % count) for i in range(count)])  29.2 us
    ppermute x12, waiting for transfers between devices, ring(): lax.ppermute(x, axis, [(i, (i + shift) % count) for i in range(count)])  25.5 us
    pallas_call x2, Pallas kernels, time_step(): pl.pallas_call(functools.partial(step_kernel, tuple(plan)), out_shape=(ja...  23.7 us
    reduce_sum x1, other arithmetic, one_block(): return jnp.sum(jnp.where(adjacent, term, 0.0), axis=1)  18.2 us
    all_gather x1, blocking collectives, per_device(): gathered = lax.all_gather(charges, 'narrow', axis=1, tiled=True)  10.5 us
    unnamed x46, local copies, waits for them, and re-layouts  4.18 us
    scatter-add x1, other arithmetic, per_device(): jnp.zeros((depth * height * width,), jnp.float32).at[index].add(values)  3.33 us
  transfers between devices with their start and end apart: 12, of which 4 were waited for; matrix products, arithmetic and copies ran while one was open for 19% of the time, Pallas kernels for 0%

profile of v9, /device:TPU:1, one launch (start us, length us, event | category | flops | bytes accessed | tf_op | source)
XLA Modules:
  0.0 124.1 jit_solution(15120038167737856149)
XLA Ops:
  0.6 0.0 copy-start.11
  0.6 0.7 convert_element_type.28
  1.4 0.8 pad_maximum_fusion.24
  2.2 0.0 copy-start.6
  2.2 10.5 %all_gather.3 = f32[5,8192]{1,0:T(8,128)S(1)} all-gather(f32[5,2048]{1,0:T(8,128)S(1)} %pad_maximum_fusion.24), channel_id=1, replica_groups=mesh['wide'=64,'narrow'=4] {'narrow'}, dimensions={1}, use_global_device_ids=true | all-gather | bytes 204800 | tf_op jit(solution)/shard_map/all_gather | solution.py:364
  12.7 1.0 fusion.36
  13.7 0.0 copy-done.11
  13.7 0.0 copy-done.6
  13.8 0.8 pad_maximum_fusion
  14.6 0.0 collective-permute-start
  14.6 0.8 pad_maximum_fusion.1
  15.5 7.0 %collective-permute-start.1 = (f32[1088,128]{1,0:T(8,128)}, f32[1088,128]{1,0:T(8,128)S(1)}, u32[]{:S(2)}, u32[]{:S(2)}) collective-permute-start(f32[1088,128]{1,0:T(8,128)} %pad_maximum_fusion.1), channel_id=1, source_target_pairs={{0,252},{4,0},{8,4},{12,8},{16,12},{20,16},{24,20},{28,24},{32,28}... | collective-permute-start | bytes 1671176 | tf_op jit(solution)/shard_map/ppermute | solution.py:125
  23.2 0.0 copy-done.21
  23.3 0.1 fusion.42
  23.4 0.0 copy-start.5
  23.4 18.2 %select_reduce_fusion.1 = (f32[256]{0:T(256)S(1)}, f32[256]{0:T(256)S(1)}) fusion(f32[8192]{0:T(1024)S(1)} %bitcast.140, f32[256]{0:T(256)S(1)} %get-tuple-element.75, f32[8192]{0:T(1024)S(1)} %bitcast.141, f32[256]{0:T(256)S(1)} %get-tuple-element.64, f32[8192]{0:T(1024)S(1)} %bitcast.142, f32[256]{0:T(256)S(1)} %get-tuple-element.73, ...), kind=kLoop, calls=%fused_computation.21 | loop fusion | flops 104857088 | bytes 174080 | tf_op jit(solution)/shard_map/reduce_sum | solution.py:116
  41.7 3.3 %scatter_custom_fusion = f32[65536]{0:T(1024)S(1)} fusion(s32[512]{0:T(512)S(1)} %bitcast.145, f32[512]{0:T(512)S(1)} %maximum_multiply_fusion, f32[]{:T(128)} %constant.72.clone.1), kind=kCustom, calls=%fused_computation.37 | custom fusion | flops 512 | bytes 262148 | tf_op jit(solution)/shard_map/scatter-add | solution.py:387
  45.0 0.1 multiply_reduce_fusion.1
  45.2 0.0 copy-start.7
  45.2 0.1 collective-permute-start.4
  45.3 5.7 %collective-permute-start.5 = (f32[384,128]{1,0:T(8,128)S(1)}, f32[384,128]{1,0:T(8,128)S(1)}, u32[]{:S(2)}, u32[]{:S(2)}) collective-permute-start(f32[384,128]{1,0:T(8,128)S(1)} %bitcast.135), channel_id=1, source_target_pairs={{0,252},{4,0},{8,4},{12,8},{16,12},{20,16},{24,20},{28,24},{32,28}... | collective-permute-start | bytes 589832 | tf_op jit(solution)/shard_map/ppermute | solution.py:125
  51.0 0.0 collective-permute-done
  51.0 0.0 collective-permute-done.1
  51.1 0.7 copy-done
  51.9 0.1 copy-done.1
  52.1 3.6 %collective-permute-start.2 = (f32[592,128]{1,0:T(8,128)S(1)}, f32[592,128]{1,0:T(8,128)S(1)}, u32[]{:S(2)}, u32[]{:S(2)}) collective-permute-start(f32[592,128]{1,0:T(8,128)S(1)} %pad_maximum_fusion.4), channel_id=1, source_target_pairs={{0,1},{1,2},{2,3},{3,0},{4,5},{5,6},{6,7},{7,4},{8,9},{9,10},{10,1... | collective-permute-start | bytes 909320 | tf_op jit(solution)/shard_map/ppermute | solution.py:125
  55.7 0.1 collective-permute-start.3
  55.8 0.0 collective-permute-done.4
  55.8 0.0 copy-start.15
  55.8 0.0 collective-permute-done.5
  55.8 0.0 copy-start.16
  55.8 0.0 copy-done.7
  55.9 1.1 collective-permute-start.7
  57.0 2.7 %collective-permute-start.6 = (f32[160,128]{1,0:T(8,128)S(1)}, f32[160,128]{1,0:T(8,128)S(1)}, u32[]{:S(2)}, u32[]{:S(2)}) collective-permute-start(f32[160,128]{1,0:T(8,128)S(1)} %get-tuple-element.39), channel_id=1, source_target_pairs={{0,1},{1,2},{2,3},{3,0},{4,5},{5,6},{6,7},{7,4},{8,9},{9,10},{10,1... | collective-permute-start | bytes 245768 | tf_op jit(solution)/shard_map/ppermute | solution.py:125
  59.7 6.4 %collective-permute-done.7 = f32[160,128]{1,0:T(8,128)S(1)} collective-permute-done((f32[160,128]{1,0:T(8,128)S(1)}, f32[160,128]{1,0:T(8,128)S(1)}, u32[]{:S(2)}, u32[]{:S(2)}) %collective-permute-start.7) | collective-permute-done | bytes 81952 | tf_op jit(solution)/shard_map/ppermute | solution.py:125
  66.0 0.0 collective-permute-done.6
  66.0 0.0 collective-permute-done.2
  66.1 0.0 collective-permute-done.3
  66.1 0.0 copy-done.15
  66.1 0.0 copy-start.10
  66.1 0.0 copy-done.16
  66.1 0.6 copy-done.17
  66.7 0.0 copy-done.18
  66.7 0.1 copy-done.9
  66.8 0.1 copy-done.10
  66.9 11.9 %shard_map.113 = (f32[8,64,128]{2,1,0:T(8,128)}, f32[3,8,64,128]{3,2,1,0:T(8,128)}) custom-call(f32[3]{0:T(128)} %dif_ref.3, f32[3]{0:T(128)} %copy-done.19, f32[8,64,128]{2,1,0:T(8,128)} %refs_0_, f32[17,64,128]{2,1,0:T(8,128)} %bitcast.73, f32[17,64,128]{2,1,0:T(8,128)} %bitcast.77, f32[74,8,128]{2,1,0:T(8,128)} %bitcast.87, f32[74,8,128]{2,1,0:T(8,128)} %bitcast.91, ...), custom_call_target="tpu_custom_call" | custom-call | flops 40755200 | bytes 4538368 | tf_op jit(solution)/shard_map/pallas_call | solution.py:301
  78.8 1.0 fusion.35
  79.8 1.3 %multiply_reduce_fusion = f32[8,64,128]{2,1,0:T(8,128)S(1)} fusion(f32[3,8,64,128]{3,2,1,0:T(8,128)} %get-tuple-element.15.refs_15_, f32[3]{0:T(128)S(1)} %copy-done.20), kind=kLoop, calls=%fused_computation.27 | loop fusion | flops 327680 | bytes 1048588 | tf_op jit(solution)/shard_map/reduce_sum | solution.py:394
  81.1 0.0 copy-start.12
  81.2 0.9 copy-done.12
  82.1 0.0 copy-start.4
  82.1 0.1 collective-permute-start.8
  82.3 5.7 %collective-permute-start.9 = (f32[1024,128]{1,0:T(8,128)S(1)}, f32[1024,128]{1,0:T(8,128)S(1)}, u32[]{:S(2)}, u32[]{:S(2)}) collective-permute-start(f32[1024,128]{1,0:T(8,128)S(1)} %pad_maximum_fusion.3), channel_id=1, source_target_pairs={{0,252},{4,0},{8,4},{12,8},{16,12},{20,16},{24,20},{28,24},{32,28}... | collective-permute-start | bytes 1572872 | tf_op jit(solution)/shard_map/ppermute | solution.py:125
  88.0 11.5 %collective-permute-done.8 = f32[1024,128]{1,0:T(8,128)S(1)} collective-permute-done((f32[1024,128]{1,0:T(8,128)S(1)}, f32[1024,128]{1,0:T(8,128)S(1)}, u32[]{:S(2)}, u32[]{:S(2)}) %collective-permute-start.8) | collective-permute-done | bytes 524320 | tf_op jit(solution)/shard_map/ppermute | solution.py:125
  99.5 0.0 collective-permute-done.9
  99.7 0.7 copy-done.2
  100.3 0.1 copy-done.3
  100.6 3.1 %collective-permute-start.10 = (f32[576,128]{1,0:T(8,128)S(1)}, f32[576,128]{1,0:T(8,128)S(1)}, u32[]{:S(2)}, u32[]{:S(2)}) collective-permute-start(f32[576,128]{1,0:T(8,128)S(1)} %pad_maximum_fusion.6), channel_id=1, source_target_pairs={{0,1},{1,2},{2,3},{3,0},{4,5},{5,6},{6,7},{7,4},{8,9},{9,10},{10,1... | collective-permute-start | bytes 884744 | tf_op jit(solution)/shard_map/ppermute | solution.py:125
  103.7 0.1 collective-permute-start.11
  103.7 6.1 %collective-permute-done.10 = f32[576,128]{1,0:T(8,128)S(1)} collective-permute-done((f32[576,128]{1,0:T(8,128)S(1)}, f32[576,128]{1,0:T(8,128)S(1)}, u32[]{:S(2)}, u32[]{:S(2)}) %collective-permute-start.10) | collective-permute-done | bytes 294944 | tf_op jit(solution)/shard_map/ppermute | solution.py:125
  109.8 1.6 %collective-permute-done.11 = f32[576,128]{1,0:T(8,128)S(1)} collective-permute-done((f32[576,128]{1,0:T(8,128)S(1)}, f32[576,128]{1,0:T(8,128)S(1)}, u32[]{:S(2)}, u32[]{:S(2)}) %collective-permute-start.11) | collective-permute-done | bytes 294944 | tf_op jit(solution)/shard_map/ppermute | solution.py:125
  111.4 0.0 copy-done.13
  111.4 0.7 copy-done.14
  112.1 11.8 %shard_map.114 = (f32[8,64,128]{2,1,0:T(8,128)}, f32[3,8,64,128]{3,2,1,0:T(8,128)}) custom-call(f32[3]{0:T(128)} %dif_ref.3, f32[3]{0:T(128)} %copy-done.19, f32[8,64,128]{2,1,0:T(8,128)} %get-tuple-element.14.refs_0_, f32[16,64,128]{2,1,0:T(8,128)} %bitcast.81, f32[16,64,128]{2,1,0:T(8,128)} %bitcast.84, f32[72,8,128]{2,1,0:T(8,128)} %bitcast.95, ...), custom_call_target="tpu_custom_call" | custom-call | flops 40755200 | bytes 4538368 | tf_op jit(solution)/shard_map/pallas_call | solution.py:301
  (56 shorter events, 0.8 us)
Async XLA Ops:
  0.6 13.0 %copy-start.11 = (f32[8,64,128]{2,1,0:T(8,128)S(1)}, f32[8,64,128]{2,1,0:T(8,128)}, u32[]{:S(2)}) copy-start(f32[8,64,128]{2,1,0:T(8,128)} %refs_0_) | copy-start | bytes 786436
  2.2 11.5 %copy-start.6 = (f32[8,64,128]{2,1,0:T(8,128)S(1)}, f32[8,64,128]{2,1,0:T(8,128)}, u32[]{:S(2)}) copy-start(f32[8,64,128]{2,1,0:T(8,128)} %refs_5_.1) | copy-start | bytes 786436
  14.6 8.6 %copy-start.22 = (s32[3]{0:T(128)S(1)}, s32[3]{0:T(128)}, u32[]{:S(2)}) copy-start(s32[3]{0:T(128)} %param.14) | copy-start | bytes 40
  14.6 8.6 %copy-start.21 = (s32[1,1,512]{2,1,0:T(1,128)S(1)}, s32[1,1,512]{2,1,0:T(1,128)}, u32[]{:S(2)}) copy-start(s32[1,1,512]{2,1,0:T(1,128)} %param.18) | copy-start | bytes 6148
  14.6 36.4 %collective-permute-start = (f32[1088,128]{1,0:T(8,128)}, f32[1088,128]{1,0:T(8,128)S(1)}, u32[]{:S(2)}, u32[]{:S(2)}) collective-permute-start(f32[1088,128]{1,0:T(8,128)} %pad_maximum_fusion), channel_id=1, source_target_pairs={{0,4},{4,8},{8,12},{12,16},{16,20},{20,24},{24,28},{28,32},{32,36}... | collective-permute-start | bytes 1671176 | tf_op jit(solution)/shard_map/ppermute | solution.py:125
  15.5 35.5 %collective-permute-start.1 = (f32[1088,128]{1,0:T(8,128)}, f32[1088,128]{1,0:T(8,128)S(1)}, u32[]{:S(2)}, u32[]{:S(2)}) collective-permute-start(f32[1088,128]{1,0:T(8,128)} %pad_maximum_fusion.1), channel_id=1, source_target_pairs={{0,252},{4,0},{8,4},{12,8},{16,12},{20,16},{24,20},{28,24},{32,28}... | collective-permute-start | bytes 1671176 | tf_op jit(solution)/shard_map/ppermute | solution.py:125
  23.2 21.8 %copy-start.19 = (f32[3]{0:T(128)}, f32[3]{0:T(128)S(1)}, u32[]{:S(2)}) copy-start(f32[3]{0:T(128)S(1)} %convert_element_type.27.val_ref) | copy-start | bytes 40
  23.4 21.6 %copy-start.5 = (f32[3,8,64,128]{3,2,1,0:T(8,128)S(1)}, f32[3,8,64,128]{3,2,1,0:T(8,128)}, u32[]{:S(2)}) copy-start(f32[3,8,64,128]{3,2,1,0:T(8,128)} %refs_15_) | copy-start | bytes 2359300
  45.2 10.7 %copy-start.7 = (f32[8,64,128]{2,1,0:T(8,128)}, f32[8,64,128]{2,1,0:T(8,128)S(1)}, u32[]{:S(2)}) copy-start(f32[8,64,128]{2,1,0:T(8,128)S(1)} %add.100.refs_10_) | copy-start | bytes 786436
  45.2 10.6 %collective-permute-start.4 = (f32[384,128]{1,0:T(8,128)S(1)}, f32[384,128]{1,0:T(8,128)S(1)}, u32[]{:S(2)}, u32[]{:S(2)}) collective-permute-start(f32[384,128]{1,0:T(8,128)S(1)} %bitcast.136), channel_id=1, source_target_pairs={{0,4},{4,8},{8,12},{12,16},{16,20},{20,24},{24,28},{28,32},{32,36}... | collective-permute-start | bytes 589832 | tf_op jit(solution)/shard_map/ppermute | solution.py:125
  45.3 10.5 %collective-permute-start.5 = (f32[384,128]{1,0:T(8,128)S(1)}, f32[384,128]{1,0:T(8,128)S(1)}, u32[]{:S(2)}, u32[]{:S(2)}) collective-permute-start(f32[384,128]{1,0:T(8,128)S(1)} %bitcast.135), channel_id=1, source_target_pairs={{0,252},{4,0},{8,4},{12,8},{16,12},{20,16},{24,20},{28,24},{32,28}... | collective-permute-start | bytes 589832 | tf_op jit(solution)/shard_map/ppermute | solution.py:125
  51.0 0.8 copy-start
  51.0 1.0 copy-start.1
  52.1 13.9 %collective-permute-start.2 = (f32[592,128]{1,0:T(8,128)S(1)}, f32[592,128]{1,0:T(8,128)S(1)}, u32[]{:S(2)}, u32[]{:S(2)}) collective-permute-start(f32[592,128]{1,0:T(8,128)S(1)} %pad_maximum_fusion.4), channel_id=1, source_target_pairs={{0,1},{1,2},{2,3},{3,0},{4,5},{5,6},{6,7},{7,4},{8,9},{9,10},{10,1... | collective-permute-start | bytes 909320 | tf_op jit(solution)/shard_map/ppermute | solution.py:125
  55.7 10.3 %collective-permute-start.3 = (f32[592,128]{1,0:T(8,128)S(1)}, f32[592,128]{1,0:T(8,128)S(1)}, u32[]{:S(2)}, u32[]{:S(2)}) collective-permute-start(f32[592,128]{1,0:T(8,128)S(1)} %pad_maximum_fusion.5), channel_id=1, source_target_pairs={{0,3},{1,0},{2,1},{3,2},{4,7},{5,4},{6,5},{7,6},{8,11},{9,8},{10,9... | collective-permute-start | bytes 909320 | tf_op jit(solution)/shard_map/ppermute | solution.py:125
  55.8 10.2 %copy-start.15 = (f32[384,128]{1,0:T(8,128)}, f32[384,128]{1,0:T(8,128)S(1)}, u32[]{:S(2)}) copy-start(f32[384,128]{1,0:T(8,128)S(1)} %collective-permute-done.4) | copy-start | bytes 589828
  55.8 10.2 %copy-start.16 = (f32[384,128]{1,0:T(8,128)}, f32[384,128]{1,0:T(8,128)S(1)}, u32[]{:S(2)}) copy-start(f32[384,128]{1,0:T(8,128)S(1)} %collective-permute-done.5) | copy-start | bytes 589828
  55.9 10.1 %collective-permute-start.7 = (f32[160,128]{1,0:T(8,128)S(1)}, f32[160,128]{1,0:T(8,128)S(1)}, u32[]{:S(2)}, u32[]{:S(2)}) collective-permute-start(f32[160,128]{1,0:T(8,128)S(1)} %get-tuple-element.38), channel_id=1, source_target_pairs={{0,3},{1,0},{2,1},{3,2},{4,7},{5,4},{6,5},{7,6},{8,11},{9,8},{10,9... | collective-permute-start | bytes 245768 | tf_op jit(solution)/shard_map/ppermute | solution.py:125
  57.0 9.1 %collective-permute-start.6 = (f32[160,128]{1,0:T(8,128)S(1)}, f32[160,128]{1,0:T(8,128)S(1)}, u32[]{:S(2)}, u32[]{:S(2)}) collective-permute-start(f32[160,128]{1,0:T(8,128)S(1)} %get-tuple-element.39), channel_id=1, source_target_pairs={{0,1},{1,2},{2,3},{3,0},{4,5},{5,6},{6,7},{7,4},{8,9},{9,10},{10,1... | collective-permute-start | bytes 245768 | tf_op jit(solution)/shard_map/ppermute | solution.py:125
  66.0 0.6 copy-start.17
  66.0 0.6 copy-start.18
  66.0 0.7 copy-start.9
  66.1 0.8 copy-start.10
  66.9 12.9 %copy-start.20 = (f32[3]{0:T(128)S(1)}, f32[3]{0:T(128)}, u32[]{:S(2)}) copy-start(f32[3]{0:T(128)} %copy-done.19) | copy-start | bytes 40
  81.1 1.0 copy-start.12
  81.1 18.5 %copy-start.8 = (f32[8,64,128]{2,1,0:T(8,128)}, f32[8,64,128]{2,1,0:T(8,128)S(1)}, u32[]{:S(2)}) copy-start(f32[8,64,128]{2,1,0:T(8,128)S(1)} %add.101.refs_10_) | copy-start | bytes 786436
  82.1 17.4 %copy-start.4 = (f32[3,8,64,128]{3,2,1,0:T(8,128)S(1)}, f32[3,8,64,128]{3,2,1,0:T(8,128)}, u32[]{:S(2)}) copy-start(f32[3,8,64,128]{3,2,1,0:T(8,128)} %get-tuple-element.15.refs_15_) | copy-start | bytes 2359300
  82.1 17.4 %collective-permute-start.8 = (f32[1024,128]{1,0:T(8,128)S(1)}, f32[1024,128]{1,0:T(8,128)S(1)}, u32[]{:S(2)}, u32[]{:S(2)}) collective-permute-start(f32[1024,128]{1,0:T(8,128)S(1)} %pad_maximum_fusion.2), channel_id=1, source_target_pairs={{0,4},{4,8},{8,12},{12,16},{16,20},{20,24},{24,28},{28,32},{32,36}... | collective-permute-start | bytes 1572872 | tf_op jit(solution)/shard_map/ppermute | solution.py:125
  82.3 17.2 %collective-permute-start.9 = (f32[1024,128]{1,0:T(8,128)S(1)}, f32[1024,128]{1,0:T(8,128)S(1)}, u32[]{:S(2)}, u32[]{:S(2)}) collective-permute-start(f32[1024,128]{1,0:T(8,128)S(1)} %pad_maximum_fusion.3), channel_id=1, source_target_pairs={{0,252},{4,0},{8,4},{12,8},{16,12},{20,16},{24,20},{28,24},{32,28}... | collective-permute-start | bytes 1572872 | tf_op jit(solution)/shard_map/ppermute | solution.py:125
  99.5 0.8 copy-start.2
  99.5 1.0 copy-start.3
  100.6 9.2 %collective-permute-start.10 = (f32[576,128]{1,0:T(8,128)S(1)}, f32[576,128]{1,0:T(8,128)S(1)}, u32[]{:S(2)}, u32[]{:S(2)}) collective-permute-start(f32[576,128]{1,0:T(8,128)S(1)} %pad_maximum_fusion.6), channel_id=1, source_target_pairs={{0,1},{1,2},{2,3},{3,0},{4,5},{5,6},{6,7},{7,4},{8,9},{9,10},{10,1... | collective-permute-start | bytes 884744 | tf_op jit(solution)/shard_map/ppermute | solution.py:125
  103.7 7.7 %collective-permute-start.11 = (f32[576,128]{1,0:T(8,128)S(1)}, f32[576,128]{1,0:T(8,128)S(1)}, u32[]{:S(2)}, u32[]{:S(2)}) collective-permute-start(f32[576,128]{1,0:T(8,128)S(1)} %pad_maximum_fusion.7), channel_id=1, source_target_pairs={{0,3},{1,0},{2,1},{3,2},{4,7},{5,4},{6,5},{7,6},{8,11},{9,8},{10,9... | collective-permute-start | bytes 884744 | tf_op jit(solution)/shard_map/ppermute | solution.py:125
  109.8 1.6 %copy-start.13 = (f32[576,128]{1,0:T(8,128)}, f32[576,128]{1,0:T(8,128)S(1)}, u32[]{:S(2)}) copy-start(f32[576,128]{1,0:T(8,128)S(1)} %collective-permute-done.10) | copy-start | bytes 884740
  111.4 0.7 copy-start.14

commit v10 on v9

--- a/solution.py
+++ b/solution.py
@@ -384,7 +384,12 @@
         tiles_all,
     )
     values = values * brick_mask[0, 0].astype(jnp.float32)
-    electrode = jnp.zeros((depth * height * width,), jnp.float32).at[index].add(values)
+    node_row = index // width
+    picks = jnp.where(
+        node_row[None, :] == jnp.arange(depth * height, dtype=jnp.int32)[:, None], values[None, :], 0.0
+    )
+    lanes_of = (local_x[:, None] == jnp.arange(width, dtype=jnp.int32)[None, :]).astype(jnp.float32)
+    electrode = jnp.dot(picks, lanes_of, precision=lax.Precision.HIGHEST, preferred_element_type=jnp.float32)
     electrode = electrode.reshape(depth, height, width)
     charge_num = valence.astype(jnp.float32)
     field = potential

time: 124 us -> 122 us (0.984)
  other arithmetic: 26.7 us -> 23.4 us
    scatter-add x1 -> x0, other arithmetic: 3.33 us -> none  [per_device(): jnp.zeros((depth * height * width,), jnp.float32).at[index].add(values)]
  transfers between devices with their start and end apart: 12 -> 12, of which waited for: 4 -> 4; matrix products, arithmetic and copies ran while one was open for 19% -> 17% of each run, Pallas kernels for 0% -> 0%
where the time goes in v10:
time: 122 us
  starting transfers between devices  29.2 us (24%)
  waiting for transfers between devices  25.5 us (21%)
  Pallas kernels  23.7 us (19%)
  other arithmetic  23.4 us (19%)
  blocking collectives  10.5 us (9%)
  local copies, waits for them, and re-layouts  6.76 us (6%)
  between operations  1.98 us (2%)
    ppermute x12, starting transfers between devices, ring(): lax.ppermute(x, axis, [(i, (i + shift) % count) for i in range(count)])  29.2 us
    ppermute x12, waiting for transfers between devices, ring(): lax.ppermute(x, axis, [(i, (i + shift) % count) for i in range(count)])  25.5 us
    pallas_call x2, Pallas kernels, time_step(): pl.pallas_call(functools.partial(step_kernel, tuple(plan)), out_shape=(ja...  23.7 us
    reduce_sum x1, other arithmetic, one_block(): return jnp.sum(jnp.where(adjacent, term, 0.0), axis=1)  18.2 us
    all_gather x1, blocking collectives, per_device(): gathered = lax.all_gather(charges, 'narrow', axis=1, tiled=True)  10.5 us
    unnamed x46, local copies, waits for them, and re-layouts  4.51 us
  transfers between devices with their start and end apart: 12, of which 4 were waited for; matrix products, arithmetic and copies ran while one was open for 17% of the time, Pallas kernels for 0%

profile of v10, /device:TPU:1, one launch (start us, length us, event | category | flops | bytes accessed | tf_op | source)
XLA Modules:
  0.0 121.8 jit_solution(4957925763724889251)
XLA Ops:
  0.6 0.0 copy-start.11
  0.6 0.7 convert_element_type.29
  1.4 0.8 pad_maximum_fusion.24
  2.2 0.0 copy-start.6
  2.2 10.5 %all_gather.3 = f32[5,8192]{1,0:T(8,128)S(1)} all-gather(f32[5,2048]{1,0:T(8,128)S(1)} %pad_maximum_fusion.24), channel_id=1, replica_groups=mesh['wide'=64,'narrow'=4] {'narrow'}, dimensions={1}, use_global_device_ids=true | all-gather | bytes 204800 | tf_op jit(solution)/shard_map/all_gather | solution.py:364
  12.7 1.0 fusion.41
  13.7 0.0 copy-done.11
  13.7 0.0 copy-done.6
  13.8 0.8 pad_maximum_fusion
  14.6 0.0 collective-permute-start
  14.6 0.8 pad_maximum_fusion.1
  15.5 7.0 %collective-permute-start.1 = (f32[1088,128]{1,0:T(8,128)}, f32[1088,128]{1,0:T(8,128)S(1)}, u32[]{:S(2)}, u32[]{:S(2)}) collective-permute-start(f32[1088,128]{1,0:T(8,128)} %pad_maximum_fusion.1), channel_id=1, source_target_pairs={{0,252},{4,0},{8,4},{12,8},{16,12},{20,16},{24,20},{28,24},{32,28}... | collective-permute-start | bytes 1671176 | tf_op jit(solution)/shard_map/ppermute | solution.py:125
  23.2 0.0 copy-done.22
  23.2 0.0 copy-start.19
  23.2 0.0 copy-done.21
  23.3 0.1 multiply_reduce_fusion.1
  23.4 0.3 copy-done.19
  23.8 0.1 fusion.47
  23.9 18.2 %select_reduce_fusion.1 = (f32[256]{0:T(256)S(1)}, f32[256]{0:T(256)S(1)}) fusion(f32[8192]{0:T(1024)S(1)} %bitcast.137, f32[256]{0:T(256)S(1)} %get-tuple-element.77, f32[8192]{0:T(1024)S(1)} %bitcast.138, f32[256]{0:T(256)S(1)} %get-tuple-element.66, f32[8192]{0:T(1024)S(1)} %bitcast.139, f32[256]{0:T(256)S(1)} %get-tuple-element.75, ...), kind=kLoop, calls=%fused_computation.20 | loop fusion | flops 104857088 | bytes 174080 | tf_op jit(solution)/shard_map/reduce_sum | solution.py:116
  42.1 0.8 fusion.18
  42.9 0.0 copy-start.7
  43.0 0.1 collective-permute-start.4
  43.1 5.7 %collective-permute-start.5 = (f32[384,128]{1,0:T(8,128)S(1)}, f32[384,128]{1,0:T(8,128)S(1)}, u32[]{:S(2)}, u32[]{:S(2)}) collective-permute-start(f32[384,128]{1,0:T(8,128)S(1)} %bitcast.132), channel_id=1, source_target_pairs={{0,252},{4,0},{8,4},{12,8},{16,12},{20,16},{24,20},{28,24},{32,28}... | collective-permute-start | bytes 589832 | tf_op jit(solution)/shard_map/ppermute | solution.py:125
  48.7 0.0 collective-permute-done
  48.8 0.0 collective-permute-done.1
  48.8 0.7 copy-done
  49.6 0.1 copy-done.1
  49.8 3.6 %collective-permute-start.2 = (f32[592,128]{1,0:T(8,128)S(1)}, f32[592,128]{1,0:T(8,128)S(1)}, u32[]{:S(2)}, u32[]{:S(2)}) collective-permute-start(f32[592,128]{1,0:T(8,128)S(1)} %pad_maximum_fusion.4), channel_id=1, source_target_pairs={{0,1},{1,2},{2,3},{3,0},{4,5},{5,6},{6,7},{7,4},{8,9},{9,10},{10,1... | collective-permute-start | bytes 909320 | tf_op jit(solution)/shard_map/ppermute | solution.py:125
  53.5 0.1 collective-permute-start.3
  53.5 0.0 collective-permute-done.4
  53.6 0.0 copy-start.15
  53.6 0.0 collective-permute-done.5
  53.6 1.1 collective-permute-start.7
  54.7 2.7 %collective-permute-start.6 = (f32[160,128]{1,0:T(8,128)S(1)}, f32[160,128]{1,0:T(8,128)S(1)}, u32[]{:S(2)}, u32[]{:S(2)}) collective-permute-start(f32[160,128]{1,0:T(8,128)S(1)} %get-tuple-element.41), channel_id=1, source_target_pairs={{0,1},{1,2},{2,3},{3,0},{4,5},{5,6},{6,7},{7,4},{8,9},{9,10},{10,1... | collective-permute-start | bytes 245768 | tf_op jit(solution)/shard_map/ppermute | solution.py:125
  57.4 6.4 %collective-permute-done.7 = f32[160,128]{1,0:T(8,128)S(1)} collective-permute-done((f32[160,128]{1,0:T(8,128)S(1)}, f32[160,128]{1,0:T(8,128)S(1)}, u32[]{:S(2)}, u32[]{:S(2)}) %collective-permute-start.7) | collective-permute-done | bytes 81952 | tf_op jit(solution)/shard_map/ppermute | solution.py:125
  63.8 0.0 collective-permute-done.6
  63.8 0.0 collective-permute-done.2
  63.8 0.0 collective-permute-done.3
  63.8 0.0 copy-done.15
  63.8 0.0 copy-start.10
  63.8 0.0 copy-done.16
  63.8 0.6 copy-done.17
  64.4 0.0 copy-done.18
  64.4 0.1 copy-done.9
  64.5 0.1 copy-done.10
  64.7 11.9 %shard_map.113 = (f32[8,64,128]{2,1,0:T(8,128)}, f32[3,8,64,128]{3,2,1,0:T(8,128)}) custom-call(f32[3]{0:T(128)} %dif_ref.3, f32[3]{0:T(128)} %copy-done.19, f32[8,64,128]{2,1,0:T(8,128)} %refs_0_, f32[17,64,128]{2,1,0:T(8,128)} %bitcast.70, f32[17,64,128]{2,1,0:T(8,128)} %bitcast.74, f32[74,8,128]{2,1,0:T(8,128)} %bitcast.84, f32[74,8,128]{2,1,0:T(8,128)} %bitcast.88, ...), custom_call_target="tpu_custom_call" | custom-call | flops 40755200 | bytes 4538368 | tf_op jit(solution)/shard_map/pallas_call | solution.py:301
  76.5 1.0 fusion.40
  77.5 0.0 copy-done.20
  77.5 1.3 %multiply_reduce_fusion = f32[8,64,128]{2,1,0:T(8,128)S(1)} fusion(f32[3,8,64,128]{3,2,1,0:T(8,128)} %get-tuple-element.15.refs_15_, f32[3]{0:T(128)S(1)} %copy-done.20), kind=kLoop, calls=%fused_computation.29 | loop fusion | flops 327680 | bytes 1048588 | tf_op jit(solution)/shard_map/reduce_sum | solution.py:399
  78.9 0.9 copy-done.12
  79.9 0.1 collective-permute-start.8
  80.0 5.7 %collective-permute-start.9 = (f32[1024,128]{1,0:T(8,128)S(1)}, f32[1024,128]{1,0:T(8,128)S(1)}, u32[]{:S(2)}, u32[]{:S(2)}) collective-permute-start(f32[1024,128]{1,0:T(8,128)S(1)} %pad_maximum_fusion.3), channel_id=1, source_target_pairs={{0,252},{4,0},{8,4},{12,8},{16,12},{20,16},{24,20},{28,24},{32,28}... | collective-permute-start | bytes 1572872 | tf_op jit(solution)/shard_map/ppermute | solution.py:125
  85.8 11.5 %collective-permute-done.8 = f32[1024,128]{1,0:T(8,128)S(1)} collective-permute-done((f32[1024,128]{1,0:T(8,128)S(1)}, f32[1024,128]{1,0:T(8,128)S(1)}, u32[]{:S(2)}, u32[]{:S(2)}) %collective-permute-start.8) | collective-permute-done | bytes 524320 | tf_op jit(solution)/shard_map/ppermute | solution.py:125
  97.2 0.0 collective-permute-done.9
  97.3 0.0 copy-done.4
  97.4 0.6 copy-done.2
  98.1 0.2 copy-done.3
  98.3 3.1 %collective-permute-start.10 = (f32[576,128]{1,0:T(8,128)S(1)}, f32[576,128]{1,0:T(8,128)S(1)}, u32[]{:S(2)}, u32[]{:S(2)}) collective-permute-start(f32[576,128]{1,0:T(8,128)S(1)} %pad_maximum_fusion.6), channel_id=1, source_target_pairs={{0,1},{1,2},{2,3},{3,0},{4,5},{5,6},{6,7},{7,4},{8,9},{9,10},{10,1... | collective-permute-start | bytes 884744 | tf_op jit(solution)/shard_map/ppermute | solution.py:125
  101.4 0.1 collective-permute-start.11
  101.5 6.1 %collective-permute-done.10 = f32[576,128]{1,0:T(8,128)S(1)} collective-permute-done((f32[576,128]{1,0:T(8,128)S(1)}, f32[576,128]{1,0:T(8,128)S(1)}, u32[]{:S(2)}, u32[]{:S(2)}) %collective-permute-start.10) | collective-permute-done | bytes 294944 | tf_op jit(solution)/shard_map/ppermute | solution.py:125
  107.5 1.6 %collective-permute-done.11 = f32[576,128]{1,0:T(8,128)S(1)} collective-permute-done((f32[576,128]{1,0:T(8,128)S(1)}, f32[576,128]{1,0:T(8,128)S(1)}, u32[]{:S(2)}, u32[]{:S(2)}) %collective-permute-start.11) | collective-permute-done | bytes 294944 | tf_op jit(solution)/shard_map/ppermute | solution.py:125
  109.1 0.0 copy-done.13
  109.1 0.7 copy-done.14
  109.8 11.8 %shard_map.114 = (f32[8,64,128]{2,1,0:T(8,128)}, f32[3,8,64,128]{3,2,1,0:T(8,128)}) custom-call(f32[3]{0:T(128)} %dif_ref.3, f32[3]{0:T(128)} %copy-done.19, f32[8,64,128]{2,1,0:T(8,128)} %get-tuple-element.14.refs_0_, f32[16,64,128]{2,1,0:T(8,128)} %bitcast.78, f32[16,64,128]{2,1,0:T(8,128)} %bitcast.81, f32[72,8,128]{2,1,0:T(8,128)} %bitcast.92, ...), custom_call_target="tpu_custom_call" | custom-call | flops 40755200 | bytes 4538368 | tf_op jit(solution)/shard_map/pallas_call | solution.py:301
  (55 shorter events, 0.8 us)
Async XLA Ops:
  0.6 13.0 %copy-start.11 = (f32[8,64,128]{2,1,0:T(8,128)S(1)}, f32[8,64,128]{2,1,0:T(8,128)}, u32[]{:S(2)}) copy-start(f32[8,64,128]{2,1,0:T(8,128)} %refs_0_) | copy-start | bytes 786436
  2.2 11.5 %copy-start.6 = (f32[8,64,128]{2,1,0:T(8,128)S(1)}, f32[8,64,128]{2,1,0:T(8,128)}, u32[]{:S(2)}) copy-start(f32[8,64,128]{2,1,0:T(8,128)} %refs_5_.1) | copy-start | bytes 786436
  14.6 8.6 %copy-start.22 = (s32[3]{0:T(128)S(1)}, s32[3]{0:T(128)}, u32[]{:S(2)}) copy-start(s32[3]{0:T(128)} %param.14) | copy-start | bytes 40
  14.6 8.6 %copy-start.21 = (s32[1,1,512]{2,1,0:T(1,128)S(1)}, s32[1,1,512]{2,1,0:T(1,128)}, u32[]{:S(2)}) copy-start(s32[1,1,512]{2,1,0:T(1,128)} %param.18) | copy-start | bytes 6148
  14.6 8.7 %copy-start.5 = (f32[3,8,64,128]{3,2,1,0:T(8,128)S(1)}, f32[3,8,64,128]{3,2,1,0:T(8,128)}, u32[]{:S(2)}) copy-start(f32[3,8,64,128]{3,2,1,0:T(8,128)} %refs_15_) | copy-start | bytes 2359300
  14.6 34.1 %collective-permute-start = (f32[1088,128]{1,0:T(8,128)}, f32[1088,128]{1,0:T(8,128)S(1)}, u32[]{:S(2)}, u32[]{:S(2)}) collective-permute-start(f32[1088,128]{1,0:T(8,128)} %pad_maximum_fusion), channel_id=1, source_target_pairs={{0,4},{4,8},{8,12},{12,16},{16,20},{20,24},{24,28},{28,32},{32,36}... | collective-permute-start | bytes 1671176 | tf_op jit(solution)/shard_map/ppermute | solution.py:125
  15.5 33.3 %collective-permute-start.1 = (f32[1088,128]{1,0:T(8,128)}, f32[1088,128]{1,0:T(8,128)S(1)}, u32[]{:S(2)}, u32[]{:S(2)}) collective-permute-start(f32[1088,128]{1,0:T(8,128)} %pad_maximum_fusion.1), channel_id=1, source_target_pairs={{0,252},{4,0},{8,4},{12,8},{16,12},{20,16},{24,20},{28,24},{32,28}... | collective-permute-start | bytes 1671176 | tf_op jit(solution)/shard_map/ppermute | solution.py:125
  23.2 0.6 copy-start.19
  42.9 10.7 %copy-start.7 = (f32[8,64,128]{2,1,0:T(8,128)}, f32[8,64,128]{2,1,0:T(8,128)S(1)}, u32[]{:S(2)}) copy-start(f32[8,64,128]{2,1,0:T(8,128)S(1)} %add.91.refs_10_) | copy-start | bytes 786436
  43.0 10.6 %collective-permute-start.4 = (f32[384,128]{1,0:T(8,128)S(1)}, f32[384,128]{1,0:T(8,128)S(1)}, u32[]{:S(2)}, u32[]{:S(2)}) collective-permute-start(f32[384,128]{1,0:T(8,128)S(1)} %bitcast.133), channel_id=1, source_target_pairs={{0,4},{4,8},{8,12},{12,16},{16,20},{20,24},{24,28},{28,32},{32,36}... | collective-permute-start | bytes 589832 | tf_op jit(solution)/shard_map/ppermute | solution.py:125
  43.1 10.5 %collective-permute-start.5 = (f32[384,128]{1,0:T(8,128)S(1)}, f32[384,128]{1,0:T(8,128)S(1)}, u32[]{:S(2)}, u32[]{:S(2)}) collective-permute-start(f32[384,128]{1,0:T(8,128)S(1)} %bitcast.132), channel_id=1, source_target_pairs={{0,252},{4,0},{8,4},{12,8},{16,12},{20,16},{24,20},{28,24},{32,28}... | collective-permute-start | bytes 589832 | tf_op jit(solution)/shard_map/ppermute | solution.py:125
  48.7 0.8 copy-start
  48.8 1.0 copy-start.1
  49.8 13.9 %collective-permute-start.2 = (f32[592,128]{1,0:T(8,128)S(1)}, f32[592,128]{1,0:T(8,128)S(1)}, u32[]{:S(2)}, u32[]{:S(2)}) collective-permute-start(f32[592,128]{1,0:T(8,128)S(1)} %pad_maximum_fusion.4), channel_id=1, source_target_pairs={{0,1},{1,2},{2,3},{3,0},{4,5},{5,6},{6,7},{7,4},{8,9},{9,10},{10,1... | collective-permute-start | bytes 909320 | tf_op jit(solution)/shard_map/ppermute | solution.py:125
  53.5 10.3 %collective-permute-start.3 = (f32[592,128]{1,0:T(8,128)S(1)}, f32[592,128]{1,0:T(8,128)S(1)}, u32[]{:S(2)}, u32[]{:S(2)}) collective-permute-start(f32[592,128]{1,0:T(8,128)S(1)} %pad_maximum_fusion.5), channel_id=1, source_target_pairs={{0,3},{1,0},{2,1},{3,2},{4,7},{5,4},{6,5},{7,6},{8,11},{9,8},{10,9... | collective-permute-start | bytes 909320 | tf_op jit(solution)/shard_map/ppermute | solution.py:125
  53.6 10.3 %copy-start.15 = (f32[384,128]{1,0:T(8,128)}, f32[384,128]{1,0:T(8,128)S(1)}, u32[]{:S(2)}) copy-start(f32[384,128]{1,0:T(8,128)S(1)} %collective-permute-done.4) | copy-start | bytes 589828
  53.6 10.3 %copy-start.16 = (f32[384,128]{1,0:T(8,128)}, f32[384,128]{1,0:T(8,128)S(1)}, u32[]{:S(2)}) copy-start(f32[384,128]{1,0:T(8,128)S(1)} %collective-permute-done.5) | copy-start | bytes 589828
  53.6 10.2 %collective-permute-start.7 = (f32[160,128]{1,0:T(8,128)S(1)}, f32[160,128]{1,0:T(8,128)S(1)}, u32[]{:S(2)}, u32[]{:S(2)}) collective-permute-start(f32[160,128]{1,0:T(8,128)S(1)} %get-tuple-element.40), channel_id=1, source_target_pairs={{0,3},{1,0},{2,1},{3,2},{4,7},{5,4},{6,5},{7,6},{8,11},{9,8},{10,9... | collective-permute-start | bytes 245768 | tf_op jit(solution)/shard_map/ppermute | solution.py:125
  54.7 9.1 %collective-permute-start.6 = (f32[160,128]{1,0:T(8,128)S(1)}, f32[160,128]{1,0:T(8,128)S(1)}, u32[]{:S(2)}, u32[]{:S(2)}) collective-permute-start(f32[160,128]{1,0:T(8,128)S(1)} %get-tuple-element.41), channel_id=1, source_target_pairs={{0,1},{1,2},{2,3},{3,0},{4,5},{5,6},{6,7},{7,4},{8,9},{9,10},{10,1... | collective-permute-start | bytes 245768 | tf_op jit(solution)/shard_map/ppermute | solution.py:125
  63.8 0.6 copy-start.17
  63.8 0.7 copy-start.18
  63.8 0.8 copy-start.9
  63.8 0.8 copy-start.10
  64.7 12.9 %copy-start.20 = (f32[3]{0:T(128)S(1)}, f32[3]{0:T(128)}, u32[]{:S(2)}) copy-start(f32[3]{0:T(128)} %copy-done.19) | copy-start | bytes 40
  78.8 1.0 copy-start.12
  78.9 18.5 %copy-start.8 = (f32[8,64,128]{2,1,0:T(8,128)}, f32[8,64,128]{2,1,0:T(8,128)S(1)}, u32[]{:S(2)}) copy-start(f32[8,64,128]{2,1,0:T(8,128)S(1)} %add.92.refs_10_) | copy-start | bytes 786436
  79.9 17.4 %copy-start.4 = (f32[3,8,64,128]{3,2,1,0:T(8,128)S(1)}, f32[3,8,64,128]{3,2,1,0:T(8,128)}, u32[]{:S(2)}) copy-start(f32[3,8,64,128]{3,2,1,0:T(8,128)} %get-tuple-element.15.refs_15_) | copy-start | bytes 2359300
  79.9 17.4 %collective-permute-start.8 = (f32[1024,128]{1,0:T(8,128)S(1)}, f32[1024,128]{1,0:T(8,128)S(1)}, u32[]{:S(2)}, u32[]{:S(2)}) collective-permute-start(f32[1024,128]{1,0:T(8,128)S(1)} %pad_maximum_fusion.2), channel_id=1, source_target_pairs={{0,4},{4,8},{8,12},{12,16},{16,20},{20,24},{24,28},{28,32},{32,36}... | collective-permute-start | bytes 1572872 | tf_op jit(solution)/shard_map/ppermute | solution.py:125
  80.0 17.2 %collective-permute-start.9 = (f32[1024,128]{1,0:T(8,128)S(1)}, f32[1024,128]{1,0:T(8,128)S(1)}, u32[]{:S(2)}, u32[]{:S(2)}) collective-permute-start(f32[1024,128]{1,0:T(8,128)S(1)} %pad_maximum_fusion.3), channel_id=1, source_target_pairs={{0,252},{4,0},{8,4},{12,8},{16,12},{20,16},{24,20},{28,24},{32,28}... | collective-permute-start | bytes 1572872 | tf_op jit(solution)/shard_map/ppermute | solution.py:125
  97.2 0.8 copy-start.2
  97.3 1.0 copy-start.3
  98.3 9.2 %collective-permute-start.10 = (f32[576,128]{1,0:T(8,128)S(1)}, f32[576,128]{1,0:T(8,128)S(1)}, u32[]{:S(2)}, u32[]{:S(2)}) collective-permute-start(f32[576,128]{1,0:T(8,128)S(1)} %pad_maximum_fusion.6), channel_id=1, source_target_pairs={{0,1},{1,2},{2,3},{3,0},{4,5},{5,6},{6,7},{7,4},{8,9},{9,10},{10,1... | collective-permute-start | bytes 884744 | tf_op jit(solution)/shard_map/ppermute | solution.py:125
  101.4 7.7 %collective-permute-start.11 = (f32[576,128]{1,0:T(8,128)S(1)}, f32[576,128]{1,0:T(8,128)S(1)}, u32[]{:S(2)}, u32[]{:S(2)}) collective-permute-start(f32[576,128]{1,0:T(8,128)S(1)} %pad_maximum_fusion.7), channel_id=1, source_target_pairs={{0,3},{1,0},{2,1},{3,2},{4,7},{5,4},{6,5},{7,6},{8,11},{9,8},{10,9... | collective-permute-start | bytes 884744 | tf_op jit(solution)/shard_map/ppermute | solution.py:125
  107.5 1.6 %copy-start.13 = (f32[576,128]{1,0:T(8,128)}, f32[576,128]{1,0:T(8,128)S(1)}, u32[]{:S(2)}) copy-start(f32[576,128]{1,0:T(8,128)S(1)} %collective-permute-done.10) | copy-start | bytes 884740
  109.1 0.7 copy-start.14

commit v11 on v10

--- a/solution.py
+++ b/solution.py
@@ -162,9 +162,13 @@
     return [(a,) + bufs + (zo, yo, wz) for (a, wz, _), zo, yo in zip(items, z_offs, y_offs)]
 
 
-def step_kernel(plan, dif_ref, val_ref, *refs):
+def step_kernel(plan, with_source, dif_ref, val_ref, *refs):
     hbm = refs[:20]
-    fo_ref, co_ref, f_ref, p_ref, s_ref, c_ref, fa, fb, w_ref, sems = refs[20:]
+    rest = list(refs[20:])
+    e_ref = rest.pop(0) if with_source else None
+    fo_ref, co_ref = rest[0], rest[1]
+    so_ref = rest.pop(2) if with_source else None
+    f_ref, p_ref, s_ref, c_ref, fa, fb, w_ref, sems = rest[2:]
     targets = (f_ref, p_ref, s_ref, c_ref)
     copies = [[] for _ in targets]
     count = 0
@@ -276,12 +280,17 @@
             total = total - xsh(across, -1)
             new = c - dif_ref[s] * total
             co_ref[s, z] = new[hy:hy + out_rows]
+            if with_source:
+                charged = drift * new[hy:hy + out_rows]
+                mix = charged if s == 0 else mix + charged
+        if with_source:
+            so_ref[z] = mix + e_ref[z]
         return carry
 
     lax.fori_loop(0, inner, move, 0, unroll=2)
 
 
-def time_step(diffusivity, charge_num, field_p, perm_p, source_p, species_p):
+def time_step(diffusivity, charge_num, field_p, perm_p, source_p, species_p, electrode=None):
     species, inner, out_rows, lanes = species_p[0].shape
     planes = inner + 2 * field_p[7]
     rows = out_rows + 2 * (SWEEPS + 2)
@@ -298,14 +307,20 @@
     hbm = pl.BlockSpec(memory_space=pl.ANY)
     points = planes * rows * lanes
     moves = sum(1 + 4 * p[0] for p in plan)
+    with_source = electrode is not None
+    out_shape = [
+        jax.ShapeDtypeStruct((inner, out_rows, lanes), jnp.float32),
+        jax.ShapeDtypeStruct((species, inner, out_rows, lanes), jnp.float32),
+    ]
+    extra = []
+    if with_source:
+        out_shape.append(jax.ShapeDtypeStruct((inner, out_rows, lanes), jnp.float32))
+        extra = [electrode]
     return pl.pallas_call(
-        functools.partial(step_kernel, tuple(plan)),
-        out_shape=(
-            jax.ShapeDtypeStruct((inner, out_rows, lanes), jnp.float32),
-            jax.ShapeDtypeStruct((species, inner, out_rows, lanes), jnp.float32),
-        ),
-        in_specs=[smem, smem] + [hbm] * len(operands),
-        out_specs=(vmem, vmem),
+        functools.partial(step_kernel, tuple(plan), with_source),
+        out_shape=tuple(out_shape),
+        in_specs=[smem, smem] + [hbm] * len(operands) + [vmem] * len(extra),
+        out_specs=tuple([vmem] * len(out_shape)),
         scratch_shapes=[pltpu.VMEM(shape, jnp.float32) for shape in boxes]
         + [
             pltpu.VMEM((planes, rows + 16, lanes), jnp.float32),
@@ -318,7 +333,7 @@
             transcendentals=0,
             bytes_accessed=4 * (3 * points + inner * out_rows * lanes * (2 * species + 1)),
         ),
-    )(diffusivity, charge_num, *operands)
+    )(diffusivity, charge_num, *operands, *extra)
 
 
 def box(a, have, want):
@@ -396,15 +411,20 @@
     species = concentration
     perm_p = first[1]
     for step in range(STEPS):
-        source = jnp.sum(charge_num[:, None, None, None] * species, axis=0) + electrode
         if step == 0:
+            source = jnp.sum(charge_num[:, None, None, None] * species, axis=0) + electrode
             field_p, species_p = first[0], first[2]
             (source_p,) = deep_halo([(source, deep - 1, wide_y)], "wide", "narrow")
         else:
             field_p, source_p, species_p = deep_halo(
                 [(field, deep, wide_y), (source, deep - 1, wide_y), (species, 1, wide_y)], "wide", "narrow"
             )
-        field, species = time_step(diffusivity, charge_num, field_p, perm_p, source_p, species_p)
+        if step + 1 < STEPS:
+            field, species, source = time_step(
+                diffusivity, charge_num, field_p, perm_p, source_p, species_p, electrode
+            )
+        else:
+            field, species = time_step(diffusivity, charge_num, field_p, perm_p, source_p, species_p)
     return (species, field)
 
 

time: 122 us -> 122 us (level)
  other arithmetic: 23.4 us -> 22.1 us
    reduce_sum x2 -> x1, other arithmetic: 1.42 us -> 0.13 us  [per_device(): jnp.sum(charge_num[:, None, None, None] * species, axis=0) + electrode]
where the time goes in v11:
time: 122 us; the launch traced here: 121 us
  starting transfers between devices  29.2 us (24%)
  waiting for transfers between devices  25.5 us (21%)
  Pallas kernels  24.1 us (20%)
  other arithmetic  22.1 us (18%)
  blocking collectives  10.5 us (9%)
  local copies, waits for them, and re-layouts  7.45 us (6%)
  between operations  1.99 us (2%)
    ppermute x12, starting transfers between devices, ring(): lax.ppermute(x, axis, [(i, (i + shift) % count) for i in range(count)])  29.2 us
    ppermute x12, waiting for transfers between devices, ring(): lax.ppermute(x, axis, [(i, (i + shift) % count) for i in range(count)])  25.5 us
    pallas_call x2, Pallas kernels, time_step(): pl.pallas_call(functools.partial(step_kernel, tuple(plan), with_source),...  24.1 us
    reduce_sum x1, other arithmetic, one_block(): return jnp.sum(jnp.where(adjacent, term, 0.0), axis=1)  18.2 us
    all_gather x1, blocking collectives, per_device(): gathered = lax.all_gather(charges, 'narrow', axis=1, tiled=True)  10.5 us
    unnamed x46, local copies, waits for them, and re-layouts  4.13 us
    slice x7, local copies, waits for them, and re-layouts, deep_halo(): bots.append(lax.slice_in_dim(a, 0, wz, axis=dim))  3.15 us
  transfers between devices with their start and end apart: 12, of which 4 were waited for; matrix products, arithmetic and copies ran while one was open for 17% of the time, Pallas kernels for 0%

profile of v11, /device:TPU:1, one launch (start us, length us, event | category | flops | bytes accessed | tf_op | source)
XLA Modules:
  0.0 121.5 jit_solution(17165098295197846332)
XLA Ops:
  0.6 0.0 copy-start.10
  0.6 0.7 convert_element_type.29
  1.4 0.8 pad_maximum_fusion.24
  2.2 0.0 copy-start.5
  2.2 10.5 %all_gather.3 = f32[5,8192]{1,0:T(8,128)S(1)} all-gather(f32[5,2048]{1,0:T(8,128)S(1)} %pad_maximum_fusion.24), channel_id=1, replica_groups=mesh['wide'=64,'narrow'=4] {'narrow'}, dimensions={1}, use_global_device_ids=true | all-gather | bytes 204800 | tf_op jit(solution)/shard_map/all_gather | solution.py:379
  12.7 1.0 fusion.41
  13.7 0.0 copy-done.10
  13.7 0.0 copy-done.5
  13.8 0.8 pad_maximum_fusion
  14.6 0.0 collective-permute-start
  14.6 0.8 pad_maximum_fusion.1
  15.5 7.0 %collective-permute-start.1 = (f32[1088,128]{1,0:T(8,128)}, f32[1088,128]{1,0:T(8,128)S(1)}, u32[]{:S(2)}, u32[]{:S(2)}) collective-permute-start(f32[1088,128]{1,0:T(8,128)} %pad_maximum_fusion.1), channel_id=1, source_target_pairs={{0,252},{4,0},{8,4},{12,8},{16,12},{20,16},{24,20},{28,24},{32,28}... | collective-permute-start | bytes 1671176 | tf_op jit(solution)/shard_map/ppermute | solution.py:125
  23.2 0.0 copy-done.22
  23.2 0.0 copy-start.20
  23.2 0.0 copy-done.21
  23.3 0.0 copy-done.4
  23.3 0.1 multiply_reduce_fusion
  23.4 0.1 fusion.47
  23.6 18.2 %select_reduce_fusion.1 = (f32[256]{0:T(256)S(1)}, f32[256]{0:T(256)S(1)}) fusion(f32[8192]{0:T(1024)S(1)} %bitcast.137, f32[256]{0:T(256)S(1)} %get-tuple-element.79, f32[8192]{0:T(1024)S(1)} %bitcast.138, f32[256]{0:T(256)S(1)} %get-tuple-element.68, f32[8192]{0:T(1024)S(1)} %bitcast.139, f32[256]{0:T(256)S(1)} %get-tuple-element.77, ...), kind=kLoop, calls=%fused_computation.20 | loop fusion | flops 104857088 | bytes 174080 | tf_op jit(solution)/shard_map/reduce_sum | solution.py:116
  41.8 0.0 copy-done.20
  41.8 0.8 fusion.18
  42.6 0.0 copy-start.15
  42.6 0.0 copy-start.6
  42.7 0.6 copy-done.15
  43.3 0.0 collective-permute-start.4
  43.3 5.7 %collective-permute-start.5 = (f32[384,128]{1,0:T(8,128)S(1)}, f32[384,128]{1,0:T(8,128)S(1)}, u32[]{:S(2)}, u32[]{:S(2)}) collective-permute-start(f32[384,128]{1,0:T(8,128)S(1)} %bitcast.132), channel_id=1, source_target_pairs={{0,252},{4,0},{8,4},{12,8},{16,12},{20,16},{24,20},{28,24},{32,28}... | collective-permute-start | bytes 589832 | tf_op jit(solution)/shard_map/ppermute | solution.py:125
  49.0 0.0 collective-permute-done
  49.0 0.0 collective-permute-done.1
  49.0 0.0 copy-start.1
  49.0 0.7 copy-done
  49.8 0.1 copy-done.1
  50.0 3.6 %collective-permute-start.2 = (f32[592,128]{1,0:T(8,128)S(1)}, f32[592,128]{1,0:T(8,128)S(1)}, u32[]{:S(2)}, u32[]{:S(2)}) collective-permute-start(f32[592,128]{1,0:T(8,128)S(1)} %pad_maximum_fusion.4), channel_id=1, source_target_pairs={{0,1},{1,2},{2,3},{3,0},{4,5},{5,6},{6,7},{7,4},{8,9},{9,10},{10,1... | collective-permute-start | bytes 909320 | tf_op jit(solution)/shard_map/ppermute | solution.py:125
  53.6 0.1 collective-permute-start.3
  53.7 0.0 collective-permute-done.4
  53.7 0.0 copy-start.16
  53.8 0.0 collective-permute-done.5
  53.8 0.0 copy-start.17
  53.8 1.1 collective-permute-start.7
  54.9 2.7 %collective-permute-start.6 = (f32[160,128]{1,0:T(8,128)S(1)}, f32[160,128]{1,0:T(8,128)S(1)}, u32[]{:S(2)}, u32[]{:S(2)}) collective-permute-start(f32[160,128]{1,0:T(8,128)S(1)} %get-tuple-element.43), channel_id=1, source_target_pairs={{0,1},{1,2},{2,3},{3,0},{4,5},{5,6},{6,7},{7,4},{8,9},{9,10},{10,1... | collective-permute-start | bytes 245768 | tf_op jit(solution)/shard_map/ppermute | solution.py:125
  57.6 6.4 %collective-permute-done.7 = f32[160,128]{1,0:T(8,128)S(1)} collective-permute-done((f32[160,128]{1,0:T(8,128)S(1)}, f32[160,128]{1,0:T(8,128)S(1)}, u32[]{:S(2)}, u32[]{:S(2)}) %collective-permute-start.7) | collective-permute-done | bytes 81952 | tf_op jit(solution)/shard_map/ppermute | solution.py:125
  64.0 0.0 collective-permute-done.6
  64.0 0.0 collective-permute-done.2
  64.0 0.0 collective-permute-done.3
  64.0 0.6 copy-done.18
  64.6 0.0 copy-done.19
  64.6 0.1 copy-done.7
  64.8 0.1 copy-done.8
  64.9 12.2 %shard_map.113 = (f32[8,64,128]{2,1,0:T(8,128)}, f32[3,8,64,128]{3,2,1,0:T(8,128)}, f32[8,64,128]{2,1,0:T(8,128)}) custom-call(f32[3]{0:T(128)} %dif_ref.3, f32[3]{0:T(128)} %copy-done.20, f32[8,64,128]{2,1,0:T(8,128)} %refs_0_, f32[17,64,128]{2,1,0:T(8,128)} %bitcast.70, f32[17,64,128]{2,1,0:T(8,128)} %bitcast.74, f32[74,8,128]{2,1,0:T(8,128)} %bitcast.84, ...), custom_call_target="tpu_custom_call" | custom-call | flops 40755200 | bytes 4538368 | tf_op jit(solution)/shard_map/pallas_call | solution.py:319
  77.1 1.0 fusion.40
  78.1 1.0 fusion.45
  79.3 0.1 collective-permute-start.8
  79.4 5.7 %collective-permute-start.9 = (f32[1024,128]{1,0:T(8,128)S(1)}, f32[1024,128]{1,0:T(8,128)S(1)}, u32[]{:S(2)}, u32[]{:S(2)}) collective-permute-start(f32[1024,128]{1,0:T(8,128)S(1)} %pad_maximum_fusion.3), channel_id=1, source_target_pairs={{0,252},{4,0},{8,4},{12,8},{16,12},{20,16},{24,20},{28,24},{32,28}... | collective-permute-start | bytes 1572872 | tf_op jit(solution)/shard_map/ppermute | solution.py:125
  85.2 11.5 %collective-permute-done.8 = f32[1024,128]{1,0:T(8,128)S(1)} collective-permute-done((f32[1024,128]{1,0:T(8,128)S(1)}, f32[1024,128]{1,0:T(8,128)S(1)}, u32[]{:S(2)}, u32[]{:S(2)}) %collective-permute-start.8) | collective-permute-done | bytes 524320 | tf_op jit(solution)/shard_map/ppermute | solution.py:125
  96.7 0.0 collective-permute-done.9
  96.7 0.0 copy-done.9
  96.7 0.0 copy-start.12
  96.8 1.1 copy-done.12
  98.0 3.1 %collective-permute-start.10 = (f32[576,128]{1,0:T(8,128)S(1)}, f32[576,128]{1,0:T(8,128)S(1)}, u32[]{:S(2)}, u32[]{:S(2)}) collective-permute-start(f32[576,128]{1,0:T(8,128)S(1)} %pad_maximum_fusion.6), channel_id=1, source_target_pairs={{0,1},{1,2},{2,3},{3,0},{4,5},{5,6},{6,7},{7,4},{8,9},{9,10},{10,1... | collective-permute-start | bytes 884744 | tf_op jit(solution)/shard_map/ppermute | solution.py:125
  101.1 0.1 collective-permute-start.11
  101.2 6.0 %collective-permute-done.10 = f32[576,128]{1,0:T(8,128)S(1)} collective-permute-done((f32[576,128]{1,0:T(8,128)S(1)}, f32[576,128]{1,0:T(8,128)S(1)}, u32[]{:S(2)}, u32[]{:S(2)}) %collective-permute-start.10) | collective-permute-done | bytes 294944 | tf_op jit(solution)/shard_map/ppermute | solution.py:125
  107.2 1.6 %collective-permute-done.11 = f32[576,128]{1,0:T(8,128)S(1)} collective-permute-done((f32[576,128]{1,0:T(8,128)S(1)}, f32[576,128]{1,0:T(8,128)S(1)}, u32[]{:S(2)}, u32[]{:S(2)}) %collective-permute-start.11) | collective-permute-done | bytes 294944 | tf_op jit(solution)/shard_map/ppermute | solution.py:125
  108.8 0.0 copy-done.13
  108.8 0.7 copy-done.14
  109.5 11.8 %shard_map.114 = (f32[8,64,128]{2,1,0:T(8,128)}, f32[3,8,64,128]{3,2,1,0:T(8,128)}) custom-call(f32[3]{0:T(128)} %dif_ref.3, f32[3]{0:T(128)} %copy-done.20, f32[8,64,128]{2,1,0:T(8,128)} %get-tuple-element.15.refs_0_, f32[16,64,128]{2,1,0:T(8,128)} %bitcast.78, f32[16,64,128]{2,1,0:T(8,128)} %bitcast.81, f32[72,8,128]{2,1,0:T(8,128)} %bitcast.92, ...), custom_call_target="tpu_custom_call" | custom-call | flops 40755200 | bytes 4538368 | tf_op jit(solution)/shard_map/pallas_call | solution.py:319
  (53 shorter events, 0.7 us)
Async XLA Ops:
  0.6 13.0 %copy-start.10 = (f32[8,64,128]{2,1,0:T(8,128)S(1)}, f32[8,64,128]{2,1,0:T(8,128)}, u32[]{:S(2)}) copy-start(f32[8,64,128]{2,1,0:T(8,128)} %refs_0_) | copy-start | bytes 786436
  2.2 11.5 %copy-start.5 = (f32[8,64,128]{2,1,0:T(8,128)S(1)}, f32[8,64,128]{2,1,0:T(8,128)}, u32[]{:S(2)}) copy-start(f32[8,64,128]{2,1,0:T(8,128)} %refs_5_.1) | copy-start | bytes 786436
  14.6 8.6 %copy-start.22 = (s32[3]{0:T(128)S(1)}, s32[3]{0:T(128)}, u32[]{:S(2)}) copy-start(s32[3]{0:T(128)} %param.14) | copy-start | bytes 40
  14.6 8.6 %copy-start.21 = (s32[1,1,512]{2,1,0:T(1,128)S(1)}, s32[1,1,512]{2,1,0:T(1,128)}, u32[]{:S(2)}) copy-start(s32[1,1,512]{2,1,0:T(1,128)} %param.18) | copy-start | bytes 6148
  14.6 8.7 %copy-start.4 = (f32[3,8,64,128]{3,2,1,0:T(8,128)S(1)}, f32[3,8,64,128]{3,2,1,0:T(8,128)}, u32[]{:S(2)}) copy-start(f32[3,8,64,128]{3,2,1,0:T(8,128)} %refs_15_) | copy-start | bytes 2359300
  14.6 34.3 %collective-permute-start = (f32[1088,128]{1,0:T(8,128)}, f32[1088,128]{1,0:T(8,128)S(1)}, u32[]{:S(2)}, u32[]{:S(2)}) collective-permute-start(f32[1088,128]{1,0:T(8,128)} %pad_maximum_fusion), channel_id=1, source_target_pairs={{0,4},{4,8},{8,12},{12,16},{16,20},{20,24},{24,28},{28,32},{32,36}... | collective-permute-start | bytes 1671176 | tf_op jit(solution)/shard_map/ppermute | solution.py:125
  15.5 33.5 %collective-permute-start.1 = (f32[1088,128]{1,0:T(8,128)}, f32[1088,128]{1,0:T(8,128)S(1)}, u32[]{:S(2)}, u32[]{:S(2)}) collective-permute-start(f32[1088,128]{1,0:T(8,128)} %pad_maximum_fusion.1), channel_id=1, source_target_pairs={{0,252},{4,0},{8,4},{12,8},{16,12},{20,16},{24,20},{28,24},{32,28}... | collective-permute-start | bytes 1671176 | tf_op jit(solution)/shard_map/ppermute | solution.py:125
  23.2 18.6 %copy-start.20 = (f32[3]{0:T(128)}, f32[3]{0:T(128)S(1)}, u32[]{:S(2)}) copy-start(f32[3]{0:T(128)S(1)} %convert_element_type.28.val_ref) | copy-start | bytes 40
  42.6 0.7 copy-start.15
  42.6 11.2 %copy-start.6 = (f32[8,64,128]{2,1,0:T(8,128)}, f32[8,64,128]{2,1,0:T(8,128)S(1)}, u32[]{:S(2)}) copy-start(f32[8,64,128]{2,1,0:T(8,128)S(1)} %add.88.refs_10_) | copy-start | bytes 786436
  43.3 10.5 %collective-permute-start.4 = (f32[384,128]{1,0:T(8,128)S(1)}, f32[384,128]{1,0:T(8,128)S(1)}, u32[]{:S(2)}, u32[]{:S(2)}) collective-permute-start(f32[384,128]{1,0:T(8,128)S(1)} %bitcast.133), channel_id=1, source_target_pairs={{0,4},{4,8},{8,12},{12,16},{16,20},{20,24},{24,28},{28,32},{32,36}... | collective-permute-start | bytes 589832 | tf_op jit(solution)/shard_map/ppermute | solution.py:125
  43.3 10.5 %collective-permute-start.5 = (f32[384,128]{1,0:T(8,128)S(1)}, f32[384,128]{1,0:T(8,128)S(1)}, u32[]{:S(2)}, u32[]{:S(2)}) collective-permute-start(f32[384,128]{1,0:T(8,128)S(1)} %bitcast.132), channel_id=1, source_target_pairs={{0,252},{4,0},{8,4},{12,8},{16,12},{20,16},{24,20},{28,24},{32,28}... | collective-permute-start | bytes 589832 | tf_op jit(solution)/shard_map/ppermute | solution.py:125
  49.0 0.8 copy-start
  49.0 1.0 copy-start.1
  50.0 14.0 %collective-permute-start.2 = (f32[592,128]{1,0:T(8,128)S(1)}, f32[592,128]{1,0:T(8,128)S(1)}, u32[]{:S(2)}, u32[]{:S(2)}) collective-permute-start(f32[592,128]{1,0:T(8,128)S(1)} %pad_maximum_fusion.4), channel_id=1, source_target_pairs={{0,1},{1,2},{2,3},{3,0},{4,5},{5,6},{6,7},{7,4},{8,9},{9,10},{10,1... | collective-permute-start | bytes 909320 | tf_op jit(solution)/shard_map/ppermute | solution.py:125
  53.6 10.4 %collective-permute-start.3 = (f32[592,128]{1,0:T(8,128)S(1)}, f32[592,128]{1,0:T(8,128)S(1)}, u32[]{:S(2)}, u32[]{:S(2)}) collective-permute-start(f32[592,128]{1,0:T(8,128)S(1)} %pad_maximum_fusion.5), channel_id=1, source_target_pairs={{0,3},{1,0},{2,1},{3,2},{4,7},{5,4},{6,5},{7,6},{8,11},{9,8},{10,9... | collective-permute-start | bytes 909320 | tf_op jit(solution)/shard_map/ppermute | solution.py:125
  53.7 10.3 %copy-start.16 = (f32[384,128]{1,0:T(8,128)}, f32[384,128]{1,0:T(8,128)S(1)}, u32[]{:S(2)}) copy-start(f32[384,128]{1,0:T(8,128)S(1)} %collective-permute-done.4) | copy-start | bytes 589828
  53.8 10.3 %copy-start.17 = (f32[384,128]{1,0:T(8,128)}, f32[384,128]{1,0:T(8,128)S(1)}, u32[]{:S(2)}) copy-start(f32[384,128]{1,0:T(8,128)S(1)} %collective-permute-done.5) | copy-start | bytes 589828
  53.8 10.2 %collective-permute-start.7 = (f32[160,128]{1,0:T(8,128)S(1)}, f32[160,128]{1,0:T(8,128)S(1)}, u32[]{:S(2)}, u32[]{:S(2)}) collective-permute-start(f32[160,128]{1,0:T(8,128)S(1)} %get-tuple-element.42), channel_id=1, source_target_pairs={{0,3},{1,0},{2,1},{3,2},{4,7},{5,4},{6,5},{7,6},{8,11},{9,8},{10,9... | collective-permute-start | bytes 245768 | tf_op jit(solution)/shard_map/ppermute | solution.py:125
  54.9 9.1 %collective-permute-start.6 = (f32[160,128]{1,0:T(8,128)S(1)}, f32[160,128]{1,0:T(8,128)S(1)}, u32[]{:S(2)}, u32[]{:S(2)}) collective-permute-start(f32[160,128]{1,0:T(8,128)S(1)} %get-tuple-element.43), channel_id=1, source_target_pairs={{0,1},{1,2},{2,3},{3,0},{4,5},{5,6},{6,7},{7,4},{8,9},{9,10},{10,1... | collective-permute-start | bytes 245768 | tf_op jit(solution)/shard_map/ppermute | solution.py:125
  64.0 0.6 copy-start.18
  64.0 0.7 copy-start.19
  64.0 0.8 copy-start.7
  64.0 0.8 copy-start.8
  77.1 2.1 %copy-start.11 = (f32[8,64,128]{2,1,0:T(8,128)S(1)}, f32[8,64,128]{2,1,0:T(8,128)}, u32[]{:S(2)}) copy-start(f32[8,64,128]{2,1,0:T(8,128)} %get-tuple-element.15.refs_0_) | copy-start | bytes 786436
  79.3 17.4 %copy-start.9 = (f32[3,8,64,128]{3,2,1,0:T(8,128)S(1)}, f32[3,8,64,128]{3,2,1,0:T(8,128)}, u32[]{:S(2)}) copy-start(f32[3,8,64,128]{3,2,1,0:T(8,128)} %get-tuple-element.17.refs_15_) | copy-start | bytes 2359300
  79.3 17.4 %collective-permute-start.8 = (f32[1024,128]{1,0:T(8,128)S(1)}, f32[1024,128]{1,0:T(8,128)S(1)}, u32[]{:S(2)}, u32[]{:S(2)}) collective-permute-start(f32[1024,128]{1,0:T(8,128)S(1)} %pad_maximum_fusion.2), channel_id=1, source_target_pairs={{0,4},{4,8},{8,12},{12,16},{16,20},{20,24},{24,28},{28,32},{32,36}... | collective-permute-start | bytes 1572872 | tf_op jit(solution)/shard_map/ppermute | solution.py:125
  79.4 17.2 %collective-permute-start.9 = (f32[1024,128]{1,0:T(8,128)S(1)}, f32[1024,128]{1,0:T(8,128)S(1)}, u32[]{:S(2)}, u32[]{:S(2)}) collective-permute-start(f32[1024,128]{1,0:T(8,128)S(1)} %pad_maximum_fusion.3), channel_id=1, source_target_pairs={{0,252},{4,0},{8,4},{12,8},{16,12},{20,16},{24,20},{28,24},{32,28}... | collective-permute-start | bytes 1572872 | tf_op jit(solution)/shard_map/ppermute | solution.py:125
  96.6 1.2 %copy-start.2 = (f32[1024,128]{1,0:T(8,128)}, f32[1024,128]{1,0:T(8,128)S(1)}, u32[]{:S(2)}) copy-start(f32[1024,128]{1,0:T(8,128)S(1)} %collective-permute-done.8) | copy-start | bytes 1572868
  96.7 1.2 %copy-start.3 = (f32[1024,128]{1,0:T(8,128)}, f32[1024,128]{1,0:T(8,128)S(1)}, u32[]{:S(2)}) copy-start(f32[1024,128]{1,0:T(8,128)S(1)} %collective-permute-done.9) | copy-start | bytes 1572868
  96.7 1.1 copy-start.12
  98.0 9.2 %collective-permute-start.10 = (f32[576,128]{1,0:T(8,128)S(1)}, f32[576,128]{1,0:T(8,128)S(1)}, u32[]{:S(2)}, u32[]{:S(2)}) collective-permute-start(f32[576,128]{1,0:T(8,128)S(1)} %pad_maximum_fusion.6), channel_id=1, source_target_pairs={{0,1},{1,2},{2,3},{3,0},{4,5},{5,6},{6,7},{7,4},{8,9},{9,10},{10,1... | collective-permute-start | bytes 884744 | tf_op jit(solution)/shard_map/ppermute | solution.py:125
  101.1 7.7 %collective-permute-start.11 = (f32[576,128]{1,0:T(8,128)S(1)}, f32[576,128]{1,0:T(8,128)S(1)}, u32[]{:S(2)}, u32[]{:S(2)}) collective-permute-start(f32[576,128]{1,0:T(8,128)S(1)} %pad_maximum_fusion.7), channel_id=1, source_target_pairs={{0,3},{1,0},{2,1},{3,2},{4,7},{5,4},{6,5},{7,6},{8,11},{9,8},{10,9... | collective-permute-start | bytes 884744 | tf_op jit(solution)/shard_map/ppermute | solution.py:125
  107.2 1.6 %copy-start.13 = (f32[576,128]{1,0:T(8,128)}, f32[576,128]{1,0:T(8,128)S(1)}, u32[]{:S(2)}) copy-start(f32[576,128]{1,0:T(8,128)S(1)} %collective-permute-done.10) | copy-start | bytes 884740
  108.8 0.7 copy-start.14

commit v12 on v11

--- a/solution.py
+++ b/solution.py
@@ -125,7 +125,7 @@
     return lax.ppermute(x, axis, [(i, (i + shift) % count) for i in range(count)])
 
 
-def deep_halo(items, axis_z, axis_y):
+def deep_halo(items, axis_z, axis_y, sends=None):
     minor = items[0][0].shape[-1]
     rows = items[0][0].shape[-2]
     tops, bots = [], []
@@ -134,8 +134,13 @@
         n = a.shape[dim]
         tops.append(lax.slice_in_dim(a, n - wz, n, axis=dim))
         bots.append(lax.slice_in_dim(a, 0, wz, axis=dim))
-    z_lo = ring(jnp.concatenate([t.reshape(-1, minor) for t in tops], axis=0), axis_z, 1)
-    z_hi = ring(jnp.concatenate([t.reshape(-1, minor) for t in bots], axis=0), axis_z, -1)
+    if sends is None:
+        top = jnp.concatenate([t.reshape(-1, minor) for t in tops], axis=0)
+        bot = jnp.concatenate([t.reshape(-1, minor) for t in bots], axis=0)
+    else:
+        top, bot = (s.reshape(-1, minor) for s in sends)
+    z_lo = ring(top, axis_z, 1)
+    z_hi = ring(bot, axis_z, -1)
     y_tops, y_bots, z_offs, at = [], [], [], 0
     for (a, wz, wy), t in zip(items, tops):
         size = t.size // minor
@@ -167,7 +172,8 @@
     rest = list(refs[20:])
     e_ref = rest.pop(0) if with_source else None
     fo_ref, co_ref = rest[0], rest[1]
-    so_ref = rest.pop(2) if with_source else None
+    if with_source:
+        so_ref, top_ref, bot_ref = rest.pop(2), rest.pop(2), rest.pop(2)
     f_ref, p_ref, s_ref, c_ref, fa, fb, w_ref, sems = rest[2:]
     targets = (f_ref, p_ref, s_ref, c_ref)
     copies = [[] for _ in targets]
@@ -288,6 +294,15 @@
         return carry
 
     lax.fori_loop(0, inner, move, 0, unroll=2)
+    if with_source:
+        wf, wsrc = hz, hz - 1
+        top_ref[0:wf] = fo_ref[inner - wf:inner]
+        bot_ref[0:wf] = fo_ref[0:wf]
+        top_ref[wf:wf + wsrc] = so_ref[inner - wsrc:inner]
+        bot_ref[wf:wf + wsrc] = so_ref[0:wsrc]
+        for s in range(species):
+            top_ref[wf + wsrc + s] = co_ref[s, inner - 1]
+            bot_ref[wf + wsrc + s] = co_ref[s, 0]
 
 
 def time_step(diffusivity, charge_num, field_p, perm_p, source_p, species_p, electrode=None):
@@ -315,6 +330,8 @@
     extra = []
     if with_source:
         out_shape.append(jax.ShapeDtypeStruct((inner, out_rows, lanes), jnp.float32))
+        send = jax.ShapeDtypeStruct((2 * SWEEPS + 1 + species, out_rows, lanes), jnp.float32)
+        out_shape += [send, send]
         extra = [electrode]
     return pl.pallas_call(
         functools.partial(step_kernel, tuple(plan), with_source),
@@ -417,10 +434,13 @@
             (source_p,) = deep_halo([(source, deep - 1, wide_y)], "wide", "narrow")
         else:
             field_p, source_p, species_p = deep_halo(
-                [(field, deep, wide_y), (source, deep - 1, wide_y), (species, 1, wide_y)], "wide", "narrow"
+                [(field, deep, wide_y), (source, deep - 1, wide_y), (species, 1, wide_y)],
+                "wide",
+                "narrow",
+                sends,
             )
         if step + 1 < STEPS:
-            field, species, source = time_step(
+            field, species, source, *sends = time_step(
                 diffusivity, charge_num, field_p, perm_p, source_p, species_p, electrode
             )
         else:

time: 122 us -> 125 us (1.025)
  waiting for transfers between devices: 25.5 us -> 31.3 us
  local copies, waits for them, and re-layouts: 7.45 us -> 5.22 us
  starting transfers between devices: 29.2 us -> 27.6 us
    ppermute x12, waiting for transfers between devices: 25.5 us -> 31.3 us  [ring(): lax.ppermute(x, axis, [(i, (i + shift) % count) for i in range(count)])]
    slice x7 -> x4, local copies, waits for them, and re-layouts: 3.15 us -> 1.06 us  [deep_halo(): bots.append(lax.slice_in_dim(a, 0, wz, axis=dim))]
    ppermute x12, starting transfers between devices: 29.2 us -> 27.6 us  [ring(): lax.ppermute(x, axis, [(i, (i + shift) % count) for i in range(count)])]
    unnamed x46 -> x44, local copies, waits for them, and re-layouts: 4.13 us -> 3.99 us
  transfers between devices with their start and end apart: 12 -> 12, of which waited for: 4 -> 5; matrix products, arithmetic and copies ran while one was open for 17% -> 16% of each run, Pallas kernels for 0% -> 0%
where the time goes in v12:
time: 125 us
  waiting for transfers between devices  31.3 us (25%)
  starting transfers between devices  27.6 us (22%)
  Pallas kernels  24.4 us (20%)
  other arithmetic  23.1 us (18%)
  blocking collectives  10.5 us (8%)
  local copies, waits for them, and re-layouts  5.22 us (4%)
  between operations  1.91 us (2%)
    ppermute x12, waiting for transfers between devices, ring(): lax.ppermute(x, axis, [(i, (i + shift) % count) for i in range(count)])  31.3 us
    ppermute x12, starting transfers between devices, ring(): lax.ppermute(x, axis, [(i, (i + shift) % count) for i in range(count)])  27.6 us
    pallas_call x2, Pallas kernels, time_step(): pl.pallas_call(functools.partial(step_kernel, tuple(plan), with_source),...  24.4 us
    reduce_sum x1, other arithmetic, one_block(): return jnp.sum(jnp.where(adjacent, term, 0.0), axis=1)  18.2 us
    all_gather x1, blocking collectives, per_device(): gathered = lax.all_gather(charges, 'narrow', axis=1, tiled=True)  10.5 us
    unnamed x44, local copies, waits for them, and re-layouts  3.99 us
  transfers between devices with their start and end apart: 12, of which 5 were waited for; matrix products, arithmetic and copies ran while one was open for 16% of the time, Pallas kernels for 0%

profile of v12, /device:TPU:1, one launch (start us, length us, event | category | flops | bytes accessed | tf_op | source)
XLA Modules:
  0.0 124.8 jit_solution(6190807882005828442)
XLA Ops:
  0.6 0.0 copy-start.9
  0.6 0.7 convert_element_type.29
  1.4 0.8 pad_maximum_fusion.22
  2.2 0.0 copy-start.5
  2.2 10.5 %all_gather.3 = f32[5,8192]{1,0:T(8,128)S(1)} all-gather(f32[5,2048]{1,0:T(8,128)S(1)} %pad_maximum_fusion.22), channel_id=1, replica_groups=mesh['wide'=64,'narrow'=4] {'narrow'}, dimensions={1}, use_global_device_ids=true | all-gather | bytes 204800 | tf_op jit(solution)/shard_map/all_gather | solution.py:396
  12.7 1.0 fusion.40
  13.7 0.0 copy-done.9
  13.7 0.0 copy-done.5
  13.8 0.8 pad_maximum_fusion
  14.6 0.0 collective-permute-start
  14.6 0.9 pad_maximum_fusion.1
  15.5 7.0 %collective-permute-start.1 = (f32[1088,128]{1,0:T(8,128)}, f32[1088,128]{1,0:T(8,128)S(1)}, u32[]{:S(2)}, u32[]{:S(2)}) collective-permute-start(f32[1088,128]{1,0:T(8,128)} %pad_maximum_fusion.1), channel_id=1, source_target_pairs={{0,252},{4,0},{8,4},{12,8},{16,12},{20,16},{24,20},{28,24},{32,28}... | collective-permute-start | bytes 1671176 | tf_op jit(solution)/shard_map/ppermute | solution.py:125
  23.2 0.0 copy-done.21
  23.2 0.0 copy-start.19
  23.2 0.0 copy-done.20
  23.3 0.0 copy-done.4
  23.3 0.1 multiply_reduce_fusion
  23.4 0.1 fusion.44
  23.6 18.2 %select_reduce_fusion.1 = (f32[256]{0:T(256)S(1)}, f32[256]{0:T(256)S(1)}) fusion(f32[8192]{0:T(1024)S(1)} %bitcast.127, f32[256]{0:T(256)S(1)} %get-tuple-element.77, f32[8192]{0:T(1024)S(1)} %bitcast.128, f32[256]{0:T(256)S(1)} %get-tuple-element.66, f32[8192]{0:T(1024)S(1)} %bitcast.129, f32[256]{0:T(256)S(1)} %get-tuple-element.75, ...), kind=kLoop, calls=%fused_computation.20 | loop fusion | flops 104857088 | bytes 174080 | tf_op jit(solution)/shard_map/reduce_sum | solution.py:116
  41.8 0.0 copy-done.19
  41.8 0.8 fusion.18
  42.6 0.0 copy-start.12
  42.6 0.0 copy-start.6
  42.7 0.6 copy-done.12
  43.3 0.0 collective-permute-start.4
  43.3 5.7 %collective-permute-start.5 = (f32[384,128]{1,0:T(8,128)S(1)}, f32[384,128]{1,0:T(8,128)S(1)}, u32[]{:S(2)}, u32[]{:S(2)}) collective-permute-start(f32[384,128]{1,0:T(8,128)S(1)} %bitcast.122), channel_id=1, source_target_pairs={{0,252},{4,0},{8,4},{12,8},{16,12},{20,16},{24,20},{28,24},{32,28}... | collective-permute-start | bytes 589832 | tf_op jit(solution)/shard_map/ppermute | solution.py:125
  49.0 0.0 collective-permute-done
  49.0 0.0 collective-permute-done.1
  49.0 0.0 copy-start.1
  49.1 0.8 copy-done
  49.8 0.1 copy-done.1
  50.1 3.6 %collective-permute-start.2 = (f32[592,128]{1,0:T(8,128)S(1)}, f32[592,128]{1,0:T(8,128)S(1)}, u32[]{:S(2)}, u32[]{:S(2)}) collective-permute-start(f32[592,128]{1,0:T(8,128)S(1)} %pad_maximum_fusion.2), channel_id=1, source_target_pairs={{0,1},{1,2},{2,3},{3,0},{4,5},{5,6},{6,7},{7,4},{8,9},{9,10},{10,1... | collective-permute-start | bytes 909320 | tf_op jit(solution)/shard_map/ppermute | solution.py:125
  53.7 0.1 collective-permute-start.3
  53.8 0.0 collective-permute-done.4
  53.8 0.0 copy-start.15
  53.8 0.0 collective-permute-done.5
  53.8 0.0 copy-start.16
  53.8 1.1 collective-permute-start.7
  54.9 2.7 %collective-permute-start.6 = (f32[160,128]{1,0:T(8,128)S(1)}, f32[160,128]{1,0:T(8,128)S(1)}, u32[]{:S(2)}, u32[]{:S(2)}) collective-permute-start(f32[160,128]{1,0:T(8,128)S(1)} %get-tuple-element.45), channel_id=1, source_target_pairs={{0,1},{1,2},{2,3},{3,0},{4,5},{5,6},{6,7},{7,4},{8,9},{9,10},{10,1... | collective-permute-start | bytes 245768 | tf_op jit(solution)/shard_map/ppermute | solution.py:125
  57.6 6.4 %collective-permute-done.7 = f32[160,128]{1,0:T(8,128)S(1)} collective-permute-done((f32[160,128]{1,0:T(8,128)S(1)}, f32[160,128]{1,0:T(8,128)S(1)}, u32[]{:S(2)}, u32[]{:S(2)}) %collective-permute-start.7) | collective-permute-done | bytes 81952 | tf_op jit(solution)/shard_map/ppermute | solution.py:125
  64.0 0.0 collective-permute-done.6
  64.0 0.0 collective-permute-done.2
  64.0 0.0 copy-start.7
  64.0 0.0 collective-permute-done.3
  64.1 0.6 copy-done.17
  64.6 0.0 copy-done.18
  64.7 0.1 copy-done.7
  64.8 0.1 copy-done.8
  64.9 12.6 %shard_map.113 = (f32[8,64,128]{2,1,0:T(8,128)}, f32[3,8,64,128]{3,2,1,0:T(8,128)}, f32[8,64,128]{2,1,0:T(8,128)}, f32[16,64,128]{2,1,0:T(8,128)}, f32[16,64,128]{2,1,0:T(8,128)}) custom-call(f32[3]{0:T(128)} %dif_ref.3, f32[3]{0:T(128)} %copy-done.19, f32[8,64,128]{2,1,0:T(8,128)} %refs_0_, f32[17,64,128]{2,1,0:T(8,128)} %bitcast.66, ...), custom_call_target="tpu_custom_call" | custom-call | flops 40755200 | bytes 4538368 | tf_op jit(solution)/shard_map/pallas_call | solution.py:336
  77.5 3.4 %collective-permute-start.9 = (f32[1024,128]{1,0:T(8,128)}, f32[1024,128]{1,0:T(8,128)S(1)}, u32[]{:S(2)}, u32[]{:S(2)}) collective-permute-start(f32[1024,128]{1,0:T(8,128)} %bitcast.133), channel_id=1, source_target_pairs={{0,252},{4,0},{8,4},{12,8},{16,12},{20,16},{24,20},{28,24},{32,28}... | collective-permute-start | bytes 1572872 | tf_op jit(solution)/shard_map/ppermute | solution.py:125
  80.9 0.0 collective-permute-start.8
  80.9 11.2 %collective-permute-done.9 = f32[1024,128]{1,0:T(8,128)S(1)} collective-permute-done((f32[1024,128]{1,0:T(8,128)}, f32[1024,128]{1,0:T(8,128)S(1)}, u32[]{:S(2)}, u32[]{:S(2)}) %collective-permute-start.9) | collective-permute-done | bytes 524320 | tf_op jit(solution)/shard_map/ppermute | solution.py:125
  92.2 6.0 %collective-permute-done.8 = f32[1024,128]{1,0:T(8,128)S(1)} collective-permute-done((f32[1024,128]{1,0:T(8,128)}, f32[1024,128]{1,0:T(8,128)S(1)}, u32[]{:S(2)}, u32[]{:S(2)}) %collective-permute-start.8) | collective-permute-done | bytes 524320 | tf_op jit(solution)/shard_map/ppermute | solution.py:125
  98.2 1.2 pad_maximum_fusion.6
  99.4 0.0 copy-done.14
  99.5 0.0 copy-done.3
  99.5 0.8 copy-done.13
  100.4 3.9 %collective-permute-start.10 = (f32[576,128]{1,0:T(8,128)S(1)}, f32[576,128]{1,0:T(8,128)S(1)}, u32[]{:S(2)}, u32[]{:S(2)}) collective-permute-start(f32[576,128]{1,0:T(8,128)S(1)} %pad_maximum_fusion.4), channel_id=1, source_target_pairs={{0,1},{1,2},{2,3},{3,0},{4,5},{5,6},{6,7},{7,4},{8,9},{9,10},{10,1... | collective-permute-start | bytes 884744 | tf_op jit(solution)/shard_map/ppermute | solution.py:125
  104.4 0.1 collective-permute-start.11
  104.5 5.5 %collective-permute-done.10 = f32[576,128]{1,0:T(8,128)S(1)} collective-permute-done((f32[576,128]{1,0:T(8,128)S(1)}, f32[576,128]{1,0:T(8,128)S(1)}, u32[]{:S(2)}, u32[]{:S(2)}) %collective-permute-start.10) | collective-permute-done | bytes 294944 | tf_op jit(solution)/shard_map/ppermute | solution.py:125
  109.9 2.2 %collective-permute-done.11 = f32[576,128]{1,0:T(8,128)S(1)} collective-permute-done((f32[576,128]{1,0:T(8,128)S(1)}, f32[576,128]{1,0:T(8,128)S(1)}, u32[]{:S(2)}, u32[]{:S(2)}) %collective-permute-start.11) | collective-permute-done | bytes 294944 | tf_op jit(solution)/shard_map/ppermute | solution.py:125
  112.1 0.0 copy-done.10
  112.1 0.7 copy-done.11
  112.9 11.8 %shard_map.114 = (f32[8,64,128]{2,1,0:T(8,128)}, f32[3,8,64,128]{3,2,1,0:T(8,128)}) custom-call(f32[3]{0:T(128)} %dif_ref.3, f32[3]{0:T(128)} %copy-done.19, f32[8,64,128]{2,1,0:T(8,128)} %get-tuple-element.17.refs_0_, f32[16,64,128]{2,1,0:T(8,128)} %bitcast.77, f32[16,64,128]{2,1,0:T(8,128)} %bitcast.74, f32[72,8,128]{2,1,0:T(8,128)} %bitcast.88, ...), custom_call_target="tpu_custom_call" | custom-call | flops 40755200 | bytes 4538368 | tf_op jit(solution)/shard_map/pallas_call | solution.py:336
  (46 shorter events, 0.6 us)
Async XLA Ops:
  0.6 13.0 %copy-start.9 = (f32[8,64,128]{2,1,0:T(8,128)S(1)}, f32[8,64,128]{2,1,0:T(8,128)}, u32[]{:S(2)}) copy-start(f32[8,64,128]{2,1,0:T(8,128)} %refs_0_) | copy-start | bytes 786436
  2.2 11.5 %copy-start.5 = (f32[8,64,128]{2,1,0:T(8,128)S(1)}, f32[8,64,128]{2,1,0:T(8,128)}, u32[]{:S(2)}) copy-start(f32[8,64,128]{2,1,0:T(8,128)} %refs_5_.1) | copy-start | bytes 786436
  14.6 8.6 %copy-start.21 = (s32[3]{0:T(128)S(1)}, s32[3]{0:T(128)}, u32[]{:S(2)}) copy-start(s32[3]{0:T(128)} %param.14) | copy-start | bytes 40
  14.6 8.6 %copy-start.20 = (s32[1,1,512]{2,1,0:T(1,128)S(1)}, s32[1,1,512]{2,1,0:T(1,128)}, u32[]{:S(2)}) copy-start(s32[1,1,512]{2,1,0:T(1,128)} %param.18) | copy-start | bytes 6148
  14.6 8.7 %copy-start.4 = (f32[3,8,64,128]{3,2,1,0:T(8,128)S(1)}, f32[3,8,64,128]{3,2,1,0:T(8,128)}, u32[]{:S(2)}) copy-start(f32[3,8,64,128]{3,2,1,0:T(8,128)} %refs_15_) | copy-start | bytes 2359300
  14.6 34.4 %collective-permute-start = (f32[1088,128]{1,0:T(8,128)}, f32[1088,128]{1,0:T(8,128)S(1)}, u32[]{:S(2)}, u32[]{:S(2)}) collective-permute-start(f32[1088,128]{1,0:T(8,128)} %pad_maximum_fusion), channel_id=1, source_target_pairs={{0,4},{4,8},{8,12},{12,16},{16,20},{20,24},{24,28},{28,32},{32,36}... | collective-permute-start | bytes 1671176 | tf_op jit(solution)/shard_map/ppermute | solution.py:125
  15.5 33.5 %collective-permute-start.1 = (f32[1088,128]{1,0:T(8,128)}, f32[1088,128]{1,0:T(8,128)S(1)}, u32[]{:S(2)}, u32[]{:S(2)}) collective-permute-start(f32[1088,128]{1,0:T(8,128)} %pad_maximum_fusion.1), channel_id=1, source_target_pairs={{0,252},{4,0},{8,4},{12,8},{16,12},{20,16},{24,20},{28,24},{32,28}... | collective-permute-start | bytes 1671176 | tf_op jit(solution)/shard_map/ppermute | solution.py:125
  23.2 18.6 %copy-start.19 = (f32[3]{0:T(128)}, f32[3]{0:T(128)S(1)}, u32[]{:S(2)}) copy-start(f32[3]{0:T(128)S(1)} %convert_element_type.28.val_ref) | copy-start | bytes 40
  42.6 0.7 copy-start.12
  42.6 11.2 %copy-start.6 = (f32[8,64,128]{2,1,0:T(8,128)}, f32[8,64,128]{2,1,0:T(8,128)S(1)}, u32[]{:S(2)}) copy-start(f32[8,64,128]{2,1,0:T(8,128)S(1)} %add.88.refs_10_) | copy-start | bytes 786436
  43.3 10.5 %collective-permute-start.4 = (f32[384,128]{1,0:T(8,128)S(1)}, f32[384,128]{1,0:T(8,128)S(1)}, u32[]{:S(2)}, u32[]{:S(2)}) collective-permute-start(f32[384,128]{1,0:T(8,128)S(1)} %bitcast.123), channel_id=1, source_target_pairs={{0,4},{4,8},{8,12},{12,16},{16,20},{20,24},{24,28},{28,32},{32,36}... | collective-permute-start | bytes 589832 | tf_op jit(solution)/shard_map/ppermute | solution.py:125
  43.3 10.5 %collective-permute-start.5 = (f32[384,128]{1,0:T(8,128)S(1)}, f32[384,128]{1,0:T(8,128)S(1)}, u32[]{:S(2)}, u32[]{:S(2)}) collective-permute-start(f32[384,128]{1,0:T(8,128)S(1)} %bitcast.122), channel_id=1, source_target_pairs={{0,252},{4,0},{8,4},{12,8},{16,12},{20,16},{24,20},{28,24},{32,28}... | collective-permute-start | bytes 589832 | tf_op jit(solution)/shard_map/ppermute | solution.py:125
  49.0 0.8 copy-start
  49.0 1.0 copy-start.1
  50.1 13.9 %collective-permute-start.2 = (f32[592,128]{1,0:T(8,128)S(1)}, f32[592,128]{1,0:T(8,128)S(1)}, u32[]{:S(2)}, u32[]{:S(2)}) collective-permute-start(f32[592,128]{1,0:T(8,128)S(1)} %pad_maximum_fusion.2), channel_id=1, source_target_pairs={{0,1},{1,2},{2,3},{3,0},{4,5},{5,6},{6,7},{7,4},{8,9},{9,10},{10,1... | collective-permute-start | bytes 909320 | tf_op jit(solution)/shard_map/ppermute | solution.py:125
  53.7 10.3 %collective-permute-start.3 = (f32[592,128]{1,0:T(8,128)S(1)}, f32[592,128]{1,0:T(8,128)S(1)}, u32[]{:S(2)}, u32[]{:S(2)}) collective-permute-start(f32[592,128]{1,0:T(8,128)S(1)} %pad_maximum_fusion.3), channel_id=1, source_target_pairs={{0,3},{1,0},{2,1},{3,2},{4,7},{5,4},{6,5},{7,6},{8,11},{9,8},{10,9... | collective-permute-start | bytes 909320 | tf_op jit(solution)/shard_map/ppermute | solution.py:125
  53.8 10.3 %copy-start.15 = (f32[384,128]{1,0:T(8,128)}, f32[384,128]{1,0:T(8,128)S(1)}, u32[]{:S(2)}) copy-start(f32[384,128]{1,0:T(8,128)S(1)} %collective-permute-done.4) | copy-start | bytes 589828
  53.8 10.3 %copy-start.16 = (f32[384,128]{1,0:T(8,128)}, f32[384,128]{1,0:T(8,128)S(1)}, u32[]{:S(2)}) copy-start(f32[384,128]{1,0:T(8,128)S(1)} %collective-permute-done.5) | copy-start | bytes 589828
  53.8 10.2 %collective-permute-start.7 = (f32[160,128]{1,0:T(8,128)S(1)}, f32[160,128]{1,0:T(8,128)S(1)}, u32[]{:S(2)}, u32[]{:S(2)}) collective-permute-start(f32[160,128]{1,0:T(8,128)S(1)} %get-tuple-element.44), channel_id=1, source_target_pairs={{0,3},{1,0},{2,1},{3,2},{4,7},{5,4},{6,5},{7,6},{8,11},{9,8},{10,9... | collective-permute-start | bytes 245768 | tf_op jit(solution)/shard_map/ppermute | solution.py:125
  54.9 9.1 %collective-permute-start.6 = (f32[160,128]{1,0:T(8,128)S(1)}, f32[160,128]{1,0:T(8,128)S(1)}, u32[]{:S(2)}, u32[]{:S(2)}) collective-permute-start(f32[160,128]{1,0:T(8,128)S(1)} %get-tuple-element.45), channel_id=1, source_target_pairs={{0,1},{1,2},{2,3},{3,0},{4,5},{5,6},{6,7},{7,4},{8,9},{9,10},{10,1... | collective-permute-start | bytes 245768 | tf_op jit(solution)/shard_map/ppermute | solution.py:125
  64.0 0.6 copy-start.17
  64.0 0.7 copy-start.18
  64.0 0.8 copy-start.7
  64.0 0.9 copy-start.8
  77.5 14.7 %collective-permute-start.9 = (f32[1024,128]{1,0:T(8,128)}, f32[1024,128]{1,0:T(8,128)S(1)}, u32[]{:S(2)}, u32[]{:S(2)}) collective-permute-start(f32[1024,128]{1,0:T(8,128)} %bitcast.133), channel_id=1, source_target_pairs={{0,252},{4,0},{8,4},{12,8},{16,12},{20,16},{24,20},{28,24},{32,28}... | collective-permute-start | bytes 1572872 | tf_op jit(solution)/shard_map/ppermute | solution.py:125
  80.9 17.2 %collective-permute-start.8 = (f32[1024,128]{1,0:T(8,128)}, f32[1024,128]{1,0:T(8,128)S(1)}, u32[]{:S(2)}, u32[]{:S(2)}) collective-permute-start(f32[1024,128]{1,0:T(8,128)} %bitcast.132), channel_id=1, source_target_pairs={{0,4},{4,8},{8,12},{12,16},{16,20},{20,24},{24,28},{28,32},{32,36}... | collective-permute-start | bytes 1572872 | tf_op jit(solution)/shard_map/ppermute | solution.py:125
  92.2 7.3 %copy-start.2 = (f32[1024,128]{1,0:T(8,128)}, f32[1024,128]{1,0:T(8,128)S(1)}, u32[]{:S(2)}) copy-start(f32[1024,128]{1,0:T(8,128)S(1)} %collective-permute-done.9) | copy-start | bytes 1572868
  98.2 1.3 %copy-start.3 = (f32[1024,128]{1,0:T(8,128)}, f32[1024,128]{1,0:T(8,128)S(1)}, u32[]{:S(2)}) copy-start(f32[1024,128]{1,0:T(8,128)S(1)} %collective-permute-done.8) | copy-start | bytes 1572868
  98.2 1.2 copy-start.14
  99.4 0.9 copy-start.13
  100.4 9.5 %collective-permute-start.10 = (f32[576,128]{1,0:T(8,128)S(1)}, f32[576,128]{1,0:T(8,128)S(1)}, u32[]{:S(2)}, u32[]{:S(2)}) collective-permute-start(f32[576,128]{1,0:T(8,128)S(1)} %pad_maximum_fusion.4), channel_id=1, source_target_pairs={{0,1},{1,2},{2,3},{3,0},{4,5},{5,6},{6,7},{7,4},{8,9},{9,10},{10,1... | collective-permute-start | bytes 884744 | tf_op jit(solution)/shard_map/ppermute | solution.py:125
  104.4 7.8 %collective-permute-start.11 = (f32[576,128]{1,0:T(8,128)S(1)}, f32[576,128]{1,0:T(8,128)S(1)}, u32[]{:S(2)}, u32[]{:S(2)}) collective-permute-start(f32[576,128]{1,0:T(8,128)S(1)} %pad_maximum_fusion.5), channel_id=1, source_target_pairs={{0,3},{1,0},{2,1},{3,2},{4,7},{5,4},{6,5},{7,6},{8,11},{9,8},{10,9... | collective-permute-start | bytes 884744 | tf_op jit(solution)/shard_map/ppermute | solution.py:125
  109.9 2.2 %copy-start.10 = (f32[576,128]{1,0:T(8,128)}, f32[576,128]{1,0:T(8,128)S(1)}, u32[]{:S(2)}) copy-start(f32[576,128]{1,0:T(8,128)S(1)} %collective-permute-done.10) | copy-start | bytes 884740
  112.1 0.7 copy-start.11

commit v13 on v11

--- a/solution.py
+++ b/solution.py
@@ -198,7 +198,7 @@
         for copy in copies[k]:
             copy.wait()
 
-    planes, rows, lanes = p_ref.shape
+    planes, rows, lanes = s_ref.shape[0] + 2, s_ref.shape[1], s_ref.shape[2]
     species, inner = c_ref.shape[0], c_ref.shape[1] - 2
     hz = (planes - inner) // 2
     hy = (rows - co_ref.shape[2]) // 2
@@ -214,12 +214,12 @@
         return pltpu.roll(a, (-d) % lanes, 1)
 
     def weights(z, carry):
-        pc = p_ref[z]
+        pc = p_ref[z, 8:88]
         ws = (
-            0.5 * (pc + p_ref[z + 1]),
-            0.5 * (pc + p_ref[z - 1]),
-            0.5 * (pc + ysh(pc, 1)),
-            0.5 * (pc + ysh(pc, -1)),
+            0.5 * (pc + p_ref[z + 1, 8:88]),
+            0.5 * (pc + p_ref[z - 1, 8:88]),
+            0.5 * (pc + p_ref[z, pl.ds(9, rows)]),
+            0.5 * (pc + p_ref[z, pl.ds(7, rows)]),
             0.5 * (pc + jnp.where(top, pc, xsh(pc, 1))),
             0.5 * (pc + jnp.where(bot, pc, xsh(pc, -1))),
         )
@@ -236,6 +236,9 @@
 
     wait(1)
     wait(2)
+    edge = jnp.zeros((planes, 8, lanes), jnp.float32)
+    p_ref[:, 0:8, :] = edge
+    p_ref[:, 88:96, :] = edge
     lax.fori_loop(1, planes - 1, weights, 0, unroll=2)
     wait(0)
     pad = jnp.zeros((planes, 8, lanes), jnp.float32)
@@ -295,7 +298,7 @@
     planes = inner + 2 * field_p[7]
     rows = out_rows + 2 * (SWEEPS + 2)
     plan, operands, boxes = [], [], []
-    for pieces, r0 in ((field_p, 8), (perm_p, 0), (source_p, 0), (species_p, 0)):
+    for pieces, r0 in ((field_p, 8), (perm_p, 8), (source_p, 0), (species_p, 0)):
         inner_arr, z_lo, z_hi, y_lo, y_hi, z_off, y_off, wz = pieces
         lead = inner_arr.shape[0] if inner_arr.ndim == 4 else 1
         plan.append((lead, z_off, y_off, wz, r0))

time: 122 us -> 122 us (level)
  no operation moved by 1% of the time
where the time goes in v13:
time: 122 us; the launch traced here: 121 us
  starting transfers between devices  29.2 us (24%)
  waiting for transfers between devices  25.5 us (21%)
  Pallas kernels  24.1 us (20%)
  other arithmetic  22.1 us (18%)
  blocking collectives  10.5 us (9%)
  local copies, waits for them, and re-layouts  7.45 us (6%)
  between operations  1.99 us (2%)
    ppermute x12, starting transfers between devices, ring(): lax.ppermute(x, axis, [(i, (i + shift) % count) for i in range(count)])  29.2 us
    ppermute x12, waiting for transfers between devices, ring(): lax.ppermute(x, axis, [(i, (i + shift) % count) for i in range(count)])  25.5 us
    pallas_call x2, Pallas kernels, time_step(): pl.pallas_call(functools.partial(step_kernel, tuple(plan), with_source),...  24.1 us
    reduce_sum x1, other arithmetic, one_block(): return jnp.sum(jnp.where(adjacent, term, 0.0), axis=1)  18.2 us
    all_gather x1, blocking collectives, per_device(): gathered = lax.all_gather(charges, 'narrow', axis=1, tiled=True)  10.5 us
    unnamed x46, local copies, waits for them, and re-layouts  4.13 us
    slice x7, local copies, waits for them, and re-layouts, deep_halo(): bots.append(lax.slice_in_dim(a, 0, wz, axis=dim))  3.15 us
  transfers between devices with their start and end apart: 12, of which 4 were waited for; matrix products, arithmetic and copies ran while one was open for 17% of the time, Pallas kernels for 0%

profile of v13, /device:TPU:1, one launch (start us, length us, event | category | flops | bytes accessed | tf_op | source)
XLA Modules:
  0.0 121.5 jit_solution(11146943306070372316)
XLA Ops:
  0.6 0.0 copy-start.10
  0.6 0.7 convert_element_type.29
  1.4 0.8 pad_maximum_fusion.24
  2.2 0.0 copy-start.5
  2.2 10.5 %all_gather.3 = f32[5,8192]{1,0:T(8,128)S(1)} all-gather(f32[5,2048]{1,0:T(8,128)S(1)} %pad_maximum_fusion.24), channel_id=1, replica_groups=mesh['wide'=64,'narrow'=4] {'narrow'}, dimensions={1}, use_global_device_ids=true | all-gather | bytes 204800 | tf_op jit(solution)/shard_map/all_gather | solution.py:382
  12.7 1.0 fusion.41
  13.7 0.0 copy-done.10
  13.7 0.0 copy-done.5
  13.8 0.8 pad_maximum_fusion
  14.6 0.0 collective-permute-start
  14.6 0.8 pad_maximum_fusion.1
  15.5 7.0 %collective-permute-start.1 = (f32[1088,128]{1,0:T(8,128)}, f32[1088,128]{1,0:T(8,128)S(1)}, u32[]{:S(2)}, u32[]{:S(2)}) collective-permute-start(f32[1088,128]{1,0:T(8,128)} %pad_maximum_fusion.1), channel_id=1, source_target_pairs={{0,252},{4,0},{8,4},{12,8},{16,12},{20,16},{24,20},{28,24},{32,28}... | collective-permute-start | bytes 1671176 | tf_op jit(solution)/shard_map/ppermute | solution.py:125
  23.2 0.0 copy-done.22
  23.2 0.0 copy-start.20
  23.2 0.0 copy-done.21
  23.3 0.0 copy-done.4
  23.3 0.1 multiply_reduce_fusion
  23.4 0.1 fusion.47
  23.6 18.2 %select_reduce_fusion.1 = (f32[256]{0:T(256)S(1)}, f32[256]{0:T(256)S(1)}) fusion(f32[8192]{0:T(1024)S(1)} %bitcast.137, f32[256]{0:T(256)S(1)} %get-tuple-element.79, f32[8192]{0:T(1024)S(1)} %bitcast.138, f32[256]{0:T(256)S(1)} %get-tuple-element.68, f32[8192]{0:T(1024)S(1)} %bitcast.139, f32[256]{0:T(256)S(1)} %get-tuple-element.77, ...), kind=kLoop, calls=%fused_computation.20 | loop fusion | flops 104857088 | bytes 174080 | tf_op jit(solution)/shard_map/reduce_sum | solution.py:116
  41.8 0.0 copy-done.20
  41.8 0.8 fusion.18
  42.6 0.0 copy-start.15
  42.6 0.0 copy-start.6
  42.7 0.6 copy-done.15
  43.3 0.0 collective-permute-start.4
  43.3 5.7 %collective-permute-start.5 = (f32[384,128]{1,0:T(8,128)S(1)}, f32[384,128]{1,0:T(8,128)S(1)}, u32[]{:S(2)}, u32[]{:S(2)}) collective-permute-start(f32[384,128]{1,0:T(8,128)S(1)} %bitcast.132), channel_id=1, source_target_pairs={{0,252},{4,0},{8,4},{12,8},{16,12},{20,16},{24,20},{28,24},{32,28}... | collective-permute-start | bytes 589832 | tf_op jit(solution)/shard_map/ppermute | solution.py:125
  49.0 0.0 collective-permute-done
  49.0 0.0 collective-permute-done.1
  49.0 0.0 copy-start.1
  49.0 0.7 copy-done
  49.8 0.1 copy-done.1
  50.0 3.6 %collective-permute-start.2 = (f32[592,128]{1,0:T(8,128)S(1)}, f32[592,128]{1,0:T(8,128)S(1)}, u32[]{:S(2)}, u32[]{:S(2)}) collective-permute-start(f32[592,128]{1,0:T(8,128)S(1)} %pad_maximum_fusion.4), channel_id=1, source_target_pairs={{0,1},{1,2},{2,3},{3,0},{4,5},{5,6},{6,7},{7,4},{8,9},{9,10},{10,1... | collective-permute-start | bytes 909320 | tf_op jit(solution)/shard_map/ppermute | solution.py:125
  53.6 0.1 collective-permute-start.3
  53.7 0.0 collective-permute-done.4
  53.7 0.0 copy-start.16
  53.8 0.0 collective-permute-done.5
  53.8 1.1 collective-permute-start.7
  54.9 2.7 %collective-permute-start.6 = (f32[160,128]{1,0:T(8,128)S(1)}, f32[160,128]{1,0:T(8,128)S(1)}, u32[]{:S(2)}, u32[]{:S(2)}) collective-permute-start(f32[160,128]{1,0:T(8,128)S(1)} %get-tuple-element.43), channel_id=1, source_target_pairs={{0,1},{1,2},{2,3},{3,0},{4,5},{5,6},{6,7},{7,4},{8,9},{9,10},{10,1... | collective-permute-start | bytes 245768 | tf_op jit(solution)/shard_map/ppermute | solution.py:125
  57.6 6.4 %collective-permute-done.7 = f32[160,128]{1,0:T(8,128)S(1)} collective-permute-done((f32[160,128]{1,0:T(8,128)S(1)}, f32[160,128]{1,0:T(8,128)S(1)}, u32[]{:S(2)}, u32[]{:S(2)}) %collective-permute-start.7) | collective-permute-done | bytes 81952 | tf_op jit(solution)/shard_map/ppermute | solution.py:125
  64.0 0.0 collective-permute-done.6
  64.0 0.0 collective-permute-done.2
  64.0 0.0 collective-permute-done.3
  64.0 0.6 copy-done.18
  64.6 0.0 copy-done.19
  64.6 0.1 copy-done.7
  64.8 0.1 copy-done.8
  64.9 12.2 %shard_map.113 = (f32[8,64,128]{2,1,0:T(8,128)}, f32[3,8,64,128]{3,2,1,0:T(8,128)}, f32[8,64,128]{2,1,0:T(8,128)}) custom-call(f32[3]{0:T(128)} %dif_ref.3, f32[3]{0:T(128)} %copy-done.20, f32[8,64,128]{2,1,0:T(8,128)} %refs_0_, f32[17,64,128]{2,1,0:T(8,128)} %bitcast.70, f32[17,64,128]{2,1,0:T(8,128)} %bitcast.74, f32[74,8,128]{2,1,0:T(8,128)} %bitcast.84, ...), custom_call_target="tpu_custom_call" | custom-call | flops 40755200 | bytes 4538368 | tf_op jit(solution)/shard_map/pallas_call | solution.py:322
  77.1 0.0 copy-start.11
  77.1 1.0 fusion.40
  78.1 1.0 fusion.45
  79.2 0.0 copy-done.11
  79.3 0.0 copy-start.9
  79.3 0.1 collective-permute-start.8
  79.4 5.7 %collective-permute-start.9 = (f32[1024,128]{1,0:T(8,128)S(1)}, f32[1024,128]{1,0:T(8,128)S(1)}, u32[]{:S(2)}, u32[]{:S(2)}) collective-permute-start(f32[1024,128]{1,0:T(8,128)S(1)} %pad_maximum_fusion.3), channel_id=1, source_target_pairs={{0,252},{4,0},{8,4},{12,8},{16,12},{20,16},{24,20},{28,24},{32,28}... | collective-permute-start | bytes 1572872 | tf_op jit(solution)/shard_map/ppermute | solution.py:125
  85.2 11.5 %collective-permute-done.8 = f32[1024,128]{1,0:T(8,128)S(1)} collective-permute-done((f32[1024,128]{1,0:T(8,128)S(1)}, f32[1024,128]{1,0:T(8,128)S(1)}, u32[]{:S(2)}, u32[]{:S(2)}) %collective-permute-start.8) | collective-permute-done | bytes 524320 | tf_op jit(solution)/shard_map/ppermute | solution.py:125
  96.7 0.0 collective-permute-done.9
  96.8 1.1 copy-done.12
  97.9 0.0 copy-done.3
  98.0 3.1 %collective-permute-start.10 = (f32[576,128]{1,0:T(8,128)S(1)}, f32[576,128]{1,0:T(8,128)S(1)}, u32[]{:S(2)}, u32[]{:S(2)}) collective-permute-start(f32[576,128]{1,0:T(8,128)S(1)} %pad_maximum_fusion.6), channel_id=1, source_target_pairs={{0,1},{1,2},{2,3},{3,0},{4,5},{5,6},{6,7},{7,4},{8,9},{9,10},{10,1... | collective-permute-start | bytes 884744 | tf_op jit(solution)/shard_map/ppermute | solution.py:125
  101.1 0.1 collective-permute-start.11
  101.1 6.0 %collective-permute-done.10 = f32[576,128]{1,0:T(8,128)S(1)} collective-permute-done((f32[576,128]{1,0:T(8,128)S(1)}, f32[576,128]{1,0:T(8,128)S(1)}, u32[]{:S(2)}, u32[]{:S(2)}) %collective-permute-start.10) | collective-permute-done | bytes 294944 | tf_op jit(solution)/shard_map/ppermute | solution.py:125
  107.2 1.6 %collective-permute-done.11 = f32[576,128]{1,0:T(8,128)S(1)} collective-permute-done((f32[576,128]{1,0:T(8,128)S(1)}, f32[576,128]{1,0:T(8,128)S(1)}, u32[]{:S(2)}, u32[]{:S(2)}) %collective-permute-start.11) | collective-permute-done | bytes 294944 | tf_op jit(solution)/shard_map/ppermute | solution.py:125
  108.8 0.7 copy-done.14
  109.5 11.8 %shard_map.114 = (f32[8,64,128]{2,1,0:T(8,128)}, f32[3,8,64,128]{3,2,1,0:T(8,128)}) custom-call(f32[3]{0:T(128)} %dif_ref.3, f32[3]{0:T(128)} %copy-done.20, f32[8,64,128]{2,1,0:T(8,128)} %get-tuple-element.15.refs_0_, f32[16,64,128]{2,1,0:T(8,128)} %bitcast.78, f32[16,64,128]{2,1,0:T(8,128)} %bitcast.81, f32[72,8,128]{2,1,0:T(8,128)} %bitcast.92, ...), custom_call_target="tpu_custom_call" | custom-call | flops 40755200 | bytes 4538368 | tf_op jit(solution)/shard_map/pallas_call | solution.py:322
  (53 shorter events, 0.7 us)
Async XLA Ops:
  0.6 13.0 %copy-start.10 = (f32[8,64,128]{2,1,0:T(8,128)S(1)}, f32[8,64,128]{2,1,0:T(8,128)}, u32[]{:S(2)}) copy-start(f32[8,64,128]{2,1,0:T(8,128)} %refs_0_) | copy-start | bytes 786436
  2.2 11.5 %copy-start.5 = (f32[8,64,128]{2,1,0:T(8,128)S(1)}, f32[8,64,128]{2,1,0:T(8,128)}, u32[]{:S(2)}) copy-start(f32[8,64,128]{2,1,0:T(8,128)} %refs_5_.1) | copy-start | bytes 786436
  14.6 8.6 %copy-start.22 = (s32[3]{0:T(128)S(1)}, s32[3]{0:T(128)}, u32[]{:S(2)}) copy-start(s32[3]{0:T(128)} %param.14) | copy-start | bytes 40
  14.6 8.6 %copy-start.21 = (s32[1,1,512]{2,1,0:T(1,128)S(1)}, s32[1,1,512]{2,1,0:T(1,128)}, u32[]{:S(2)}) copy-start(s32[1,1,512]{2,1,0:T(1,128)} %param.18) | copy-start | bytes 6148
  14.6 8.7 %copy-start.4 = (f32[3,8,64,128]{3,2,1,0:T(8,128)S(1)}, f32[3,8,64,128]{3,2,1,0:T(8,128)}, u32[]{:S(2)}) copy-start(f32[3,8,64,128]{3,2,1,0:T(8,128)} %refs_15_) | copy-start | bytes 2359300
  14.6 34.3 %collective-permute-start = (f32[1088,128]{1,0:T(8,128)}, f32[1088,128]{1,0:T(8,128)S(1)}, u32[]{:S(2)}, u32[]{:S(2)}) collective-permute-start(f32[1088,128]{1,0:T(8,128)} %pad_maximum_fusion), channel_id=1, source_target_pairs={{0,4},{4,8},{8,12},{12,16},{16,20},{20,24},{24,28},{28,32},{32,36}... | collective-permute-start | bytes 1671176 | tf_op jit(solution)/shard_map/ppermute | solution.py:125
  15.5 33.5 %collective-permute-start.1 = (f32[1088,128]{1,0:T(8,128)}, f32[1088,128]{1,0:T(8,128)S(1)}, u32[]{:S(2)}, u32[]{:S(2)}) collective-permute-start(f32[1088,128]{1,0:T(8,128)} %pad_maximum_fusion.1), channel_id=1, source_target_pairs={{0,252},{4,0},{8,4},{12,8},{16,12},{20,16},{24,20},{28,24},{32,28}... | collective-permute-start | bytes 1671176 | tf_op jit(solution)/shard_map/ppermute | solution.py:125
  23.2 18.6 %copy-start.20 = (f32[3]{0:T(128)}, f32[3]{0:T(128)S(1)}, u32[]{:S(2)}) copy-start(f32[3]{0:T(128)S(1)} %convert_element_type.28.val_ref) | copy-start | bytes 40
  42.6 0.7 copy-start.15
  42.6 11.2 %copy-start.6 = (f32[8,64,128]{2,1,0:T(8,128)}, f32[8,64,128]{2,1,0:T(8,128)S(1)}, u32[]{:S(2)}) copy-start(f32[8,64,128]{2,1,0:T(8,128)S(1)} %add.88.refs_10_) | copy-start | bytes 786436
  43.3 10.5 %collective-permute-start.4 = (f32[384,128]{1,0:T(8,128)S(1)}, f32[384,128]{1,0:T(8,128)S(1)}, u32[]{:S(2)}, u32[]{:S(2)}) collective-permute-start(f32[384,128]{1,0:T(8,128)S(1)} %bitcast.133), channel_id=1, source_target_pairs={{0,4},{4,8},{8,12},{12,16},{16,20},{20,24},{24,28},{28,32},{32,36}... | collective-permute-start | bytes 589832 | tf_op jit(solution)/shard_map/ppermute | solution.py:125
  43.3 10.5 %collective-permute-start.5 = (f32[384,128]{1,0:T(8,128)S(1)}, f32[384,128]{1,0:T(8,128)S(1)}, u32[]{:S(2)}, u32[]{:S(2)}) collective-permute-start(f32[384,128]{1,0:T(8,128)S(1)} %bitcast.132), channel_id=1, source_target_pairs={{0,252},{4,0},{8,4},{12,8},{16,12},{20,16},{24,20},{28,24},{32,28}... | collective-permute-start | bytes 589832 | tf_op jit(solution)/shard_map/ppermute | solution.py:125
  49.0 0.8 copy-start
  49.0 1.0 copy-start.1
  50.0 14.0 %collective-permute-start.2 = (f32[592,128]{1,0:T(8,128)S(1)}, f32[592,128]{1,0:T(8,128)S(1)}, u32[]{:S(2)}, u32[]{:S(2)}) collective-permute-start(f32[592,128]{1,0:T(8,128)S(1)} %pad_maximum_fusion.4), channel_id=1, source_target_pairs={{0,1},{1,2},{2,3},{3,0},{4,5},{5,6},{6,7},{7,4},{8,9},{9,10},{10,1... | collective-permute-start | bytes 909320 | tf_op jit(solution)/shard_map/ppermute | solution.py:125
  53.6 10.4 %collective-permute-start.3 = (f32[592,128]{1,0:T(8,128)S(1)}, f32[592,128]{1,0:T(8,128)S(1)}, u32[]{:S(2)}, u32[]{:S(2)}) collective-permute-start(f32[592,128]{1,0:T(8,128)S(1)} %pad_maximum_fusion.5), channel_id=1, source_target_pairs={{0,3},{1,0},{2,1},{3,2},{4,7},{5,4},{6,5},{7,6},{8,11},{9,8},{10,9... | collective-permute-start | bytes 909320 | tf_op jit(solution)/shard_map/ppermute | solution.py:125
  53.7 10.3 %copy-start.16 = (f32[384,128]{1,0:T(8,128)}, f32[384,128]{1,0:T(8,128)S(1)}, u32[]{:S(2)}) copy-start(f32[384,128]{1,0:T(8,128)S(1)} %collective-permute-done.4) | copy-start | bytes 589828
  53.8 10.3 %copy-start.17 = (f32[384,128]{1,0:T(8,128)}, f32[384,128]{1,0:T(8,128)S(1)}, u32[]{:S(2)}) copy-start(f32[384,128]{1,0:T(8,128)S(1)} %collective-permute-done.5) | copy-start | bytes 589828
  53.8 10.2 %collective-permute-start.7 = (f32[160,128]{1,0:T(8,128)S(1)}, f32[160,128]{1,0:T(8,128)S(1)}, u32[]{:S(2)}, u32[]{:S(2)}) collective-permute-start(f32[160,128]{1,0:T(8,128)S(1)} %get-tuple-element.42), channel_id=1, source_target_pairs={{0,3},{1,0},{2,1},{3,2},{4,7},{5,4},{6,5},{7,6},{8,11},{9,8},{10,9... | collective-permute-start | bytes 245768 | tf_op jit(solution)/shard_map/ppermute | solution.py:125
  54.9 9.1 %collective-permute-start.6 = (f32[160,128]{1,0:T(8,128)S(1)}, f32[160,128]{1,0:T(8,128)S(1)}, u32[]{:S(2)}, u32[]{:S(2)}) collective-permute-start(f32[160,128]{1,0:T(8,128)S(1)} %get-tuple-element.43), channel_id=1, source_target_pairs={{0,1},{1,2},{2,3},{3,0},{4,5},{5,6},{6,7},{7,4},{8,9},{9,10},{10,1... | collective-permute-start | bytes 245768 | tf_op jit(solution)/shard_map/ppermute | solution.py:125
  64.0 0.6 copy-start.18
  64.0 0.7 copy-start.19
  64.0 0.8 copy-start.7
  64.0 0.8 copy-start.8
  77.1 2.1 %copy-start.11 = (f32[8,64,128]{2,1,0:T(8,128)S(1)}, f32[8,64,128]{2,1,0:T(8,128)}, u32[]{:S(2)}) copy-start(f32[8,64,128]{2,1,0:T(8,128)} %get-tuple-element.15.refs_0_) | copy-start | bytes 786436
  79.3 17.4 %copy-start.9 = (f32[3,8,64,128]{3,2,1,0:T(8,128)S(1)}, f32[3,8,64,128]{3,2,1,0:T(8,128)}, u32[]{:S(2)}) copy-start(f32[3,8,64,128]{3,2,1,0:T(8,128)} %get-tuple-element.17.refs_15_) | copy-start | bytes 2359300
  79.3 17.4 %collective-permute-start.8 = (f32[1024,128]{1,0:T(8,128)S(1)}, f32[1024,128]{1,0:T(8,128)S(1)}, u32[]{:S(2)}, u32[]{:S(2)}) collective-permute-start(f32[1024,128]{1,0:T(8,128)S(1)} %pad_maximum_fusion.2), channel_id=1, source_target_pairs={{0,4},{4,8},{8,12},{12,16},{16,20},{20,24},{24,28},{28,32},{32,36}... | collective-permute-start | bytes 1572872 | tf_op jit(solution)/shard_map/ppermute | solution.py:125
  79.4 17.2 %collective-permute-start.9 = (f32[1024,128]{1,0:T(8,128)S(1)}, f32[1024,128]{1,0:T(8,128)S(1)}, u32[]{:S(2)}, u32[]{:S(2)}) collective-permute-start(f32[1024,128]{1,0:T(8,128)S(1)} %pad_maximum_fusion.3), channel_id=1, source_target_pairs={{0,252},{4,0},{8,4},{12,8},{16,12},{20,16},{24,20},{28,24},{32,28}... | collective-permute-start | bytes 1572872 | tf_op jit(solution)/shard_map/ppermute | solution.py:125
  96.6 1.2 %copy-start.2 = (f32[1024,128]{1,0:T(8,128)}, f32[1024,128]{1,0:T(8,128)S(1)}, u32[]{:S(2)}) copy-start(f32[1024,128]{1,0:T(8,128)S(1)} %collective-permute-done.8) | copy-start | bytes 1572868
  96.7 1.2 %copy-start.3 = (f32[1024,128]{1,0:T(8,128)}, f32[1024,128]{1,0:T(8,128)S(1)}, u32[]{:S(2)}) copy-start(f32[1024,128]{1,0:T(8,128)S(1)} %collective-permute-done.9) | copy-start | bytes 1572868
  96.7 1.1 copy-start.12
  98.0 9.2 %collective-permute-start.10 = (f32[576,128]{1,0:T(8,128)S(1)}, f32[576,128]{1,0:T(8,128)S(1)}, u32[]{:S(2)}, u32[]{:S(2)}) collective-permute-start(f32[576,128]{1,0:T(8,128)S(1)} %pad_maximum_fusion.6), channel_id=1, source_target_pairs={{0,1},{1,2},{2,3},{3,0},{4,5},{5,6},{6,7},{7,4},{8,9},{9,10},{10,1... | collective-permute-start | bytes 884744 | tf_op jit(solution)/shard_map/ppermute | solution.py:125
  101.1 7.7 %collective-permute-start.11 = (f32[576,128]{1,0:T(8,128)S(1)}, f32[576,128]{1,0:T(8,128)S(1)}, u32[]{:S(2)}, u32[]{:S(2)}) collective-permute-start(f32[576,128]{1,0:T(8,128)S(1)} %pad_maximum_fusion.7), channel_id=1, source_target_pairs={{0,3},{1,0},{2,1},{3,2},{4,7},{5,4},{6,5},{7,6},{8,11},{9,8},{10,9... | collective-permute-start | bytes 884744 | tf_op jit(solution)/shard_map/ppermute | solution.py:125
  107.2 1.6 %copy-start.13 = (f32[576,128]{1,0:T(8,128)}, f32[576,128]{1,0:T(8,128)S(1)}, u32[]{:S(2)}) copy-start(f32[576,128]{1,0:T(8,128)S(1)} %collective-permute-done.10) | copy-start | bytes 884740
  108.8 0.7 copy-start.14

commit v14 on v11

--- a/solution.py
+++ b/solution.py
@@ -138,6 +138,7 @@
     z_hi = ring(jnp.concatenate([t.reshape(-1, minor) for t in bots], axis=0), axis_z, -1)
     y_tops, y_bots, z_offs, at = [], [], [], 0
     for (a, wz, wy), t in zip(items, tops):
+        wy = 1 if a.ndim == 4 else wy
         size = t.size // minor
         z_offs.append(at // rows)
         ext = jnp.concatenate(
@@ -147,19 +148,30 @@
         y_tops.append(ext[..., rows - wy:rows, :])
         y_bots.append(ext[..., 0:wy, :])
     wy = items[0][2]
-    y_lo = ring(jnp.concatenate([t.reshape(-1, minor) for t in y_tops], axis=0), axis_y, 1)
-    y_hi = ring(jnp.concatenate([t.reshape(-1, minor) for t in y_bots], axis=0), axis_y, -1)
+
+    def pack(parts):
+        flat = [t.reshape(-1, minor) for t in parts]
+        flat = [jnp.pad(f, ((0, -f.shape[0] % wy), (0, 0))) for f in flat]
+        return jnp.concatenate(flat, axis=0)
+
+    y_lo = ring(pack(y_tops), axis_y, 1)
+    y_hi = ring(pack(y_bots), axis_y, -1)
     y_offs, at = [], 0
     for t in y_tops:
-        y_offs.append(at // wy)
-        at += t.size // minor
+        y_offs.append(at if t.ndim == 4 else at // wy)
+        at += -(-(t.size // minor) // wy) * wy
     bufs = (
         z_lo.reshape(-1, rows, minor),
         z_hi.reshape(-1, rows, minor),
         y_lo.reshape(-1, wy, minor),
         y_hi.reshape(-1, wy, minor),
     )
-    return [(a,) + bufs + (zo, yo, wz) for (a, wz, _), zo, yo in zip(items, z_offs, y_offs)]
+    thin = (y_lo.reshape(-1, 1, minor), y_hi.reshape(-1, 1, minor))
+    out = []
+    for (a, wz, _), zo, yo in zip(items, z_offs, y_offs):
+        y_pair = thin if a.ndim == 4 else bufs[2:]
+        out.append((a,) + bufs[:2] + y_pair + (zo, yo, wz))
+    return out
 
 
 def step_kernel(plan, with_source, dif_ref, val_ref, *refs):
@@ -185,8 +197,8 @@
             moves += [
                 (z_lo.at[zs], part.at[0:wz, mid, :]),
                 (z_hi.at[zs], part.at[span - wz:span, mid, :]),
-                (y_lo.at[ys], part.at[:, r0:r0 + 8, :]),
-                (y_hi.at[ys], part.at[:, mid.stop:mid.stop + 8, :]),
+                (y_lo.at[ys], part.at[:, r0 + 8 - y_lo.shape[1]:r0 + 8, :]),
+                (y_hi.at[ys], part.at[:, mid.stop:mid.stop + y_hi.shape[1], :]),
             ]
         for src, dst in moves:
             copy = pltpu.make_async_copy(src, dst, sems.at[count])

time: 122 us -> 119 us (0.975)
  waiting for transfers between devices: 25.5 us -> 21.8 us
    ppermute x12, waiting for transfers between devices: 25.5 us -> 21.8 us  [ring(): lax.ppermute(x, axis, [(i, (i + shift) % count) for i in range(count)])]
  transfers between devices with their start and end apart: 12 -> 12, of which waited for: 4 -> 4; matrix products, arithmetic and copies ran while one was open for 17% -> 18% of each run, Pallas kernels for 0% -> 0%
where the time goes in v14:
time: 119 us; the launch traced here: 118 us
  starting transfers between devices  29.7 us (25%)
  Pallas kernels  24.1 us (20%)
  other arithmetic  22.1 us (19%)
  waiting for transfers between devices  21.8 us (18%)
  blocking collectives  10.5 us (9%)
  local copies, waits for them, and re-layouts  7.38 us (6%)
  between operations  2.02 us (2%)
    ppermute x12, starting transfers between devices, ring(): lax.ppermute(x, axis, [(i, (i + shift) % count) for i in range(count)])  29.7 us
    pallas_call x2, Pallas kernels, time_step(): pl.pallas_call(functools.partial(step_kernel, tuple(plan), with_source),...  24.1 us
    ppermute x12, waiting for transfers between devices, ring(): lax.ppermute(x, axis, [(i, (i + shift) % count) for i in range(count)])  21.8 us
    reduce_sum x1, other arithmetic, one_block(): return jnp.sum(jnp.where(adjacent, term, 0.0), axis=1)  18.2 us
    all_gather x1, blocking collectives, per_device(): gathered = lax.all_gather(charges, 'narrow', axis=1, tiled=True)  10.5 us
    slice x7, local copies, waits for them, and re-layouts, deep_halo(): bots.append(lax.slice_in_dim(a, 0, wz, axis=dim))  3.9 us
    unnamed x46, local copies, waits for them, and re-layouts  3.3 us
  transfers between devices with their start and end apart: 12, of which 4 were waited for; matrix products, arithmetic and copies ran while one was open for 18% of the time, Pallas kernels for 0%

profile of v14, /device:TPU:1, one launch (start us, length us, event | category | flops | bytes accessed | tf_op | source)
XLA Modules:
  0.0 118.4 jit_solution(11878447467167876150)
XLA Ops:
  0.6 0.0 copy-start.8
  0.6 0.7 convert_element_type.34
  1.4 0.8 pad_maximum_fusion.14
  2.2 0.0 copy-start.5
  2.2 10.5 %all_gather.3 = f32[5,8192]{1,0:T(8,128)S(1)} all-gather(f32[5,2048]{1,0:T(8,128)S(1)} %pad_maximum_fusion.14), channel_id=1, replica_groups=mesh['wide'=64,'narrow'=4] {'narrow'}, dimensions={1}, use_global_device_ids=true | all-gather | bytes 204800 | tf_op jit(solution)/shard_map/all_gather | solution.py:391
  12.7 1.0 fusion.43
  13.7 0.0 copy-done.8
  13.7 0.0 copy-done.5
  13.8 0.8 pad_maximum_fusion
  14.6 0.0 collective-permute-start
  14.6 0.8 pad_maximum_fusion.1
  15.5 7.0 %collective-permute-start.1 = (f32[1088,128]{1,0:T(8,128)}, f32[1088,128]{1,0:T(8,128)S(1)}, u32[]{:S(2)}, u32[]{:S(2)}) collective-permute-start(f32[1088,128]{1,0:T(8,128)} %pad_maximum_fusion.1), channel_id=1, source_target_pairs={{0,252},{4,0},{8,4},{12,8},{16,12},{20,16},{24,20},{28,24},{32,28}... | collective-permute-start | bytes 1671176 | tf_op jit(solution)/shard_map/ppermute | solution.py:125
  23.2 0.0 copy-done.22
  23.2 0.0 copy-start.20
  23.2 0.0 copy-done.21
  23.3 0.0 copy-done.4
  23.3 0.1 multiply_reduce_fusion
  23.4 0.1 fusion.49
  23.6 18.2 %select_reduce_fusion.1 = (f32[256]{0:T(256)S(1)}, f32[256]{0:T(256)S(1)}) fusion(f32[8192]{0:T(1024)S(1)} %bitcast.132, f32[256]{0:T(256)S(1)} %get-tuple-element.79, f32[8192]{0:T(1024)S(1)} %bitcast.133, f32[256]{0:T(256)S(1)} %get-tuple-element.68, f32[8192]{0:T(1024)S(1)} %bitcast.134, f32[256]{0:T(256)S(1)} %get-tuple-element.77, ...), kind=kLoop, calls=%fused_computation.20 | loop fusion | flops 104857088 | bytes 174080 | tf_op jit(solution)/shard_map/reduce_sum | solution.py:116
  41.8 0.0 copy-done.20
  41.8 0.8 fusion.18
  42.6 0.0 copy-start.15
  42.6 0.0 copy-start.6
  42.6 0.8 fusion.48
  43.4 0.0 collective-permute-start.4
  43.4 5.7 %collective-permute-start.5 = (f32[384,128]{1,0:T(8,128)S(1)}, f32[384,128]{1,0:T(8,128)S(1)}, u32[]{:S(2)}, u32[]{:S(2)}) collective-permute-start(f32[384,128]{1,0:T(8,128)S(1)} %bitcast.128), channel_id=1, source_target_pairs={{0,252},{4,0},{8,4},{12,8},{16,12},{20,16},{24,20},{28,24},{32,28}... | collective-permute-start | bytes 589832 | tf_op jit(solution)/shard_map/ppermute | solution.py:125
  49.1 0.0 collective-permute-done
  49.1 0.0 collective-permute-done.1
  49.2 0.1 fusion.30
  49.3 0.6 copy-done
  49.9 0.2 copy-done.1
  50.2 3.6 %collective-permute-start.2 = (f32[384,128]{1,0:T(8,128)S(1)}, f32[384,128]{1,0:T(8,128)S(1)}, u32[]{:S(2)}, u32[]{:S(2)}) collective-permute-start(f32[384,128]{1,0:T(8,128)S(1)} %select_maximum_fusion.1), channel_id=1, source_target_pairs={{0,1},{1,2},{2,3},{3,0},{4,5},{5,6},{6,7},{7,4},{8,9},{9,10},{10,1... | collective-permute-start | bytes 589832 | tf_op jit(solution)/shard_map/ppermute | solution.py:125
  53.8 0.1 collective-permute-start.3
  53.9 0.0 collective-permute-done.4
  53.9 0.0 copy-start.16
  53.9 0.0 collective-permute-done.5
  54.0 1.3 %collective-permute-start.7 = (f32[160,128]{1,0:T(8,128)S(1)}, f32[160,128]{1,0:T(8,128)S(1)}, u32[]{:S(2)}, u32[]{:S(2)}) collective-permute-start(f32[160,128]{1,0:T(8,128)S(1)} %get-tuple-element.42), channel_id=1, source_target_pairs={{0,3},{1,0},{2,1},{3,2},{4,7},{5,4},{6,5},{7,6},{8,11},{9,8},{10,9... | collective-permute-start | bytes 245768 | tf_op jit(solution)/shard_map/ppermute | solution.py:125
  55.3 2.7 %collective-permute-start.6 = (f32[160,128]{1,0:T(8,128)S(1)}, f32[160,128]{1,0:T(8,128)S(1)}, u32[]{:S(2)}, u32[]{:S(2)}) collective-permute-start(f32[160,128]{1,0:T(8,128)S(1)} %get-tuple-element.43), channel_id=1, source_target_pairs={{0,1},{1,2},{2,3},{3,0},{4,5},{5,6},{6,7},{7,4},{8,9},{9,10},{10,1... | collective-permute-start | bytes 245768 | tf_op jit(solution)/shard_map/ppermute | solution.py:125
  58.0 4.2 %collective-permute-done.7 = f32[160,128]{1,0:T(8,128)S(1)} collective-permute-done((f32[160,128]{1,0:T(8,128)S(1)}, f32[160,128]{1,0:T(8,128)S(1)}, u32[]{:S(2)}, u32[]{:S(2)}) %collective-permute-start.7) | collective-permute-done | bytes 81952 | tf_op jit(solution)/shard_map/ppermute | solution.py:125
  62.1 0.0 collective-permute-done.6
  62.1 0.0 collective-permute-done.2
  62.2 0.0 collective-permute-done.3
  62.2 0.6 copy-done.18
  62.8 0.0 copy-done.19
  62.8 0.1 copy-done.11
  62.9 0.1 copy-done.12
  62.9 12.2 %shard_map.113 = (f32[8,64,128]{2,1,0:T(8,128)}, f32[3,8,64,128]{3,2,1,0:T(8,128)}, f32[8,64,128]{2,1,0:T(8,128)}) custom-call(f32[3]{0:T(128)} %dif_ref.3, f32[3]{0:T(128)} %copy-done.20, f32[8,64,128]{2,1,0:T(8,128)} %refs_0_, f32[17,64,128]{2,1,0:T(8,128)} %bitcast.70, f32[17,64,128]{2,1,0:T(8,128)} %bitcast.74, f32[48,8,128]{2,1,0:T(8,128)} %bitcast.84, ...), custom_call_target="tpu_custom_call" | custom-call | flops 40755200 | bytes 4538368 | tf_op jit(solution)/shard_map/pallas_call | solution.py:331
  75.2 0.0 copy-start.9
  75.2 1.0 fusion.42
  76.2 1.0 fusion.47
  77.4 0.1 collective-permute-start.8
  77.5 5.7 %collective-permute-start.9 = (f32[1024,128]{1,0:T(8,128)S(1)}, f32[1024,128]{1,0:T(8,128)S(1)}, u32[]{:S(2)}, u32[]{:S(2)}) collective-permute-start(f32[1024,128]{1,0:T(8,128)S(1)} %pad_maximum_fusion.3), channel_id=1, source_target_pairs={{0,252},{4,0},{8,4},{12,8},{16,12},{20,16},{24,20},{28,24},{32,28}... | collective-permute-start | bytes 1572872 | tf_op jit(solution)/shard_map/ppermute | solution.py:125
  83.2 11.1 %collective-permute-done.8 = f32[1024,128]{1,0:T(8,128)S(1)} collective-permute-done((f32[1024,128]{1,0:T(8,128)S(1)}, f32[1024,128]{1,0:T(8,128)S(1)}, u32[]{:S(2)}, u32[]{:S(2)}) %collective-permute-start.8) | collective-permute-done | bytes 524320 | tf_op jit(solution)/shard_map/ppermute | solution.py:125
  94.4 0.0 collective-permute-done.9
  94.4 0.1 fusion.29
  94.6 1.0 copy-done.10
  95.6 0.0 copy-done.2
  95.7 3.4 %collective-permute-start.10 = (f32[368,128]{1,0:T(8,128)S(1)}, f32[368,128]{1,0:T(8,128)S(1)}, u32[]{:S(2)}, u32[]{:S(2)}) collective-permute-start(f32[368,128]{1,0:T(8,128)S(1)} %select_maximum_fusion.3), channel_id=1, source_target_pairs={{0,1},{1,2},{2,3},{3,0},{4,5},{5,6},{6,7},{7,4},{8,9},{9,10},{10,1... | collective-permute-start | bytes 565256 | tf_op jit(solution)/shard_map/ppermute | solution.py:125
  99.1 0.1 collective-permute-start.11
  99.2 2.4 %collective-permute-done.10 = f32[368,128]{1,0:T(8,128)S(1)} collective-permute-done((f32[368,128]{1,0:T(8,128)S(1)}, f32[368,128]{1,0:T(8,128)S(1)}, u32[]{:S(2)}, u32[]{:S(2)}) %collective-permute-start.10) | collective-permute-done | bytes 188448 | tf_op jit(solution)/shard_map/ppermute | solution.py:125
  101.6 4.1 %collective-permute-done.11 = f32[368,128]{1,0:T(8,128)S(1)} collective-permute-done((f32[368,128]{1,0:T(8,128)S(1)}, f32[368,128]{1,0:T(8,128)S(1)}, u32[]{:S(2)}, u32[]{:S(2)}) %collective-permute-start.11) | collective-permute-done | bytes 188448 | tf_op jit(solution)/shard_map/ppermute | solution.py:125
  105.7 0.0 copy-done.13
  105.7 0.7 copy-done.14
  106.4 11.8 %shard_map.114 = (f32[8,64,128]{2,1,0:T(8,128)}, f32[3,8,64,128]{3,2,1,0:T(8,128)}) custom-call(f32[3]{0:T(128)} %dif_ref.3, f32[3]{0:T(128)} %copy-done.20, f32[8,64,128]{2,1,0:T(8,128)} %get-tuple-element.15.refs_0_, f32[16,64,128]{2,1,0:T(8,128)} %bitcast.78, f32[16,64,128]{2,1,0:T(8,128)} %bitcast.81, f32[46,8,128]{2,1,0:T(8,128)} %bitcast.92, ...), custom_call_target="tpu_custom_call" | custom-call | flops 40755200 | bytes 4538368 | tf_op jit(solution)/shard_map/pallas_call | solution.py:331
  (57 shorter events, 0.6 us)
Async XLA Ops:
  0.6 13.0 %copy-start.8 = (f32[8,64,128]{2,1,0:T(8,128)S(1)}, f32[8,64,128]{2,1,0:T(8,128)}, u32[]{:S(2)}) copy-start(f32[8,64,128]{2,1,0:T(8,128)} %refs_0_) | copy-start | bytes 786436
  2.2 11.5 %copy-start.5 = (f32[8,64,128]{2,1,0:T(8,128)S(1)}, f32[8,64,128]{2,1,0:T(8,128)}, u32[]{:S(2)}) copy-start(f32[8,64,128]{2,1,0:T(8,128)} %refs_5_.1) | copy-start | bytes 786436
  14.6 8.6 %copy-start.22 = (s32[3]{0:T(128)S(1)}, s32[3]{0:T(128)}, u32[]{:S(2)}) copy-start(s32[3]{0:T(128)} %param.14) | copy-start | bytes 40
  14.6 8.6 %copy-start.21 = (s32[1,1,512]{2,1,0:T(1,128)S(1)}, s32[1,1,512]{2,1,0:T(1,128)}, u32[]{:S(2)}) copy-start(s32[1,1,512]{2,1,0:T(1,128)} %param.18) | copy-start | bytes 6148
  14.6 8.6 %copy-start.4 = (f32[3,8,64,128]{3,2,1,0:T(8,128)S(1)}, f32[3,8,64,128]{3,2,1,0:T(8,128)}, u32[]{:S(2)}) copy-start(f32[3,8,64,128]{3,2,1,0:T(8,128)} %refs_15_) | copy-start | bytes 2359300
  14.6 34.5 %collective-permute-start = (f32[1088,128]{1,0:T(8,128)}, f32[1088,128]{1,0:T(8,128)S(1)}, u32[]{:S(2)}, u32[]{:S(2)}) collective-permute-start(f32[1088,128]{1,0:T(8,128)} %pad_maximum_fusion), channel_id=1, source_target_pairs={{0,4},{4,8},{8,12},{12,16},{16,20},{20,24},{24,28},{28,32},{32,36}... | collective-permute-start | bytes 1671176 | tf_op jit(solution)/shard_map/ppermute | solution.py:125
  15.5 33.6 %collective-permute-start.1 = (f32[1088,128]{1,0:T(8,128)}, f32[1088,128]{1,0:T(8,128)S(1)}, u32[]{:S(2)}, u32[]{:S(2)}) collective-permute-start(f32[1088,128]{1,0:T(8,128)} %pad_maximum_fusion.1), channel_id=1, source_target_pairs={{0,252},{4,0},{8,4},{12,8},{16,12},{20,16},{24,20},{28,24},{32,28}... | collective-permute-start | bytes 1671176 | tf_op jit(solution)/shard_map/ppermute | solution.py:125
  23.2 18.6 %copy-start.20 = (f32[3]{0:T(128)}, f32[3]{0:T(128)S(1)}, u32[]{:S(2)}) copy-start(f32[3]{0:T(128)S(1)} %convert_element_type.33.val_ref) | copy-start | bytes 40
  42.6 0.9 copy-start.15
  42.6 11.3 %copy-start.6 = (f32[8,64,128]{2,1,0:T(8,128)}, f32[8,64,128]{2,1,0:T(8,128)S(1)}, u32[]{:S(2)}) copy-start(f32[8,64,128]{2,1,0:T(8,128)S(1)} %add.96.refs_10_) | copy-start | bytes 786436
  43.4 10.5 %collective-permute-start.4 = (f32[384,128]{1,0:T(8,128)}, f32[384,128]{1,0:T(8,128)S(1)}, u32[]{:S(2)}, u32[]{:S(2)}) collective-permute-start(f32[384,128]{1,0:T(8,128)} %bitcast.28), channel_id=1, source_target_pairs={{0,4},{4,8},{8,12},{12,16},{16,20},{20,24},{24,28},{28,32},{32,36}... | collective-permute-start | bytes 589832 | tf_op jit(solution)/shard_map/ppermute | solution.py:125
  43.4 10.5 %collective-permute-start.5 = (f32[384,128]{1,0:T(8,128)S(1)}, f32[384,128]{1,0:T(8,128)S(1)}, u32[]{:S(2)}, u32[]{:S(2)}) collective-permute-start(f32[384,128]{1,0:T(8,128)S(1)} %bitcast.128), channel_id=1, source_target_pairs={{0,252},{4,0},{8,4},{12,8},{16,12},{20,16},{24,20},{28,24},{32,28}... | collective-permute-start | bytes 589832 | tf_op jit(solution)/shard_map/ppermute | solution.py:125
  49.1 0.8 copy-start
  49.1 1.0 copy-start.1
  50.2 11.9 %collective-permute-start.2 = (f32[384,128]{1,0:T(8,128)S(1)}, f32[384,128]{1,0:T(8,128)S(1)}, u32[]{:S(2)}, u32[]{:S(2)}) collective-permute-start(f32[384,128]{1,0:T(8,128)S(1)} %select_maximum_fusion.1), channel_id=1, source_target_pairs={{0,1},{1,2},{2,3},{3,0},{4,5},{5,6},{6,7},{7,4},{8,9},{9,10},{10,1... | collective-permute-start | bytes 589832 | tf_op jit(solution)/shard_map/ppermute | solution.py:125
  53.8 8.4 %collective-permute-start.3 = (f32[384,128]{1,0:T(8,128)S(1)}, f32[384,128]{1,0:T(8,128)S(1)}, u32[]{:S(2)}, u32[]{:S(2)}) collective-permute-start(f32[384,128]{1,0:T(8,128)S(1)} %select_maximum_fusion), channel_id=1, source_target_pairs={{0,3},{1,0},{2,1},{3,2},{4,7},{5,4},{6,5},{7,6},{8,11},{9,8},{10,9... | collective-permute-start | bytes 589832 | tf_op jit(solution)/shard_map/ppermute | solution.py:125
  53.9 8.3 %copy-start.16 = (f32[384,128]{1,0:T(8,128)}, f32[384,128]{1,0:T(8,128)S(1)}, u32[]{:S(2)}) copy-start(f32[384,128]{1,0:T(8,128)S(1)} %collective-permute-done.4) | copy-start | bytes 589828
  53.9 8.3 %copy-start.17 = (f32[384,128]{1,0:T(8,128)}, f32[384,128]{1,0:T(8,128)S(1)}, u32[]{:S(2)}) copy-start(f32[384,128]{1,0:T(8,128)S(1)} %collective-permute-done.5) | copy-start | bytes 589828
  54.0 8.2 %collective-permute-start.7 = (f32[160,128]{1,0:T(8,128)S(1)}, f32[160,128]{1,0:T(8,128)S(1)}, u32[]{:S(2)}, u32[]{:S(2)}) collective-permute-start(f32[160,128]{1,0:T(8,128)S(1)} %get-tuple-element.42), channel_id=1, source_target_pairs={{0,3},{1,0},{2,1},{3,2},{4,7},{5,4},{6,5},{7,6},{8,11},{9,8},{10,9... | collective-permute-start | bytes 245768 | tf_op jit(solution)/shard_map/ppermute | solution.py:125
  55.3 6.9 %collective-permute-start.6 = (f32[160,128]{1,0:T(8,128)S(1)}, f32[160,128]{1,0:T(8,128)S(1)}, u32[]{:S(2)}, u32[]{:S(2)}) collective-permute-start(f32[160,128]{1,0:T(8,128)S(1)} %get-tuple-element.43), channel_id=1, source_target_pairs={{0,1},{1,2},{2,3},{3,0},{4,5},{5,6},{6,7},{7,4},{8,9},{9,10},{10,1... | collective-permute-start | bytes 245768 | tf_op jit(solution)/shard_map/ppermute | solution.py:125
  62.1 0.6 copy-start.18
  62.1 0.7 copy-start.19
  62.1 0.7 copy-start.11
  62.2 0.8 copy-start.12
  75.2 2.1 %copy-start.9 = (f32[8,64,128]{2,1,0:T(8,128)S(1)}, f32[8,64,128]{2,1,0:T(8,128)}, u32[]{:S(2)}) copy-start(f32[8,64,128]{2,1,0:T(8,128)} %get-tuple-element.15.refs_0_) | copy-start | bytes 786436
  77.4 17.1 %copy-start.7 = (f32[3,8,64,128]{3,2,1,0:T(8,128)S(1)}, f32[3,8,64,128]{3,2,1,0:T(8,128)}, u32[]{:S(2)}) copy-start(f32[3,8,64,128]{3,2,1,0:T(8,128)} %get-tuple-element.17.refs_15_) | copy-start | bytes 2359300
  77.4 17.0 %collective-permute-start.8 = (f32[1024,128]{1,0:T(8,128)S(1)}, f32[1024,128]{1,0:T(8,128)S(1)}, u32[]{:S(2)}, u32[]{:S(2)}) collective-permute-start(f32[1024,128]{1,0:T(8,128)S(1)} %pad_maximum_fusion.2), channel_id=1, source_target_pairs={{0,4},{4,8},{8,12},{12,16},{16,20},{20,24},{24,28},{28,32},{32,36}... | collective-permute-start | bytes 1572872 | tf_op jit(solution)/shard_map/ppermute | solution.py:125
  77.5 16.9 %collective-permute-start.9 = (f32[1024,128]{1,0:T(8,128)S(1)}, f32[1024,128]{1,0:T(8,128)S(1)}, u32[]{:S(2)}, u32[]{:S(2)}) collective-permute-start(f32[1024,128]{1,0:T(8,128)S(1)} %pad_maximum_fusion.3), channel_id=1, source_target_pairs={{0,252},{4,0},{8,4},{12,8},{16,12},{20,16},{24,20},{28,24},{32,28}... | collective-permute-start | bytes 1572872 | tf_op jit(solution)/shard_map/ppermute | solution.py:125
  94.4 1.2 %copy-start.2 = (f32[1024,128]{1,0:T(8,128)}, f32[1024,128]{1,0:T(8,128)S(1)}, u32[]{:S(2)}) copy-start(f32[1024,128]{1,0:T(8,128)S(1)} %collective-permute-done.8) | copy-start | bytes 1572868
  94.4 1.2 %copy-start.3 = (f32[1024,128]{1,0:T(8,128)}, f32[1024,128]{1,0:T(8,128)S(1)}, u32[]{:S(2)}) copy-start(f32[1024,128]{1,0:T(8,128)S(1)} %collective-permute-done.9) | copy-start | bytes 1572868
  94.4 1.1 copy-start.10
  95.7 5.9 %collective-permute-start.10 = (f32[368,128]{1,0:T(8,128)S(1)}, f32[368,128]{1,0:T(8,128)S(1)}, u32[]{:S(2)}, u32[]{:S(2)}) collective-permute-start(f32[368,128]{1,0:T(8,128)S(1)} %select_maximum_fusion.3), channel_id=1, source_target_pairs={{0,1},{1,2},{2,3},{3,0},{4,5},{5,6},{6,7},{7,4},{8,9},{9,10},{10,1... | collective-permute-start | bytes 565256 | tf_op jit(solution)/shard_map/ppermute | solution.py:125
  99.1 6.6 %collective-permute-start.11 = (f32[368,128]{1,0:T(8,128)S(1)}, f32[368,128]{1,0:T(8,128)S(1)}, u32[]{:S(2)}, u32[]{:S(2)}) collective-permute-start(f32[368,128]{1,0:T(8,128)S(1)} %select_maximum_fusion.2), channel_id=1, source_target_pairs={{0,3},{1,0},{2,1},{3,2},{4,7},{5,4},{6,5},{7,6},{8,11},{9,8},{10,9... | collective-permute-start | bytes 565256 | tf_op jit(solution)/shard_map/ppermute | solution.py:125
  101.6 4.1 %copy-start.13 = (f32[368,128]{1,0:T(8,128)}, f32[368,128]{1,0:T(8,128)S(1)}, u32[]{:S(2)}) copy-start(f32[368,128]{1,0:T(8,128)S(1)} %collective-permute-done.10) | copy-start | bytes 565252
  105.7 0.7 copy-start.14

commit v15 on v14

--- a/solution.py
+++ b/solution.py
@@ -248,7 +248,7 @@
 
     wait(1)
     wait(2)
-    lax.fori_loop(1, planes - 1, weights, 0, unroll=2)
+    lax.fori_loop(1, planes - 1, weights, 0, unroll=4)
     wait(0)
     pad = jnp.zeros((planes, 8, lanes), jnp.float32)
     for buf in (f_ref, fa, fb):
@@ -299,7 +299,7 @@
             so_ref[z] = mix + e_ref[z]
         return carry
 
-    lax.fori_loop(0, inner, move, 0, unroll=2)
+    lax.fori_loop(0, inner, move, 0, unroll=4)
 
 
 def time_step(diffusivity, charge_num, field_p, perm_p, source_p, species_p, electrode=None):

time: 119 us -> 119 us (level)
  no operation moved by 1% of the time
where the time goes in v15:
time: 119 us; the launch traced here: 118 us
  starting transfers between devices  29.7 us (25%)
  Pallas kernels  23.9 us (20%)
  other arithmetic  22.1 us (19%)
  waiting for transfers between devices  21.8 us (18%)
  blocking collectives  10.5 us (9%)
  local copies, waits for them, and re-layouts  7.38 us (6%)
  between operations  2.02 us (2%)
    ppermute x12, starting transfers between devices, ring(): lax.ppermute(x, axis, [(i, (i + shift) % count) for i in range(count)])  29.7 us
    pallas_call x2, Pallas kernels, time_step(): pl.pallas_call(functools.partial(step_kernel, tuple(plan), with_source),...  23.9 us
    ppermute x12, waiting for transfers between devices, ring(): lax.ppermute(x, axis, [(i, (i + shift) % count) for i in range(count)])  21.8 us
    reduce_sum x1, other arithmetic, one_block(): return jnp.sum(jnp.where(adjacent, term, 0.0), axis=1)  18.2 us
    all_gather x1, blocking collectives, per_device(): gathered = lax.all_gather(charges, 'narrow', axis=1, tiled=True)  10.5 us
    slice x7, local copies, waits for them, and re-layouts, deep_halo(): bots.append(lax.slice_in_dim(a, 0, wz, axis=dim))  3.9 us
    unnamed x46, local copies, waits for them, and re-layouts  3.3 us
  transfers between devices with their start and end apart: 12, of which 4 were waited for; matrix products, arithmetic and copies ran while one was open for 18% of the time, Pallas kernels for 0%

profile of v15, /device:TPU:1, one launch (start us, length us, event | category | flops | bytes accessed | tf_op | source)
XLA Modules:
  0.0 118.3 jit_solution(2381324542313668221)
XLA Ops:
  0.6 0.0 copy-start.8
  0.6 0.7 convert_element_type.34
  1.4 0.8 pad_maximum_fusion.14
  2.2 0.0 copy-start.5
  2.2 10.5 %all_gather.3 = f32[5,8192]{1,0:T(8,128)S(1)} all-gather(f32[5,2048]{1,0:T(8,128)S(1)} %pad_maximum_fusion.14), channel_id=1, replica_groups=mesh['wide'=64,'narrow'=4] {'narrow'}, dimensions={1}, use_global_device_ids=true | all-gather | bytes 204800 | tf_op jit(solution)/shard_map/all_gather | solution.py:391
  12.7 1.0 fusion.43
  13.7 0.0 copy-done.8
  13.7 0.0 copy-done.5
  13.8 0.8 pad_maximum_fusion
  14.6 0.0 collective-permute-start
  14.6 0.8 pad_maximum_fusion.1
  15.5 7.0 %collective-permute-start.1 = (f32[1088,128]{1,0:T(8,128)}, f32[1088,128]{1,0:T(8,128)S(1)}, u32[]{:S(2)}, u32[]{:S(2)}) collective-permute-start(f32[1088,128]{1,0:T(8,128)} %pad_maximum_fusion.1), channel_id=1, source_target_pairs={{0,252},{4,0},{8,4},{12,8},{16,12},{20,16},{24,20},{28,24},{32,28}... | collective-permute-start | bytes 1671176 | tf_op jit(solution)/shard_map/ppermute | solution.py:125
  23.2 0.0 copy-done.22
  23.2 0.0 copy-start.20
  23.2 0.0 copy-done.21
  23.3 0.0 copy-done.4
  23.3 0.1 multiply_reduce_fusion
  23.4 0.1 fusion.49
  23.6 18.2 %select_reduce_fusion.1 = (f32[256]{0:T(256)S(1)}, f32[256]{0:T(256)S(1)}) fusion(f32[8192]{0:T(1024)S(1)} %bitcast.132, f32[256]{0:T(256)S(1)} %get-tuple-element.79, f32[8192]{0:T(1024)S(1)} %bitcast.133, f32[256]{0:T(256)S(1)} %get-tuple-element.68, f32[8192]{0:T(1024)S(1)} %bitcast.134, f32[256]{0:T(256)S(1)} %get-tuple-element.77, ...), kind=kLoop, calls=%fused_computation.20 | loop fusion | flops 104857088 | bytes 174080 | tf_op jit(solution)/shard_map/reduce_sum | solution.py:116
  41.8 0.0 copy-done.20
  41.8 0.8 fusion.18
  42.6 0.0 copy-start.15
  42.6 0.0 copy-start.6
  42.6 0.8 fusion.48
  43.4 0.0 copy-done.15
  43.4 0.0 collective-permute-start.4
  43.4 5.7 %collective-permute-start.5 = (f32[384,128]{1,0:T(8,128)S(1)}, f32[384,128]{1,0:T(8,128)S(1)}, u32[]{:S(2)}, u32[]{:S(2)}) collective-permute-start(f32[384,128]{1,0:T(8,128)S(1)} %bitcast.128), channel_id=1, source_target_pairs={{0,252},{4,0},{8,4},{12,8},{16,12},{20,16},{24,20},{28,24},{32,28}... | collective-permute-start | bytes 589832 | tf_op jit(solution)/shard_map/ppermute | solution.py:125
  49.1 0.0 collective-permute-done
  49.1 0.0 collective-permute-done.1
  49.1 0.0 copy-start.1
  49.2 0.1 fusion.30
  49.3 0.6 copy-done
  49.9 0.2 copy-done.1
  50.2 3.6 %collective-permute-start.2 = (f32[384,128]{1,0:T(8,128)S(1)}, f32[384,128]{1,0:T(8,128)S(1)}, u32[]{:S(2)}, u32[]{:S(2)}) collective-permute-start(f32[384,128]{1,0:T(8,128)S(1)} %select_maximum_fusion.1), channel_id=1, source_target_pairs={{0,1},{1,2},{2,3},{3,0},{4,5},{5,6},{6,7},{7,4},{8,9},{9,10},{10,1... | collective-permute-start | bytes 589832 | tf_op jit(solution)/shard_map/ppermute | solution.py:125
  53.8 0.1 collective-permute-start.3
  53.9 0.0 collective-permute-done.4
  53.9 0.0 copy-start.16
  53.9 0.0 collective-permute-done.5
  54.0 1.3 %collective-permute-start.7 = (f32[160,128]{1,0:T(8,128)S(1)}, f32[160,128]{1,0:T(8,128)S(1)}, u32[]{:S(2)}, u32[]{:S(2)}) collective-permute-start(f32[160,128]{1,0:T(8,128)S(1)} %get-tuple-element.42), channel_id=1, source_target_pairs={{0,3},{1,0},{2,1},{3,2},{4,7},{5,4},{6,5},{7,6},{8,11},{9,8},{10,9... | collective-permute-start | bytes 245768 | tf_op jit(solution)/shard_map/ppermute | solution.py:125
  55.3 2.7 %collective-permute-start.6 = (f32[160,128]{1,0:T(8,128)S(1)}, f32[160,128]{1,0:T(8,128)S(1)}, u32[]{:S(2)}, u32[]{:S(2)}) collective-permute-start(f32[160,128]{1,0:T(8,128)S(1)} %get-tuple-element.43), channel_id=1, source_target_pairs={{0,1},{1,2},{2,3},{3,0},{4,5},{5,6},{6,7},{7,4},{8,9},{9,10},{10,1... | collective-permute-start | bytes 245768 | tf_op jit(solution)/shard_map/ppermute | solution.py:125
  58.0 4.2 %collective-permute-done.7 = f32[160,128]{1,0:T(8,128)S(1)} collective-permute-done((f32[160,128]{1,0:T(8,128)S(1)}, f32[160,128]{1,0:T(8,128)S(1)}, u32[]{:S(2)}, u32[]{:S(2)}) %collective-permute-start.7) | collective-permute-done | bytes 81952 | tf_op jit(solution)/shard_map/ppermute | solution.py:125
  62.1 0.0 collective-permute-done.6
  62.1 0.0 collective-permute-done.2
  62.2 0.0 collective-permute-done.3
  62.2 0.6 copy-done.18
  62.8 0.0 copy-done.19
  62.8 0.1 copy-done.11
  62.9 0.1 copy-done.12
  62.9 12.1 %shard_map.113 = (f32[8,64,128]{2,1,0:T(8,128)}, f32[3,8,64,128]{3,2,1,0:T(8,128)}, f32[8,64,128]{2,1,0:T(8,128)}) custom-call(f32[3]{0:T(128)} %dif_ref.3, f32[3]{0:T(128)} %copy-done.20, f32[8,64,128]{2,1,0:T(8,128)} %refs_0_, f32[17,64,128]{2,1,0:T(8,128)} %bitcast.70, f32[17,64,128]{2,1,0:T(8,128)} %bitcast.74, f32[48,8,128]{2,1,0:T(8,128)} %bitcast.84, ...), custom_call_target="tpu_custom_call" | custom-call | flops 40755200 | bytes 4538368 | tf_op jit(solution)/shard_map/pallas_call | solution.py:331
  75.1 1.0 fusion.42
  76.1 1.0 fusion.47
  77.3 0.1 collective-permute-start.8
  77.4 5.7 %collective-permute-start.9 = (f32[1024,128]{1,0:T(8,128)S(1)}, f32[1024,128]{1,0:T(8,128)S(1)}, u32[]{:S(2)}, u32[]{:S(2)}) collective-permute-start(f32[1024,128]{1,0:T(8,128)S(1)} %pad_maximum_fusion.3), channel_id=1, source_target_pairs={{0,252},{4,0},{8,4},{12,8},{16,12},{20,16},{24,20},{28,24},{32,28}... | collective-permute-start | bytes 1572872 | tf_op jit(solution)/shard_map/ppermute | solution.py:125
  83.1 11.1 %collective-permute-done.8 = f32[1024,128]{1,0:T(8,128)S(1)} collective-permute-done((f32[1024,128]{1,0:T(8,128)S(1)}, f32[1024,128]{1,0:T(8,128)S(1)}, u32[]{:S(2)}, u32[]{:S(2)}) %collective-permute-start.8) | collective-permute-done | bytes 524320 | tf_op jit(solution)/shard_map/ppermute | solution.py:125
  94.3 0.0 collective-permute-done.9
  94.3 0.0 copy-start.3
  94.3 0.1 fusion.29
  94.5 1.0 copy-done.10
  95.6 3.4 %collective-permute-start.10 = (f32[368,128]{1,0:T(8,128)S(1)}, f32[368,128]{1,0:T(8,128)S(1)}, u32[]{:S(2)}, u32[]{:S(2)}) collective-permute-start(f32[368,128]{1,0:T(8,128)S(1)} %select_maximum_fusion.3), channel_id=1, source_target_pairs={{0,1},{1,2},{2,3},{3,0},{4,5},{5,6},{6,7},{7,4},{8,9},{9,10},{10,1... | collective-permute-start | bytes 565256 | tf_op jit(solution)/shard_map/ppermute | solution.py:125
  99.0 0.1 collective-permute-start.11
  99.1 2.4 %collective-permute-done.10 = f32[368,128]{1,0:T(8,128)S(1)} collective-permute-done((f32[368,128]{1,0:T(8,128)S(1)}, f32[368,128]{1,0:T(8,128)S(1)}, u32[]{:S(2)}, u32[]{:S(2)}) %collective-permute-start.10) | collective-permute-done | bytes 188448 | tf_op jit(solution)/shard_map/ppermute | solution.py:125
  101.5 4.1 %collective-permute-done.11 = f32[368,128]{1,0:T(8,128)S(1)} collective-permute-done((f32[368,128]{1,0:T(8,128)S(1)}, f32[368,128]{1,0:T(8,128)S(1)}, u32[]{:S(2)}, u32[]{:S(2)}) %collective-permute-start.11) | collective-permute-done | bytes 188448 | tf_op jit(solution)/shard_map/ppermute | solution.py:125
  105.6 0.7 copy-done.14
  106.3 11.8 %shard_map.114 = (f32[8,64,128]{2,1,0:T(8,128)}, f32[3,8,64,128]{3,2,1,0:T(8,128)}) custom-call(f32[3]{0:T(128)} %dif_ref.3, f32[3]{0:T(128)} %copy-done.20, f32[8,64,128]{2,1,0:T(8,128)} %get-tuple-element.15.refs_0_, f32[16,64,128]{2,1,0:T(8,128)} %bitcast.78, f32[16,64,128]{2,1,0:T(8,128)} %bitcast.81, f32[46,8,128]{2,1,0:T(8,128)} %bitcast.92, ...), custom_call_target="tpu_custom_call" | custom-call | flops 40755200 | bytes 4538368 | tf_op jit(solution)/shard_map/pallas_call | solution.py:331
  (57 shorter events, 0.6 us)
Async XLA Ops:
  0.6 13.0 %copy-start.8 = (f32[8,64,128]{2,1,0:T(8,128)S(1)}, f32[8,64,128]{2,1,0:T(8,128)}, u32[]{:S(2)}) copy-start(f32[8,64,128]{2,1,0:T(8,128)} %refs_0_) | copy-start | bytes 786436
  2.2 11.5 %copy-start.5 = (f32[8,64,128]{2,1,0:T(8,128)S(1)}, f32[8,64,128]{2,1,0:T(8,128)}, u32[]{:S(2)}) copy-start(f32[8,64,128]{2,1,0:T(8,128)} %refs_5_.1) | copy-start | bytes 786436
  14.6 8.6 %copy-start.22 = (s32[3]{0:T(128)S(1)}, s32[3]{0:T(128)}, u32[]{:S(2)}) copy-start(s32[3]{0:T(128)} %param.14) | copy-start | bytes 40
  14.6 8.6 %copy-start.21 = (s32[1,1,512]{2,1,0:T(1,128)S(1)}, s32[1,1,512]{2,1,0:T(1,128)}, u32[]{:S(2)}) copy-start(s32[1,1,512]{2,1,0:T(1,128)} %param.18) | copy-start | bytes 6148
  14.6 8.6 %copy-start.4 = (f32[3,8,64,128]{3,2,1,0:T(8,128)S(1)}, f32[3,8,64,128]{3,2,1,0:T(8,128)}, u32[]{:S(2)}) copy-start(f32[3,8,64,128]{3,2,1,0:T(8,128)} %refs_15_) | copy-start | bytes 2359300
  14.6 34.5 %collective-permute-start = (f32[1088,128]{1,0:T(8,128)}, f32[1088,128]{1,0:T(8,128)S(1)}, u32[]{:S(2)}, u32[]{:S(2)}) collective-permute-start(f32[1088,128]{1,0:T(8,128)} %pad_maximum_fusion), channel_id=1, source_target_pairs={{0,4},{4,8},{8,12},{12,16},{16,20},{20,24},{24,28},{28,32},{32,36}... | collective-permute-start | bytes 1671176 | tf_op jit(solution)/shard_map/ppermute | solution.py:125
  15.5 33.6 %collective-permute-start.1 = (f32[1088,128]{1,0:T(8,128)}, f32[1088,128]{1,0:T(8,128)S(1)}, u32[]{:S(2)}, u32[]{:S(2)}) collective-permute-start(f32[1088,128]{1,0:T(8,128)} %pad_maximum_fusion.1), channel_id=1, source_target_pairs={{0,252},{4,0},{8,4},{12,8},{16,12},{20,16},{24,20},{28,24},{32,28}... | collective-permute-start | bytes 1671176 | tf_op jit(solution)/shard_map/ppermute | solution.py:125
  23.2 18.6 %copy-start.20 = (f32[3]{0:T(128)}, f32[3]{0:T(128)S(1)}, u32[]{:S(2)}) copy-start(f32[3]{0:T(128)S(1)} %convert_element_type.33.val_ref) | copy-start | bytes 40
  42.6 0.9 copy-start.15
  42.6 11.3 %copy-start.6 = (f32[8,64,128]{2,1,0:T(8,128)}, f32[8,64,128]{2,1,0:T(8,128)S(1)}, u32[]{:S(2)}) copy-start(f32[8,64,128]{2,1,0:T(8,128)S(1)} %add.96.refs_10_) | copy-start | bytes 786436
  43.4 10.5 %collective-permute-start.4 = (f32[384,128]{1,0:T(8,128)}, f32[384,128]{1,0:T(8,128)S(1)}, u32[]{:S(2)}, u32[]{:S(2)}) collective-permute-start(f32[384,128]{1,0:T(8,128)} %bitcast.28), channel_id=1, source_target_pairs={{0,4},{4,8},{8,12},{12,16},{16,20},{20,24},{24,28},{28,32},{32,36}... | collective-permute-start | bytes 589832 | tf_op jit(solution)/shard_map/ppermute | solution.py:125
  43.4 10.5 %collective-permute-start.5 = (f32[384,128]{1,0:T(8,128)S(1)}, f32[384,128]{1,0:T(8,128)S(1)}, u32[]{:S(2)}, u32[]{:S(2)}) collective-permute-start(f32[384,128]{1,0:T(8,128)S(1)} %bitcast.128), channel_id=1, source_target_pairs={{0,252},{4,0},{8,4},{12,8},{16,12},{20,16},{24,20},{28,24},{32,28}... | collective-permute-start | bytes 589832 | tf_op jit(solution)/shard_map/ppermute | solution.py:125
  49.1 0.8 copy-start
  49.1 1.0 copy-start.1
  50.2 11.9 %collective-permute-start.2 = (f32[384,128]{1,0:T(8,128)S(1)}, f32[384,128]{1,0:T(8,128)S(1)}, u32[]{:S(2)}, u32[]{:S(2)}) collective-permute-start(f32[384,128]{1,0:T(8,128)S(1)} %select_maximum_fusion.1), channel_id=1, source_target_pairs={{0,1},{1,2},{2,3},{3,0},{4,5},{5,6},{6,7},{7,4},{8,9},{9,10},{10,1... | collective-permute-start | bytes 589832 | tf_op jit(solution)/shard_map/ppermute | solution.py:125
  53.8 8.4 %collective-permute-start.3 = (f32[384,128]{1,0:T(8,128)S(1)}, f32[384,128]{1,0:T(8,128)S(1)}, u32[]{:S(2)}, u32[]{:S(2)}) collective-permute-start(f32[384,128]{1,0:T(8,128)S(1)} %select_maximum_fusion), channel_id=1, source_target_pairs={{0,3},{1,0},{2,1},{3,2},{4,7},{5,4},{6,5},{7,6},{8,11},{9,8},{10,9... | collective-permute-start | bytes 589832 | tf_op jit(solution)/shard_map/ppermute | solution.py:125
  53.9 8.3 %copy-start.16 = (f32[384,128]{1,0:T(8,128)}, f32[384,128]{1,0:T(8,128)S(1)}, u32[]{:S(2)}) copy-start(f32[384,128]{1,0:T(8,128)S(1)} %collective-permute-done.4) | copy-start | bytes 589828
  53.9 8.3 %copy-start.17 = (f32[384,128]{1,0:T(8,128)}, f32[384,128]{1,0:T(8,128)S(1)}, u32[]{:S(2)}) copy-start(f32[384,128]{1,0:T(8,128)S(1)} %collective-permute-done.5) | copy-start | bytes 589828
  54.0 8.2 %collective-permute-start.7 = (f32[160,128]{1,0:T(8,128)S(1)}, f32[160,128]{1,0:T(8,128)S(1)}, u32[]{:S(2)}, u32[]{:S(2)}) collective-permute-start(f32[160,128]{1,0:T(8,128)S(1)} %get-tuple-element.42), channel_id=1, source_target_pairs={{0,3},{1,0},{2,1},{3,2},{4,7},{5,4},{6,5},{7,6},{8,11},{9,8},{10,9... | collective-permute-start | bytes 245768 | tf_op jit(solution)/shard_map/ppermute | solution.py:125
  55.3 6.9 %collective-permute-start.6 = (f32[160,128]{1,0:T(8,128)S(1)}, f32[160,128]{1,0:T(8,128)S(1)}, u32[]{:S(2)}, u32[]{:S(2)}) collective-permute-start(f32[160,128]{1,0:T(8,128)S(1)} %get-tuple-element.43), channel_id=1, source_target_pairs={{0,1},{1,2},{2,3},{3,0},{4,5},{5,6},{6,7},{7,4},{8,9},{9,10},{10,1... | collective-permute-start | bytes 245768 | tf_op jit(solution)/shard_map/ppermute | solution.py:125
  62.1 0.6 copy-start.18
  62.1 0.7 copy-start.19
  62.1 0.7 copy-start.11
  62.2 0.8 copy-start.12
  75.1 2.1 %copy-start.9 = (f32[8,64,128]{2,1,0:T(8,128)S(1)}, f32[8,64,128]{2,1,0:T(8,128)}, u32[]{:S(2)}) copy-start(f32[8,64,128]{2,1,0:T(8,128)} %get-tuple-element.15.refs_0_) | copy-start | bytes 786436
  77.2 17.1 %copy-start.7 = (f32[3,8,64,128]{3,2,1,0:T(8,128)S(1)}, f32[3,8,64,128]{3,2,1,0:T(8,128)}, u32[]{:S(2)}) copy-start(f32[3,8,64,128]{3,2,1,0:T(8,128)} %get-tuple-element.17.refs_15_) | copy-start | bytes 2359300
  77.3 17.0 %collective-permute-start.8 = (f32[1024,128]{1,0:T(8,128)S(1)}, f32[1024,128]{1,0:T(8,128)S(1)}, u32[]{:S(2)}, u32[]{:S(2)}) collective-permute-start(f32[1024,128]{1,0:T(8,128)S(1)} %pad_maximum_fusion.2), channel_id=1, source_target_pairs={{0,4},{4,8},{8,12},{12,16},{16,20},{20,24},{24,28},{28,32},{32,36}... | collective-permute-start | bytes 1572872 | tf_op jit(solution)/shard_map/ppermute | solution.py:125
  77.4 16.9 %collective-permute-start.9 = (f32[1024,128]{1,0:T(8,128)S(1)}, f32[1024,128]{1,0:T(8,128)S(1)}, u32[]{:S(2)}, u32[]{:S(2)}) collective-permute-start(f32[1024,128]{1,0:T(8,128)S(1)} %pad_maximum_fusion.3), channel_id=1, source_target_pairs={{0,252},{4,0},{8,4},{12,8},{16,12},{20,16},{24,20},{28,24},{32,28}... | collective-permute-start | bytes 1572872 | tf_op jit(solution)/shard_map/ppermute | solution.py:125
  94.3 1.2 %copy-start.2 = (f32[1024,128]{1,0:T(8,128)}, f32[1024,128]{1,0:T(8,128)S(1)}, u32[]{:S(2)}) copy-start(f32[1024,128]{1,0:T(8,128)S(1)} %collective-permute-done.8) | copy-start | bytes 1572868
  94.3 1.2 %copy-start.3 = (f32[1024,128]{1,0:T(8,128)}, f32[1024,128]{1,0:T(8,128)S(1)}, u32[]{:S(2)}) copy-start(f32[1024,128]{1,0:T(8,128)S(1)} %collective-permute-done.9) | copy-start | bytes 1572868
  94.3 1.1 copy-start.10
  95.6 5.9 %collective-permute-start.10 = (f32[368,128]{1,0:T(8,128)S(1)}, f32[368,128]{1,0:T(8,128)S(1)}, u32[]{:S(2)}, u32[]{:S(2)}) collective-permute-start(f32[368,128]{1,0:T(8,128)S(1)} %select_maximum_fusion.3), channel_id=1, source_target_pairs={{0,1},{1,2},{2,3},{3,0},{4,5},{5,6},{6,7},{7,4},{8,9},{9,10},{10,1... | collective-permute-start | bytes 565256 | tf_op jit(solution)/shard_map/ppermute | solution.py:125
  99.0 6.6 %collective-permute-start.11 = (f32[368,128]{1,0:T(8,128)S(1)}, f32[368,128]{1,0:T(8,128)S(1)}, u32[]{:S(2)}, u32[]{:S(2)}) collective-permute-start(f32[368,128]{1,0:T(8,128)S(1)} %select_maximum_fusion.2), channel_id=1, source_target_pairs={{0,3},{1,0},{2,1},{3,2},{4,7},{5,4},{6,5},{7,6},{8,11},{9,8},{10,9... | collective-permute-start | bytes 565256 | tf_op jit(solution)/shard_map/ppermute | solution.py:125
  101.5 4.1 %copy-start.13 = (f32[368,128]{1,0:T(8,128)}, f32[368,128]{1,0:T(8,128)S(1)}, u32[]{:S(2)}) copy-start(f32[368,128]{1,0:T(8,128)S(1)} %collective-permute-done.10) | copy-start | bytes 565252
  105.6 0.7 copy-start.14
